TPU v7x, 32 devices: a whole 2x2x4 slice. The times are simulated.
32 devices in a mesh: gx: 8 (over z, core), gy: 4 (over y, x).
Axes of the slice: x: 2, y: 2, z: 4, core: 2. Of those that a mesh axis runs over, the one named last changes fastest.
Arguments:
- tokens_in: bfloat16 [2048, 8192], P('gy', 'gx'), may hold values from -230 to 230, as said below
- norm_gain: bfloat16 [8192], replicated, may hold values from 0.099609375 to 1.8984375
- query_weight: bfloat16 [8192, 2048], P('gy', 'gx'), may hold values from -0.044194174 to 0.044194174
- key_weight: bfloat16 [8192, 256], P('gy', 'gx'), may hold values from -1.08275726 to 1.08275726
- value_weight: bfloat16 [8192, 256], P('gy', 'gx'), may hold values from -0.0625 to 0.0625
- segment_ids: int32 [2048], P('gy'), may hold values from -1 to 389, as said below
- positions: int32 [2048], P('gy'), may hold values from 0 to 511, as said below
- page_owner: int32 [128, 1], P('gy'), may hold values from 0 to 3; in each aligned block of 32 rows (0 to 31, 32 to 63, ...) at most 16 rows name the same one
Outputs:
- context: bfloat16 [2048, 2048], P('gy', 'gx')
- key_cache: bfloat16 [256, 16, 256], P('gy', None, 'gx')
- value_cache: bfloat16 [256, 16, 256], P('gy', None, 'gx')
Inputs may be any that keep to these rules, and one draw needn't show every extreme that they name: `tokens_in`: activations with row and column scales. `segment_ids`: two requests are prompts of exactly 512 tokens, one starting in the first half of the stream and one in the second; every other request has 16 to 64 consecutive tokens; padding tokens have -1. The tokens of a request are consecutive. Inside a request, positions rise by one from token to token; padding has 0. `page_owner`: among the 32 pages of one index of gy, at most 16 have the same owner.
All inputs are finite; a program needn't handle non-finite values.
Results may differ from a plain program's by a relative error of at most 0.006.
The roundings to bfloat16 on the way count: a program that leaves them out, or rounds other values in their place, can miss the bound.
Values may be sent and summed in bfloat16 or wider, within the bound.
No kernel may reach another device: no remote copies, remote signals or barrier semaphores. Data moves between devices by JAX's collectives and lax.ppermute only.
A program may use at most 64 MiB of HBM per device.

v0:
```python
import jax
import jax.numpy as jnp
from jax import lax
from jax.sharding import PartitionSpec as P

D = 8192
HD = 128
PAGE = 16


EPSILON = 1e-05
THETA = 500000.0
MASKED = -1e30


def swapped(block, axis, bit):
    count = lax.axis_size(axis)
    route = []
    for low in range(count):
        high = low | 1 << bit
        if high != low and high < count:
            route += [(low, high), (high, low)]
    return lax.ppermute(block, axis, route)


def shifted(value, axis, by):
    count = lax.axis_size(axis)
    pairs = [(i, i + by) for i in range(count) if 0 <= i + by < count]
    return lax.ppermute(value, axis, pairs)


def rotate(matrix, places, group_width):
    row_count = matrix.shape[0]
    pair_count = group_width // 2
    shaped = matrix.reshape(row_count, -1, pair_count, 2)
    pair_index = jnp.arange(pair_count, dtype=jnp.int32)
    frequency = jnp.power(THETA, -(2.0 * pair_index.astype(jnp.float32)) / HD)
    angles = places.astype(jnp.float32)[:, None] * frequency[None, :]
    cosine = jnp.cos(angles)[:, None, :]
    sine_of = jnp.sin(angles)[:, None, :]
    even_part = shaped[..., 0]
    odd_part = shaped[..., 1]
    turned = jnp.stack(
        [even_part * cosine - odd_part * sine_of, even_part * sine_of + odd_part * cosine], axis=-1
    )
    return turned.reshape(row_count, -1)


def shards(
    tokens_in, norm_gain, query_weight, key_weight, value_weight, segment_ids, positions, page_owner
):
    token_count = tokens_in.shape[0]
    quarter = key_weight.shape[1]
    head_local = query_weight.shape[1] // HD
    quarters = HD // quarter
    bit_count = quarters.bit_length() - 1
    spot = lax.axis_index("gx") % quarters
    stacked_weights = jnp.stack([key_weight, value_weight])
    for bit_index in range(bit_count):
        other_side = swapped(stacked_weights, "gx", bit_index)
        upper_half = spot // (1 << bit_index) % 2 == 1
        stacked_weights = jnp.where(
            upper_half,
            jnp.concatenate([other_side, stacked_weights], axis=2),
            jnp.concatenate([stacked_weights, other_side], axis=2),
        )
    key_cols = HD
    local_weights = jnp.concatenate([query_weight, stacked_weights[0], stacked_weights[1]], axis=1)
    all_rows = lax.all_gather(local_weights, "gy", axis=0, tiled=True)
    gain_part = norm_gain.astype(jnp.float32)
    piece_float = lax.all_gather(tokens_in, "gx", axis=1, tiled=True).astype(jnp.float32)
    normed = (piece_float * gain_part[None, :]).astype(jnp.bfloat16)
    products = jnp.dot(normed, all_rows, preferred_element_type=jnp.float32)
    squares = jnp.sum(piece_float * piece_float, axis=1)
    products, squares = (products, squares)
    scaling = 1.0 / jnp.sqrt(squares / D + EPSILON)
    projected = products * scaling[:, None]
    query_cols = head_local * HD
    queries = rotate(projected[:, :query_cols], positions, HD).astype(jnp.bfloat16)
    key_proj = projected[:, query_cols : query_cols + key_cols]
    value_proj = projected[:, query_cols + key_cols :]
    full_keys = rotate(key_proj, positions, HD).astype(jnp.bfloat16)
    full_values = value_proj.astype(jnp.bfloat16)
    key_piece = lax.dynamic_slice_in_dim(full_keys, spot * quarter, quarter, 1)
    value_piece = lax.dynamic_slice_in_dim(full_values, spot * quarter, quarter, 1)
    span_count = lax.axis_size("gy") // 4
    marks = segment_ids + 1
    key_list = [full_keys]
    value_list = [full_values]
    mark_list = [marks]
    for shift_by in range(1, span_count + 1):
        moved_keys, moved_values, moved_marks = shifted(
            (full_keys, full_values, marks), "gy", shift_by
        )
        key_list.insert(0, moved_keys)
        value_list.insert(0, moved_values)
        mark_list.insert(0, moved_marks)
    window_keys = jnp.concatenate(key_list, axis=0)
    window_values = jnp.concatenate(value_list, axis=0)
    window_marks = jnp.concatenate(mark_list, axis=0)
    reach_rows = span_count * token_count
    query_rows = (
        queries.reshape(token_count, head_local, HD)
        .transpose(1, 0, 2)
        .reshape(head_local * token_count, HD)
    )
    scores = lax.dot_general(
        query_rows, window_keys, (((1,), (1,)), ((), ())), preferred_element_type=jnp.float32
    ) * HD ** (-0.5)
    query_marks = jnp.tile(segment_ids, head_local)
    query_place = jnp.tile(jnp.arange(token_count, dtype=jnp.int32), head_local)
    key_place = jnp.arange(window_keys.shape[0], dtype=jnp.int32)
    allowed = (window_marks[None, :] == query_marks[:, None] + 1) & (window_marks[None, :] > 0)
    allowed = allowed & (key_place[None, :] <= query_place[:, None] + reach_rows)
    masked = jnp.where(allowed, scores, MASKED)
    highest = jnp.max(masked, axis=1, keepdims=True)
    exponent = jnp.exp(masked - highest)
    totals = jnp.sum(exponent, axis=1)
    weights = exponent.astype(jnp.bfloat16)
    summed = jnp.dot(weights, window_values, preferred_element_type=jnp.float32)
    result = summed / totals[:, None]
    result = jnp.where((query_marks >= 0)[:, None], result, 0.0)
    context = (
        result.reshape(head_local, token_count, HD)
        .transpose(1, 0, 2)
        .reshape(token_count, head_local * HD)
        .astype(jnp.bfloat16)
    )
    owner_count = lax.axis_size("gy")
    page_rows = token_count // PAGE
    capacity = max(2, 2 * page_rows // owner_count)
    owner_of = page_owner[:, 0]
    one_hot = (owner_of[:, None] == jnp.arange(owner_count, dtype=jnp.int32)[None, :]).astype(
        jnp.int32
    )
    earlier = jnp.cumsum(one_hot, axis=0) - one_hot
    rank_in = jnp.sum(earlier * one_hot, axis=1)
    slot_of = owner_of * capacity + rank_in
    key_pages = key_piece.reshape(page_rows, PAGE * quarter)
    value_pages = value_piece.reshape(page_rows, PAGE * quarter)
    send_keys = (
        jnp.zeros((owner_count * capacity, PAGE * quarter), jnp.bfloat16).at[slot_of].set(key_pages)
    )
    send_values = (
        jnp.zeros((owner_count * capacity, PAGE * quarter), jnp.bfloat16)
        .at[slot_of]
        .set(value_pages)
    )
    send_keys = send_keys.reshape(owner_count, capacity, PAGE * quarter)
    send_values = send_values.reshape(owner_count, capacity, PAGE * quarter)
    got_keys, got_values = (
        lax.all_to_all(send_keys, "gy", split_axis=0, concat_axis=0, tiled=True),
        lax.all_to_all(send_values, "gy", split_axis=0, concat_axis=0, tiled=True),
    )
    key_cache = got_keys.reshape(owner_count * capacity, PAGE, quarter)
    value_cache = got_values.reshape(owner_count * capacity, PAGE, quarter)
    return (context, key_cache, value_cache)


def solution(mesh):
    placed = (
        P("gy", "gx"),
        P(),
        P("gy", "gx"),
        P("gy", "gx"),
        P("gy", "gx"),
        P("gy"),
        P("gy"),
        P("gy", None),
    )
    return jax.shard_map(
        shards,
        mesh=mesh,
        in_specs=placed,
        out_specs=(P("gy", "gx"), P("gy", None, "gx"), P("gy", None, "gx")),
        check_vma=False,
    )
```

profile of v0, /device:TPU:0, one launch (start us, length us, event | category | flops | bytes accessed | tf_op | source)
XLA Modules:
  0.0 235.4 jit_solution(4119033207739403095)
XLA Ops:
  7.2 0.7 all-gather.3.cloned.1.call-update
  8.0 1.1 pad_maximum_fusion.1
  9.0 0.5 collective-permute-start.1
  9.5 1.2 collective-permute-done.1
  10.7 1.2 maximum_select_fusion.1
  11.9 3.0 %collective-permute-start.2 = (bf16[2,2048,64]{1,2,0:T(8,128)(2,1)S(1)}, bf16[2,2048,64]{1,2,0:T(8,128)(2,1)S(1)}, u32[]{:S(2)}, u32[]{:S(2)}) collective-permute-start(bf16[2,2048,64]{1,2,0:T(8,128)(2,1)S(1)} %maximum_select_fusion.1), channel_id=1, source_target_pairs={{0,8},{8,0},{4,12},{12,4},{16,24},{24,16},{20,28},{28,20},{1,9},{9... | collective-permute-start | bytes 1572872 | tf_op jit(solution)/shard_map/ppermute | solution.py:23
  14.9 26.6 %collective-permute-done.2 = bf16[2,2048,64]{1,2,0:T(8,128)(2,1)S(1)} collective-permute-done((bf16[2,2048,64]{1,2,0:T(8,128)(2,1)S(1)}, bf16[2,2048,64]{1,2,0:T(8,128)(2,1)S(1)}, u32[]{:S(2)}, u32[]{:S(2)}) %collective-permute-start.2) | collective-permute-done | bytes 524320 | tf_op jit(solution)/shard_map/ppermute | solution.py:23
  41.6 0.2 maximum_select_fusion
  42.0 0.3 copy.43
  42.2 0.3 copy.44
  42.5 1.5 pad_maximum_fusion
  44.1 4.1 %collective-permute-start = (s32[512]{0:T(512)S(1)}, s32[512]{0:T(512)S(1)}, u32[]{:S(2)}, u32[]{:S(2)}) collective-permute-start(s32[512]{0:T(512)S(1)} %broadcast_add_fusion), channel_id=1, source_target_pairs={{0,1},{1,2},{2,3},{4,5},{5,6},{6,7},{8,9},{9,10},{10,11},{12,13},{... | collective-permute-start | bytes 6152 | tf_op jit(solution)/shard_map/ppermute | solution.py:29
  48.4 0.2 select_reduce_fusion
  48.6 0.5 multiply_cosine_fusion.1
  49.2 0.3 collective-permute-done
  49.5 46.9 %all-gather.3.cloned.1.call-done = bf16[512,8192]{1,0:T(8,128)(2,1)} async-done(((bf16[512,1024]{1,0:T(8,128)(2,1)}), bf16[512,8192]{1,0:T(8,128)(2,1)}) %all-gather.3.cloned.1.call-update) | async-done | bytes 8388624 | tf_op jit(solution)/shard_map/all_gather | solution.py:71
  96.4 5.1 %fusion.1 = f32[512]{0:T(512)S(1)} fusion(bf16[512,8192]{1,0:T(8,128)(2,1)} %all-gather.3.cloned.1.call-done), kind=kLoop, calls=%fused_computation.5 | loop fusion | flops 12582400 | bytes 8390656 | tf_op jit(solution)/shard_map/reduce_sum | solution.py:74
  101.5 85.8 %all-gather.5.cloned.1.call-done = bf16[8192,512]{1,0:T(8,128)(2,1)} async-done(((bf16[2048,512]{1,0:T(8,128)(2,1)}), bf16[8192,512]{1,0:T(8,128)(2,1)}) %all-gather.5.cloned.1.call-update) | async-done | bytes 8388624 | tf_op jit(solution)/shard_map/all_gather | solution.py:69
  187.3 9.5 %fusion.11 = f32[512,512]{0,1:T(8,128)S(1)} fusion(bf16[8192,512]{1,0:T(8,128)(2,1)} %all-gather.5.cloned.1.call-done, bf16[512,8192]{1,0:T(8,128)(2,1)} %all-gather.3.cloned.1.call-done, f32[8192]{0:T(1024)S(1)} %convert_element_type.52, f32[512]{0:T(512)S(1)} %add_rsqrt_fusion), kind=kOutput, calls=%fused_computation.17 | convolution fusion | flops 4307812352 | bytes 17860608 | tf_op jit(solution)/shard_map/dot_general | solution.py:73
  196.9 0.1 reshape.251
  197.0 0.2 fusion.46
  197.3 0.6 fusion.34
  197.9 0.1 copy.50
  198.1 3.4 %collective-permute-start.3 = (bf16[512,128]{0,1:T(8,128)(2,1)S(1)}, bf16[512,128]{0,1:T(8,128)(2,1)S(1)}, u32[]{:S(2)}, u32[]{:S(2)}) collective-permute-start(bf16[512,128]{0,1:T(8,128)(2,1)S(1)} %convert_element_type.57), channel_id=1, source_target_pairs={{0,1},{1,2},{2,3},{4,5},{5,6},{6,7},{8,9},{9,10},{10,11},{12,13},{... | collective-permute-start | bytes 393224 | tf_op jit(solution)/shard_map/ppermute | solution.py:29
  201.4 0.3 reshape.249
  201.8 0.4 fusion.45
  202.2 3.4 %collective-permute-start.4 = (bf16[512,128]{0,1:T(8,128)(2,1)S(1)}, bf16[512,128]{0,1:T(8,128)(2,1)S(1)}, u32[]{:S(2)}, u32[]{:S(2)}) collective-permute-start(bf16[512,128]{0,1:T(8,128)(2,1)S(1)} %slice.49), channel_id=1, source_target_pairs={{0,1},{1,2},{2,3},{4,5},{5,6},{6,7},{8,9},{9,10},{10,11},{12,13},{... | collective-permute-start | bytes 393224 | tf_op jit(solution)/shard_map/ppermute | solution.py:29
  205.6 0.1 copy.52
  205.7 0.2 reshape.262
  205.9 1.3 scatter_custom_fusion
  207.2 3.3 %all-to-all-start = ((bf16[4,16,512]{2,1,0:T(8,128)(2,1)}), bf16[4,16,512]{2,1,0:T(8,128)(2,1)S(1)}, u32[]{:S(2)}, u32[]{:S(2)}) async-start(bf16[4,16,512]{2,1,0:T(8,128)(2,1)} %bitcast.12), calls=%async_computation | async-start | bytes 131072 | tf_op jit(solution)/shard_map/all_to_all | solution.py:152
  210.5 0.5 subtract_convert_fusion
  211.0 0.1 copy.53
  211.2 0.2 reshape.270
  211.3 1.3 scatter_custom_fusion.1
  212.6 2.7 %all-to-all-done = bf16[4,16,512]{2,1,0:T(8,128)(2,1)S(1)} async-done(((bf16[4,16,512]{2,1,0:T(8,128)(2,1)}), bf16[4,16,512]{2,1,0:T(8,128)(2,1)S(1)}, u32[]{:S(2)}, u32[]{:S(2)}) %all-to-all-start) | async-done | bytes 65568 | tf_op jit(solution)/shard_map/all_to_all | solution.py:152
  215.3 3.5 %all-to-all-start.1 = ((bf16[4,16,512]{2,1,0:T(8,128)(2,1)}), bf16[4,16,512]{2,1,0:T(8,128)(2,1)S(1)}, u32[]{:S(2)}, u32[]{:S(2)}) async-start(bf16[4,16,512]{2,1,0:T(8,128)(2,1)} %bitcast.13), calls=%async_computation.1 | async-start | bytes 131072 | tf_op jit(solution)/shard_map/all_to_all | solution.py:153
  218.8 0.3 pad_maximum_fusion.2
  219.1 0.2 copy.47
  219.4 0.2 reshape.254
  219.6 0.9 copy.54
  220.5 2.9 %all-to-all-done.1 = bf16[4,16,512]{2,1,0:T(8,128)(2,1)S(1)} async-done(((bf16[4,16,512]{2,1,0:T(8,128)(2,1)}), bf16[4,16,512]{2,1,0:T(8,128)(2,1)S(1)}, u32[]{:S(2)}, u32[]{:S(2)}) %all-to-all-start.1) | async-done | bytes 65568 | tf_op jit(solution)/shard_map/all_to_all | solution.py:153
  223.4 0.2 reshape.257
  223.6 0.9 copy.55
  224.5 1.7 fusion.47
  226.3 0.6 fusion.6
  226.9 0.9 fusion.20
  227.8 0.7 copy.72
  (40 shorter events, 0.6 us)
Async XLA Ops:
  7.2 89.2 %all-gather.3.cloned.1.call-start = ((), (), s32[]{:S(2)}) async-start(), calls=%async_computation.2 | async-start | bytes 9437184 | tf_op jit(solution)/shard_map/all_gather | solution.py:71
  7.9 34.6 %copy-start = (bf16[2048,256]{1,0:T(8,128)(2,1)S(1)}, bf16[2048,256]{1,0:T(8,128)(2,1)}, u32[]{:S(2)}) copy-start(bf16[2048,256]{1,0:T(8,128)(2,1)} %param.10) | copy-start | bytes 3145732
  7.9 179.4 %all-gather.5.cloned.1.call-start = ((), (), s32[]{:S(2)}) async-start(), calls=%async_computation.3 | async-start | bytes 10485760 | tf_op jit(solution)/shard_map/all_gather | solution.py:69
  9.0 1.7 collective-permute-start.1
  11.9 29.6 %collective-permute-start.2 = (bf16[2,2048,64]{1,2,0:T(8,128)(2,1)S(1)}, bf16[2,2048,64]{1,2,0:T(8,128)(2,1)S(1)}, u32[]{:S(2)}, u32[]{:S(2)}) collective-permute-start(bf16[2,2048,64]{1,2,0:T(8,128)(2,1)S(1)} %maximum_select_fusion.1), channel_id=1, source_target_pairs={{0,8},{8,0},{4,12},{12,4},{16,24},{24,16},{20,28},{28,20},{1,9},{9... | collective-permute-start | bytes 1572872 | tf_op jit(solution)/shard_map/ppermute | solution.py:23
  41.9 2.2 copy-start.2
  41.9 6.3 %copy-start.4 = (s32[512]{0:T(512)S(1)}, s32[512]{0:T(512)}, u32[]{:S(2)}) copy-start(s32[512]{0:T(512)} %param.14) | copy-start | bytes 6148
  41.9 6.3 %copy-start.3 = (s32[32,1]{0,1:T(1,128)S(1)}, s32[32,1]{0,1:T(1,128)}, u32[]{:S(2)}) copy-start(s32[32,1]{0,1:T(1,128)} %param.15) | copy-start | bytes 388
  41.9 7.2 %copy-start.1 = (bf16[8192]{0:T(1024)(128)(2,1)S(1)}, bf16[8192]{0:T(1024)(128)(2,1)}, u32[]{:S(2)}) copy-start(bf16[8192]{0:T(1024)(128)(2,1)} %param.9) | copy-start | bytes 49156
  44.1 5.4 %collective-permute-start = (s32[512]{0:T(512)S(1)}, s32[512]{0:T(512)S(1)}, u32[]{:S(2)}, u32[]{:S(2)}) collective-permute-start(s32[512]{0:T(512)S(1)} %broadcast_add_fusion), channel_id=1, source_target_pairs={{0,1},{1,2},{2,3},{4,5},{5,6},{6,7},{8,9},{9,10},{10,11},{12,13},{... | collective-permute-start | bytes 6152 | tf_op jit(solution)/shard_map/ppermute | solution.py:29
  198.1 26.4 %collective-permute-start.3 = (bf16[512,128]{0,1:T(8,128)(2,1)S(1)}, bf16[512,128]{0,1:T(8,128)(2,1)S(1)}, u32[]{:S(2)}, u32[]{:S(2)}) collective-permute-start(bf16[512,128]{0,1:T(8,128)(2,1)S(1)} %convert_element_type.57), channel_id=1, source_target_pairs={{0,1},{1,2},{2,3},{4,5},{5,6},{6,7},{8,9},{9,10},{10,11},{12,13},{... | collective-permute-start | bytes 393224 | tf_op jit(solution)/shard_map/ppermute | solution.py:29
  202.2 24.7 %collective-permute-start.4 = (bf16[512,128]{0,1:T(8,128)(2,1)S(1)}, bf16[512,128]{0,1:T(8,128)(2,1)S(1)}, u32[]{:S(2)}, u32[]{:S(2)}) collective-permute-start(bf16[512,128]{0,1:T(8,128)(2,1)S(1)} %slice.49), channel_id=1, source_target_pairs={{0,1},{1,2},{2,3},{4,5},{5,6},{6,7},{8,9},{9,10},{10,11},{12,13},{... | collective-permute-start | bytes 393224 | tf_op jit(solution)/shard_map/ppermute | solution.py:29
  207.2 8.1 %all-to-all-start = ((bf16[4,16,512]{2,1,0:T(8,128)(2,1)}), bf16[4,16,512]{2,1,0:T(8,128)(2,1)S(1)}, u32[]{:S(2)}, u32[]{:S(2)}) async-start(bf16[4,16,512]{2,1,0:T(8,128)(2,1)} %bitcast.12), calls=%async_computation | async-start | bytes 131072 | tf_op jit(solution)/shard_map/all_to_all | solution.py:152
  215.3 8.1 %all-to-all-start.1 = ((bf16[4,16,512]{2,1,0:T(8,128)(2,1)}), bf16[4,16,512]{2,1,0:T(8,128)(2,1)S(1)}, u32[]{:S(2)}, u32[]{:S(2)}) async-start(bf16[4,16,512]{2,1,0:T(8,128)(2,1)} %bitcast.13), calls=%async_computation.1 | async-start | bytes 131072 | tf_op jit(solution)/shard_map/all_to_all | solution.py:153
Sparse Core Ops, SparseCore 0:
  9.6 86.7 all-gather.2
  98.2 89.0 all-gather.4
where the time goes:
time: 236 us; the launch traced here: 235 us
  waiting for transfers between devices  167 us (71%)
  starting transfers between devices  21.2 us (9%)
  between operations  14.5 us (6%)
  other arithmetic  12.2 us (5%)
  matrix products  12.1 us (5%)
  local copies, waits for them, and re-layouts  8.42 us (4%)
    all_gather x1, waiting for transfers between devices, shards(): all_rows = lax.all_gather(local_weights, 'gy', axis=0, tiled=True)  85.8 us
    all_gather x1, waiting for transfers between devices, shards(): lax.all_gather(tokens_in, 'gx', axis=1, tiled=True).astype(jnp.float32)  46.9 us
    ppermute x2, waiting for transfers between devices, swapped(): return lax.ppermute(block, axis, route)  27.8 us
    ppermute x3, starting transfers between devices, shifted(): return lax.ppermute(value, axis, pairs)  10.8 us
    dot_general x1, matrix products, shards(): products = jnp.dot(normed, all_rows, preferred_element_type=jnp.float32)  9.46 us
    reduce_sum x1, other arithmetic, shards(): squares = jnp.sum(piece_float * piece_float, axis=1)  5.1 us
  transfers between devices with their start and end apart: 9, of which 7 were waited for; matrix products, arithmetic and copies ran while one was open for 9% of the time, Pallas kernels for 0%

commit v1 on v0

--- a/solution.py
+++ b/solution.py
@@ -13,28 +13,27 @@
 MASKED = -1e30
 
 
-def swapped(block, axis, bit):
-    count = lax.axis_size(axis)
-    route = []
-    for low in range(count):
-        high = low | 1 << bit
-        if high != low and high < count:
-            route += [(low, high), (high, low)]
-    return lax.ppermute(block, axis, route)
-
-
 def shifted(value, axis, by):
     count = lax.axis_size(axis)
     pairs = [(i, i + by) for i in range(count) if 0 <= i + by < count]
     return lax.ppermute(value, axis, pairs)
 
 
-def rotate(matrix, places, group_width):
+def partner_route(count, group, k):
+    route = []
+    for i in range(count):
+        base = i - i % group
+        route.append((i, base + ((i % group) ^ k)))
+    return route
+
+
+def rotate(matrix, places, group_width, first_pair):
     row_count = matrix.shape[0]
     pair_count = group_width // 2
     shaped = matrix.reshape(row_count, -1, pair_count, 2)
-    pair_index = jnp.arange(pair_count, dtype=jnp.int32)
-    frequency = jnp.power(THETA, -(2.0 * pair_index.astype(jnp.float32)) / HD)
+    all_pairs = jnp.arange(HD // 2, dtype=jnp.int32)
+    all_freq = jnp.power(THETA, -(2.0 * all_pairs.astype(jnp.float32)) / HD)
+    frequency = lax.dynamic_slice_in_dim(all_freq, first_pair, pair_count, 0)
     angles = places.astype(jnp.float32)[:, None] * frequency[None, :]
     cosine = jnp.cos(angles)[:, None, :]
     sine_of = jnp.sin(angles)[:, None, :]
@@ -53,37 +52,48 @@
     quarter = key_weight.shape[1]
     head_local = query_weight.shape[1] // HD
     quarters = HD // quarter
-    bit_count = quarters.bit_length() - 1
+    gx_count = lax.axis_size("gx")
+    gy_count = lax.axis_size("gy")
     spot = lax.axis_index("gx") % quarters
-    stacked_weights = jnp.stack([key_weight, value_weight])
-    for bit_index in range(bit_count):
-        other_side = swapped(stacked_weights, "gx", bit_index)
-        upper_half = spot // (1 << bit_index) % 2 == 1
-        stacked_weights = jnp.where(
-            upper_half,
-            jnp.concatenate([other_side, stacked_weights], axis=2),
-            jnp.concatenate([stacked_weights, other_side], axis=2),
-        )
-    key_cols = HD
-    local_weights = jnp.concatenate([query_weight, stacked_weights[0], stacked_weights[1]], axis=1)
-    all_rows = lax.all_gather(local_weights, "gy", axis=0, tiled=True)
+    my_gy = lax.axis_index("gy")
+    row_block = query_weight.shape[0]
+
+    local_weights = jnp.concatenate([query_weight, key_weight, value_weight], axis=1)
+    pieces = [(my_gy, local_weights)]
+    for k in range(1, gy_count):
+        got = lax.ppermute(local_weights, "gy", partner_route(gy_count, gy_count, k))
+        pieces.append((my_gy ^ k, got))
+
     gain_part = norm_gain.astype(jnp.float32)
     piece_float = lax.all_gather(tokens_in, "gx", axis=1, tiled=True).astype(jnp.float32)
     normed = (piece_float * gain_part[None, :]).astype(jnp.bfloat16)
-    products = jnp.dot(normed, all_rows, preferred_element_type=jnp.float32)
     squares = jnp.sum(piece_float * piece_float, axis=1)
-    products, squares = (products, squares)
+    products = None
+    for source, block in pieces:
+        rows = lax.dynamic_slice_in_dim(normed, source * row_block, row_block, 1)
+        part = jnp.dot(rows, block, preferred_element_type=jnp.float32)
+        products = part if products is None else products + part
     scaling = 1.0 / jnp.sqrt(squares / D + EPSILON)
     projected = products * scaling[:, None]
     query_cols = head_local * HD
-    queries = rotate(projected[:, :query_cols], positions, HD).astype(jnp.bfloat16)
-    key_proj = projected[:, query_cols : query_cols + key_cols]
-    value_proj = projected[:, query_cols + key_cols :]
-    full_keys = rotate(key_proj, positions, HD).astype(jnp.bfloat16)
-    full_values = value_proj.astype(jnp.bfloat16)
-    key_piece = lax.dynamic_slice_in_dim(full_keys, spot * quarter, quarter, 1)
-    value_piece = lax.dynamic_slice_in_dim(full_values, spot * quarter, quarter, 1)
-    span_count = lax.axis_size("gy") // 4
+    queries = rotate(projected[:, :query_cols], positions, HD, 0).astype(jnp.bfloat16)
+    key_proj = projected[:, query_cols : query_cols + quarter]
+    value_proj = projected[:, query_cols + quarter :]
+    key_piece = rotate(key_proj, positions, quarter, spot * (quarter // 2)).astype(jnp.bfloat16)
+    value_piece = value_proj.astype(jnp.bfloat16)
+
+    own_kv = jnp.stack([key_piece, value_piece])
+    kv_parts = [own_kv]
+    for k in range(1, quarters):
+        kv_parts.append(lax.ppermute(own_kv, "gx", partner_route(gx_count, quarters, k)))
+    kv_stack = jnp.stack(kv_parts)
+    order = jnp.arange(quarters, dtype=jnp.int32) ^ spot
+    kv_full = jnp.take(kv_stack, order, axis=0)
+    kv_full = kv_full.transpose(1, 2, 0, 3).reshape(2, token_count, HD)
+    full_keys = kv_full[0]
+    full_values = kv_full[1]
+
+    span_count = gy_count // 4
     marks = segment_ids + 1
     key_list = [full_keys]
     value_list = [full_values]
@@ -126,7 +136,7 @@
         .reshape(token_count, head_local * HD)
         .astype(jnp.bfloat16)
     )
-    owner_count = lax.axis_size("gy")
+    owner_count = gy_count
     page_rows = token_count // PAGE
     capacity = max(2, 2 * page_rows // owner_count)
     owner_of = page_owner[:, 0]

time: 236 us -> 163 us (0.69)
  waiting for transfers between devices: 167 us -> 76.9 us
  local copies, waits for them, and re-layouts: 8.42 us -> 17.4 us
  other arithmetic: 12.2 us -> 16 us
  starting transfers between devices: 21.2 us -> 24 us
    all_gather x1 -> x0, waiting for transfers between devices: 85.8 us -> none  [shards(): all_rows = lax.all_gather(local_weights, 'gy', axis=0, tiled=True)]
    ppermute x3, waiting for transfers between devices: 0.28 us -> 49.3 us  [shifted(): return lax.ppermute(value, axis, pairs)]
    ppermute x2 -> x6, waiting for transfers between devices: 27.8 us -> 0.02 us  [the longest x3 0.01 us: shards(): lax.ppermute(local_weights, 'gy', partner_route(gy_count, gy_count, k))]
    all_gather x1, waiting for transfers between devices: 46.9 us -> 23.8 us  [shards(): lax.all_gather(tokens_in, 'gx', axis=1, tiled=True).astype(jnp.float32)]
    convert_element_type x1 -> x4, local copies, waits for them, and re-layouts: 0.06 us -> 6.67 us  [shards(): rotate(key_proj, positions, quarter, spot * (quarter // 2))]
    reduce_sum x1, other arithmetic: 5.1 us -> 9.88 us  [shards(): squares = jnp.sum(piece_float * piece_float, axis=1)]
    ppermute x2 -> x6, starting transfers between devices: 3.53 us -> 6.43 us  [the longest x3 4.57 us: shards(): lax.ppermute(local_weights, 'gy', partner_route(gy_count, gy_count, k))]
    all_to_all x1, waiting for transfers between devices: 2.65 us -> 0.01 us  [shards(): lax.all_to_all(send_keys, 'gy', split_axis=0, concat_axis=0, tiled=True)]
  transfers between devices with their start and end apart: 9 -> 12, of which waited for: 7 -> 4; matrix products, arithmetic and copies ran while one was open for 9% -> 25% of each run, Pallas kernels for 0% -> 0%
where the time goes in v1:
time: 163 us; the launch traced here: 162 us
  waiting for transfers between devices  76.9 us (47%)
  starting transfers between devices  24 us (15%)
  local copies, waits for them, and re-layouts  17.4 us (11%)
  other arithmetic  16 us (10%)
  between operations  14.5 us (9%)
  matrix products  12.9 us (8%)
    ppermute x3, waiting for transfers between devices, shifted(): return lax.ppermute(value, axis, pairs)  49.3 us
    all_gather x1, waiting for transfers between devices, shards(): lax.all_gather(tokens_in, 'gx', axis=1, tiled=True).astype(jnp.float32)  23.8 us
    ppermute x3, starting transfers between devices, shifted(): return lax.ppermute(value, axis, pairs)  10.6 us
    dot_general x4, matrix products, shards(): part = jnp.dot(rows, block, preferred_element_type=jnp.float32)  10.3 us
    reduce_sum x1, other arithmetic, shards(): squares = jnp.sum(piece_float * piece_float, axis=1)  9.88 us
    convert_element_type x4, local copies, waits for them, and re-layouts, shards(): rotate(key_proj, positions, quarter, spot * (quarter // 2))  6.67 us
    ppermute x3, starting transfers between devices, shards(): lax.ppermute(local_weights, 'gy', partner_route(gy_count, gy_count, k))  4.57 us
    unnamed x28, local copies, waits for them, and re-layouts  4 us
  transfers between devices with their start and end apart: 12, of which 4 were waited for; matrix products, arithmetic and copies ran while one was open for 25% of the time, Pallas kernels for 0%

profile of v1, /device:TPU:0, one launch (start us, length us, event | category | flops | bytes accessed | tf_op | source)
XLA Modules:
  0.0 161.8 jit_solution(10147811337922431939)
XLA Ops:
  7.2 0.7 all-gather.2.cloned.1.call-update
  8.0 1.5 copy.36
  9.6 3.0 %collective-permute-start.2 = (bf16[2048,320]{0,1:T(8,128)(2,1)S(1)}, bf16[2048,320]{0,1:T(8,128)(2,1)}, u32[]{:S(2)}, u32[]{:S(2)}) collective-permute-start(bf16[2048,320]{0,1:T(8,128)(2,1)S(1)} %pad_maximum_fusion), channel_id=1, source_target_pairs={{0,2},{1,3},{2,0},{3,1},{4,6},{5,7},{6,4},{7,5},{8,10},{9,11},{10,... | collective-permute-start | bytes 3932168 | tf_op jit(solution)/shard_map/ppermute | solution.py:64
  12.7 1.4 collective-permute-start.3
  14.2 3.8 %collective-permute-start = (s32[512]{0:T(512)S(1)}, s32[512]{0:T(512)S(1)}, u32[]{:S(2)}, u32[]{:S(2)}) collective-permute-start(s32[512]{0:T(512)S(1)} %broadcast_add_fusion), channel_id=1, source_target_pairs={{0,1},{1,2},{2,3},{4,5},{5,6},{6,7},{8,9},{9,10},{10,11},{12,13},{... | collective-permute-start | bytes 6152 | tf_op jit(solution)/shard_map/ppermute | solution.py:19
  18.3 0.2 select_reduce_fusion
  18.4 0.6 fusion.59
  19.0 0.5 multiply_cosine_fusion
  19.6 0.5 compare_and_fusion
  20.2 0.6 ge.25
  20.8 49.2 %collective-permute-done = s32[512]{0:T(512)S(1)} collective-permute-done((s32[512]{0:T(512)S(1)}, s32[512]{0:T(512)S(1)}, u32[]{:S(2)}, u32[]{:S(2)}) %collective-permute-start) | collective-permute-done | bytes 2080 | tf_op jit(solution)/shard_map/ppermute | solution.py:19
  70.0 0.6 broadcast_compare_fusion
  70.6 23.8 %all-gather.2.cloned.1.call-done = bf16[512,8192]{1,0:T(8,128)(2,1)} async-done(((bf16[512,1024]{1,0:T(8,128)(2,1)}), bf16[512,8192]{1,0:T(8,128)(2,1)}) %all-gather.2.cloned.1.call-update) | async-done | bytes 8388624 | tf_op jit(solution)/shard_map/all_gather | solution.py:68
  94.4 9.9 %fusion.1 = (f32[512]{0:T(512)S(1)}, bf16[512,8192]{1,0:T(8,128)(2,1)}) fusion(bf16[512,8192]{1,0:T(8,128)(2,1)} %all-gather.2.cloned.1.call-done, f32[8192]{0:T(1024)S(1)} %convert_element_type.65), kind=kLoop, calls=%fused_computation.6 | loop fusion | flops 20971008 | bytes 16812032 | tf_op jit(solution)/shard_map/reduce_sum | solution.py:70
  104.3 2.6 %fusion.14 = f32[512,320]{0,1:T(8,128)S(1)} fusion(bf16[512,8192]{1,0:T(8,128)(2,1)} %get-tuple-element.13, s32[]{:T(128)S(6)} %select_n.59, bf16[2048,32]{0,1:T(8,128)(2,1)S(1)} %copy-done.2, bf16[2048,32]{0,1:T(8,128)(2,1)S(1)} %copy-done.3, bf16[2048,256]{0,1:T(8,128)(2,1)S(1)} %copy.36), kind=kOutput, calls=%fused_computation.21 | convolution fusion | flops 675020800 | bytes 4063236 | tf_op jit(solution)/shard_map/dot_general | solution.py:74
  107.0 3.2 %fusion.10 = f32[512,320]{0,1:T(8,128)S(1)} fusion(bf16[2048,320]{0,1:T(8,128)(2,1)} %collective-permute-done.2, bf16[512,8192]{1,0:T(8,128)(2,1)} %get-tuple-element.13, s32[]{:T(128)S(6)} %select_n.61), kind=kOutput, calls=%fused_computation.17 | convolution fusion | flops 671088640 | bytes 4063236 | tf_op jit(solution)/shard_map/dot_general | solution.py:74
  110.2 2.2 %fusion.8 = f32[512,320]{0,1:T(8,128)S(1)} fusion(bf16[2048,320]{0,1:T(8,128)(2,1)} %collective-permute-done.3, bf16[512,8192]{1,0:T(8,128)(2,1)S(1)} %copy-done, s32[]{:T(128)S(6)} %select_n.62), kind=kOutput, calls=%fused_computation.15 | convolution fusion | flops 671088640 | bytes 4063236 | tf_op jit(solution)/shard_map/dot_general | solution.py:74
  112.4 2.2 %fusion.28 = f32[512,320]{0,1:T(8,128)S(1)} fusion(f32[512,320]{0,1:T(8,128)S(1)} %fusion.8, f32[512,320]{0,1:T(8,128)S(1)} %fusion.10, f32[512,320]{0,1:T(8,128)S(1)} %fusion.14, bf16[2048,320]{0,1:T(8,128)(2,1)} %collective-permute-done.1, bf16[512,8192]{1,0:T(8,128)(2,1)S(1)} %copy-done, s32[]{:T(128)S(6)} %select_n.60, f32[512]{0:T(512)S(1)} %add_rsqrt_fusion), kind=kOutput, calls=%fused_computation.28 | convolution fusion | flops 671744000 | bytes 6031364 | tf_op jit(solution)/shard_map/dot_general | solution.py:74
  114.8 0.2 fusion.47
  115.0 0.6 copy-done.1
  115.7 0.7 fusion.62
  116.3 0.2 collective-permute-start.4
  116.6 1.6 collective-permute-start.6
  118.2 0.3 reshape.283
  118.6 0.4 fusion.63
  119.0 2.8 %copy.44 = bf16[512,1,16,2]{3,2,0,1:T(8,128)(2,1)S(1)} copy(bf16[512,1,16,2]{0,2,3,1:T(8,128)(2,1)} %copy-done.1) | data formatting | bytes 65536 | tf_op jit(solution)/shard_map/convert_element_type | solution.py:82
  121.8 3.8 %reshape.303 = bf16[32,512]{1,0:T(8,128)(2,1)} reshape(bf16[512,1,16,2]{3,2,0,1:T(8,128)(2,1)S(1)} %copy.44) | data formatting | bytes 65536 | tf_op jit(solution)/shard_map/convert_element_type | solution.py:82
  125.6 1.5 scatter_custom_fusion
  127.1 3.6 %all-to-all-start = ((bf16[4,16,512]{2,1,0:T(8,128)(2,1)}), bf16[4,16,512]{2,1,0:T(8,128)(2,1)S(1)}, u32[]{:S(2)}, u32[]{:S(2)}) async-start(bf16[4,16,512]{2,1,0:T(8,128)(2,1)} %bitcast.17), calls=%async_computation | async-start | bytes 131072 | tf_op jit(solution)/shard_map/all_to_all | solution.py:162
  130.8 1.0 pad_maximum_fusion.2
  131.8 0.6 gather_fusion
  132.5 4.1 %collective-permute-start.7 = (bf16[512,128]{0,1:T(8,128)(2,1)S(1)}, bf16[512,128]{0,1:T(8,128)(2,1)S(1)}, u32[]{:S(2)}, u32[]{:S(2)}) collective-permute-start(bf16[512,128]{0,1:T(8,128)(2,1)S(1)} %bitcast.59), channel_id=1, source_target_pairs={{0,1},{1,2},{2,3},{4,5},{5,6},{6,7},{8,9},{9,10},{10,11},{12,13},{... | collective-permute-start | bytes 393224 | tf_op jit(solution)/shard_map/ppermute | solution.py:19
  136.6 0.5 subtract_convert_fusion
  137.3 0.2 reshape.311
  137.4 1.4 scatter_custom_fusion.1
  138.9 3.3 %all-to-all-start.1 = ((bf16[4,16,512]{2,1,0:T(8,128)(2,1)}), bf16[4,16,512]{2,1,0:T(8,128)(2,1)S(1)}, u32[]{:S(2)}, u32[]{:S(2)}) async-start(bf16[4,16,512]{2,1,0:T(8,128)(2,1)} %bitcast.18), calls=%async_computation.1 | async-start | bytes 131072 | tf_op jit(solution)/shard_map/all_to_all | solution.py:163
  142.2 0.3 pad_maximum_fusion.1
  142.5 0.2 copy.39
  142.8 0.2 reshape.287
  142.9 0.9 copy.46
  143.9 3.1 %all-to-all-done.1 = bf16[4,16,512]{2,1,0:T(8,128)(2,1)S(1)} async-done(((bf16[4,16,512]{2,1,0:T(8,128)(2,1)}), bf16[4,16,512]{2,1,0:T(8,128)(2,1)S(1)}, u32[]{:S(2)}, u32[]{:S(2)}) %all-to-all-start.1) | async-done | bytes 65568 | tf_op jit(solution)/shard_map/all_to_all | solution.py:163
  147.0 0.2 reshape.290
  147.2 0.9 copy.47
  148.1 2.6 %collective-permute-start.8 = (bf16[512,128]{0,1:T(8,128)(2,1)S(1)}, bf16[512,128]{0,1:T(8,128)(2,1)S(1)}, u32[]{:S(2)}, u32[]{:S(2)}) collective-permute-start(bf16[512,128]{0,1:T(8,128)(2,1)S(1)} %bitcast.57), channel_id=1, source_target_pairs={{0,1},{1,2},{2,3},{4,5},{5,6},{6,7},{8,9},{9,10},{10,11},{12,13},{... | collective-permute-start | bytes 393224 | tf_op jit(solution)/shard_map/ppermute | solution.py:19
  150.8 1.7 %fusion.66 = (f32[1024]{0:T(1024)S(1)}, f32[1024,1024]{0,1:T(8,128)S(1)}) fusion(bf16[1024,128]{1,0:T(8,128)(2,1)S(1)} %bitcast.54, bf16[512,128]{0,1:T(8,128)(2,1)S(1)} %bitcast.60, bf16[512,128]{0,1:T(8,128)(2,1)S(1)} %collective-permute-done.7, s32[1024]{0:T(1024)S(1)} %bitcast.62, pred[1024]{0:T(1024)(128)(4,1)S(1)} %copy-done.9, ...), kind=kOutput, calls=%fused_computation.89 | convolution fusion | flops 276298752 | bytes 4736000 | tf_op jit(solution)/shard_map/dot_general | solution.py:117
  152.5 0.6 fusion.3
  153.2 0.9 fusion.34
  154.2 0.7 copy.64
  (63 shorter events, 1.2 us)
Async XLA Ops:
  7.2 2.3 %copy-start.3 = (bf16[2048,32]{0,1:T(8,128)(2,1)S(1)}, bf16[2048,32]{0,1:T(8,128)(2,1)}, u32[]{:S(2)}) copy-start(bf16[2048,32]{0,1:T(8,128)(2,1)} %param.11) | copy-start | bytes 393220
  7.2 2.3 %copy-start.2 = (bf16[2048,32]{0,1:T(8,128)(2,1)S(1)}, bf16[2048,32]{0,1:T(8,128)(2,1)}, u32[]{:S(2)}) copy-start(bf16[2048,32]{0,1:T(8,128)(2,1)} %param.12) | copy-start | bytes 393220
  7.2 7.0 %copy-start.5 = (s32[512]{0:T(512)S(1)}, s32[512]{0:T(512)}, u32[]{:S(2)}) copy-start(s32[512]{0:T(512)} %param.13) | copy-start | bytes 6148
  7.2 87.2 %all-gather.2.cloned.1.call-start = ((), (), s32[]{:S(2)}) async-start(), calls=%async_computation.2 | async-start | bytes 9437184 | tf_op jit(solution)/shard_map/all_gather | solution.py:68
  7.9 10.1 %copy-start.7 = (s32[512]{0:T(512)S(1)}, s32[512]{0:T(512)}, u32[]{:S(2)}) copy-start(s32[512]{0:T(512)} %param.14) | copy-start | bytes 6148
  7.9 10.1 %copy-start.6 = (s32[32,1]{0,1:T(1,128)S(1)}, s32[32,1]{0,1:T(1,128)}, u32[]{:S(2)}) copy-start(s32[32,1]{0,1:T(1,128)} %param.15) | copy-start | bytes 388
  8.0 12.2 %copy-start.4 = (bf16[8192]{0:T(1024)(128)(2,1)S(1)}, bf16[8192]{0:T(1024)(128)(2,1)}, u32[]{:S(2)}) copy-start(bf16[8192]{0:T(1024)(128)(2,1)} %param.9) | copy-start | bytes 49156
  9.6 97.3 %collective-permute-start.2 = (bf16[2048,320]{0,1:T(8,128)(2,1)S(1)}, bf16[2048,320]{0,1:T(8,128)(2,1)}, u32[]{:S(2)}, u32[]{:S(2)}) collective-permute-start(bf16[2048,320]{0,1:T(8,128)(2,1)S(1)} %pad_maximum_fusion), channel_id=1, source_target_pairs={{0,2},{1,3},{2,0},{3,1},{4,6},{5,7},{6,4},{7,5},{8,10},{9,11},{10,... | collective-permute-start | bytes 3932168 | tf_op jit(solution)/shard_map/ppermute | solution.py:64
  12.7 97.5 %collective-permute-start.3 = (bf16[2048,320]{0,1:T(8,128)(2,1)S(1)}, bf16[2048,320]{0,1:T(8,128)(2,1)}, u32[]{:S(2)}, u32[]{:S(2)}) collective-permute-start(bf16[2048,320]{0,1:T(8,128)(2,1)S(1)} %pad_maximum_fusion), channel_id=1, source_target_pairs={{0,3},{1,2},{2,1},{3,0},{4,7},{5,6},{6,5},{7,4},{8,11},{9,10},{10,... | collective-permute-start | bytes 3932168 | tf_op jit(solution)/shard_map/ppermute | solution.py:64
  14.1 98.3 %collective-permute-start.1 = (bf16[2048,320]{0,1:T(8,128)(2,1)S(1)}, bf16[2048,320]{0,1:T(8,128)(2,1)}, u32[]{:S(2)}, u32[]{:S(2)}) collective-permute-start(bf16[2048,320]{0,1:T(8,128)(2,1)S(1)} %pad_maximum_fusion), channel_id=1, source_target_pairs={{0,1},{1,0},{2,3},{3,2},{4,5},{5,4},{6,7},{7,6},{8,9},{9,8},{10,11... | collective-permute-start | bytes 3932168 | tf_op jit(solution)/shard_map/ppermute | solution.py:64
  14.2 55.8 %collective-permute-start = (s32[512]{0:T(512)S(1)}, s32[512]{0:T(512)S(1)}, u32[]{:S(2)}, u32[]{:S(2)}) collective-permute-start(s32[512]{0:T(512)S(1)} %broadcast_add_fusion), channel_id=1, source_target_pairs={{0,1},{1,2},{2,3},{4,5},{5,6},{6,7},{8,9},{9,10},{10,11},{12,13},{... | collective-permute-start | bytes 6152 | tf_op jit(solution)/shard_map/ppermute | solution.py:19
  104.3 5.9 %copy-start = (bf16[512,8192]{1,0:T(8,128)(2,1)S(1)}, bf16[512,8192]{1,0:T(8,128)(2,1)}, u32[]{:S(2)}) copy-start(bf16[512,8192]{1,0:T(8,128)(2,1)} %get-tuple-element.13) | copy-start | bytes 25165828
  115.0 0.6 copy-start.1
  116.3 14.4 %collective-permute-start.4 = (bf16[2,512,32]{1,2,0:T(8,128)(2,1)}, bf16[2,512,32]{1,2,0:T(8,128)(2,1)}, u32[]{:S(2)}, u32[]{:S(2)}) collective-permute-start(bf16[2,512,32]{1,2,0:T(8,128)(2,1)} %get-tuple-element.23), channel_id=1, source_target_pairs={{0,4},{4,0},{8,12},{12,8},{16,20},{20,16},{24,28},{28,24},{1,5},{5... | collective-permute-start | bytes 196616 | tf_op jit(solution)/shard_map/ppermute | solution.py:88
  116.6 14.2 %collective-permute-start.5 = (bf16[2,512,32]{1,2,0:T(8,128)(2,1)}, bf16[2,512,32]{1,2,0:T(8,128)(2,1)}, u32[]{:S(2)}, u32[]{:S(2)}) collective-permute-start(bf16[2,512,32]{1,2,0:T(8,128)(2,1)} %get-tuple-element.23), channel_id=1, source_target_pairs={{0,8},{4,12},{8,0},{12,4},{16,24},{20,28},{24,16},{28,20},{1,9},{5... | collective-permute-start | bytes 196616 | tf_op jit(solution)/shard_map/ppermute | solution.py:88
  116.6 14.2 %collective-permute-start.6 = (bf16[2,512,32]{1,2,0:T(8,128)(2,1)}, bf16[2,512,32]{1,2,0:T(8,128)(2,1)}, u32[]{:S(2)}, u32[]{:S(2)}) collective-permute-start(bf16[2,512,32]{1,2,0:T(8,128)(2,1)} %get-tuple-element.23), channel_id=1, source_target_pairs={{0,12},{4,8},{8,4},{12,0},{16,28},{20,24},{24,20},{28,16},{1,13},{... | collective-permute-start | bytes 196616 | tf_op jit(solution)/shard_map/ppermute | solution.py:88
  125.6 6.7 %copy-start.10 = (pred[4]{0:T(512)(128)(4,1)S(1)}, pred[4]{0:T(512)(128)(4,1)}, u32[]{:S(2)}) copy-start(pred[4]{0:T(512)(128)(4,1)} %compare_and_fusion) | copy-start | bytes 16
  127.1 11.7 %all-to-all-start = ((bf16[4,16,512]{2,1,0:T(8,128)(2,1)}), bf16[4,16,512]{2,1,0:T(8,128)(2,1)S(1)}, u32[]{:S(2)}, u32[]{:S(2)}) async-start(bf16[4,16,512]{2,1,0:T(8,128)(2,1)} %bitcast.17), calls=%async_computation | async-start | bytes 131072 | tf_op jit(solution)/shard_map/all_to_all | solution.py:162
  132.4 18.4 %copy-start.9 = (pred[1024]{0:T(1024)(128)(4,1)S(1)}, pred[1024]{0:T(1024)(128)(4,1)}, u32[]{:S(2)}) copy-start(pred[1024]{0:T(1024)(128)(4,1)} %broadcast_compare_fusion) | copy-start | bytes 3076
  132.5 18.3 %collective-permute-start.7 = (bf16[512,128]{0,1:T(8,128)(2,1)S(1)}, bf16[512,128]{0,1:T(8,128)(2,1)S(1)}, u32[]{:S(2)}, u32[]{:S(2)}) collective-permute-start(bf16[512,128]{0,1:T(8,128)(2,1)S(1)} %bitcast.59), channel_id=1, source_target_pairs={{0,1},{1,2},{2,3},{4,5},{5,6},{6,7},{8,9},{9,10},{10,11},{12,13},{... | collective-permute-start | bytes 393224 | tf_op jit(solution)/shard_map/ppermute | solution.py:19
  138.9 8.1 %all-to-all-start.1 = ((bf16[4,16,512]{2,1,0:T(8,128)(2,1)}), bf16[4,16,512]{2,1,0:T(8,128)(2,1)S(1)}, u32[]{:S(2)}, u32[]{:S(2)}) async-start(bf16[4,16,512]{2,1,0:T(8,128)(2,1)} %bitcast.18), calls=%async_computation.1 | async-start | bytes 131072 | tf_op jit(solution)/shard_map/all_to_all | solution.py:163
  148.1 5.1 %collective-permute-start.8 = (bf16[512,128]{0,1:T(8,128)(2,1)S(1)}, bf16[512,128]{0,1:T(8,128)(2,1)S(1)}, u32[]{:S(2)}, u32[]{:S(2)}) collective-permute-start(bf16[512,128]{0,1:T(8,128)(2,1)S(1)} %bitcast.57), channel_id=1, source_target_pairs={{0,1},{1,2},{2,3},{4,5},{5,6},{6,7},{8,9},{9,10},{10,11},{12,13},{... | collective-permute-start | bytes 393224 | tf_op jit(solution)/shard_map/ppermute | solution.py:19
  152.5 0.7 copy-start.8
Sparse Core Ops, SparseCore 0:
  9.6 84.7 all-gather.1

commit v2 on v1

--- a/solution.py
+++ b/solution.py
@@ -64,10 +64,18 @@
         got = lax.ppermute(local_weights, "gy", partner_route(gy_count, gy_count, k))
         pieces.append((my_gy ^ k, got))
 
-    gain_part = norm_gain.astype(jnp.float32)
-    piece_float = lax.all_gather(tokens_in, "gx", axis=1, tiled=True).astype(jnp.float32)
-    normed = (piece_float * gain_part[None, :]).astype(jnp.bfloat16)
-    squares = jnp.sum(piece_float * piece_float, axis=1)
+    local_float = tokens_in.astype(jnp.float32)
+    my_gx = lax.axis_index("gx")
+    feature_block = tokens_in.shape[1]
+    local_gain = lax.dynamic_slice_in_dim(norm_gain, my_gx * feature_block, feature_block, 0)
+    local_normed = (local_float * local_gain.astype(jnp.float32)[None, :]).astype(jnp.bfloat16)
+    local_squares = jnp.sum(local_float * local_float, axis=1)
+    square_parts = [local_squares]
+    for k in range(1, gx_count):
+        square_parts.append(lax.ppermute(local_squares, "gx", partner_route(gx_count, gx_count, k)))
+    square_order = jnp.arange(gx_count, dtype=jnp.int32) ^ my_gx
+    squares = jnp.sum(jnp.take(jnp.stack(square_parts), square_order, axis=0), axis=0)
+    normed = lax.all_gather(local_normed, "gx", axis=1, tiled=True)
     products = None
     for source, block in pieces:
         rows = lax.dynamic_slice_in_dim(normed, source * row_block, row_block, 1)
@@ -82,31 +90,34 @@
     key_piece = rotate(key_proj, positions, quarter, spot * (quarter // 2)).astype(jnp.bfloat16)
     value_piece = value_proj.astype(jnp.bfloat16)
 
-    own_kv = jnp.stack([key_piece, value_piece])
-    kv_parts = [own_kv]
-    for k in range(1, quarters):
-        kv_parts.append(lax.ppermute(own_kv, "gx", partner_route(gx_count, quarters, k)))
-    kv_stack = jnp.stack(kv_parts)
-    order = jnp.arange(quarters, dtype=jnp.int32) ^ spot
-    kv_full = jnp.take(kv_stack, order, axis=0)
-    kv_full = kv_full.transpose(1, 2, 0, 3).reshape(2, token_count, HD)
-    full_keys = kv_full[0]
-    full_values = kv_full[1]
-
     span_count = gy_count // 4
     marks = segment_ids + 1
-    key_list = [full_keys]
-    value_list = [full_values]
+    own_kv = jnp.stack([key_piece, value_piece])
+    order = jnp.arange(quarters, dtype=jnp.int32) ^ spot
+
+    def assembled(parts):
+        stack = jnp.take(jnp.stack(parts), order, axis=0)
+        return stack.transpose(1, 2, 0, 3).reshape(2, token_count, HD)
+
+    here = [own_kv]
+    for k in range(1, quarters):
+        here.append(lax.ppermute(own_kv, "gx", partner_route(gx_count, quarters, k)))
+    kv_blocks = [assembled(here)]
     mark_list = [marks]
     for shift_by in range(1, span_count + 1):
-        moved_keys, moved_values, moved_marks = shifted(
-            (full_keys, full_values, marks), "gy", shift_by
-        )
-        key_list.insert(0, moved_keys)
-        value_list.insert(0, moved_values)
-        mark_list.insert(0, moved_marks)
-    window_keys = jnp.concatenate(key_list, axis=0)
-    window_values = jnp.concatenate(value_list, axis=0)
+        earlier_parts = []
+        for k in range(quarters):
+            route = []
+            for i in range(gx_count):
+                peer = i - i % quarters + ((i % quarters) ^ k)
+                for j in range(gy_count - shift_by):
+                    route.append((i * gy_count + j, peer * gy_count + j + shift_by))
+            earlier_parts.append(lax.ppermute(own_kv, ("gx", "gy"), route))
+        kv_blocks.insert(0, assembled(earlier_parts))
+        mark_list.insert(0, shifted(marks, "gy", shift_by))
+    window_kv = jnp.concatenate(kv_blocks, axis=1)
+    window_keys = window_kv[0]
+    window_values = window_kv[1]
     window_marks = jnp.concatenate(mark_list, axis=0)
     reach_rows = span_count * token_count
     query_rows = (
@@ -146,24 +157,17 @@
     earlier = jnp.cumsum(one_hot, axis=0) - one_hot
     rank_in = jnp.sum(earlier * one_hot, axis=1)
     slot_of = owner_of * capacity + rank_in
-    key_pages = key_piece.reshape(page_rows, PAGE * quarter)
-    value_pages = value_piece.reshape(page_rows, PAGE * quarter)
-    send_keys = (
-        jnp.zeros((owner_count * capacity, PAGE * quarter), jnp.bfloat16).at[slot_of].set(key_pages)
+    kv_pages = own_kv.reshape(2, page_rows, PAGE * quarter).transpose(1, 0, 2)
+    send_kv = (
+        jnp.zeros((owner_count * capacity, 2, PAGE * quarter), jnp.bfloat16)
+        .at[slot_of]
+        .set(kv_pages)
     )
-    send_values = (
-        jnp.zeros((owner_count * capacity, PAGE * quarter), jnp.bfloat16)
-        .at[slot_of]
-        .set(value_pages)
-    )
-    send_keys = send_keys.reshape(owner_count, capacity, PAGE * quarter)
-    send_values = send_values.reshape(owner_count, capacity, PAGE * quarter)
-    got_keys, got_values = (
-        lax.all_to_all(send_keys, "gy", split_axis=0, concat_axis=0, tiled=True),
-        lax.all_to_all(send_values, "gy", split_axis=0, concat_axis=0, tiled=True),
-    )
-    key_cache = got_keys.reshape(owner_count * capacity, PAGE, quarter)
-    value_cache = got_values.reshape(owner_count * capacity, PAGE, quarter)
+    send_kv = send_kv.reshape(owner_count, capacity, 2, PAGE * quarter)
+    got_kv = lax.all_to_all(send_kv, "gy", split_axis=0, concat_axis=0, tiled=True)
+    got_kv = got_kv.reshape(owner_count * capacity, 2, PAGE, quarter)
+    key_cache = got_kv[:, 0]
+    value_cache = got_kv[:, 1]
     return (context, key_cache, value_cache)
 
 

time: 163 us -> 156 us (0.957)
  waiting for transfers between devices: 76.9 us -> 65.5 us
  starting transfers between devices: 24 us -> 35.3 us
  other arithmetic: 16 us -> 10.5 us
    ppermute x0 -> x11, starting transfers between devices: none -> 22.7 us  [the longest x4 12.7 us: shards(): earlier_parts.append(lax.ppermute(own_kv, ('gx', 'gy'), route))]
    ppermute x3 -> x1, starting transfers between devices: 10.6 us -> 3.08 us  [shifted(): return lax.ppermute(value, axis, pairs)]
    reduce_sum x1 -> x2, other arithmetic: 9.88 us -> 2.68 us  [the longest x1 2.6 us: shards(): local_squares = jnp.sum(local_float * local_float, axis=1)]
    ppermute x3 -> x1, waiting for transfers between devices: 49.3 us -> 42.4 us  [shifted(): return lax.ppermute(value, axis, pairs)]
    all_to_all x2 -> x1, starting transfers between devices: 6.93 us -> 3.51 us  [shards(): lax.all_to_all(send_kv, 'gy', split_axis=0, concat_axis=0, tiled=True)]
    all_to_all x2 -> x1, waiting for transfers between devices: 3.12 us -> 0.01 us  [shards(): lax.all_to_all(send_kv, 'gy', split_axis=0, concat_axis=0, tiled=True)]
    all_gather x1, waiting for transfers between devices: 23.8 us -> 20.8 us  [shards(): normed = lax.all_gather(local_normed, 'gx', axis=1, tiled=True)]
    ppermute x3, waiting for transfers between devices: 0.01 us -> 1.98 us  [shards(): lax.ppermute(own_kv, 'gx', partner_route(gx_count, quarters, k))]
  transfers between devices with their start and end apart: 12 -> 20, of which waited for: 4 -> 4; matrix products, arithmetic and copies ran while one was open for 25% -> 18% of each run, Pallas kernels for 0% -> 0%
where the time goes in v2:
time: 156 us; the launch traced here: 155 us
  waiting for transfers between devices  65.5 us (42%)
  starting transfers between devices  35.3 us (23%)
  local copies, waits for them, and re-layouts  16.5 us (11%)
  between operations  14.6 us (9%)
  matrix products  13 us (8%)
  other arithmetic  10.5 us (7%)
    ppermute x1, waiting for transfers between devices, shifted(): return lax.ppermute(value, axis, pairs)  42.4 us
    all_gather x1, waiting for transfers between devices, shards(): normed = lax.all_gather(local_normed, 'gx', axis=1, tiled=True)  20.8 us
    ppermute x4, starting transfers between devices, shards(): earlier_parts.append(lax.ppermute(own_kv, ('gx', 'gy'), route))  12.7 us
    dot_general x4, matrix products, shards(): part = jnp.dot(rows, block, preferred_element_type=jnp.float32)  10.3 us
    ppermute x7, starting transfers between devices, shards(): lax.ppermute(local_squares, 'gx', partner_route(gx_count, gx_count, k))  10 us
    convert_element_type x4, local copies, waits for them, and re-layouts, shards(): rotate(key_proj, positions, quarter, spot * (quarter // 2))  5.36 us
    ppermute x3, starting transfers between devices, shards(): lax.ppermute(local_weights, 'gy', partner_route(gy_count, gy_count, k))  3.7 us
    all_to_all x1, starting transfers between devices, shards(): lax.all_to_all(send_kv, 'gy', split_axis=0, concat_axis=0, tiled=True)  3.51 us
  transfers between devices with their start and end apart: 20, of which 4 were waited for; matrix products, arithmetic and copies ran while one was open for 18% of the time, Pallas kernels for 0%

profile of v2, /device:TPU:0, one launch (start us, length us, event | category | flops | bytes accessed | tf_op | source)
XLA Modules:
  0.0 155.4 jit_solution(303463831903954331)
XLA Ops:
  7.2 0.8 dynamic-slice_convert_fusion
  8.0 2.6 %fusion.4 = (f32[512]{0:T(512)S(1)}, bf16[512,1024]{1,0:T(8,128)(2,1)}) fusion(bf16[512,1024]{1,0:T(8,128)(2,1)} %param.10, f32[1024]{0:T(1024)S(1)} %dynamic-slice_convert_fusion), kind=kLoop, calls=%fused_computation.13 | loop fusion | flops 2620928 | bytes 2103296 | tf_op jit(solution)/shard_map/reduce_sum | solution.py:72
  11.2 2.6 %collective-permute-start.5 = (f32[512]{0:T(512)S(1)}, f32[512]{0:T(512)S(1)}, u32[]{:S(2)}, u32[]{:S(2)}) collective-permute-start(f32[512]{0:T(512)S(1)} %get-tuple-element.13), channel_id=1, source_target_pairs={{0,8},{4,12},{8,0},{12,4},{16,24},{20,28},{24,16},{28,20},{1,9},{5... | collective-permute-start | bytes 6152 | tf_op jit(solution)/shard_map/ppermute | solution.py:75
  13.9 0.6 copy.46
  14.7 1.7 %collective-permute-start.2 = (bf16[2048,320]{0,1:T(8,128)(2,1)S(1)}, bf16[2048,320]{0,1:T(8,128)(2,1)}, u32[]{:S(2)}, u32[]{:S(2)}) collective-permute-start(bf16[2048,320]{0,1:T(8,128)(2,1)S(1)} %pad_maximum_fusion), channel_id=1, source_target_pairs={{0,2},{1,3},{2,0},{3,1},{4,6},{5,7},{6,4},{7,5},{8,10},{9,11},{10,... | collective-permute-start | bytes 3932168 | tf_op jit(solution)/shard_map/ppermute | solution.py:64
  16.4 1.4 collective-permute-start.3
  18.8 0.5 multiply_cosine_fusion
  19.4 2.7 %collective-permute-start.7 = (f32[512]{0:T(512)S(1)}, f32[512]{0:T(512)S(1)}, u32[]{:S(2)}, u32[]{:S(2)}) collective-permute-start(f32[512]{0:T(512)S(1)} %get-tuple-element.13), channel_id=1, source_target_pairs={{0,16},{4,20},{8,24},{12,28},{16,0},{20,4},{24,8},{28,12},{1,17},{... | collective-permute-start | bytes 6152 | tf_op jit(solution)/shard_map/ppermute | solution.py:75
  22.1 3.1 %collective-permute-start.9 = (f32[512]{0:T(512)S(1)}, f32[512]{0:T(512)S(1)}, u32[]{:S(2)}, u32[]{:S(2)}) collective-permute-start(f32[512]{0:T(512)S(1)} %get-tuple-element.13), channel_id=1, source_target_pairs={{0,24},{4,28},{8,16},{12,20},{16,8},{20,12},{24,0},{28,4},{1,25},{... | collective-permute-start | bytes 6152 | tf_op jit(solution)/shard_map/ppermute | solution.py:75
  25.2 1.0 collective-permute-start.10
  26.2 0.5 collective-permute-start.1
  26.7 0.6 compare_and_fusion
  27.6 3.1 %collective-permute-start = (s32[512]{0:T(512)S(1)}, s32[512]{0:T(512)S(1)}, u32[]{:S(2)}, u32[]{:S(2)}) collective-permute-start(s32[512]{0:T(512)S(1)} %broadcast_add_fusion), channel_id=1, source_target_pairs={{0,1},{1,2},{2,3},{4,5},{5,6},{6,7},{8,9},{9,10},{10,11},{12,13},{... | collective-permute-start | bytes 6152 | tf_op jit(solution)/shard_map/ppermute | solution.py:19
  30.8 0.6 ge.29
  31.4 0.6 gather_fusion
  31.9 42.4 %collective-permute-done = s32[512]{0:T(512)S(1)} collective-permute-done((s32[512]{0:T(512)S(1)}, s32[512]{0:T(512)S(1)}, u32[]{:S(2)}, u32[]{:S(2)}) %collective-permute-start) | collective-permute-done | bytes 2080 | tf_op jit(solution)/shard_map/ppermute | solution.py:19
  74.3 0.6 broadcast_compare_fusion
  75.0 20.8 %all-gather.2.cloned.1.call-done = bf16[512,8192]{1,0:T(8,128)(2,1)} async-done(((bf16[512,1024]{1,0:T(8,128)(2,1)}), bf16[512,8192]{1,0:T(8,128)(2,1)}) %all-gather.2.cloned.1.call-update) | async-done | bytes 8388624 | tf_op jit(solution)/shard_map/all_gather | solution.py:78
  95.8 2.6 %fusion.14 = f32[512,320]{0,1:T(8,128)S(1)} fusion(bf16[512,8192]{1,0:T(8,128)(2,1)} %all-gather.2.cloned.1.call-done, s32[]{:T(128)S(6)} %select_n.65, bf16[2048,32]{0,1:T(8,128)(2,1)S(1)} %copy-done.2, bf16[2048,32]{0,1:T(8,128)(2,1)S(1)} %copy-done.3, bf16[2048,256]{0,1:T(8,128)(2,1)S(1)} %copy.46), kind=kOutput, calls=%fused_computation.22 | convolution fusion | flops 675020800 | bytes 4063236 | tf_op jit(solution)/shard_map/dot_general | solution.py:82
  98.4 3.2 %fusion.10 = f32[512,320]{0,1:T(8,128)S(1)} fusion(bf16[2048,320]{0,1:T(8,128)(2,1)} %collective-permute-done.2, bf16[512,8192]{1,0:T(8,128)(2,1)} %all-gather.2.cloned.1.call-done, s32[]{:T(128)S(6)} %select_n.67), kind=kOutput, calls=%fused_computation.18 | convolution fusion | flops 671088640 | bytes 4063236 | tf_op jit(solution)/shard_map/dot_general | solution.py:82
  101.7 2.2 %fusion.8 = f32[512,320]{0,1:T(8,128)S(1)} fusion(bf16[2048,320]{0,1:T(8,128)(2,1)} %collective-permute-done.3, bf16[512,8192]{1,0:T(8,128)(2,1)S(1)} %copy-done.10, s32[]{:T(128)S(6)} %select_n.68), kind=kOutput, calls=%fused_computation.16 | convolution fusion | flops 671088640 | bytes 4063236 | tf_op jit(solution)/shard_map/dot_general | solution.py:82
  103.9 2.3 %fusion.28 = f32[512,320]{0,1:T(8,128)S(1)} fusion(f32[512,320]{0,1:T(8,128)S(1)} %fusion.8, f32[512,320]{0,1:T(8,128)S(1)} %fusion.10, f32[512,320]{0,1:T(8,128)S(1)} %fusion.14, bf16[2048,320]{0,1:T(8,128)(2,1)} %collective-permute-done.1, bf16[512,8192]{1,0:T(8,128)(2,1)S(1)} %copy-done.10, s32[]{:T(128)S(6)} %select_n.66, f32[512]{0:T(512)S(1)} %add_rsqrt_fusion), kind=kOutput, calls=%fused_computation.29 | convolution fusion | flops 671744000 | bytes 6031364 | tf_op jit(solution)/shard_map/dot_general | solution.py:82
  106.2 0.6 slice.77
  107.1 2.1 %copy.56 = bf16[512,1,16,2]{3,2,0,1:T(8,128)(2,1)S(1)} copy(bf16[512,1,16,2]{0,2,3,1:T(8,128)(2,1)S(1)} %maximum_convert_fusion) | data formatting | bytes 65536 | tf_op jit(solution)/shard_map/convert_element_type | solution.py:90
  109.3 0.7 fusion.61
  109.9 3.8 %collective-permute-start.11 = (bf16[2,512,32]{1,2,0:T(8,128)(2,1)}, bf16[2,512,32]{1,2,0:T(8,128)(2,1)}, u32[]{:S(2)}, u32[]{:S(2)}) collective-permute-start(bf16[2,512,32]{1,2,0:T(8,128)(2,1)} %get-tuple-element.24), channel_id=1, source_target_pairs={{0,1},{1,2},{2,3},{4,5},{5,6},{6,7},{8,9},{9,10},{10,11},{12,13},{... | collective-permute-start | bytes 196616 | tf_op jit(solution)/shard_map/ppermute | solution.py:115
  113.8 3.1 %collective-permute-start.12 = (bf16[2,512,32]{1,2,0:T(8,128)(2,1)}, bf16[2,512,32]{1,2,0:T(8,128)(2,1)}, u32[]{:S(2)}, u32[]{:S(2)}) collective-permute-start(bf16[2,512,32]{1,2,0:T(8,128)(2,1)} %get-tuple-element.24), channel_id=1, source_target_pairs={{0,5},{1,6},{2,7},{4,1},{5,2},{6,3},{8,13},{9,14},{10,15},{12,9},{... | collective-permute-start | bytes 196616 | tf_op jit(solution)/shard_map/ppermute | solution.py:115
  116.9 1.9 %collective-permute-start.13 = (bf16[2,512,32]{1,2,0:T(8,128)(2,1)}, bf16[2,512,32]{1,2,0:T(8,128)(2,1)}, u32[]{:S(2)}, u32[]{:S(2)}) collective-permute-start(bf16[2,512,32]{1,2,0:T(8,128)(2,1)} %get-tuple-element.24), channel_id=1, source_target_pairs={{0,9},{1,10},{2,11},{4,13},{5,14},{6,15},{8,1},{9,2},{10,3},{12,5}... | collective-permute-start | bytes 196616 | tf_op jit(solution)/shard_map/ppermute | solution.py:115
  118.8 3.9 %collective-permute-start.14 = (bf16[2,512,32]{1,2,0:T(8,128)(2,1)}, bf16[2,512,32]{1,2,0:T(8,128)(2,1)}, u32[]{:S(2)}, u32[]{:S(2)}) collective-permute-start(bf16[2,512,32]{1,2,0:T(8,128)(2,1)} %get-tuple-element.24), channel_id=1, source_target_pairs={{0,13},{1,14},{2,15},{4,9},{5,10},{6,11},{8,5},{9,6},{10,7},{12,1}... | collective-permute-start | bytes 196616 | tf_op jit(solution)/shard_map/ppermute | solution.py:115
  122.7 0.8 collective-permute-start.15
  123.5 3.2 %convert_element_type.84 = bf16[1,32,512]{2,1,0:T(8,128)(2,1)S(1)} reshape(bf16[512,1,16,2]{3,2,0,1:T(8,128)(2,1)S(1)} %copy.56) | data formatting | bytes 65536 | tf_op jit(solution)/shard_map/convert_element_type | solution.py:90
  126.8 0.9 copy.57
  128.0 1.6 %scatter_fusion = bf16[64,2,512]{2,1,0:T(2,128)(2,1)S(1)} fusion(bf16[64,2,512]{2,1,0:T(2,128)(2,1)S(1)} %broadcast_in_dim.61, s32[32]{0:T(128)} %fusion.58, bf16[32,2,512]{2,1,0:T(2,128)(2,1)S(1)} %copy.58), kind=kCustom, calls=%fused_computation.3 | custom fusion | bytes 196736 | tf_op jit(solution)/shard_map/scatter | solution.py:164
  129.6 0.7 copy.59
  130.3 3.5 %all-to-all-start = ((bf16[4,16,2,512]{3,1,2,0:T(8,128)(2,1)}), bf16[4,16,2,512]{3,1,2,0:T(8,128)(2,1)S(1)}, u32[]{:S(2)}, u32[]{:S(2)}) async-start(bf16[4,16,2,512]{3,1,2,0:T(8,128)(2,1)} %copy.59), calls=%async_computation | async-start | bytes 262144 | tf_op jit(solution)/shard_map/all_to_all | solution.py:167
  134.5 0.5 subtract_convert_fusion
  136.0 1.1 collective-permute-start.17
  137.1 1.0 pad_maximum_fusion.3
  138.1 0.6 gather_fusion.1
  138.7 2.0 %collective-permute-done.16 = bf16[2,512,32]{1,2,0:T(8,128)(2,1)S(1)} collective-permute-done((bf16[2,512,32]{1,2,0:T(8,128)(2,1)}, bf16[2,512,32]{1,2,0:T(8,128)(2,1)S(1)}, u32[]{:S(2)}, u32[]{:S(2)}) %collective-permute-start.16) | collective-permute-done | bytes 65568 | tf_op jit(solution)/shard_map/ppermute | solution.py:104
  140.6 0.9 pad_maximum_fusion.4
  141.5 0.6 gather_fusion.2
  142.3 1.7 %fusion.64 = (f32[1024]{0:T(1024)S(1)}, f32[1024,1024]{0,1:T(8,128)S(1)}) fusion(bf16[1024,128]{1,0:T(8,128)(2,1)S(1)} %bitcast.88, bf16[2,512,128]{1,2,0:T(8,128)(2,1)S(1)} %bitcast.90, bf16[2,512,128]{1,2,0:T(8,128)(2,1)S(1)} %bitcast.92, s32[1024]{0:T(1024)S(1)} %bitcast.99, pred[1024]{0:T(1024)(128)(4,1)S(1)} %copy-done.8, s32[1024]{0:T(1024)S(1)} %bitcast.98, ...), kind=kOutput, calls=%fused_computation.97 | convolution fusion | flops 276298752 | bytes 4998144 | tf_op jit(solution)/shard_map/dot_general | solution.py:128
  144.1 0.6 fusion.1
  144.7 0.9 fusion.34
  145.6 0.7 copy.79
  146.7 0.9 copy.61
  147.6 0.9 copy.62
  (92 shorter events, 5.1 us)
Async XLA Ops:
  7.2 6.7 %copy-start = (bf16[2048,256]{1,0:T(8,128)(2,1)S(1)}, bf16[2048,256]{1,0:T(8,128)(2,1)}, u32[]{:S(2)}) copy-start(bf16[2048,256]{1,0:T(8,128)(2,1)} %param.12) | copy-start | bytes 3145732
  7.2 88.6 %all-gather.2.cloned.1.call-start = ((), (), s32[]{:S(2)}) async-start(), calls=%async_computation.1 | async-start | bytes 9437184 | tf_op jit(solution)/shard_map/all_gather | solution.py:78
  8.0 6.5 %copy-start.2 = (bf16[2048,32]{0,1:T(8,128)(2,1)S(1)}, bf16[2048,32]{0,1:T(8,128)(2,1)}, u32[]{:S(2)}) copy-start(bf16[2048,32]{0,1:T(8,128)(2,1)} %param.14) | copy-start | bytes 393220
  8.0 6.6 %copy-start.3 = (bf16[2048,32]{0,1:T(8,128)(2,1)S(1)}, bf16[2048,32]{0,1:T(8,128)(2,1)}, u32[]{:S(2)}) copy-start(bf16[2048,32]{0,1:T(8,128)(2,1)} %param.13) | copy-start | bytes 393220
  10.6 7.3 %copy-start.5 = (s32[32,1]{0,1:T(1,128)S(1)}, s32[32,1]{0,1:T(1,128)}, u32[]{:S(2)}) copy-start(s32[32,1]{0,1:T(1,128)} %param.17) | copy-start | bytes 388
  10.6 8.1 %copy-start.4 = (s32[512]{0:T(512)S(1)}, s32[512]{0:T(512)}, u32[]{:S(2)}) copy-start(s32[512]{0:T(512)} %param.15) | copy-start | bytes 6148
  10.6 8.2 %copy-start.6 = (s32[512]{0:T(512)S(1)}, s32[512]{0:T(512)}, u32[]{:S(2)}) copy-start(s32[512]{0:T(512)} %param.16) | copy-start | bytes 6148
  10.7 8.7 %collective-permute-start.4 = (f32[512]{0:T(512)S(1)}, f32[512]{0:T(512)S(1)}, u32[]{:S(2)}, u32[]{:S(2)}) collective-permute-start(f32[512]{0:T(512)S(1)} %get-tuple-element.13), channel_id=1, source_target_pairs={{0,4},{4,0},{8,12},{12,8},{16,20},{20,16},{24,28},{28,24},{1,5},{5... | collective-permute-start | bytes 6152 | tf_op jit(solution)/shard_map/ppermute | solution.py:75
  11.2 10.9 %collective-permute-start.5 = (f32[512]{0:T(512)S(1)}, f32[512]{0:T(512)S(1)}, u32[]{:S(2)}, u32[]{:S(2)}) collective-permute-start(f32[512]{0:T(512)S(1)} %get-tuple-element.13), channel_id=1, source_target_pairs={{0,8},{4,12},{8,0},{12,4},{16,24},{20,28},{24,16},{28,20},{1,9},{5... | collective-permute-start | bytes 6152 | tf_op jit(solution)/shard_map/ppermute | solution.py:75
  13.8 8.2 %collective-permute-start.6 = (f32[512]{0:T(512)S(1)}, f32[512]{0:T(512)S(1)}, u32[]{:S(2)}, u32[]{:S(2)}) collective-permute-start(f32[512]{0:T(512)S(1)} %get-tuple-element.13), channel_id=1, source_target_pairs={{0,12},{4,8},{8,4},{12,0},{16,28},{20,24},{24,20},{28,16},{1,13},{... | collective-permute-start | bytes 6152 | tf_op jit(solution)/shard_map/ppermute | solution.py:75
  14.7 83.7 %collective-permute-start.2 = (bf16[2048,320]{0,1:T(8,128)(2,1)S(1)}, bf16[2048,320]{0,1:T(8,128)(2,1)}, u32[]{:S(2)}, u32[]{:S(2)}) collective-permute-start(bf16[2048,320]{0,1:T(8,128)(2,1)S(1)} %pad_maximum_fusion), channel_id=1, source_target_pairs={{0,2},{1,3},{2,0},{3,1},{4,6},{5,7},{6,4},{7,5},{8,10},{9,11},{10,... | collective-permute-start | bytes 3932168 | tf_op jit(solution)/shard_map/ppermute | solution.py:64
  16.4 85.2 %collective-permute-start.3 = (bf16[2048,320]{0,1:T(8,128)(2,1)S(1)}, bf16[2048,320]{0,1:T(8,128)(2,1)}, u32[]{:S(2)}, u32[]{:S(2)}) collective-permute-start(bf16[2048,320]{0,1:T(8,128)(2,1)S(1)} %pad_maximum_fusion), channel_id=1, source_target_pairs={{0,3},{1,2},{2,1},{3,0},{4,7},{5,6},{6,5},{7,4},{8,11},{9,10},{10,... | collective-permute-start | bytes 3932168 | tf_op jit(solution)/shard_map/ppermute | solution.py:64
  19.4 5.8 %collective-permute-start.7 = (f32[512]{0:T(512)S(1)}, f32[512]{0:T(512)S(1)}, u32[]{:S(2)}, u32[]{:S(2)}) collective-permute-start(f32[512]{0:T(512)S(1)} %get-tuple-element.13), channel_id=1, source_target_pairs={{0,16},{4,20},{8,24},{12,28},{16,0},{20,4},{24,8},{28,12},{1,17},{... | collective-permute-start | bytes 6152 | tf_op jit(solution)/shard_map/ppermute | solution.py:75
  22.0 4.1 %collective-permute-start.8 = (f32[512]{0:T(512)S(1)}, f32[512]{0:T(512)S(1)}, u32[]{:S(2)}, u32[]{:S(2)}) collective-permute-start(f32[512]{0:T(512)S(1)} %get-tuple-element.13), channel_id=1, source_target_pairs={{0,20},{4,16},{8,28},{12,24},{16,4},{20,0},{24,12},{28,8},{1,21},{... | collective-permute-start | bytes 6152 | tf_op jit(solution)/shard_map/ppermute | solution.py:75
  22.1 5.5 %collective-permute-start.9 = (f32[512]{0:T(512)S(1)}, f32[512]{0:T(512)S(1)}, u32[]{:S(2)}, u32[]{:S(2)}) collective-permute-start(f32[512]{0:T(512)S(1)} %get-tuple-element.13), channel_id=1, source_target_pairs={{0,24},{4,28},{8,16},{12,20},{16,8},{20,12},{24,0},{28,4},{1,25},{... | collective-permute-start | bytes 6152 | tf_op jit(solution)/shard_map/ppermute | solution.py:75
  25.2 6.2 %collective-permute-start.10 = (f32[512]{0:T(512)S(1)}, f32[512]{0:T(512)S(1)}, u32[]{:S(2)}, u32[]{:S(2)}) collective-permute-start(f32[512]{0:T(512)S(1)} %get-tuple-element.13), channel_id=1, source_target_pairs={{0,28},{4,24},{8,20},{12,16},{16,12},{20,8},{24,4},{28,0},{1,29},{... | collective-permute-start | bytes 6152 | tf_op jit(solution)/shard_map/ppermute | solution.py:75
  26.2 77.7 %collective-permute-start.1 = (bf16[2048,320]{0,1:T(8,128)(2,1)S(1)}, bf16[2048,320]{0,1:T(8,128)(2,1)}, u32[]{:S(2)}, u32[]{:S(2)}) collective-permute-start(bf16[2048,320]{0,1:T(8,128)(2,1)S(1)} %pad_maximum_fusion), channel_id=1, source_target_pairs={{0,1},{1,0},{2,3},{3,2},{4,5},{5,4},{6,7},{7,6},{8,9},{9,8},{10,11... | collective-permute-start | bytes 3932168 | tf_op jit(solution)/shard_map/ppermute | solution.py:64
  27.6 46.7 %collective-permute-start = (s32[512]{0:T(512)S(1)}, s32[512]{0:T(512)S(1)}, u32[]{:S(2)}, u32[]{:S(2)}) collective-permute-start(s32[512]{0:T(512)S(1)} %broadcast_add_fusion), channel_id=1, source_target_pairs={{0,1},{1,2},{2,3},{4,5},{5,6},{6,7},{8,9},{9,10},{10,11},{12,13},{... | collective-permute-start | bytes 6152 | tf_op jit(solution)/shard_map/ppermute | solution.py:19
  95.8 5.9 %copy-start.10 = (bf16[512,8192]{1,0:T(8,128)(2,1)S(1)}, bf16[512,8192]{1,0:T(8,128)(2,1)}, u32[]{:S(2)}) copy-start(bf16[512,8192]{1,0:T(8,128)(2,1)} %all-gather.2.cloned.1.call-done) | copy-start | bytes 25165828
  109.9 25.7 %collective-permute-start.11 = (bf16[2,512,32]{1,2,0:T(8,128)(2,1)}, bf16[2,512,32]{1,2,0:T(8,128)(2,1)}, u32[]{:S(2)}, u32[]{:S(2)}) collective-permute-start(bf16[2,512,32]{1,2,0:T(8,128)(2,1)} %get-tuple-element.24), channel_id=1, source_target_pairs={{0,1},{1,2},{2,3},{4,5},{5,6},{6,7},{8,9},{9,10},{10,11},{12,13},{... | collective-permute-start | bytes 196616 | tf_op jit(solution)/shard_map/ppermute | solution.py:115
  113.8 22.2 %collective-permute-start.12 = (bf16[2,512,32]{1,2,0:T(8,128)(2,1)}, bf16[2,512,32]{1,2,0:T(8,128)(2,1)}, u32[]{:S(2)}, u32[]{:S(2)}) collective-permute-start(bf16[2,512,32]{1,2,0:T(8,128)(2,1)} %get-tuple-element.24), channel_id=1, source_target_pairs={{0,5},{1,6},{2,7},{4,1},{5,2},{6,3},{8,13},{9,14},{10,15},{12,9},{... | collective-permute-start | bytes 196616 | tf_op jit(solution)/shard_map/ppermute | solution.py:115
  116.9 20.2 %collective-permute-start.13 = (bf16[2,512,32]{1,2,0:T(8,128)(2,1)}, bf16[2,512,32]{1,2,0:T(8,128)(2,1)}, u32[]{:S(2)}, u32[]{:S(2)}) collective-permute-start(bf16[2,512,32]{1,2,0:T(8,128)(2,1)} %get-tuple-element.24), channel_id=1, source_target_pairs={{0,9},{1,10},{2,11},{4,13},{5,14},{6,15},{8,1},{9,2},{10,3},{12,5}... | collective-permute-start | bytes 196616 | tf_op jit(solution)/shard_map/ppermute | solution.py:115
  118.8 18.3 %collective-permute-start.14 = (bf16[2,512,32]{1,2,0:T(8,128)(2,1)}, bf16[2,512,32]{1,2,0:T(8,128)(2,1)}, u32[]{:S(2)}, u32[]{:S(2)}) collective-permute-start(bf16[2,512,32]{1,2,0:T(8,128)(2,1)} %get-tuple-element.24), channel_id=1, source_target_pairs={{0,13},{1,14},{2,15},{4,9},{5,10},{6,11},{8,5},{9,6},{10,7},{12,1}... | collective-permute-start | bytes 196616 | tf_op jit(solution)/shard_map/ppermute | solution.py:115
  122.7 16.0 %collective-permute-start.15 = (bf16[2,512,32]{1,2,0:T(8,128)(2,1)}, bf16[2,512,32]{1,2,0:T(8,128)(2,1)}, u32[]{:S(2)}, u32[]{:S(2)}) collective-permute-start(bf16[2,512,32]{1,2,0:T(8,128)(2,1)} %get-tuple-element.24), channel_id=1, source_target_pairs={{0,4},{4,0},{8,12},{12,8},{16,20},{20,16},{24,28},{28,24},{1,5},{5... | collective-permute-start | bytes 196616 | tf_op jit(solution)/shard_map/ppermute | solution.py:104
  130.3 16.1 %all-to-all-start = ((bf16[4,16,2,512]{3,1,2,0:T(8,128)(2,1)}), bf16[4,16,2,512]{3,1,2,0:T(8,128)(2,1)S(1)}, u32[]{:S(2)}, u32[]{:S(2)}) async-start(bf16[4,16,2,512]{3,1,2,0:T(8,128)(2,1)} %copy.59), calls=%async_computation | async-start | bytes 262144 | tf_op jit(solution)/shard_map/all_to_all | solution.py:167
  134.5 6.1 %copy-start.1 = (bf16[1,2,512,32]{2,3,1,0:T(8,128)(2,1)S(1)}, bf16[1,2,512,32]{2,3,1,0:T(8,128)(2,1)}, u32[]{:S(2)}) copy-start(bf16[1,2,512,32]{2,3,1,0:T(8,128)(2,1)} %get-tuple-element.23) | copy-start | bytes 196612
  135.7 5.0 %collective-permute-start.16 = (bf16[2,512,32]{1,2,0:T(8,128)(2,1)}, bf16[2,512,32]{1,2,0:T(8,128)(2,1)S(1)}, u32[]{:S(2)}, u32[]{:S(2)}) collective-permute-start(bf16[2,512,32]{1,2,0:T(8,128)(2,1)} %get-tuple-element.24), channel_id=1, source_target_pairs={{0,8},{4,12},{8,0},{12,4},{16,24},{20,28},{24,16},{28,20},{1,9},{5... | collective-permute-start | bytes 196616 | tf_op jit(solution)/shard_map/ppermute | solution.py:104
  136.0 4.6 %collective-permute-start.17 = (bf16[2,512,32]{1,2,0:T(8,128)(2,1)}, bf16[2,512,32]{1,2,0:T(8,128)(2,1)S(1)}, u32[]{:S(2)}, u32[]{:S(2)}) collective-permute-start(bf16[2,512,32]{1,2,0:T(8,128)(2,1)} %get-tuple-element.24), channel_id=1, source_target_pairs={{0,12},{4,8},{8,4},{12,0},{16,28},{20,24},{24,20},{28,16},{1,13},{... | collective-permute-start | bytes 196616 | tf_op jit(solution)/shard_map/ppermute | solution.py:104
  137.1 5.0 %copy-start.9 = (pred[4]{0:T(512)(128)(4,1)S(1)}, pred[4]{0:T(512)(128)(4,1)}, u32[]{:S(2)}) copy-start(pred[4]{0:T(512)(128)(4,1)} %compare_and_fusion) | copy-start | bytes 16
  138.6 3.6 %copy-start.8 = (pred[1024]{0:T(1024)(128)(4,1)S(1)}, pred[1024]{0:T(1024)(128)(4,1)}, u32[]{:S(2)}) copy-start(pred[1024]{0:T(1024)(128)(4,1)} %broadcast_compare_fusion) | copy-start | bytes 3076
  144.0 0.6 copy-start.7
Sparse Core Ops, SparseCore 0:
  10.7 85.0 all-gather.1

commit v3 on v2

--- a/solution.py
+++ b/solution.py
@@ -58,11 +58,31 @@
     my_gy = lax.axis_index("gy")
     row_block = query_weight.shape[0]
 
-    local_weights = jnp.concatenate([query_weight, key_weight, value_weight], axis=1)
+    kv_weights = jnp.stack([key_weight, value_weight])
+    kv_order = jnp.arange(quarters, dtype=jnp.int32) ^ spot
+    kv_parts = [kv_weights]
+    for k in range(1, quarters):
+        kv_parts.append(lax.ppermute(kv_weights, "gx", partner_route(gx_count, quarters, k)))
+    kv_full = jnp.take(jnp.stack(kv_parts), kv_order, axis=0)
+    kv_full = kv_full.transpose(1, 2, 0, 3).reshape(2, row_block, HD)
+    local_weights = jnp.concatenate([query_weight, kv_full[0], kv_full[1]], axis=1)
+
     pieces = [(my_gy, local_weights)]
-    for k in range(1, gy_count):
-        got = lax.ppermute(local_weights, "gy", partner_route(gy_count, gy_count, k))
-        pieces.append((my_gy ^ k, got))
+    if gy_count == 4:
+        from_one = lax.ppermute(local_weights, "gy", partner_route(4, 4, 1))
+        from_two = lax.ppermute(local_weights, "gy", partner_route(4, 4, 2))
+        half = row_block // 2
+        far_low = lax.ppermute(from_two[:half], "gy", partner_route(4, 4, 1))
+        far_high = lax.ppermute(from_one[half:], "gy", partner_route(4, 4, 2))
+        pieces += [(my_gy ^ 1, from_one), (my_gy ^ 2, from_two)]
+        pieces.append((my_gy ^ 3, jnp.concatenate([far_low, far_high], axis=0)))
+    else:
+        for k in range(1, gy_count):
+            got = lax.ppermute(local_weights, "gy", partner_route(gy_count, gy_count, k))
+            pieces.append((my_gy ^ k, got))
+    all_rows = jnp.zeros((gy_count * row_block, local_weights.shape[1]), local_weights.dtype)
+    for source, block in pieces:
+        all_rows = lax.dynamic_update_slice_in_dim(all_rows, block, source * row_block, 0)
 
     local_float = tokens_in.astype(jnp.float32)
     my_gx = lax.axis_index("gx")
@@ -76,44 +96,26 @@
     square_order = jnp.arange(gx_count, dtype=jnp.int32) ^ my_gx
     squares = jnp.sum(jnp.take(jnp.stack(square_parts), square_order, axis=0), axis=0)
     normed = lax.all_gather(local_normed, "gx", axis=1, tiled=True)
-    products = None
-    for source, block in pieces:
-        rows = lax.dynamic_slice_in_dim(normed, source * row_block, row_block, 1)
-        part = jnp.dot(rows, block, preferred_element_type=jnp.float32)
-        products = part if products is None else products + part
+    products = jnp.dot(normed, all_rows, preferred_element_type=jnp.float32)
     scaling = 1.0 / jnp.sqrt(squares / D + EPSILON)
     projected = products * scaling[:, None]
     query_cols = head_local * HD
     queries = rotate(projected[:, :query_cols], positions, HD, 0).astype(jnp.bfloat16)
-    key_proj = projected[:, query_cols : query_cols + quarter]
-    value_proj = projected[:, query_cols + quarter :]
-    key_piece = rotate(key_proj, positions, quarter, spot * (quarter // 2)).astype(jnp.bfloat16)
-    value_piece = value_proj.astype(jnp.bfloat16)
+    key_proj = projected[:, query_cols : query_cols + HD]
+    value_proj = projected[:, query_cols + HD :]
+    full_keys = rotate(key_proj, positions, HD, 0).astype(jnp.bfloat16)
+    full_values = value_proj.astype(jnp.bfloat16)
+    key_piece = lax.dynamic_slice_in_dim(full_keys, spot * quarter, quarter, 1)
+    value_piece = lax.dynamic_slice_in_dim(full_values, spot * quarter, quarter, 1)
+    own_kv = jnp.stack([key_piece, value_piece])
 
     span_count = gy_count // 4
     marks = segment_ids + 1
-    own_kv = jnp.stack([key_piece, value_piece])
-    order = jnp.arange(quarters, dtype=jnp.int32) ^ spot
-
-    def assembled(parts):
-        stack = jnp.take(jnp.stack(parts), order, axis=0)
-        return stack.transpose(1, 2, 0, 3).reshape(2, token_count, HD)
-
-    here = [own_kv]
-    for k in range(1, quarters):
-        here.append(lax.ppermute(own_kv, "gx", partner_route(gx_count, quarters, k)))
-    kv_blocks = [assembled(here)]
+    head_kv = jnp.stack([full_keys, full_values])
+    kv_blocks = [head_kv]
     mark_list = [marks]
     for shift_by in range(1, span_count + 1):
-        earlier_parts = []
-        for k in range(quarters):
-            route = []
-            for i in range(gx_count):
-                peer = i - i % quarters + ((i % quarters) ^ k)
-                for j in range(gy_count - shift_by):
-                    route.append((i * gy_count + j, peer * gy_count + j + shift_by))
-            earlier_parts.append(lax.ppermute(own_kv, ("gx", "gy"), route))
-        kv_blocks.insert(0, assembled(earlier_parts))
+        kv_blocks.insert(0, shifted(head_kv, "gy", shift_by))
         mark_list.insert(0, shifted(marks, "gy", shift_by))
     window_kv = jnp.concatenate(kv_blocks, axis=1)
     window_keys = window_kv[0]

time: 156 us -> 177 us (1.13)
  waiting for transfers between devices: 65.5 us -> 83.1 us
  local copies, waits for them, and re-layouts: 16.5 us -> 21.1 us
  starting transfers between devices: 35.3 us -> 31 us
  other arithmetic: 10.5 us -> 12.8 us
    ppermute x10 -> x7, waiting for transfers between devices: 2 us -> 79.9 us  [the longest x1 42.1 us: shards(): from_one = lax.ppermute(local_weights, 'gy', partner_route(4, 4, 1))]
    ppermute x1 -> x2, waiting for transfers between devices: 42.4 us -> 0.16 us  [shifted(): return lax.ppermute(value, axis, pairs)]
    all_gather x1, waiting for transfers between devices: 20.8 us -> 0.01 us  [shards(): normed = lax.all_gather(local_normed, 'gx', axis=1, tiled=True)]
    ppermute x10 -> x7, starting transfers between devices: 18.7 us -> 8.01 us  [the longest x3 3.24 us: shards(): lax.ppermute(kv_weights, 'gx', partner_route(gx_count, quarters, k))]
    convert_element_type x4 -> x3, local copies, waits for them, and re-layouts: 5.36 us -> 0.25 us  [shards(): full_keys = rotate(key_proj, positions, HD, 0).astype(jnp.bfloat16)]
    dynamic_update_slice x0 -> x2, local copies, waits for them, and re-layouts: none -> 4.54 us  [shards(): lax.dynamic_update_slice_in_dim(all_rows, block, source * row_block, 0)]
    ppermute x1 -> x2, starting transfers between devices: 3.08 us -> 7.28 us  [shifted(): return lax.ppermute(value, axis, pairs)]
    broadcast_in_dim x0 -> x1, local copies, waits for them, and re-layouts: none -> 3.79 us  [shards(): jnp.zeros((gy_count * row_block, local_weights.shape[1]), local_weights.d...]
  transfers between devices with their start and end apart: 20 -> 18, of which waited for: 4 -> 7; matrix products, arithmetic and copies ran while one was open for 18% -> 14% of each run, Pallas kernels for 0% -> 0%
where the time goes in v3:
time: 177 us; the launch traced here: 175 us
  waiting for transfers between devices  83.1 us (47%)
  starting transfers between devices  31 us (18%)
  local copies, waits for them, and re-layouts  21.1 us (12%)
  between operations  14.5 us (8%)
  other arithmetic  12.8 us (7%)
  matrix products  12.1 us (7%)
    ppermute x1, waiting for transfers between devices, shards(): from_one = lax.ppermute(local_weights, 'gy', partner_route(4, 4, 1))  42.1 us
    ppermute x3, waiting for transfers between devices, shards(): lax.ppermute(kv_weights, 'gx', partner_route(gx_count, quarters, k))  21 us
    ppermute x1, waiting for transfers between devices, shards(): far_low = lax.ppermute(from_two[:half], 'gy', partner_route(4, 4, 1))  15.4 us
    ppermute x7, starting transfers between devices, shards(): lax.ppermute(local_squares, 'gx', partner_route(gx_count, gx_count, k))  12.4 us
    dot_general x1, matrix products, shards(): products = jnp.dot(normed, all_rows, preferred_element_type=jnp.float32)  9.45 us
    ppermute x2, starting transfers between devices, shifted(): return lax.ppermute(value, axis, pairs)  7.28 us
    dynamic_update_slice x2, local copies, waits for them, and re-layouts, shards(): lax.dynamic_update_slice_in_dim(all_rows, block, source * row_block, 0)  4.54 us
    broadcast_in_dim x1, local copies, waits for them, and re-layouts, shards(): jnp.zeros((gy_count * row_block, local_weights.shape[1]), local_weights.d...  3.79 us
  transfers between devices with their start and end apart: 18, of which 7 were waited for; matrix products, arithmetic and copies ran while one was open for 14% of the time, Pallas kernels for 0%

profile of v3, /device:TPU:0, one launch (start us, length us, event | category | flops | bytes accessed | tf_op | source)
XLA Modules:
  0.0 174.6 jit_solution(103366804590310294)
XLA Ops:
  7.2 0.7 dynamic-slice_convert_fusion
  7.9 2.5 %fusion.4 = (f32[512]{0:T(512)S(1)}, bf16[512,1024]{1,0:T(8,128)(2,1)}) fusion(bf16[512,1024]{1,0:T(8,128)(2,1)} %param.8, f32[1024]{0:T(1024)S(1)} %dynamic-slice_convert_fusion), kind=kLoop, calls=%fused_computation.12 | loop fusion | flops 2620928 | bytes 2103296 | tf_op jit(solution)/shard_map/reduce_sum | solution.py:92
  10.4 1.0 fusion.27
  11.4 0.5 collective-permute-start.1
  12.0 2.6 %collective-permute-start.2 = (bf16[2,2048,32]{1,2,0:T(8,128)(2,1)S(1)}, bf16[2,2048,32]{1,2,0:T(8,128)(2,1)S(1)}, u32[]{:S(2)}, u32[]{:S(2)}) collective-permute-start(bf16[2,2048,32]{1,2,0:T(8,128)(2,1)S(1)} %get-tuple-element.35), channel_id=1, source_target_pairs={{0,8},{4,12},{8,0},{12,4},{16,24},{20,28},{24,16},{28,20},{1,9},{5... | collective-permute-start | bytes 786440 | tf_op jit(solution)/shard_map/ppermute | solution.py:65
  14.7 7.0 %collective-permute-done.2 = bf16[2,2048,32]{1,2,0:T(8,128)(2,1)S(1)} collective-permute-done((bf16[2,2048,32]{1,2,0:T(8,128)(2,1)S(1)}, bf16[2,2048,32]{1,2,0:T(8,128)(2,1)S(1)}, u32[]{:S(2)}, u32[]{:S(2)}) %collective-permute-start.2) | collective-permute-done | bytes 262176 | tf_op jit(solution)/shard_map/ppermute | solution.py:65
  21.8 14.0 %collective-permute-done.3 = bf16[2,2048,32]{1,2,0:T(8,128)(2,1)S(1)} collective-permute-done((bf16[2,2048,32]{1,2,0:T(8,128)(2,1)S(1)}, bf16[2,2048,32]{1,2,0:T(8,128)(2,1)S(1)}, u32[]{:S(2)}, u32[]{:S(2)}) %collective-permute-start.3) | collective-permute-done | bytes 262176 | tf_op jit(solution)/shard_map/ppermute | solution.py:65
  35.9 0.6 gather_fusion
  36.8 0.3 copy.65
  37.1 0.3 copy.66
  37.4 3.8 %broadcast_in_dim.41 = bf16[8192,512]{1,0:T(8,128)(2,1)} broadcast(bf16[]{:T(256)} %constant.37.clone.1), dimensions={} | broadcast | bytes 8388610 | tf_op jit(solution)/shard_map/broadcast_in_dim | solution.py:83
  41.2 2.4 %pad_maximum_fusion = (bf16[2048,512]{1,0:T(8,128)(2,1)}, bf16[8192,512]{1,0:T(8,128)(2,1)}) fusion(bf16[2048,128]{1,0:T(8,128)(2,1)S(1)} %copy.66, bf16[2048,128]{1,0:T(8,128)(2,1)S(1)} %copy.65, bf16[2048,256]{1,0:T(8,128)(2,1)S(1)} %copy-done, bf16[8192,512]{1,0:T(8,128)(2,1)} %broadcast_in_dim.41, s32[]{:T(128)S(6)} %select_n.88), kind=kLoop, calls=%fused_computation.14 | loop fusion | flops 6291456 | bytes 6291460 | tf_op jit(solution)/shard_map/concatenate | solution.py:68
  43.6 1.4 collective-permute-start.4
  45.0 1.6 collective-permute-start.5
  46.6 1.0 collective-permute-start.8
  47.6 1.4 collective-permute-start.10
  49.4 0.5 multiply_cosine_fusion.1
  49.9 42.1 %collective-permute-done.4 = bf16[2048,512]{1,0:T(8,128)(2,1)S(1)} collective-permute-done((bf16[2048,512]{1,0:T(8,128)(2,1)}, bf16[2048,512]{1,0:T(8,128)(2,1)S(1)}, u32[]{:S(2)}, u32[]{:S(2)}) %collective-permute-start.4) | collective-permute-done | bytes 2097184 | tf_op jit(solution)/shard_map/ppermute | solution.py:72
  92.0 5.4 %collective-permute-start.11 = (f32[512]{0:T(512)S(1)}, f32[512]{0:T(512)S(1)}, u32[]{:S(2)}, u32[]{:S(2)}) collective-permute-start(f32[512]{0:T(512)S(1)} %get-tuple-element.20), channel_id=1, source_target_pairs={{0,16},{4,20},{8,24},{12,28},{16,0},{20,4},{24,8},{28,12},{1,17},{... | collective-permute-start | bytes 6152 | tf_op jit(solution)/shard_map/ppermute | solution.py:95
  97.4 3.2 %collective-permute-start = (s32[512]{0:T(512)S(1)}, s32[512]{0:T(512)S(1)}, u32[]{:S(2)}, u32[]{:S(2)}) collective-permute-start(s32[512]{0:T(512)S(1)} %broadcast_add_fusion), channel_id=1, source_target_pairs={{0,1},{1,2},{2,3},{4,5},{5,6},{6,7},{8,9},{9,10},{10,11},{12,13},{... | collective-permute-start | bytes 6152 | tf_op jit(solution)/shard_map/ppermute | solution.py:19
  100.7 2.3 %slice.69 = bf16[1024,512]{1,0:T(8,128)(2,1)} slice(bf16[2048,512]{1,0:T(8,128)(2,1)} %collective-permute-done.5), slice={[0:1024], [0:512]} | slice | bytes 2097152 | tf_op jit(solution)/shard_map/slice | solution.py:75
  103.0 1.1 slice.70
  104.1 4.6 %collective-permute-start.13 = (f32[512]{0:T(512)S(1)}, f32[512]{0:T(512)S(1)}, u32[]{:S(2)}, u32[]{:S(2)}) collective-permute-start(f32[512]{0:T(512)S(1)} %get-tuple-element.20), channel_id=1, source_target_pairs={{0,24},{4,28},{8,16},{12,20},{16,8},{20,12},{24,0},{28,4},{1,25},{... | collective-permute-start | bytes 6152 | tf_op jit(solution)/shard_map/ppermute | solution.py:95
  108.7 1.6 collective-permute-start.6
  110.5 3.0 %collective-permute-done.14 = f32[512]{0:T(512)S(1)} collective-permute-done((f32[512]{0:T(512)S(1)}, f32[512]{0:T(512)S(1)}, u32[]{:S(2)}, u32[]{:S(2)}) %collective-permute-start.14) | collective-permute-done | bytes 2080 | tf_op jit(solution)/shard_map/ppermute | solution.py:95
  113.6 0.6 gather_fusion.1
  114.2 1.5 constant_dynamic-update-slice_fusion.1
  115.7 3.1 %constant_dynamic-update-slice_fusion = bf16[8192,512]{1,0:T(8,128)(2,1)} fusion(bf16[8192,512]{1,0:T(8,128)(2,1)} %constant_dynamic-update-slice_fusion.1, bf16[2048,512]{1,0:T(8,128)(2,1)} %collective-permute-done.5, s32[]{:T(128)S(6)} %select_n.90), kind=kLoop, calls=%fused_computation.68 | loop fusion | bytes 4194308 | tf_op jit(solution)/shard_map/dynamic_update_slice | solution.py:85
  118.8 15.4 %collective-permute-done.6 = bf16[1024,512]{1,0:T(8,128)(2,1)S(1)} collective-permute-done((bf16[1024,512]{1,0:T(8,128)(2,1)}, bf16[1024,512]{1,0:T(8,128)(2,1)S(1)}, u32[]{:S(2)}, u32[]{:S(2)}) %collective-permute-start.6) | collective-permute-done | bytes 1048608 | tf_op jit(solution)/shard_map/ppermute | solution.py:75
  134.2 1.4 collective-permute-done.7
  135.6 2.7 %maximum_dynamic-update-slice_fusion = bf16[8192,512]{1,0:T(8,128)(2,1)} fusion(bf16[8192,512]{1,0:T(8,128)(2,1)} %constant_dynamic-update-slice_fusion, s32[]{:T(128)S(6)} %select_n.91, bf16[1024,512]{1,0:T(8,128)(2,1)} %collective-permute-done.7, bf16[1024,512]{1,0:T(8,128)(2,1)S(1)} %collective-permute-done.6), kind=kLoop, calls=%fused_computation.15 | loop fusion | flops 4194304 | bytes 4194308 | tf_op jit(solution)/shard_map/dynamic_update_slice | solution.py:85
  138.2 9.4 %convolution_multiply_fusion = f32[512,512]{0,1:T(8,128)S(1)} fusion(bf16[512,8192]{1,0:T(8,128)(2,1)} %all-gather.2.cloned.1.call-done, bf16[8192,512]{1,0:T(8,128)(2,1)} %maximum_dynamic-update-slice_fusion, f32[512]{0:T(512)S(1)} %add_rsqrt_fusion), kind=kOutput, calls=%fused_computation.17 | convolution fusion | flops 4295229440 | bytes 17827840 | tf_op jit(solution)/shard_map/dot_general | solution.py:99
  148.1 0.6 fusion.21
  149.8 1.5 scatter_fusion
  151.3 0.7 copy.78
  152.0 3.3 %all-to-all-start = ((bf16[4,16,2,512]{3,1,2,0:T(8,128)(2,1)}), bf16[4,16,2,512]{3,1,2,0:T(8,128)(2,1)S(1)}, u32[]{:S(2)}, u32[]{:S(2)}) async-start(bf16[4,16,2,512]{3,1,2,0:T(8,128)(2,1)} %copy.78), calls=%async_computation | async-start | bytes 262144 | tf_op jit(solution)/shard_map/all_to_all | solution.py:169
  155.4 4.1 %collective-permute-start.15 = (bf16[2,512,128]{1,2,0:T(8,128)(2,1)S(1)}, bf16[2,512,128]{1,2,0:T(8,128)(2,1)S(1)}, u32[]{:S(2)}, u32[]{:S(2)}) collective-permute-start(bf16[2,512,128]{1,2,0:T(8,128)(2,1)S(1)} %pad_maximum_fusion.4), channel_id=1, source_target_pairs={{0,1},{1,2},{2,3},{4,5},{5,6},{6,7},{8,9},{9,10},{10,11},{12,13},{... | collective-permute-start | bytes 786440 | tf_op jit(solution)/shard_map/ppermute | solution.py:19
  159.4 0.3 reshape.300
  159.8 0.4 fusion.29
  160.2 0.5 subtract_convert_fusion
  160.7 0.3 pad_maximum_fusion.3
  161.3 0.3 reshape.304
  161.7 0.9 copy.80
  162.6 0.9 copy.81
  163.7 1.8 %fusion.31 = (f32[1024]{0:T(1024)S(1)}, f32[1024,1024]{0,1:T(8,128)S(1)}) fusion(bf16[1024,128]{1,0:T(8,128)(2,1)S(1)} %bitcast.83, bf16[2,1024,128]{1,2,0:T(8,128)(2,1)S(1)} %maximum_maximum_fusion, s32[1024]{0:T(1024)S(1)} %bitcast.93, pred[1024]{0:T(1024)(128)(4,1)S(1)} %broadcast_compare_fusion, s32[1024]{0:T(1024)S(1)} %bitcast.92, ...), kind=kOutput, calls=%fused_computation.82 | convolution fusion | flops 275774464 | bytes 4736000 | tf_op jit(solution)/shard_map/dot_general | solution.py:130
  165.5 0.6 fusion.1
  166.1 0.9 fusion.14
  167.0 0.7 copy.98
  (78 shorter events, 3.2 us)
Async XLA Ops:
  7.2 131.1 %all-gather.2.cloned.1.call-start = ((), (), s32[]{:S(2)}) async-start(), calls=%async_computation.1 | async-start | bytes 9437184 | tf_op jit(solution)/shard_map/all_gather | solution.py:98
  11.4 3.3 %collective-permute-start.1 = (bf16[2,2048,32]{1,2,0:T(8,128)(2,1)S(1)}, bf16[2,2048,32]{1,2,0:T(8,128)(2,1)S(1)}, u32[]{:S(2)}, u32[]{:S(2)}) collective-permute-start(bf16[2,2048,32]{1,2,0:T(8,128)(2,1)S(1)} %get-tuple-element.35), channel_id=1, source_target_pairs={{0,4},{4,0},{8,12},{12,8},{16,20},{20,16},{24,28},{28,24},{1,5},{5... | collective-permute-start | bytes 786440 | tf_op jit(solution)/shard_map/ppermute | solution.py:65
  12.0 9.8 %collective-permute-start.2 = (bf16[2,2048,32]{1,2,0:T(8,128)(2,1)S(1)}, bf16[2,2048,32]{1,2,0:T(8,128)(2,1)S(1)}, u32[]{:S(2)}, u32[]{:S(2)}) collective-permute-start(bf16[2,2048,32]{1,2,0:T(8,128)(2,1)S(1)} %get-tuple-element.35), channel_id=1, source_target_pairs={{0,8},{4,12},{8,0},{12,4},{16,24},{20,28},{24,16},{28,20},{1,9},{5... | collective-permute-start | bytes 786440 | tf_op jit(solution)/shard_map/ppermute | solution.py:65
  14.6 21.1 %collective-permute-start.3 = (bf16[2,2048,32]{1,2,0:T(8,128)(2,1)S(1)}, bf16[2,2048,32]{1,2,0:T(8,128)(2,1)S(1)}, u32[]{:S(2)}, u32[]{:S(2)}) collective-permute-start(bf16[2,2048,32]{1,2,0:T(8,128)(2,1)S(1)} %get-tuple-element.35), channel_id=1, source_target_pairs={{0,12},{4,8},{8,4},{12,0},{16,28},{20,24},{24,20},{28,16},{1,13},{... | collective-permute-start | bytes 786440 | tf_op jit(solution)/shard_map/ppermute | solution.py:65
  37.4 3.8 %copy-start = (bf16[2048,256]{1,0:T(8,128)(2,1)S(1)}, bf16[2048,256]{1,0:T(8,128)(2,1)}, u32[]{:S(2)}) copy-start(bf16[2048,256]{1,0:T(8,128)(2,1)} %param.10) | copy-start | bytes 3145732
  41.2 7.8 %copy-start.3 = (s32[512]{0:T(512)S(1)}, s32[512]{0:T(512)}, u32[]{:S(2)}) copy-start(s32[512]{0:T(512)} %param.14) | copy-start | bytes 6148
  41.2 7.8 %copy-start.2 = (s32[32,1]{0,1:T(1,128)S(1)}, s32[32,1]{0,1:T(1,128)}, u32[]{:S(2)}) copy-start(s32[32,1]{0,1:T(1,128)} %param.15) | copy-start | bytes 388
  41.2 8.2 %copy-start.1 = (s32[512]{0:T(512)S(1)}, s32[512]{0:T(512)}, u32[]{:S(2)}) copy-start(s32[512]{0:T(512)} %param.13) | copy-start | bytes 6148
  43.6 48.4 %collective-permute-start.4 = (bf16[2048,512]{1,0:T(8,128)(2,1)}, bf16[2048,512]{1,0:T(8,128)(2,1)S(1)}, u32[]{:S(2)}, u32[]{:S(2)}) collective-permute-start(bf16[2048,512]{1,0:T(8,128)(2,1)} %get-tuple-element.18), channel_id=1, source_target_pairs={{0,1},{1,0},{2,3},{3,2},{4,5},{5,4},{6,7},{7,6},{8,9},{9,8},{10,11... | collective-permute-start | bytes 6291464 | tf_op jit(solution)/shard_map/ppermute | solution.py:72
  45.0 52.4 %collective-permute-start.5 = (bf16[2048,512]{1,0:T(8,128)(2,1)}, bf16[2048,512]{1,0:T(8,128)(2,1)}, u32[]{:S(2)}, u32[]{:S(2)}) collective-permute-start(bf16[2048,512]{1,0:T(8,128)(2,1)} %get-tuple-element.18), channel_id=1, source_target_pairs={{0,2},{1,3},{2,0},{3,1},{4,6},{5,7},{6,4},{7,5},{8,10},{9,11},{10,... | collective-permute-start | bytes 6291464 | tf_op jit(solution)/shard_map/ppermute | solution.py:73
  46.6 57.5 %collective-permute-start.8 = (f32[512]{0:T(512)S(1)}, f32[512]{0:T(512)S(1)}, u32[]{:S(2)}, u32[]{:S(2)}) collective-permute-start(f32[512]{0:T(512)S(1)} %get-tuple-element.20), channel_id=1, source_target_pairs={{0,4},{4,0},{8,12},{12,8},{16,20},{20,16},{24,28},{28,24},{1,5},{5... | collective-permute-start | bytes 6152 | tf_op jit(solution)/shard_map/ppermute | solution.py:95
  47.6 56.5 %collective-permute-start.9 = (f32[512]{0:T(512)S(1)}, f32[512]{0:T(512)S(1)}, u32[]{:S(2)}, u32[]{:S(2)}) collective-permute-start(f32[512]{0:T(512)S(1)} %get-tuple-element.20), channel_id=1, source_target_pairs={{0,8},{4,12},{8,0},{12,4},{16,24},{20,28},{24,16},{28,20},{1,9},{5... | collective-permute-start | bytes 6152 | tf_op jit(solution)/shard_map/ppermute | solution.py:95
  47.6 61.1 %collective-permute-start.10 = (f32[512]{0:T(512)S(1)}, f32[512]{0:T(512)S(1)}, u32[]{:S(2)}, u32[]{:S(2)}) collective-permute-start(f32[512]{0:T(512)S(1)} %get-tuple-element.20), channel_id=1, source_target_pairs={{0,12},{4,8},{8,4},{12,0},{16,28},{20,24},{24,20},{28,16},{1,13},{... | collective-permute-start | bytes 6152 | tf_op jit(solution)/shard_map/ppermute | solution.py:95
  92.0 16.7 %collective-permute-start.11 = (f32[512]{0:T(512)S(1)}, f32[512]{0:T(512)S(1)}, u32[]{:S(2)}, u32[]{:S(2)}) collective-permute-start(f32[512]{0:T(512)S(1)} %get-tuple-element.20), channel_id=1, source_target_pairs={{0,16},{4,20},{8,24},{12,28},{16,0},{20,4},{24,8},{28,12},{1,17},{... | collective-permute-start | bytes 6152 | tf_op jit(solution)/shard_map/ppermute | solution.py:95
  97.4 12.9 %collective-permute-start = (s32[512]{0:T(512)S(1)}, s32[512]{0:T(512)S(1)}, u32[]{:S(2)}, u32[]{:S(2)}) collective-permute-start(s32[512]{0:T(512)S(1)} %broadcast_add_fusion), channel_id=1, source_target_pairs={{0,1},{1,2},{2,3},{4,5},{5,6},{6,7},{8,9},{9,10},{10,11},{12,13},{... | collective-permute-start | bytes 6152 | tf_op jit(solution)/shard_map/ppermute | solution.py:19
  104.1 6.4 %collective-permute-start.12 = (f32[512]{0:T(512)S(1)}, f32[512]{0:T(512)S(1)}, u32[]{:S(2)}, u32[]{:S(2)}) collective-permute-start(f32[512]{0:T(512)S(1)} %get-tuple-element.20), channel_id=1, source_target_pairs={{0,20},{4,16},{8,28},{12,24},{16,4},{20,0},{24,12},{28,8},{1,21},{... | collective-permute-start | bytes 6152 | tf_op jit(solution)/shard_map/ppermute | solution.py:95
  104.1 6.4 %collective-permute-start.13 = (f32[512]{0:T(512)S(1)}, f32[512]{0:T(512)S(1)}, u32[]{:S(2)}, u32[]{:S(2)}) collective-permute-start(f32[512]{0:T(512)S(1)} %get-tuple-element.20), channel_id=1, source_target_pairs={{0,24},{4,28},{8,16},{12,20},{16,8},{20,12},{24,0},{28,4},{1,25},{... | collective-permute-start | bytes 6152 | tf_op jit(solution)/shard_map/ppermute | solution.py:95
  108.7 4.8 %collective-permute-start.14 = (f32[512]{0:T(512)S(1)}, f32[512]{0:T(512)S(1)}, u32[]{:S(2)}, u32[]{:S(2)}) collective-permute-start(f32[512]{0:T(512)S(1)} %get-tuple-element.20), channel_id=1, source_target_pairs={{0,28},{4,24},{8,20},{12,16},{16,12},{20,8},{24,4},{28,0},{1,29},{... | collective-permute-start | bytes 6152 | tf_op jit(solution)/shard_map/ppermute | solution.py:95
  108.7 25.5 %collective-permute-start.6 = (bf16[1024,512]{1,0:T(8,128)(2,1)}, bf16[1024,512]{1,0:T(8,128)(2,1)S(1)}, u32[]{:S(2)}, u32[]{:S(2)}) collective-permute-start(bf16[1024,512]{1,0:T(8,128)(2,1)} %slice.69), channel_id=1, source_target_pairs={{0,1},{1,0},{2,3},{3,2},{4,5},{5,4},{6,7},{7,6},{8,9},{9,8},{10,11... | collective-permute-start | bytes 3145736 | tf_op jit(solution)/shard_map/ppermute | solution.py:75
  110.3 25.2 %collective-permute-start.7 = (bf16[1024,512]{1,0:T(8,128)(2,1)}, bf16[1024,512]{1,0:T(8,128)(2,1)}, u32[]{:S(2)}, u32[]{:S(2)}) collective-permute-start(bf16[1024,512]{1,0:T(8,128)(2,1)} %slice.70), channel_id=1, source_target_pairs={{0,2},{1,3},{2,0},{3,1},{4,6},{5,7},{6,4},{7,5},{8,10},{9,11},{10,... | collective-permute-start | bytes 3145736 | tf_op jit(solution)/shard_map/ppermute | solution.py:76
  152.0 9.3 %all-to-all-start = ((bf16[4,16,2,512]{3,1,2,0:T(8,128)(2,1)}), bf16[4,16,2,512]{3,1,2,0:T(8,128)(2,1)S(1)}, u32[]{:S(2)}, u32[]{:S(2)}) async-start(bf16[4,16,2,512]{3,1,2,0:T(8,128)(2,1)} %copy.78), calls=%async_computation | async-start | bytes 262144 | tf_op jit(solution)/shard_map/all_to_all | solution.py:169
  155.4 8.3 %collective-permute-start.15 = (bf16[2,512,128]{1,2,0:T(8,128)(2,1)S(1)}, bf16[2,512,128]{1,2,0:T(8,128)(2,1)S(1)}, u32[]{:S(2)}, u32[]{:S(2)}) collective-permute-start(bf16[2,512,128]{1,2,0:T(8,128)(2,1)S(1)} %pad_maximum_fusion.4), channel_id=1, source_target_pairs={{0,1},{1,2},{2,3},{4,5},{5,6},{6,7},{8,9},{9,10},{10,11},{12,13},{... | collective-permute-start | bytes 786440 | tf_op jit(solution)/shard_map/ppermute | solution.py:19
Sparse Core Ops, SparseCore 0:
  10.6 85.8 all-gather.1

commit v4 on v2

--- a/solution.py
+++ b/solution.py
@@ -27,22 +27,19 @@
     return route
 
 
-def rotate(matrix, places, group_width, first_pair):
-    row_count = matrix.shape[0]
-    pair_count = group_width // 2
-    shaped = matrix.reshape(row_count, -1, pair_count, 2)
-    all_pairs = jnp.arange(HD // 2, dtype=jnp.int32)
-    all_freq = jnp.power(THETA, -(2.0 * all_pairs.astype(jnp.float32)) / HD)
-    frequency = lax.dynamic_slice_in_dim(all_freq, first_pair, pair_count, 0)
+def rope(matrix, places, width, first_pair):
+    cols = jnp.arange(matrix.shape[1], dtype=jnp.int32)
+    pair_index = first_pair + (cols % width) // 2
+    frequency = jnp.power(THETA, -(2.0 * pair_index.astype(jnp.float32)) / HD)
     angles = places.astype(jnp.float32)[:, None] * frequency[None, :]
-    cosine = jnp.cos(angles)[:, None, :]
-    sine_of = jnp.sin(angles)[:, None, :]
-    even_part = shaped[..., 0]
-    odd_part = shaped[..., 1]
-    turned = jnp.stack(
-        [even_part * cosine - odd_part * sine_of, even_part * sine_of + odd_part * cosine], axis=-1
+    cosine = jnp.cos(angles)
+    sine_of = jnp.sin(angles)
+    following = jnp.roll(matrix, -1, axis=1)
+    preceding = jnp.roll(matrix, 1, axis=1)
+    even = (cols % 2 == 0)[None, :]
+    return jnp.where(
+        even, matrix * cosine - following * sine_of, matrix * cosine + preceding * sine_of
     )
-    return turned.reshape(row_count, -1)
 
 
 def shards(
@@ -54,18 +51,19 @@
     quarters = HD // quarter
     gx_count = lax.axis_size("gx")
     gy_count = lax.axis_size("gy")
-    spot = lax.axis_index("gx") % quarters
+    my_gx = lax.axis_index("gx")
     my_gy = lax.axis_index("gy")
+    spot = my_gx % quarters
     row_block = query_weight.shape[0]
 
     local_weights = jnp.concatenate([query_weight, key_weight, value_weight], axis=1)
-    pieces = [(my_gy, local_weights)]
+    all_rows = jnp.zeros((gy_count * row_block, local_weights.shape[1]), local_weights.dtype)
+    all_rows = lax.dynamic_update_slice_in_dim(all_rows, local_weights, my_gy * row_block, 0)
     for k in range(1, gy_count):
         got = lax.ppermute(local_weights, "gy", partner_route(gy_count, gy_count, k))
-        pieces.append((my_gy ^ k, got))
+        all_rows = lax.dynamic_update_slice_in_dim(all_rows, got, (my_gy ^ k) * row_block, 0)
 
     local_float = tokens_in.astype(jnp.float32)
-    my_gx = lax.axis_index("gx")
     feature_block = tokens_in.shape[1]
     local_gain = lax.dynamic_slice_in_dim(norm_gain, my_gx * feature_block, feature_block, 0)
     local_normed = (local_float * local_gain.astype(jnp.float32)[None, :]).astype(jnp.bfloat16)
@@ -76,49 +74,35 @@
     square_order = jnp.arange(gx_count, dtype=jnp.int32) ^ my_gx
     squares = jnp.sum(jnp.take(jnp.stack(square_parts), square_order, axis=0), axis=0)
     normed = lax.all_gather(local_normed, "gx", axis=1, tiled=True)
-    products = None
-    for source, block in pieces:
-        rows = lax.dynamic_slice_in_dim(normed, source * row_block, row_block, 1)
-        part = jnp.dot(rows, block, preferred_element_type=jnp.float32)
-        products = part if products is None else products + part
+    products = jnp.dot(normed, all_rows, preferred_element_type=jnp.float32)
     scaling = 1.0 / jnp.sqrt(squares / D + EPSILON)
     projected = products * scaling[:, None]
     query_cols = head_local * HD
-    queries = rotate(projected[:, :query_cols], positions, HD, 0).astype(jnp.bfloat16)
-    key_proj = projected[:, query_cols : query_cols + quarter]
-    value_proj = projected[:, query_cols + quarter :]
-    key_piece = rotate(key_proj, positions, quarter, spot * (quarter // 2)).astype(jnp.bfloat16)
-    value_piece = value_proj.astype(jnp.bfloat16)
+    key_piece = rope(
+        projected[:, query_cols : query_cols + quarter], positions, quarter, spot * (quarter // 2)
+    ).astype(jnp.bfloat16)
+    value_piece = projected[:, query_cols + quarter :].astype(jnp.bfloat16)
+    queries = rope(projected[:, :query_cols], positions, HD, 0).astype(jnp.bfloat16)
+    own_kv = jnp.stack([key_piece, value_piece])
 
     span_count = gy_count // 4
     marks = segment_ids + 1
-    own_kv = jnp.stack([key_piece, value_piece])
-    order = jnp.arange(quarters, dtype=jnp.int32) ^ spot
-
-    def assembled(parts):
-        stack = jnp.take(jnp.stack(parts), order, axis=0)
-        return stack.transpose(1, 2, 0, 3).reshape(2, token_count, HD)
-
-    here = [own_kv]
-    for k in range(1, quarters):
-        here.append(lax.ppermute(own_kv, "gx", partner_route(gx_count, quarters, k)))
-    kv_blocks = [assembled(here)]
+    kv_list = [own_kv]
     mark_list = [marks]
     for shift_by in range(1, span_count + 1):
-        earlier_parts = []
-        for k in range(quarters):
-            route = []
-            for i in range(gx_count):
-                peer = i - i % quarters + ((i % quarters) ^ k)
-                for j in range(gy_count - shift_by):
-                    route.append((i * gy_count + j, peer * gy_count + j + shift_by))
-            earlier_parts.append(lax.ppermute(own_kv, ("gx", "gy"), route))
-        kv_blocks.insert(0, assembled(earlier_parts))
+        kv_list.insert(0, shifted(own_kv, "gy", shift_by))
         mark_list.insert(0, shifted(marks, "gy", shift_by))
-    window_kv = jnp.concatenate(kv_blocks, axis=1)
+    window_quarter = jnp.concatenate(kv_list, axis=1)
+    window_rows = window_quarter.shape[1]
+    sent = jnp.broadcast_to(window_quarter[None], (gx_count,) + window_quarter.shape)
+    got = lax.all_to_all(sent, "gx", split_axis=0, concat_axis=0, tiled=True)
+    group_start = my_gx - spot
+    head_parts = lax.dynamic_slice_in_dim(got, group_start, quarters, 0)
+    window_kv = head_parts.transpose(1, 2, 0, 3).reshape(2, window_rows, HD)
     window_keys = window_kv[0]
     window_values = window_kv[1]
     window_marks = jnp.concatenate(mark_list, axis=0)
+
     reach_rows = span_count * token_count
     query_rows = (
         queries.reshape(token_count, head_local, HD)
@@ -130,7 +114,7 @@
     ) * HD ** (-0.5)
     query_marks = jnp.tile(segment_ids, head_local)
     query_place = jnp.tile(jnp.arange(token_count, dtype=jnp.int32), head_local)
-    key_place = jnp.arange(window_keys.shape[0], dtype=jnp.int32)
+    key_place = jnp.arange(window_rows, dtype=jnp.int32)
     allowed = (window_marks[None, :] == query_marks[:, None] + 1) & (window_marks[None, :] > 0)
     allowed = allowed & (key_place[None, :] <= query_place[:, None] + reach_rows)
     masked = jnp.where(allowed, scores, MASKED)
@@ -147,6 +131,7 @@
         .reshape(token_count, head_local * HD)
         .astype(jnp.bfloat16)
     )
+
     owner_count = gy_count
     page_rows = token_count // PAGE
     capacity = max(2, 2 * page_rows // owner_count)

time: 156 us -> 166 us (1.064)
  waiting for transfers between devices: 65.5 us -> 76.3 us
  starting transfers between devices: 35.3 us -> 30.4 us
  local copies, waits for them, and re-layouts: 16.5 us -> 20.3 us
    ppermute x1 -> x2, waiting for transfers between devices: 42.4 us -> 0.99 us  [shifted(): return lax.ppermute(value, axis, pairs)]
    ppermute x3, waiting for transfers between devices: 0.01 us -> 40.4 us  [shards(): lax.ppermute(local_weights, 'gy', partner_route(gy_count, gy_count, k))]
    all_to_all x0 -> x1, waiting for transfers between devices: none -> 17.2 us  [shards(): got = lax.all_to_all(sent, 'gx', split_axis=0, concat_axis=0, tiled=True)]
    ppermute x7 -> x0, starting transfers between devices: 15 us -> none  [the longest x4 12.7 us: shards(): earlier_parts.append(lax.ppermute(own_kv, ('gx', 'gy'), route))]
    all_gather x1, waiting for transfers between devices: 20.8 us -> 10.5 us  [shards(): normed = lax.all_gather(local_normed, 'gx', axis=1, tiled=True)]
    dynamic_update_slice x0 -> x3, local copies, waits for them, and re-layouts: none -> 7.83 us  [shards(): lax.dynamic_update_slice_in_dim(all_rows, got, (my_gy ^ k) * row_block, 0)]
    convert_element_type x4 -> x1, local copies, waits for them, and re-layouts: 5.36 us -> 0.13 us  [shards(): key_piece = rope(projected[:, query_cols:query_cols + quarter], positions...]
    all_to_all x1, waiting for transfers between devices: 0.01 us -> 4.96 us  [shards(): lax.all_to_all(send_kv, 'gy', split_axis=0, concat_axis=0, tiled=True)]
  transfers between devices with their start and end apart: 20 -> 15, of which waited for: 4 -> 9; matrix products, arithmetic and copies ran while one was open for 18% -> 13% of each run, Pallas kernels for 0% -> 0%
where the time goes in v4:
time: 166 us
  waiting for transfers between devices  76.3 us (46%)
  starting transfers between devices  30.4 us (18%)
  local copies, waits for them, and re-layouts  20.3 us (12%)
  between operations  14.5 us (9%)
  matrix products  14.2 us (9%)
  other arithmetic  10.3 us (6%)
    ppermute x3, waiting for transfers between devices, shards(): lax.ppermute(local_weights, 'gy', partner_route(gy_count, gy_count, k))  40.4 us
    all_to_all x1, waiting for transfers between devices, shards(): got = lax.all_to_all(sent, 'gx', split_axis=0, concat_axis=0, tiled=True)  17.2 us
    ppermute x7, starting transfers between devices, shards(): lax.ppermute(local_squares, 'gx', partner_route(gx_count, gx_count, k))  13.6 us
    all_gather x1, waiting for transfers between devices, shards(): normed = lax.all_gather(local_normed, 'gx', axis=1, tiled=True)  10.5 us
    dot_general x1, matrix products, shards(): products = jnp.dot(normed, all_rows, preferred_element_type=jnp.float32)  10.1 us
    dynamic_update_slice x3, local copies, waits for them, and re-layouts, shards(): lax.dynamic_update_slice_in_dim(all_rows, got, (my_gy ^ k) * row_block, 0)  7.83 us
    ppermute x2, starting transfers between devices, shifted(): return lax.ppermute(value, axis, pairs)  6.41 us
    all_to_all x1, waiting for transfers between devices, shards(): lax.all_to_all(send_kv, 'gy', split_axis=0, concat_axis=0, tiled=True)  4.96 us
  transfers between devices with their start and end apart: 15, of which 9 were waited for; matrix products, arithmetic and copies ran while one was open for 13% of the time, Pallas kernels for 0%

profile of v4, /device:TPU:0, one launch (start us, length us, event | category | flops | bytes accessed | tf_op | source)
XLA Modules:
  0.0 166.0 jit_solution(11421061111481541227)
XLA Ops:
  7.2 0.7 dynamic-slice_convert_fusion
  7.9 2.5 %fusion.4 = (f32[512]{0:T(512)S(1)}, bf16[512,1024]{1,0:T(8,128)(2,1)}) fusion(bf16[512,1024]{1,0:T(8,128)(2,1)} %param.8, f32[1024]{0:T(1024)S(1)} %dynamic-slice_convert_fusion), kind=kLoop, calls=%fused_computation.11 | loop fusion | flops 2620928 | bytes 2103296 | tf_op jit(solution)/shard_map/reduce_sum | solution.py:70
  10.5 0.5 collective-permute-start.4
  11.0 2.6 %collective-permute-start.5 = (f32[512]{0:T(512)S(1)}, f32[512]{0:T(512)S(1)}, u32[]{:S(2)}, u32[]{:S(2)}) collective-permute-start(f32[512]{0:T(512)S(1)} %get-tuple-element.11), channel_id=1, source_target_pairs={{0,8},{4,12},{8,0},{12,4},{16,24},{20,28},{24,16},{28,20},{1,9},{5... | collective-permute-start | bytes 6152 | tf_op jit(solution)/shard_map/ppermute | solution.py:73
  13.6 1.5 copy.26
  15.2 3.0 %broadcast_in_dim.72 = bf16[8192,320]{0,1:T(8,128)(2,1)} broadcast(bf16[]{:T(256)} %constant.136.clone.1), dimensions={} | broadcast | bytes 5242882 | tf_op jit(solution)/shard_map/broadcast_in_dim | solution.py:60
  18.2 1.5 pad_maximum_fusion
  19.6 1.6 collective-permute-start.1
  21.2 1.5 collective-permute-start.2
  22.7 0.4 collective-permute-start.3
  23.3 0.2 select_reduce_fusion
  23.6 2.7 %collective-permute-start.7 = (f32[512]{0:T(512)S(1)}, f32[512]{0:T(512)S(1)}, u32[]{:S(2)}, u32[]{:S(2)}) collective-permute-start(f32[512]{0:T(512)S(1)} %get-tuple-element.11), channel_id=1, source_target_pairs={{0,16},{4,20},{8,24},{12,28},{16,0},{20,4},{24,8},{28,12},{1,17},{... | collective-permute-start | bytes 6152 | tf_op jit(solution)/shard_map/ppermute | solution.py:73
  26.3 0.3 collective-permute-done.6
  26.6 1.9 %collective-permute-start.8 = (f32[512]{0:T(512)S(1)}, f32[512]{0:T(512)S(1)}, u32[]{:S(2)}, u32[]{:S(2)}) collective-permute-start(f32[512]{0:T(512)S(1)} %get-tuple-element.11), channel_id=1, source_target_pairs={{0,20},{4,16},{8,28},{12,24},{16,4},{20,0},{24,12},{28,8},{1,21},{... | collective-permute-start | bytes 6152 | tf_op jit(solution)/shard_map/ppermute | solution.py:73
  28.5 0.5 collective-permute-done.7
  29.0 2.2 %collective-permute-start.9 = (f32[512]{0:T(512)S(1)}, f32[512]{0:T(512)S(1)}, u32[]{:S(2)}, u32[]{:S(2)}) collective-permute-start(f32[512]{0:T(512)S(1)} %get-tuple-element.11), channel_id=1, source_target_pairs={{0,24},{4,28},{8,16},{12,20},{16,8},{20,12},{24,0},{28,4},{1,25},{... | collective-permute-start | bytes 6152 | tf_op jit(solution)/shard_map/ppermute | solution.py:73
  31.2 3.7 %collective-permute-start.10 = (f32[512]{0:T(512)S(1)}, f32[512]{0:T(512)S(1)}, u32[]{:S(2)}, u32[]{:S(2)}) collective-permute-start(f32[512]{0:T(512)S(1)} %get-tuple-element.11), channel_id=1, source_target_pairs={{0,28},{4,24},{8,20},{12,16},{16,12},{20,8},{24,4},{28,0},{1,29},{... | collective-permute-start | bytes 6152 | tf_op jit(solution)/shard_map/ppermute | solution.py:73
  34.9 1.3 collective-permute-done.10
  36.3 0.6 gather_fusion
  37.0 14.4 %collective-permute-done.1 = bf16[2048,320]{0,1:T(8,128)(2,1)} collective-permute-done((bf16[2048,320]{0,1:T(8,128)(2,1)S(1)}, bf16[2048,320]{0,1:T(8,128)(2,1)}, u32[]{:S(2)}, u32[]{:S(2)}) %collective-permute-start.1) | collective-permute-done | bytes 1310752 | tf_op jit(solution)/shard_map/ppermute | solution.py:63
  51.4 2.6 %constant_dynamic-update-slice_fusion.2 = bf16[8192,320]{0,1:T(8,128)(2,1)} fusion(bf16[8192,320]{0,1:T(8,128)(2,1)} %get-tuple-element.10, bf16[2048,320]{0,1:T(8,128)(2,1)} %collective-permute-done.1, s32[]{:T(128)S(6)} %select_n.122), kind=kLoop, calls=%fused_computation.72 | loop fusion | bytes 2621444 | tf_op jit(solution)/shard_map/dynamic_update_slice | solution.py:64
  54.0 26.0 %collective-permute-done.2 = bf16[2048,320]{0,1:T(8,128)(2,1)} collective-permute-done((bf16[2048,320]{0,1:T(8,128)(2,1)S(1)}, bf16[2048,320]{0,1:T(8,128)(2,1)}, u32[]{:S(2)}, u32[]{:S(2)}) %collective-permute-start.2) | collective-permute-done | bytes 1310752 | tf_op jit(solution)/shard_map/ppermute | solution.py:63
  80.0 2.6 %constant_dynamic-update-slice_fusion.1 = bf16[8192,320]{0,1:T(8,128)(2,1)} fusion(bf16[8192,320]{0,1:T(8,128)(2,1)} %constant_dynamic-update-slice_fusion.2, bf16[2048,320]{0,1:T(8,128)(2,1)} %collective-permute-done.2, s32[]{:T(128)S(6)} %select_n.123), kind=kLoop, calls=%fused_computation.71 | loop fusion | bytes 2621444 | tf_op jit(solution)/shard_map/dynamic_update_slice | solution.py:64
  82.6 2.6 %constant_dynamic-update-slice_fusion = bf16[8192,320]{0,1:T(8,128)(2,1)} fusion(bf16[8192,320]{0,1:T(8,128)(2,1)} %constant_dynamic-update-slice_fusion.1, bf16[2048,320]{0,1:T(8,128)(2,1)} %collective-permute-done.3, s32[]{:T(128)S(6)} %select_n.124), kind=kLoop, calls=%fused_computation.70 | loop fusion | bytes 2621444 | tf_op jit(solution)/shard_map/dynamic_update_slice | solution.py:64
  85.2 10.5 %all-gather.2.cloned.1.call-done = bf16[512,8192]{1,0:T(8,128)(2,1)} async-done(((bf16[512,1024]{1,0:T(8,128)(2,1)}), bf16[512,8192]{1,0:T(8,128)(2,1)}) %all-gather.2.cloned.1.call-update) | async-done | bytes 8388624 | tf_op jit(solution)/shard_map/all_gather | solution.py:76
  95.7 10.1 %convolution_multiply_fusion = f32[512,320]{0,1:T(8,128)S(1)} fusion(bf16[512,8192]{1,0:T(8,128)(2,1)} %all-gather.2.cloned.1.call-done, bf16[8192,320]{0,1:T(8,128)(2,1)} %constant_dynamic-update-slice_fusion, f32[512]{0:T(512)S(1)} %add_rsqrt_fusion), kind=kOutput, calls=%fused_computation.15 | convolution fusion | flops 2684518400 | bytes 14288896 | tf_op jit(solution)/shard_map/dot_general | solution.py:77
  105.9 0.3 fusion.28
  106.3 0.2 stack.54
  106.6 0.2 stack.55
  106.8 3.4 %collective-permute-start.11 = (bf16[2,512,32]{1,2,0:T(8,128)(2,1)S(1)}, bf16[2,512,32]{1,2,0:T(8,128)(2,1)S(1)}, u32[]{:S(2)}, u32[]{:S(2)}) collective-permute-start(bf16[2,512,32]{1,2,0:T(8,128)(2,1)S(1)} %pad_maximum_fusion.1), channel_id=1, source_target_pairs={{0,1},{1,2},{2,3},{4,5},{5,6},{6,7},{8,9},{9,10},{10,11},{12,13},{... | collective-permute-start | bytes 196616 | tf_op jit(solution)/shard_map/ppermute | solution.py:19
  110.4 1.5 scatter_fusion
  111.9 0.7 copy.33
  112.5 3.3 %all-to-all-start.1 = ((bf16[4,16,2,512]{3,1,2,0:T(8,128)(2,1)}), bf16[4,16,2,512]{3,1,2,0:T(8,128)(2,1)S(1)}, u32[]{:S(2)}, u32[]{:S(2)}) async-start(bf16[4,16,2,512]{3,1,2,0:T(8,128)(2,1)} %copy.33), calls=%async_computation.1 | async-start | bytes 262144 | tf_op jit(solution)/shard_map/all_to_all | solution.py:152
  115.9 5.0 %all-to-all-done.1 = bf16[4,16,2,512]{3,1,2,0:T(8,128)(2,1)S(1)} async-done(((bf16[4,16,2,512]{3,1,2,0:T(8,128)(2,1)}), bf16[4,16,2,512]{3,1,2,0:T(8,128)(2,1)S(1)}, u32[]{:S(2)}, u32[]{:S(2)}) %all-to-all-start.1) | async-done | bytes 131104 | tf_op jit(solution)/shard_map/all_to_all | solution.py:152
  120.9 1.1 broadcast_in_dim.76
  122.0 3.6 %all-to-all-start = ((bf16[8,2,1024,32]{2,3,1,0:T(8,128)(2,1)}), bf16[8,2,1024,32]{2,3,1,0:T(8,128)(2,1)S(1)}, u32[]{:S(2)}, u32[]{:S(2)}) async-start(bf16[8,2,1024,32]{2,3,1,0:T(8,128)(2,1)} %broadcast_in_dim.76), calls=%async_computation | async-start | bytes 2097152 | tf_op jit(solution)/shard_map/all_to_all | solution.py:98
  125.6 3.0 %collective-permute-start = (s32[512]{0:T(512)S(1)}, s32[512]{0:T(512)S(1)}, u32[]{:S(2)}, u32[]{:S(2)}) collective-permute-start(s32[512]{0:T(512)S(1)} %broadcast_add_fusion), channel_id=1, source_target_pairs={{0,1},{1,2},{2,3},{4,5},{5,6},{6,7},{8,9},{9,10},{10,11},{12,13},{... | collective-permute-start | bytes 6152 | tf_op jit(solution)/shard_map/ppermute | solution.py:19
  128.7 1.0 collective-permute-done
  129.8 2.6 %fusion.21 = bf16[512,256]{0,1:T(8,128)(2,1)S(1)} fusion(f32[512,320]{0,1:T(8,128)S(1)} %convolution_multiply_fusion, f32[512,1]{0,1:T(1,128)S(1)} %get-tuple-element.16, f32[512,255]{0,1:T(8,128)S(1)} %get-tuple-element.18, f32[512,255]{0,1:T(8,128)S(1)} %get-tuple-element.17, f32[512,1]{0,1:T(1,128)S(1)} %get-tuple-element.13, ...), kind=kLoop, calls=%fused_computation.25 | loop fusion | flops 1310720 | bytes 1838336 | tf_op jit(solution)/shard_map/convert_element_type | solution.py:85
  132.4 0.2 copy.27
  132.6 0.3 reshape.189
  133.0 0.9 copy.35
  133.9 0.9 copy.36
  134.8 17.2 %all-to-all-done = bf16[8,2,1024,32]{2,3,1,0:T(8,128)(2,1)S(1)} async-done(((bf16[8,2,1024,32]{2,3,1,0:T(8,128)(2,1)}), bf16[8,2,1024,32]{2,3,1,0:T(8,128)(2,1)S(1)}, u32[]{:S(2)}, u32[]{:S(2)}) %all-to-all-start) | async-done | bytes 1048608 | tf_op jit(solution)/shard_map/all_to_all | solution.py:98
  152.1 1.8 %fusion.36 = (f32[1024]{0:T(1024)S(1)}, f32[1024,1024]{0,1:T(8,128)S(1)}) fusion(s32[1024]{0:T(1024)S(1)} %bitcast.69, pred[1024]{0:T(1024)(128)(4,1)S(1)} %broadcast_compare_fusion, s32[1024]{0:T(1024)S(1)} %bitcast.66, s32[1024]{0:T(1024)S(1)} %pad_add_fusion, bf16[1024,128]{1,0:T(8,128)(2,1)S(1)} %bitcast.61, bf16[1024,128]{0,1:T(8,128)(2,1)S(1)} %bitcast.65), kind=kOutput, calls=%fused_computation.86 | convolution fusion | flops 275774464 | bytes 4736000 | tf_op jit(solution)/shard_map/dot_general | solution.py:112
  153.9 2.1 %fusion.1 = f32[1024]{0:T(1024)S(1)} fusion(f32[1024]{0:T(1024)S(1)} %get-tuple-element.25, f32[1024,1024]{0,1:T(8,128)S(1)} %get-tuple-element.26, s32[1024]{0:T(1024)S(1)} %bitcast.70, pred[1024]{0:T(1024)(128)(4,1)S(1)} %broadcast_compare_fusion, s32[1024]{0:T(1024)S(1)} %bitcast.67, s32[1024]{0:T(1024)S(1)} %pad_add_fusion), kind=kLoop, calls=%fused_computation.6 | loop fusion | flops 8387584 | bytes 4215808 | tf_op jit(solution)/shard_map/reduce_sum | solution.py:123
  156.0 2.3 %fusion.14 = bf16[1024,128]{1,0:T(8,128)(2,1)S(1)} fusion(bf16[1024,128]{0,1:T(8,128)(2,1)S(1)} %bitcast.64, f32[1024]{0:T(1024)S(1)} %get-tuple-element.25, f32[1024]{0:T(1024)S(1)} %fusion.1, pred[1024]{0:T(1024)(128)(4,1)S(1)} %ge.25, f32[1024,1024]{0,1:T(8,128)S(1)} %get-tuple-element.26, s32[1024]{0:T(1024)S(1)} %bitcast.71, s32[1024]{0:T(1024)S(1)} %bitcast.68, ...), kind=kOutput, calls=%fused_computation.18 | convolution fusion | flops 277217280 | bytes 4741120 | tf_op jit(solution)/shard_map/dot_general | solution.py:125
  158.4 0.7 copy.43
  (59 shorter events, 1.2 us)
Async XLA Ops:
  7.2 88.5 %all-gather.2.cloned.1.call-start = ((), (), s32[]{:S(2)}) async-start(), calls=%async_computation.2 | async-start | bytes 9437184 | tf_op jit(solution)/shard_map/all_gather | solution.py:76
  10.4 7.7 %copy-start = (bf16[2048,32]{0,1:T(8,128)(2,1)S(1)}, bf16[2048,32]{0,1:T(8,128)(2,1)}, u32[]{:S(2)}) copy-start(bf16[2048,32]{0,1:T(8,128)(2,1)} %param.12) | copy-start | bytes 393220
  10.4 7.7 %copy-start.1 = (bf16[2048,32]{0,1:T(8,128)(2,1)S(1)}, bf16[2048,32]{0,1:T(8,128)(2,1)}, u32[]{:S(2)}) copy-start(bf16[2048,32]{0,1:T(8,128)(2,1)} %param.11) | copy-start | bytes 393220
  10.5 13.0 %collective-permute-start.4 = (f32[512]{0:T(512)S(1)}, f32[512]{0:T(512)S(1)}, u32[]{:S(2)}, u32[]{:S(2)}) collective-permute-start(f32[512]{0:T(512)S(1)} %get-tuple-element.11), channel_id=1, source_target_pairs={{0,4},{4,0},{8,12},{12,8},{16,20},{20,16},{24,28},{28,24},{1,5},{5... | collective-permute-start | bytes 6152 | tf_op jit(solution)/shard_map/ppermute | solution.py:73
  11.0 12.6 %collective-permute-start.5 = (f32[512]{0:T(512)S(1)}, f32[512]{0:T(512)S(1)}, u32[]{:S(2)}, u32[]{:S(2)}) collective-permute-start(f32[512]{0:T(512)S(1)} %get-tuple-element.11), channel_id=1, source_target_pairs={{0,8},{4,12},{8,0},{12,4},{16,24},{20,28},{24,16},{28,20},{1,9},{5... | collective-permute-start | bytes 6152 | tf_op jit(solution)/shard_map/ppermute | solution.py:73
  15.1 8.0 %copy-start.3 = (s32[32,1]{0,1:T(1,128)S(1)}, s32[32,1]{0,1:T(1,128)}, u32[]{:S(2)}) copy-start(s32[32,1]{0,1:T(1,128)} %param.15) | copy-start | bytes 388
  15.1 19.7 %copy-start.4 = (s32[512]{0:T(512)S(1)}, s32[512]{0:T(512)}, u32[]{:S(2)}) copy-start(s32[512]{0:T(512)} %param.14) | copy-start | bytes 6148
  19.6 31.7 %collective-permute-start.1 = (bf16[2048,320]{0,1:T(8,128)(2,1)S(1)}, bf16[2048,320]{0,1:T(8,128)(2,1)}, u32[]{:S(2)}, u32[]{:S(2)}) collective-permute-start(bf16[2048,320]{0,1:T(8,128)(2,1)S(1)} %get-tuple-element.9), channel_id=1, source_target_pairs={{0,1},{1,0},{2,3},{3,2},{4,5},{5,4},{6,7},{7,6},{8,9},{9,8},{10,11... | collective-permute-start | bytes 3932168 | tf_op jit(solution)/shard_map/ppermute | solution.py:63
  21.2 58.8 %collective-permute-start.2 = (bf16[2048,320]{0,1:T(8,128)(2,1)S(1)}, bf16[2048,320]{0,1:T(8,128)(2,1)}, u32[]{:S(2)}, u32[]{:S(2)}) collective-permute-start(bf16[2048,320]{0,1:T(8,128)(2,1)S(1)} %get-tuple-element.9), channel_id=1, source_target_pairs={{0,2},{1,3},{2,0},{3,1},{4,6},{5,7},{6,4},{7,5},{8,10},{9,11},{10,... | collective-permute-start | bytes 3932168 | tf_op jit(solution)/shard_map/ppermute | solution.py:63
  22.7 59.9 %collective-permute-start.3 = (bf16[2048,320]{0,1:T(8,128)(2,1)S(1)}, bf16[2048,320]{0,1:T(8,128)(2,1)}, u32[]{:S(2)}, u32[]{:S(2)}) collective-permute-start(bf16[2048,320]{0,1:T(8,128)(2,1)S(1)} %get-tuple-element.9), channel_id=1, source_target_pairs={{0,3},{1,2},{2,1},{3,0},{4,7},{5,6},{6,5},{7,4},{8,11},{9,10},{10,... | collective-permute-start | bytes 3932168 | tf_op jit(solution)/shard_map/ppermute | solution.py:63
  23.5 3.1 %collective-permute-start.6 = (f32[512]{0:T(512)S(1)}, f32[512]{0:T(512)S(1)}, u32[]{:S(2)}, u32[]{:S(2)}) collective-permute-start(f32[512]{0:T(512)S(1)} %get-tuple-element.11), channel_id=1, source_target_pairs={{0,12},{4,8},{8,4},{12,0},{16,28},{20,24},{24,20},{28,16},{1,13},{... | collective-permute-start | bytes 6152 | tf_op jit(solution)/shard_map/ppermute | solution.py:73
  23.6 5.4 %collective-permute-start.7 = (f32[512]{0:T(512)S(1)}, f32[512]{0:T(512)S(1)}, u32[]{:S(2)}, u32[]{:S(2)}) collective-permute-start(f32[512]{0:T(512)S(1)} %get-tuple-element.11), channel_id=1, source_target_pairs={{0,16},{4,20},{8,24},{12,28},{16,0},{20,4},{24,8},{28,12},{1,17},{... | collective-permute-start | bytes 6152 | tf_op jit(solution)/shard_map/ppermute | solution.py:73
  26.6 4.6 %collective-permute-start.8 = (f32[512]{0:T(512)S(1)}, f32[512]{0:T(512)S(1)}, u32[]{:S(2)}, u32[]{:S(2)}) collective-permute-start(f32[512]{0:T(512)S(1)} %get-tuple-element.11), channel_id=1, source_target_pairs={{0,20},{4,16},{8,28},{12,24},{16,4},{20,0},{24,12},{28,8},{1,21},{... | collective-permute-start | bytes 6152 | tf_op jit(solution)/shard_map/ppermute | solution.py:73
  29.0 5.9 %collective-permute-start.9 = (f32[512]{0:T(512)S(1)}, f32[512]{0:T(512)S(1)}, u32[]{:S(2)}, u32[]{:S(2)}) collective-permute-start(f32[512]{0:T(512)S(1)} %get-tuple-element.11), channel_id=1, source_target_pairs={{0,24},{4,28},{8,16},{12,20},{16,8},{20,12},{24,0},{28,4},{1,25},{... | collective-permute-start | bytes 6152 | tf_op jit(solution)/shard_map/ppermute | solution.py:73
  31.2 5.1 %collective-permute-start.10 = (f32[512]{0:T(512)S(1)}, f32[512]{0:T(512)S(1)}, u32[]{:S(2)}, u32[]{:S(2)}) collective-permute-start(f32[512]{0:T(512)S(1)} %get-tuple-element.11), channel_id=1, source_target_pairs={{0,28},{4,24},{8,20},{12,16},{16,12},{20,8},{24,4},{28,0},{1,29},{... | collective-permute-start | bytes 6152 | tf_op jit(solution)/shard_map/ppermute | solution.py:73
  105.8 19.8 %copy-start.2 = (s32[512]{0:T(512)S(1)}, s32[512]{0:T(512)}, u32[]{:S(2)}) copy-start(s32[512]{0:T(512)} %param.13) | copy-start | bytes 6148
  106.8 9.1 %collective-permute-start.11 = (bf16[2,512,32]{1,2,0:T(8,128)(2,1)S(1)}, bf16[2,512,32]{1,2,0:T(8,128)(2,1)S(1)}, u32[]{:S(2)}, u32[]{:S(2)}) collective-permute-start(bf16[2,512,32]{1,2,0:T(8,128)(2,1)S(1)} %pad_maximum_fusion.1), channel_id=1, source_target_pairs={{0,1},{1,2},{2,3},{4,5},{5,6},{6,7},{8,9},{9,10},{10,11},{12,13},{... | collective-permute-start | bytes 196616 | tf_op jit(solution)/shard_map/ppermute | solution.py:19
  112.5 8.3 %all-to-all-start.1 = ((bf16[4,16,2,512]{3,1,2,0:T(8,128)(2,1)}), bf16[4,16,2,512]{3,1,2,0:T(8,128)(2,1)S(1)}, u32[]{:S(2)}, u32[]{:S(2)}) async-start(bf16[4,16,2,512]{3,1,2,0:T(8,128)(2,1)} %copy.33), calls=%async_computation.1 | async-start | bytes 262144 | tf_op jit(solution)/shard_map/all_to_all | solution.py:152
  122.0 30.1 %all-to-all-start = ((bf16[8,2,1024,32]{2,3,1,0:T(8,128)(2,1)}), bf16[8,2,1024,32]{2,3,1,0:T(8,128)(2,1)S(1)}, u32[]{:S(2)}, u32[]{:S(2)}) async-start(bf16[8,2,1024,32]{2,3,1,0:T(8,128)(2,1)} %broadcast_in_dim.76), calls=%async_computation | async-start | bytes 2097152 | tf_op jit(solution)/shard_map/all_to_all | solution.py:98
  125.6 4.1 %collective-permute-start = (s32[512]{0:T(512)S(1)}, s32[512]{0:T(512)S(1)}, u32[]{:S(2)}, u32[]{:S(2)}) collective-permute-start(s32[512]{0:T(512)S(1)} %broadcast_add_fusion), channel_id=1, source_target_pairs={{0,1},{1,2},{2,3},{4,5},{5,6},{6,7},{8,9},{9,10},{10,11},{12,13},{... | collective-permute-start | bytes 6152 | tf_op jit(solution)/shard_map/ppermute | solution.py:19
Sparse Core Ops, SparseCore 0:
  10.6 85.0 all-gather.1

commit v5 on v4

--- a/solution.py
+++ b/solution.py
@@ -42,6 +42,14 @@
     )
 
 
+def joined(mine, theirs, mine_first):
+    return jnp.where(
+        mine_first,
+        jnp.concatenate([mine, theirs], axis=-1),
+        jnp.concatenate([theirs, mine], axis=-1),
+    )
+
+
 def shards(
     tokens_in, norm_gain, query_weight, key_weight, value_weight, segment_ids, positions, page_owner
 ):
@@ -51,19 +59,18 @@
     quarters = HD // quarter
     gx_count = lax.axis_size("gx")
     gy_count = lax.axis_size("gy")
-    my_gx = lax.axis_index("gx")
+    spot = lax.axis_index("gx") % quarters
     my_gy = lax.axis_index("gy")
-    spot = my_gx % quarters
     row_block = query_weight.shape[0]
 
     local_weights = jnp.concatenate([query_weight, key_weight, value_weight], axis=1)
-    all_rows = jnp.zeros((gy_count * row_block, local_weights.shape[1]), local_weights.dtype)
-    all_rows = lax.dynamic_update_slice_in_dim(all_rows, local_weights, my_gy * row_block, 0)
+    pieces = [(my_gy, local_weights)]
     for k in range(1, gy_count):
         got = lax.ppermute(local_weights, "gy", partner_route(gy_count, gy_count, k))
-        all_rows = lax.dynamic_update_slice_in_dim(all_rows, got, (my_gy ^ k) * row_block, 0)
+        pieces.append((my_gy ^ k, got))
 
     local_float = tokens_in.astype(jnp.float32)
+    my_gx = lax.axis_index("gx")
     feature_block = tokens_in.shape[1]
     local_gain = lax.dynamic_slice_in_dim(norm_gain, my_gx * feature_block, feature_block, 0)
     local_normed = (local_float * local_gain.astype(jnp.float32)[None, :]).astype(jnp.bfloat16)
@@ -73,36 +80,53 @@
         square_parts.append(lax.ppermute(local_squares, "gx", partner_route(gx_count, gx_count, k)))
     square_order = jnp.arange(gx_count, dtype=jnp.int32) ^ my_gx
     squares = jnp.sum(jnp.take(jnp.stack(square_parts), square_order, axis=0), axis=0)
-    normed = lax.all_gather(local_normed, "gx", axis=1, tiled=True)
-    products = jnp.dot(normed, all_rows, preferred_element_type=jnp.float32)
-    scaling = 1.0 / jnp.sqrt(squares / D + EPSILON)
-    projected = products * scaling[:, None]
-    query_cols = head_local * HD
-    key_piece = rope(
-        projected[:, query_cols : query_cols + quarter], positions, quarter, spot * (quarter // 2)
-    ).astype(jnp.bfloat16)
-    value_piece = projected[:, query_cols + quarter :].astype(jnp.bfloat16)
-    queries = rope(projected[:, :query_cols], positions, HD, 0).astype(jnp.bfloat16)
-    own_kv = jnp.stack([key_piece, value_piece])
-
     span_count = gy_count // 4
     marks = segment_ids + 1
-    kv_list = [own_kv]
     mark_list = [marks]
     for shift_by in range(1, span_count + 1):
-        kv_list.insert(0, shifted(own_kv, "gy", shift_by))
         mark_list.insert(0, shifted(marks, "gy", shift_by))
-    window_quarter = jnp.concatenate(kv_list, axis=1)
-    window_rows = window_quarter.shape[1]
-    sent = jnp.broadcast_to(window_quarter[None], (gx_count,) + window_quarter.shape)
-    got = lax.all_to_all(sent, "gx", split_axis=0, concat_axis=0, tiled=True)
-    group_start = my_gx - spot
-    head_parts = lax.dynamic_slice_in_dim(got, group_start, quarters, 0)
-    window_kv = head_parts.transpose(1, 2, 0, 3).reshape(2, window_rows, HD)
+    scaling = 1.0 / jnp.sqrt(squares / D + EPSILON)
+    query_cols = head_local * HD
+    halves = 2
+    half_rows = token_count // halves
+    query_halves, kv_halves, head_halves = [], [], []
+    for h in range(halves):
+        rows_of = slice(h * half_rows, (h + 1) * half_rows)
+        normed = lax.all_gather(local_normed[rows_of], "gx", axis=1, tiled=True)
+        if head_halves:
+            normed, head_halves[-1] = lax.optimization_barrier((normed, head_halves[-1]))
+        products = None
+        for source, block in pieces:
+            rows = lax.dynamic_slice_in_dim(normed, source * row_block, row_block, 1)
+            part = jnp.dot(rows, block, preferred_element_type=jnp.float32)
+            products = part if products is None else products + part
+        projected = products * scaling[rows_of, None]
+        places = positions[rows_of]
+        key_piece = rope(
+            projected[:, query_cols : query_cols + quarter], places, quarter, spot * (quarter // 2)
+        ).astype(jnp.bfloat16)
+        value_piece = projected[:, query_cols + quarter :].astype(jnp.bfloat16)
+        query_halves.append(rope(projected[:, :query_cols], places, HD, 0).astype(jnp.bfloat16))
+        own_kv = jnp.stack([key_piece, value_piece])
+        kv_halves.append(own_kv)
+        window_list = [own_kv]
+        for shift_by in range(1, span_count + 1):
+            window_list.insert(0, shifted(own_kv, "gy", shift_by))
+        held = jnp.concatenate(window_list, axis=1)
+        step = 1
+        while step < quarters:
+            theirs = lax.ppermute(held, "gx", partner_route(gx_count, quarters, step))
+            held = joined(held, theirs, (spot // step) % 2 == 0)
+            step *= 2
+        head_halves.append(held.reshape(2, span_count + 1, half_rows, HD))
+    queries = jnp.concatenate(query_halves, axis=0)
+    own_kv = jnp.concatenate(kv_halves, axis=1)
+    key_piece = own_kv[0]
+    value_piece = own_kv[1]
+    window_kv = jnp.stack(head_halves, axis=2).reshape(2, (span_count + 1) * token_count, HD)
     window_keys = window_kv[0]
     window_values = window_kv[1]
     window_marks = jnp.concatenate(mark_list, axis=0)
-
     reach_rows = span_count * token_count
     query_rows = (
         queries.reshape(token_count, head_local, HD)
@@ -114,7 +138,7 @@
     ) * HD ** (-0.5)
     query_marks = jnp.tile(segment_ids, head_local)
     query_place = jnp.tile(jnp.arange(token_count, dtype=jnp.int32), head_local)
-    key_place = jnp.arange(window_rows, dtype=jnp.int32)
+    key_place = jnp.arange(window_keys.shape[0], dtype=jnp.int32)
     allowed = (window_marks[None, :] == query_marks[:, None] + 1) & (window_marks[None, :] > 0)
     allowed = allowed & (key_place[None, :] <= query_place[:, None] + reach_rows)
     masked = jnp.where(allowed, scores, MASKED)
@@ -131,7 +155,6 @@
         .reshape(token_count, head_local * HD)
         .astype(jnp.bfloat16)
     )
-
     owner_count = gy_count
     page_rows = token_count // PAGE
     capacity = max(2, 2 * page_rows // owner_count)

time: 166 us -> 152 us (0.916)
  waiting for transfers between devices: 76.3 us -> 64.3 us
  local copies, waits for them, and re-layouts: 20.3 us -> 14 us
  other arithmetic: 10.3 us -> 14.2 us
    ppermute x3, waiting for transfers between devices: 40.4 us -> 20 us  [shards(): lax.ppermute(local_weights, 'gy', partner_route(gy_count, gy_count, k))]
    all_to_all x1 -> x0, waiting for transfers between devices: 17.2 us -> none  [shards(): got = lax.all_to_all(sent, 'gx', split_axis=0, concat_axis=0, tiled=True)]
    all_gather x1 -> x2, waiting for transfers between devices: 10.5 us -> 24.1 us  [shards(): normed = lax.all_gather(local_normed[rows_of], 'gx', axis=1, tiled=True)]
    ppermute x0 -> x4, waiting for transfers between devices: none -> 10.9 us  [shards(): theirs = lax.ppermute(held, 'gx', partner_route(gx_count, quarters, step))]
    dynamic_update_slice x3 -> x0, local copies, waits for them, and re-layouts: 7.83 us -> none  [shards(): lax.dynamic_update_slice_in_dim(all_rows, got, (my_gy ^ k) * row_block, 0)]
    ppermute x7, starting transfers between devices: 13.6 us -> 9.24 us  [shards(): lax.ppermute(local_squares, 'gx', partner_route(gx_count, gx_count, k))]
    ppermute x2 -> x3, starting transfers between devices: 6.41 us -> 10.7 us  [shifted(): return lax.ppermute(value, axis, pairs)]
    broadcast_in_dim x2 -> x0, local copies, waits for them, and re-layouts: 4.12 us -> none  [the longest x1 3.02 us: shards(): jnp.zeros((gy_count * row_block, local_weights.shape[1]), local_weights.d...]
  transfers between devices with their start and end apart: 15 -> 20, of which waited for: 9 -> 9; matrix products, arithmetic and copies ran while one was open for 13% -> 16% of each run, Pallas kernels for 0% -> 0%
where the time goes in v5:
time: 152 us; the launch traced here: 151 us
  waiting for transfers between devices  64.3 us (42%)
  starting transfers between devices  29.4 us (19%)
  matrix products  14.8 us (10%)
  between operations  14.7 us (10%)
  other arithmetic  14.2 us (9%)
  local copies, waits for them, and re-layouts  14 us (9%)
    all_gather x2, waiting for transfers between devices, shards(): normed = lax.all_gather(local_normed[rows_of], 'gx', axis=1, tiled=True)  24.1 us
    ppermute x3, waiting for transfers between devices, shards(): lax.ppermute(local_weights, 'gy', partner_route(gy_count, gy_count, k))  20 us
    ppermute x4, waiting for transfers between devices, shards(): theirs = lax.ppermute(held, 'gx', partner_route(gx_count, quarters, step))  10.9 us
    dot_general x8, matrix products, shards(): part = jnp.dot(rows, block, preferred_element_type=jnp.float32)  10.9 us
    ppermute x3, starting transfers between devices, shifted(): return lax.ppermute(value, axis, pairs)  10.7 us
    ppermute x7, starting transfers between devices, shards(): lax.ppermute(local_squares, 'gx', partner_route(gx_count, gx_count, k))  9.24 us
    unnamed x36, local copies, waits for them, and re-layouts  4.08 us
    all_to_all x1, waiting for transfers between devices, shards(): lax.all_to_all(send_kv, 'gy', split_axis=0, concat_axis=0, tiled=True)  3.91 us
  transfers between devices with their start and end apart: 20, of which 9 were waited for; matrix products, arithmetic and copies ran while one was open for 16% of the time, Pallas kernels for 0%

profile of v5, /device:TPU:0, one launch (start us, length us, event | category | flops | bytes accessed | tf_op | source)
XLA Modules:
  0.0 151.5 jit_solution(1812020111824778495)
XLA Ops:
  7.2 0.7 dynamic-slice_convert_fusion
  7.9 1.7 %fusion.4 = (f32[512]{0:T(512)S(1)}, bf16[512,1024]{1,0:T(8,128)(2,1)S(1)}) fusion(bf16[512,1024]{1,0:T(8,128)(2,1)} %param.8, f32[1024]{0:T(1024)S(1)} %dynamic-slice_convert_fusion), kind=kLoop, calls=%fused_computation.11 | loop fusion | flops 2620928 | bytes 2103296 | tf_op jit(solution)/shard_map/reduce_sum | solution.py:77
  9.6 1.1 fusion.81
  10.8 0.7 all-gather.5.cloned.1.call-update
  12.0 2.6 %collective-permute-start.5 = (f32[512]{0:T(512)S(1)}, f32[512]{0:T(512)S(1)}, u32[]{:S(2)}, u32[]{:S(2)}) collective-permute-start(f32[512]{0:T(512)S(1)} %get-tuple-element.13), channel_id=1, source_target_pairs={{0,8},{4,12},{8,0},{12,4},{16,24},{20,28},{24,16},{28,20},{1,9},{5... | collective-permute-start | bytes 6152 | tf_op jit(solution)/shard_map/ppermute | solution.py:80
  14.7 0.6 copy.37
  15.4 1.0 copy-done
  16.4 1.2 pad_maximum_fusion
  17.6 1.6 %collective-permute-start.1 = (bf16[2048,320]{0,1:T(8,128)(2,1)}, bf16[2048,320]{0,1:T(8,128)(2,1)S(1)}, u32[]{:S(2)}, u32[]{:S(2)}) collective-permute-start(bf16[2048,320]{0,1:T(8,128)(2,1)} %pad_maximum_fusion), channel_id=1, source_target_pairs={{0,1},{1,0},{2,3},{3,2},{4,5},{5,4},{6,7},{7,6},{8,9},{9,8},{10,11... | collective-permute-start | bytes 3932168 | tf_op jit(solution)/shard_map/ppermute | solution.py:69
  19.2 1.5 collective-permute-start.3
  22.3 2.6 %collective-permute-start.7 = (f32[512]{0:T(512)S(1)}, f32[512]{0:T(512)S(1)}, u32[]{:S(2)}, u32[]{:S(2)}) collective-permute-start(f32[512]{0:T(512)S(1)} %get-tuple-element.13), channel_id=1, source_target_pairs={{0,16},{4,20},{8,24},{12,28},{16,0},{20,4},{24,8},{28,12},{1,17},{... | collective-permute-start | bytes 6152 | tf_op jit(solution)/shard_map/ppermute | solution.py:80
  25.5 1.7 %collective-permute-done.7 = f32[512]{0:T(512)S(1)} collective-permute-done((f32[512]{0:T(512)S(1)}, f32[512]{0:T(512)S(1)}, u32[]{:S(2)}, u32[]{:S(2)}) %collective-permute-start.7) | collective-permute-done | bytes 2080 | tf_op jit(solution)/shard_map/ppermute | solution.py:80
  27.3 3.4 %collective-permute-start.9 = (f32[512]{0:T(512)S(1)}, f32[512]{0:T(512)S(1)}, u32[]{:S(2)}, u32[]{:S(2)}) collective-permute-start(f32[512]{0:T(512)S(1)} %get-tuple-element.13), channel_id=1, source_target_pairs={{0,24},{4,28},{8,16},{12,20},{16,8},{20,12},{24,0},{28,4},{1,25},{... | collective-permute-start | bytes 6152 | tf_op jit(solution)/shard_map/ppermute | solution.py:80
  31.3 1.4 collective-permute-done.9
  32.7 3.5 %collective-permute-start = (s32[512]{0:T(512)S(1)}, s32[512]{0:T(512)S(1)}, u32[]{:S(2)}, u32[]{:S(2)}) collective-permute-start(s32[512]{0:T(512)S(1)} %broadcast_add_fusion), channel_id=1, source_target_pairs={{0,1},{1,2},{2,3},{4,5},{5,6},{6,7},{8,9},{9,10},{10,11},{12,13},{... | collective-permute-start | bytes 6152 | tf_op jit(solution)/shard_map/ppermute | solution.py:19
  36.9 24.1 %all-gather.3.cloned.1.call-done = bf16[256,8192]{1,0:T(8,128)(2,1)} async-done(((bf16[256,1024]{1,0:T(8,128)(2,1)}), bf16[256,8192]{1,0:T(8,128)(2,1)}) %all-gather.3.cloned.1.call-update) | async-done | bytes 4194320 | tf_op jit(solution)/shard_map/all_gather | solution.py:95
  61.0 2.2 %fusion.31 = f32[256,320]{0,1:T(8,128)S(1)} fusion(bf16[256,8192]{1,0:T(8,128)(2,1)} %all-gather.3.cloned.1.call-done, s32[]{:T(128)S(6)} %select_n.215, bf16[2048,32]{0,1:T(8,128)(2,1)S(1)} %copy-done.7, bf16[2048,32]{0,1:T(8,128)(2,1)S(1)} %copy-done.8, bf16[2048,256]{0,1:T(8,128)(2,1)} %copy-done), kind=kOutput, calls=%fused_computation.36 | convolution fusion | flops 339476480 | bytes 2686980 | tf_op jit(solution)/shard_map/dot_general | solution.py:101
  63.3 14.9 %collective-permute-done.3 = bf16[2048,320]{0,1:T(8,128)(2,1)S(1)} collective-permute-done((bf16[2048,320]{0,1:T(8,128)(2,1)}, bf16[2048,320]{0,1:T(8,128)(2,1)S(1)}, u32[]{:S(2)}, u32[]{:S(2)}) %collective-permute-start.3) | collective-permute-done | bytes 1310752 | tf_op jit(solution)/shard_map/ppermute | solution.py:69
  78.1 0.6 fusion.27
  78.7 0.6 convolution_add_fusion.3
  79.4 5.1 %collective-permute-done.2 = bf16[2048,320]{0,1:T(8,128)(2,1)} collective-permute-done((bf16[2048,320]{0,1:T(8,128)(2,1)}, bf16[2048,320]{0,1:T(8,128)(2,1)}, u32[]{:S(2)}, u32[]{:S(2)}) %collective-permute-start.2) | collective-permute-done | bytes 1310752 | tf_op jit(solution)/shard_map/ppermute | solution.py:69
  84.5 1.9 %fusion.19 = f32[256,320]{0,1:T(8,128)S(1)} fusion(f32[256,320]{0,1:T(8,128)S(1)} %fusion.27, f32[256,320]{0,1:T(8,128)S(1)} %convolution_add_fusion.3, bf16[2048,320]{0,1:T(8,128)(2,1)} %collective-permute-done.2, bf16[256,8192]{1,0:T(8,128)(2,1)S(1)} %copy-done.2, s32[]{:T(128)S(6)} %select_n.217, f32[256]{0:T(256)S(1)} %get-tuple-element.42), kind=kOutput, calls=%fused_computation.24 | convolution fusion | flops 335790080 | bytes 3343364 | tf_op jit(solution)/shard_map/dot_general | solution.py:101
  86.7 3.4 %collective-permute-start.11 = (bf16[2,256,32]{1,2,0:T(8,128)(2,1)S(1)}, bf16[2,256,32]{1,2,0:T(8,128)(2,1)S(1)}, u32[]{:S(2)}, u32[]{:S(2)}) collective-permute-start(bf16[2,256,32]{1,2,0:T(8,128)(2,1)S(1)} %pad_maximum_fusion.5), channel_id=1, source_target_pairs={{0,1},{1,2},{2,3},{4,5},{5,6},{6,7},{8,9},{9,10},{10,11},{12,13},{... | collective-permute-start | bytes 98312 | tf_op jit(solution)/shard_map/ppermute | solution.py:19
  90.1 1.6 %collective-permute-done.11 = bf16[2,256,32]{1,2,0:T(8,128)(2,1)S(1)} collective-permute-done((bf16[2,256,32]{1,2,0:T(8,128)(2,1)S(1)}, bf16[2,256,32]{1,2,0:T(8,128)(2,1)S(1)}, u32[]{:S(2)}, u32[]{:S(2)}) %collective-permute-start.11) | collective-permute-done | bytes 32800 | tf_op jit(solution)/shard_map/ppermute | solution.py:19
  91.7 1.2 collective-permute-done.12
  92.9 0.7 maximum_select_fusion.4
  93.6 1.6 %collective-permute-start.13 = (bf16[2,512,64]{1,2,0:T(8,128)(2,1)}, bf16[2,512,64]{1,2,0:T(8,128)(2,1)}, u32[]{:S(2)}, u32[]{:S(2)}) collective-permute-start(bf16[2,512,64]{1,2,0:T(8,128)(2,1)} %maximum_select_fusion.4), channel_id=1, source_target_pairs={{0,8},{4,12},{8,0},{12,4},{16,24},{20,28},{24,16},{28,20},{1,9},{5... | collective-permute-start | bytes 393224 | tf_op jit(solution)/shard_map/ppermute | solution.py:118
  95.2 0.8 fusion.83
  96.2 1.0 copy.60
  97.2 1.0 maximum_select_fusion
  98.2 9.7 %collective-permute-done.13 = bf16[2,512,64]{1,2,0:T(8,128)(2,1)} collective-permute-done((bf16[2,512,64]{1,2,0:T(8,128)(2,1)}, bf16[2,512,64]{1,2,0:T(8,128)(2,1)}, u32[]{:S(2)}, u32[]{:S(2)}) %collective-permute-start.13) | collective-permute-done | bytes 131104 | tf_op jit(solution)/shard_map/ppermute | solution.py:118
  107.9 1.1 copy.61
  109.0 1.3 maximum_select_fusion.1
  110.3 2.3 %fusion.25 = f32[256,320]{0,1:T(8,128)S(1)} fusion(bf16[256,8192]{1,0:T(8,128)(2,1)} %all-gather.5.cloned.1.call-done, s32[]{:T(128)S(6)} %select_n.215, bf16[2048,32]{0,1:T(8,128)(2,1)} %param.12, bf16[2048,32]{0,1:T(8,128)(2,1)} %param.11, bf16[2048,256]{0,1:T(8,128)(2,1)} %copy-done), kind=kOutput, calls=%fused_computation.30 | convolution fusion | flops 339476480 | bytes 2686980 | tf_op jit(solution)/shard_map/dot_general | solution.py:101
  113.8 0.6 convolution_add_fusion.1
  114.5 2.0 %fusion.20 = f32[256,320]{0,1:T(8,128)S(1)} fusion(f32[256,320]{0,1:T(8,128)S(1)} %fusion.21, f32[256,320]{0,1:T(8,128)S(1)} %convolution_add_fusion.1, bf16[2048,320]{0,1:T(8,128)(2,1)} %collective-permute-done.2, bf16[256,8192]{1,0:T(8,128)(2,1)S(1)} %copy-done.1, s32[]{:T(128)S(6)} %select_n.217, f32[256]{0:T(256)S(1)} %get-tuple-element.41), kind=kOutput, calls=%fused_computation.25 | convolution fusion | flops 335790080 | bytes 3343364 | tf_op jit(solution)/shard_map/dot_general | solution.py:101
  116.8 3.8 %collective-permute-start.14 = (bf16[2,256,32]{1,2,0:T(8,128)(2,1)S(1)}, bf16[2,256,32]{1,2,0:T(8,128)(2,1)S(1)}, u32[]{:S(2)}, u32[]{:S(2)}) collective-permute-start(bf16[2,256,32]{1,2,0:T(8,128)(2,1)S(1)} %pad_maximum_fusion.6), channel_id=1, source_target_pairs={{0,1},{1,2},{2,3},{4,5},{5,6},{6,7},{8,9},{9,10},{10,11},{12,13},{... | collective-permute-start | bytes 98312 | tf_op jit(solution)/shard_map/ppermute | solution.py:19
  120.6 2.7 %fusion.43 = (bf16[256,256]{0,1:T(8,128)(2,1)S(1)}, bf16[256,256]{0,1:T(8,128)(2,1)S(1)}) fusion(f32[256,320]{0,1:T(8,128)S(1)} %fusion.19, f32[256,1]{0,1:T(1,128)S(1)} %get-tuple-element.24, f32[256,255]{0,1:T(8,128)S(1)} %copy-done.5, f32[256,255]{0,1:T(8,128)S(1)} %copy-done.4, f32[256,1]{0,1:T(1,128)S(1)} %get-tuple-element.21, ...), kind=kLoop, calls=%fused_computation.54 | loop fusion | flops 1310720 | bytes 1838336 | tf_op jit(solution)/shard_map/convert_element_type | solution.py:109
  124.4 1.5 scatter_fusion
  125.9 0.7 copy.55
  126.5 3.5 %all-to-all-start = ((bf16[4,16,2,512]{3,1,2,0:T(8,128)(2,1)}), bf16[4,16,2,512]{3,1,2,0:T(8,128)(2,1)S(1)}, u32[]{:S(2)}, u32[]{:S(2)}) async-start(bf16[4,16,2,512]{3,1,2,0:T(8,128)(2,1)} %copy.55), calls=%async_computation | async-start | bytes 262144 | tf_op jit(solution)/shard_map/all_to_all | solution.py:175
  131.2 3.9 %all-to-all-done = bf16[4,16,2,512]{3,1,2,0:T(8,128)(2,1)S(1)} async-done(((bf16[4,16,2,512]{3,1,2,0:T(8,128)(2,1)}), bf16[4,16,2,512]{3,1,2,0:T(8,128)(2,1)S(1)}, u32[]{:S(2)}, u32[]{:S(2)}) %all-to-all-start) | async-done | bytes 131104 | tf_op jit(solution)/shard_map/all_to_all | solution.py:175
  135.4 0.9 copy.57
  136.3 0.9 copy.58
  137.8 1.6 %fusion.80 = (f32[1024]{0:T(1024)S(1)}, f32[1024,1024]{0,1:T(8,128)S(1)}) fusion(s32[1024]{0:T(1024)S(1)} %bitcast.92, pred[1024]{0:T(1024)(128)(4,1)S(1)} %broadcast_compare_fusion, s32[1024]{0:T(1024)S(1)} %bitcast.89, s32[1024]{0:T(1024)S(1)} %pad_add_fusion, bf16[1024,128]{1,0:T(8,128)(2,1)S(1)} %bitcast.84, bf16[1024,128]{1,0:T(8,128)(2,1)S(1)} %bitcast.88), kind=kOutput, calls=%fused_computation.147 | convolution fusion | flops 275774464 | bytes 4736000 | tf_op jit(solution)/shard_map/dot_general | solution.py:136
  139.5 2.1 %fusion.1 = f32[1024]{0:T(1024)S(1)} fusion(f32[1024]{0:T(1024)S(1)} %get-tuple-element.45, f32[1024,1024]{0,1:T(8,128)S(1)} %get-tuple-element.46, s32[1024]{0:T(1024)S(1)} %bitcast.93, pred[1024]{0:T(1024)(128)(4,1)S(1)} %broadcast_compare_fusion, s32[1024]{0:T(1024)S(1)} %bitcast.90, s32[1024]{0:T(1024)S(1)} %pad_add_fusion), kind=kLoop, calls=%fused_computation.6 | loop fusion | flops 8387584 | bytes 4215808 | tf_op jit(solution)/shard_map/reduce_sum | solution.py:147
  141.6 2.3 %fusion.14 = bf16[1024,128]{1,0:T(8,128)(2,1)S(1)} fusion(bf16[1024,128]{1,0:T(8,128)(2,1)S(1)} %bitcast.87, f32[1024]{0:T(1024)S(1)} %get-tuple-element.45, f32[1024]{0:T(1024)S(1)} %fusion.1, pred[1024]{0:T(1024)(128)(4,1)S(1)} %copy-done.12, f32[1024,1024]{0,1:T(8,128)S(1)} %get-tuple-element.46, s32[1024]{0:T(1024)S(1)} %bitcast.94, ...), kind=kOutput, calls=%fused_computation.17 | convolution fusion | flops 277217280 | bytes 4741120 | tf_op jit(solution)/shard_map/dot_general | solution.py:149
  143.9 0.7 copy.69
  (109 shorter events, 9.0 us)
Async XLA Ops:
  7.2 53.9 %all-gather.3.cloned.1.call-start = ((), (), s32[]{:S(2)}) async-start(), calls=%async_computation.1 | async-start | bytes 4718592 | tf_op jit(solution)/shard_map/all_gather | solution.py:95
  7.9 6.8 %copy-start.3 = (bf16[2048,256]{1,0:T(8,128)(2,1)S(1)}, bf16[2048,256]{1,0:T(8,128)(2,1)}, u32[]{:S(2)}) copy-start(bf16[2048,256]{1,0:T(8,128)(2,1)} %param.10) | copy-start | bytes 3145732
  9.6 6.8 %copy-start.7 = (bf16[2048,32]{0,1:T(8,128)(2,1)S(1)}, bf16[2048,32]{0,1:T(8,128)(2,1)}, u32[]{:S(2)}) copy-start(bf16[2048,32]{0,1:T(8,128)(2,1)} %param.12) | copy-start | bytes 393220
  9.6 6.8 %copy-start.8 = (bf16[2048,32]{0,1:T(8,128)(2,1)S(1)}, bf16[2048,32]{0,1:T(8,128)(2,1)}, u32[]{:S(2)}) copy-start(bf16[2048,32]{0,1:T(8,128)(2,1)} %param.11) | copy-start | bytes 393220
  10.7 99.6 %all-gather.5.cloned.1.call-start = ((), (), s32[]{:S(2)}) async-start(), calls=%async_computation.2 | async-start | bytes 4718592 | tf_op jit(solution)/shard_map/all_gather | solution.py:95
  10.8 9.9 %copy-start.10 = (s32[32,1]{0,1:T(1,128)S(1)}, s32[32,1]{0,1:T(1,128)}, u32[]{:S(2)}) copy-start(s32[32,1]{0,1:T(1,128)} %param.15) | copy-start | bytes 388
  10.8 10.3 %copy-start.9 = (s32[512]{0:T(512)S(1)}, s32[512]{0:T(512)}, u32[]{:S(2)}) copy-start(s32[512]{0:T(512)} %param.13) | copy-start | bytes 6148
  10.8 10.3 %copy-start.11 = (s32[512]{0:T(512)S(1)}, s32[512]{0:T(512)}, u32[]{:S(2)}) copy-start(s32[512]{0:T(512)} %param.14) | copy-start | bytes 6148
  11.5 10.8 %collective-permute-start.4 = (f32[512]{0:T(512)S(1)}, f32[512]{0:T(512)S(1)}, u32[]{:S(2)}, u32[]{:S(2)}) collective-permute-start(f32[512]{0:T(512)S(1)} %get-tuple-element.13), channel_id=1, source_target_pairs={{0,4},{4,0},{8,12},{12,8},{16,20},{20,16},{24,28},{28,24},{1,5},{5... | collective-permute-start | bytes 6152 | tf_op jit(solution)/shard_map/ppermute | solution.py:80
  12.0 12.9 %collective-permute-start.5 = (f32[512]{0:T(512)S(1)}, f32[512]{0:T(512)S(1)}, u32[]{:S(2)}, u32[]{:S(2)}) collective-permute-start(f32[512]{0:T(512)S(1)} %get-tuple-element.13), channel_id=1, source_target_pairs={{0,8},{4,12},{8,0},{12,4},{16,24},{20,28},{24,16},{28,20},{1,9},{5... | collective-permute-start | bytes 6152 | tf_op jit(solution)/shard_map/ppermute | solution.py:80
  14.7 10.3 %collective-permute-start.6 = (f32[512]{0:T(512)S(1)}, f32[512]{0:T(512)S(1)}, u32[]{:S(2)}, u32[]{:S(2)}) collective-permute-start(f32[512]{0:T(512)S(1)} %get-tuple-element.13), channel_id=1, source_target_pairs={{0,12},{4,8},{8,4},{12,0},{16,28},{20,24},{24,20},{28,16},{1,13},{... | collective-permute-start | bytes 6152 | tf_op jit(solution)/shard_map/ppermute | solution.py:80
  15.4 1.0 copy-start
  17.6 61.2 %collective-permute-start.1 = (bf16[2048,320]{0,1:T(8,128)(2,1)}, bf16[2048,320]{0,1:T(8,128)(2,1)S(1)}, u32[]{:S(2)}, u32[]{:S(2)}) collective-permute-start(bf16[2048,320]{0,1:T(8,128)(2,1)} %pad_maximum_fusion), channel_id=1, source_target_pairs={{0,1},{1,0},{2,3},{3,2},{4,5},{5,4},{6,7},{7,6},{8,9},{9,8},{10,11... | collective-permute-start | bytes 3932168 | tf_op jit(solution)/shard_map/ppermute | solution.py:69
  19.2 58.9 %collective-permute-start.3 = (bf16[2048,320]{0,1:T(8,128)(2,1)}, bf16[2048,320]{0,1:T(8,128)(2,1)S(1)}, u32[]{:S(2)}, u32[]{:S(2)}) collective-permute-start(bf16[2048,320]{0,1:T(8,128)(2,1)} %pad_maximum_fusion), channel_id=1, source_target_pairs={{0,3},{1,2},{2,1},{3,0},{4,7},{5,6},{6,5},{7,4},{8,11},{9,10},{10,... | collective-permute-start | bytes 3932168 | tf_op jit(solution)/shard_map/ppermute | solution.py:69
  22.3 4.9 %collective-permute-start.7 = (f32[512]{0:T(512)S(1)}, f32[512]{0:T(512)S(1)}, u32[]{:S(2)}, u32[]{:S(2)}) collective-permute-start(f32[512]{0:T(512)S(1)} %get-tuple-element.13), channel_id=1, source_target_pairs={{0,16},{4,20},{8,24},{12,28},{16,0},{20,4},{24,8},{28,12},{1,17},{... | collective-permute-start | bytes 6152 | tf_op jit(solution)/shard_map/ppermute | solution.py:80
  24.9 5.8 %collective-permute-start.8 = (f32[512]{0:T(512)S(1)}, f32[512]{0:T(512)S(1)}, u32[]{:S(2)}, u32[]{:S(2)}) collective-permute-start(f32[512]{0:T(512)S(1)} %get-tuple-element.13), channel_id=1, source_target_pairs={{0,20},{4,16},{8,28},{12,24},{16,4},{20,0},{24,12},{28,8},{1,21},{... | collective-permute-start | bytes 6152 | tf_op jit(solution)/shard_map/ppermute | solution.py:80
  24.9 59.5 %collective-permute-start.2 = (bf16[2048,320]{0,1:T(8,128)(2,1)}, bf16[2048,320]{0,1:T(8,128)(2,1)}, u32[]{:S(2)}, u32[]{:S(2)}) collective-permute-start(bf16[2048,320]{0,1:T(8,128)(2,1)} %pad_maximum_fusion), channel_id=1, source_target_pairs={{0,2},{1,3},{2,0},{3,1},{4,6},{5,7},{6,4},{7,5},{8,10},{9,11},{10,... | collective-permute-start | bytes 3932168 | tf_op jit(solution)/shard_map/ppermute | solution.py:69
  27.3 5.5 %collective-permute-start.9 = (f32[512]{0:T(512)S(1)}, f32[512]{0:T(512)S(1)}, u32[]{:S(2)}, u32[]{:S(2)}) collective-permute-start(f32[512]{0:T(512)S(1)} %get-tuple-element.13), channel_id=1, source_target_pairs={{0,24},{4,28},{8,16},{12,20},{16,8},{20,12},{24,0},{28,4},{1,25},{... | collective-permute-start | bytes 6152 | tf_op jit(solution)/shard_map/ppermute | solution.py:80
  30.7 5.5 %collective-permute-start.10 = (f32[512]{0:T(512)S(1)}, f32[512]{0:T(512)S(1)}, u32[]{:S(2)}, u32[]{:S(2)}) collective-permute-start(f32[512]{0:T(512)S(1)} %get-tuple-element.13), channel_id=1, source_target_pairs={{0,28},{4,24},{8,20},{12,16},{16,12},{20,8},{24,4},{28,0},{1,29},{... | collective-permute-start | bytes 6152 | tf_op jit(solution)/shard_map/ppermute | solution.py:80
  32.7 57.3 %collective-permute-start = (s32[512]{0:T(512)S(1)}, s32[512]{0:T(512)S(1)}, u32[]{:S(2)}, u32[]{:S(2)}) collective-permute-start(s32[512]{0:T(512)S(1)} %broadcast_add_fusion), channel_id=1, source_target_pairs={{0,1},{1,2},{2,3},{4,5},{5,6},{6,7},{8,9},{9,10},{10,11},{12,13},{... | collective-permute-start | bytes 6152 | tf_op jit(solution)/shard_map/ppermute | solution.py:19
  61.0 17.1 %copy-start.2 = (bf16[256,8192]{1,0:T(8,128)(2,1)S(1)}, bf16[256,8192]{1,0:T(8,128)(2,1)}, u32[]{:S(2)}) copy-start(bf16[256,8192]{1,0:T(8,128)(2,1)} %all-gather.3.cloned.1.call-done) | copy-start | bytes 12582916
  86.7 5.0 %collective-permute-start.11 = (bf16[2,256,32]{1,2,0:T(8,128)(2,1)S(1)}, bf16[2,256,32]{1,2,0:T(8,128)(2,1)S(1)}, u32[]{:S(2)}, u32[]{:S(2)}) collective-permute-start(bf16[2,256,32]{1,2,0:T(8,128)(2,1)S(1)} %pad_maximum_fusion.5), channel_id=1, source_target_pairs={{0,1},{1,2},{2,3},{4,5},{5,6},{6,7},{8,9},{9,10},{10,11},{12,13},{... | collective-permute-start | bytes 98312 | tf_op jit(solution)/shard_map/ppermute | solution.py:19
  91.6 1.3 collective-permute-start.12
  92.9 3.1 %copy-start.6 = (bf16[2,512,32]{1,2,0:T(8,128)(2,1)}, bf16[2,512,32]{1,2,0:T(8,128)(2,1)S(1)}, u32[]{:S(2)}) copy-start(bf16[2,512,32]{1,2,0:T(8,128)(2,1)S(1)} %collective-permute-done.12) | copy-start | bytes 196612
  93.6 14.3 %collective-permute-start.13 = (bf16[2,512,64]{1,2,0:T(8,128)(2,1)}, bf16[2,512,64]{1,2,0:T(8,128)(2,1)}, u32[]{:S(2)}, u32[]{:S(2)}) collective-permute-start(bf16[2,512,64]{1,2,0:T(8,128)(2,1)} %maximum_select_fusion.4), channel_id=1, source_target_pairs={{0,8},{4,12},{8,0},{12,4},{16,24},{20,28},{24,16},{28,20},{1,9},{5... | collective-permute-start | bytes 393224 | tf_op jit(solution)/shard_map/ppermute | solution.py:118
  110.3 2.9 %copy-start.1 = (bf16[256,8192]{1,0:T(8,128)(2,1)S(1)}, bf16[256,8192]{1,0:T(8,128)(2,1)}, u32[]{:S(2)}) copy-start(bf16[256,8192]{1,0:T(8,128)(2,1)} %all-gather.5.cloned.1.call-done) | copy-start | bytes 12582916
  114.5 6.2 %copy-start.4 = (f32[256,255]{0,1:T(8,128)S(1)}, f32[256,255]{0,1:T(8,128)}, u32[]{:S(2)}) copy-start(f32[256,255]{0,1:T(8,128)} %get-tuple-element.25) | copy-start | bytes 783364
  114.5 6.2 %copy-start.5 = (f32[256,255]{0,1:T(8,128)S(1)}, f32[256,255]{0,1:T(8,128)}, u32[]{:S(2)}) copy-start(f32[256,255]{0,1:T(8,128)} %get-tuple-element.26) | copy-start | bytes 783364
  114.5 6.2 %copy-start.14 = (pred[256]{0:T(512)(128)(4,1)S(1)}, pred[256]{0:T(512)(128)(4,1)}, u32[]{:S(2)}) copy-start(pred[256]{0:T(512)(128)(4,1)} %fusion.76) | copy-start | bytes 772
  116.5 7.9 %copy-start.13 = (s32[32]{0:T(128)S(1)}, s32[32]{0:T(128)}, u32[]{:S(2)}) copy-start(s32[32]{0:T(128)} %fusion.79) | copy-start | bytes 388
  116.8 6.5 %collective-permute-start.14 = (bf16[2,256,32]{1,2,0:T(8,128)(2,1)S(1)}, bf16[2,256,32]{1,2,0:T(8,128)(2,1)S(1)}, u32[]{:S(2)}, u32[]{:S(2)}) collective-permute-start(bf16[2,256,32]{1,2,0:T(8,128)(2,1)S(1)} %pad_maximum_fusion.6), channel_id=1, source_target_pairs={{0,1},{1,2},{2,3},{4,5},{5,6},{6,7},{8,9},{9,10},{10,11},{12,13},{... | collective-permute-start | bytes 98312 | tf_op jit(solution)/shard_map/ppermute | solution.py:19
  123.3 6.7 %collective-permute-start.15 = (bf16[2,512,32]{1,2,0:T(8,128)(2,1)S(1)}, bf16[2,512,32]{1,2,0:T(8,128)(2,1)S(1)}, u32[]{:S(2)}, u32[]{:S(2)}) collective-permute-start(bf16[2,512,32]{1,2,0:T(8,128)(2,1)S(1)} %get-tuple-element.38), channel_id=1, source_target_pairs={{0,4},{4,0},{8,12},{12,8},{16,20},{20,16},{24,28},{28,24},{1,5},{5... | collective-permute-start | bytes 196616 | tf_op jit(solution)/shard_map/ppermute | solution.py:118
  126.5 8.5 %all-to-all-start = ((bf16[4,16,2,512]{3,1,2,0:T(8,128)(2,1)}), bf16[4,16,2,512]{3,1,2,0:T(8,128)(2,1)S(1)}, u32[]{:S(2)}, u32[]{:S(2)}) async-start(bf16[4,16,2,512]{3,1,2,0:T(8,128)(2,1)} %copy.55), calls=%async_computation | async-start | bytes 262144 | tf_op jit(solution)/shard_map/all_to_all | solution.py:175
  130.1 7.2 %collective-permute-start.16 = (bf16[2,512,64]{1,2,0:T(8,128)(2,1)S(1)}, bf16[2,512,64]{1,2,0:T(8,128)(2,1)S(1)}, u32[]{:S(2)}, u32[]{:S(2)}) collective-permute-start(bf16[2,512,64]{1,2,0:T(8,128)(2,1)S(1)} %maximum_select_fusion.5), channel_id=1, source_target_pairs={{0,8},{4,12},{8,0},{12,4},{16,24},{20,28},{24,16},{28,20},{1,9},{5... | collective-permute-start | bytes 393224 | tf_op jit(solution)/shard_map/ppermute | solution.py:118
  139.4 2.1 %copy-start.12 = (pred[1024]{0:T(1024)(128)(4,1)S(1)}, pred[1024]{0:T(1024)(128)(4,1)}, u32[]{:S(2)}) copy-start(pred[1024]{0:T(1024)(128)(4,1)} %ge.25) | copy-start | bytes 3076
Sparse Core Ops, SparseCore 0:
  10.9 50.1 all-gather.2
  62.6 47.3 all-gather.4

commit v6 on v5

--- a/solution.py
+++ b/solution.py
@@ -63,7 +63,11 @@
     my_gy = lax.axis_index("gy")
     row_block = query_weight.shape[0]
 
-    local_weights = jnp.concatenate([query_weight, key_weight, value_weight], axis=1)
+    kv_weights = jnp.stack([key_weight, value_weight])
+    sibling = lax.ppermute(kv_weights, "gx", partner_route(gx_count, quarters, 1))
+    half_weights = joined(kv_weights, sibling, spot % 2 == 0)
+    local_weights = jnp.concatenate([query_weight, half_weights[0], half_weights[1]], axis=1)
+    half_cols = 2 * quarter
     pieces = [(my_gy, local_weights)]
     for k in range(1, gy_count):
         got = lax.ppermute(local_weights, "gy", partner_route(gy_count, gy_count, k))
@@ -102,22 +106,30 @@
             products = part if products is None else products + part
         projected = products * scaling[rows_of, None]
         places = positions[rows_of]
-        key_piece = rope(
-            projected[:, query_cols : query_cols + quarter], places, quarter, spot * (quarter // 2)
+        key_half = rope(
+            projected[:, query_cols : query_cols + half_cols],
+            places,
+            half_cols,
+            (spot // 2) * quarter,
         ).astype(jnp.bfloat16)
-        value_piece = projected[:, query_cols + quarter :].astype(jnp.bfloat16)
+        value_half = projected[:, query_cols + half_cols :].astype(jnp.bfloat16)
         query_halves.append(rope(projected[:, :query_cols], places, HD, 0).astype(jnp.bfloat16))
-        own_kv = jnp.stack([key_piece, value_piece])
-        kv_halves.append(own_kv)
-        window_list = [own_kv]
+        half_kv = jnp.stack([key_half, value_half])
+        kv_halves.append(lax.dynamic_slice_in_dim(half_kv, (spot % 2) * quarter, quarter, 2))
+        low_half = (spot // 2) % 2 == 0
+        window_list = [
+            joined(half_kv, lax.ppermute(half_kv, "gx", partner_route(gx_count, quarters, 2)), low_half)
+        ]
         for shift_by in range(1, span_count + 1):
-            window_list.insert(0, shifted(own_kv, "gy", shift_by))
+            route = []
+            for i in range(gx_count):
+                peer = i - i % quarters + ((i % quarters) ^ 2)
+                for j in range(gy_count - shift_by):
+                    route.append((i * gy_count + j, peer * gy_count + j + shift_by))
+            same = shifted(half_kv, "gy", shift_by)
+            other = lax.ppermute(half_kv, ("gx", "gy"), route)
+            window_list.insert(0, joined(same, other, low_half))
         held = jnp.concatenate(window_list, axis=1)
-        step = 1
-        while step < quarters:
-            theirs = lax.ppermute(held, "gx", partner_route(gx_count, quarters, step))
-            held = joined(held, theirs, (spot // step) % 2 == 0)
-            step *= 2
         head_halves.append(held.reshape(2, span_count + 1, half_rows, HD))
     queries = jnp.concatenate(query_halves, axis=0)
     own_kv = jnp.concatenate(kv_halves, axis=1)

time: 152 us -> 164 us (1.079)
  starting transfers between devices: 29.4 us -> 37 us
  matrix products: 14.8 us -> 21.3 us
  other arithmetic: 14.2 us -> 19.2 us
  waiting for transfers between devices: 64.3 us -> 60.2 us
  local copies, waits for them, and re-layouts: 14 us -> 11.4 us
    ppermute x3, waiting for transfers between devices: 1.56 us -> 55.6 us  [shifted(): return lax.ppermute(value, axis, pairs)]
    all_gather x2, waiting for transfers between devices: 24.1 us -> 0.01 us  [shards(): normed = lax.all_gather(local_normed[rows_of], 'gx', axis=1, tiled=True)]
    ppermute x3, waiting for transfers between devices: 20 us -> 0.01 us  [shards(): lax.ppermute(local_weights, 'gy', partner_route(gy_count, gy_count, k))]
    ppermute x4 -> x5, starting transfers between devices: 2.25 us -> 9.95 us  [the longest x2 5.42 us: shards(): other = lax.ppermute(half_kv, ('gx', 'gy'), route)]
    ppermute x4 -> x5, waiting for transfers between devices: 10.9 us -> 3.85 us  [the longest x2 3.84 us: shards(): lax.ppermute(half_kv, 'gx', partner_route(gx_count, quarters, 2))]
    dot_general x8, matrix products: 10.9 us -> 16.6 us  [shards(): part = jnp.dot(rows, block, preferred_element_type=jnp.float32)]
    all_to_all x1, waiting for transfers between devices: 3.91 us -> 0.01 us  [shards(): lax.all_to_all(send_kv, 'gy', split_axis=0, concat_axis=0, tiled=True)]
    ppermute x7, waiting for transfers between devices: 3.18 us -> 0.02 us  [shards(): lax.ppermute(local_squares, 'gx', partner_route(gx_count, gx_count, k))]
  transfers between devices with their start and end apart: 20 -> 21, of which waited for: 9 -> 2; matrix products, arithmetic and copies ran while one was open for 16% -> 22% of each run, Pallas kernels for 0% -> 0%
where the time goes in v6:
time: 164 us
  waiting for transfers between devices  60.2 us (37%)
  starting transfers between devices  37 us (23%)
  matrix products  21.3 us (13%)
  other arithmetic  19.2 us (12%)
  between operations  14.8 us (9%)
  local copies, waits for them, and re-layouts  11.4 us (7%)
    ppermute x3, waiting for transfers between devices, shifted(): return lax.ppermute(value, axis, pairs)  55.6 us
    dot_general x8, matrix products, shards(): part = jnp.dot(rows, block, preferred_element_type=jnp.float32)  16.6 us
    ppermute x3, starting transfers between devices, shifted(): return lax.ppermute(value, axis, pairs)  10.3 us
    ppermute x7, starting transfers between devices, shards(): lax.ppermute(local_squares, 'gx', partner_route(gx_count, gx_count, k))  9.7 us
    ppermute x2, starting transfers between devices, shards(): other = lax.ppermute(half_kv, ('gx', 'gy'), route)  5.42 us
    ppermute x2, starting transfers between devices, shards(): lax.ppermute(half_kv, 'gx', partner_route(gx_count, quarters, 2))  4.14 us
    ppermute x2, waiting for transfers between devices, shards(): lax.ppermute(half_kv, 'gx', partner_route(gx_count, quarters, 2))  3.84 us
    ppermute x3, starting transfers between devices, shards(): lax.ppermute(local_weights, 'gy', partner_route(gy_count, gy_count, k))  3.63 us
  transfers between devices with their start and end apart: 21, of which 2 were waited for; matrix products, arithmetic and copies ran while one was open for 22% of the time, Pallas kernels for 0%

profile of v6, /device:TPU:0, one launch (start us, length us, event | category | flops | bytes accessed | tf_op | source)
XLA Modules:
  0.0 163.8 jit_solution(18251412076862381261)
XLA Ops:
  7.3 0.8 dynamic-slice_convert_fusion
  8.0 1.6 fusion.4
  9.6 1.1 fusion.82
  10.8 0.7 all-gather.5.cloned.1.call-update
  11.5 5.1 %collective-permute-start.10 = (f32[512]{0:T(512)S(1)}, f32[512]{0:T(512)S(1)}, u32[]{:S(2)}, u32[]{:S(2)}) collective-permute-start(f32[512]{0:T(512)S(1)} %get-tuple-element.16), channel_id=1, source_target_pairs={{0,24},{4,28},{8,16},{12,20},{16,8},{20,12},{24,0},{28,4},{1,25},{... | collective-permute-start | bytes 6152 | tf_op jit(solution)/shard_map/ppermute | solution.py:84
  19.4 1.6 pad_maximum_fusion
  21.1 2.5 %collective-permute-start.4 = (bf16[2048,384]{1,0:T(8,128)(2,1)S(1)}, bf16[2048,384]{1,0:T(8,128)(2,1)S(1)}, u32[]{:S(2)}, u32[]{:S(2)}) collective-permute-start(bf16[2048,384]{1,0:T(8,128)(2,1)S(1)} %pad_maximum_fusion), channel_id=1, source_target_pairs={{0,3},{1,2},{2,1},{3,0},{4,7},{5,6},{6,5},{7,4},{8,11},{9,10},{10,... | collective-permute-start | bytes 4718600 | tf_op jit(solution)/shard_map/ppermute | solution.py:73
  25.8 1.1 collective-permute-start.7
  27.4 2.9 %collective-permute-start.8 = (f32[512]{0:T(512)S(1)}, f32[512]{0:T(512)S(1)}, u32[]{:S(2)}, u32[]{:S(2)}) collective-permute-start(f32[512]{0:T(512)S(1)} %get-tuple-element.16), channel_id=1, source_target_pairs={{0,16},{4,20},{8,24},{12,28},{16,0},{20,4},{24,8},{28,12},{1,17},{... | collective-permute-start | bytes 6152 | tf_op jit(solution)/shard_map/ppermute | solution.py:84
  30.7 3.4 %collective-permute-start = (s32[512]{0:T(512)S(1)}, s32[512]{0:T(512)S(1)}, u32[]{:S(2)}, u32[]{:S(2)}) collective-permute-start(s32[512]{0:T(512)S(1)} %broadcast_add_fusion), channel_id=1, source_target_pairs={{0,1},{1,2},{2,3},{4,5},{5,6},{6,7},{8,9},{9,10},{10,11},{12,13},{... | collective-permute-start | bytes 6152 | tf_op jit(solution)/shard_map/ppermute | solution.py:19
  34.2 0.6 ge.25
  35.4 0.6 collective-permute-start.3
  36.0 55.6 %collective-permute-done = s32[512]{0:T(512)S(1)} collective-permute-done((s32[512]{0:T(512)S(1)}, s32[512]{0:T(512)S(1)}, u32[]{:S(2)}, u32[]{:S(2)}) %collective-permute-start) | collective-permute-done | bytes 2080 | tf_op jit(solution)/shard_map/ppermute | solution.py:19
  91.5 0.6 broadcast_compare_fusion
  92.2 0.6 fusion.89
  92.8 2.1 %fusion.31 = f32[256,384]{1,0:T(8,128)S(1)} fusion(bf16[2048,384]{1,0:T(8,128)(2,1)S(1)} %pad_maximum_fusion, bf16[256,8192]{1,0:T(8,128)(2,1)} %all-gather.3.cloned.1.call-done, s32[]{:T(128)S(6)} %select_n.199), kind=kOutput, calls=%fused_computation.36 | convolution fusion | flops 402653184 | bytes 3014660 | tf_op jit(solution)/shard_map/dot_general | solution.py:105
  94.9 1.9 %fusion.27 = f32[256,384]{1,0:T(8,128)S(1)} fusion(bf16[2048,384]{1,0:T(8,128)(2,1)S(1)} %collective-permute-done.4, bf16[256,8192]{1,0:T(8,128)(2,1)} %all-gather.3.cloned.1.call-done, s32[]{:T(128)S(6)} %select_n.206), kind=kOutput, calls=%fused_computation.32 | convolution fusion | flops 402653184 | bytes 3014660 | tf_op jit(solution)/shard_map/dot_general | solution.py:105
  96.9 2.1 %convolution_add_fusion.3 = f32[256,384]{1,0:T(8,128)S(1)} fusion(f32[256,384]{1,0:T(8,128)S(1)} %fusion.31, bf16[2048,384]{1,0:T(8,128)(2,1)} %collective-permute-done.2, bf16[256,8192]{1,0:T(8,128)(2,1)S(1)} %copy-done.1, s32[]{:T(128)S(6)} %select_n.204), kind=kOutput, calls=%fused_computation.21 | convolution fusion | flops 402751488 | bytes 3407876 | tf_op jit(solution)/shard_map/dot_general | solution.py:105
  99.0 2.2 %fusion.18 = f32[256,384]{1,0:T(8,128)S(1)} fusion(f32[256,384]{1,0:T(8,128)S(1)} %fusion.27, f32[256,384]{1,0:T(8,128)S(1)} %convolution_add_fusion.3, bf16[2048,384]{1,0:T(8,128)(2,1)} %collective-permute-done.3, bf16[256,8192]{1,0:T(8,128)(2,1)S(1)} %copy-done.1, s32[]{:T(128)S(6)} %select_n.205, f32[256]{0:T(256)S(1)} %copy-done.13), kind=kOutput, calls=%fused_computation.23 | convolution fusion | flops 402948096 | bytes 3802116 | tf_op jit(solution)/shard_map/dot_general | solution.py:105
  101.4 0.8 fusion.83
  102.2 0.6 fusion.66
  102.8 4.5 %collective-permute-start.12 = (bf16[2,256,64]{2,1,0:T(8,128)(2,1)S(1)}, bf16[2,256,64]{2,1,0:T(8,128)(2,1)S(1)}, u32[]{:S(2)}, u32[]{:S(2)}) collective-permute-start(bf16[2,256,64]{2,1,0:T(8,128)(2,1)S(1)} %pad_maximum_fusion.6), channel_id=1, source_target_pairs={{0,1},{1,2},{2,3},{4,5},{5,6},{6,7},{8,9},{9,10},{10,11},{12,13},{... | collective-permute-start | bytes 196616 | tf_op jit(solution)/shard_map/ppermute | solution.py:19
  107.3 2.4 %collective-permute-start.13 = (bf16[2,256,64]{2,1,0:T(8,128)(2,1)S(1)}, bf16[2,256,64]{2,1,0:T(8,128)(2,1)S(1)}, u32[]{:S(2)}, u32[]{:S(2)}) collective-permute-start(bf16[2,256,64]{2,1,0:T(8,128)(2,1)S(1)} %pad_maximum_fusion.6), channel_id=1, source_target_pairs={{0,9},{1,10},{2,11},{4,13},{5,14},{6,15},{8,1},{9,2},{10,3},{12,5}... | collective-permute-start | bytes 196616 | tf_op jit(solution)/shard_map/ppermute | solution.py:130
  109.8 2.3 %collective-permute-start.14 = (bf16[2,256,64]{2,1,0:T(8,128)(2,1)S(1)}, bf16[2,256,64]{2,1,0:T(8,128)(2,1)S(1)}, u32[]{:S(2)}, u32[]{:S(2)}) collective-permute-start(bf16[2,256,64]{2,1,0:T(8,128)(2,1)S(1)} %pad_maximum_fusion.6), channel_id=1, source_target_pairs={{0,8},{4,12},{8,0},{12,4},{16,24},{20,28},{24,16},{28,20},{1,9},{5... | collective-permute-start | bytes 196616 | tf_op jit(solution)/shard_map/ppermute | solution.py:121
  112.1 0.9 fusion.84
  113.0 0.8 fusion.53
  113.7 3.8 %collective-permute-done.14 = bf16[2,256,64]{2,1,0:T(8,128)(2,1)S(1)} collective-permute-done((bf16[2,256,64]{2,1,0:T(8,128)(2,1)S(1)}, bf16[2,256,64]{2,1,0:T(8,128)(2,1)S(1)}, u32[]{:S(2)}, u32[]{:S(2)}) %collective-permute-start.14) | collective-permute-done | bytes 65568 | tf_op jit(solution)/shard_map/ppermute | solution.py:121
  117.9 0.7 pad_maximum_fusion.3
  118.6 2.1 %fusion.25 = f32[256,384]{1,0:T(8,128)S(1)} fusion(bf16[2048,384]{1,0:T(8,128)(2,1)S(1)} %pad_maximum_fusion, bf16[256,8192]{1,0:T(8,128)(2,1)} %all-gather.5.cloned.1.call-done, s32[]{:T(128)S(6)} %select_n.199), kind=kOutput, calls=%fused_computation.30 | convolution fusion | flops 402653184 | bytes 3014660 | tf_op jit(solution)/shard_map/dot_general | solution.py:105
  120.7 1.9 %fusion.21 = f32[256,384]{1,0:T(8,128)S(1)} fusion(bf16[2048,384]{1,0:T(8,128)(2,1)S(1)} %collective-permute-done.4, bf16[256,8192]{1,0:T(8,128)(2,1)} %all-gather.5.cloned.1.call-done, s32[]{:T(128)S(6)} %select_n.206), kind=kOutput, calls=%fused_computation.26 | convolution fusion | flops 402653184 | bytes 3014660 | tf_op jit(solution)/shard_map/dot_general | solution.py:105
  122.7 2.1 %convolution_add_fusion.1 = f32[256,384]{1,0:T(8,128)S(1)} fusion(f32[256,384]{1,0:T(8,128)S(1)} %fusion.25, bf16[2048,384]{1,0:T(8,128)(2,1)} %collective-permute-done.2, bf16[256,8192]{1,0:T(8,128)(2,1)S(1)} %copy-done, s32[]{:T(128)S(6)} %select_n.204), kind=kOutput, calls=%fused_computation.19 | convolution fusion | flops 402751488 | bytes 3407876 | tf_op jit(solution)/shard_map/dot_general | solution.py:105
  124.9 2.2 %fusion.20 = f32[256,384]{1,0:T(8,128)S(1)} fusion(f32[256,384]{1,0:T(8,128)S(1)} %fusion.21, f32[256,384]{1,0:T(8,128)S(1)} %convolution_add_fusion.1, bf16[2048,384]{1,0:T(8,128)(2,1)} %collective-permute-done.3, bf16[256,8192]{1,0:T(8,128)(2,1)S(1)} %copy-done, s32[]{:T(128)S(6)} %select_n.205, f32[256]{0:T(256)S(1)} %copy-done.12), kind=kOutput, calls=%fused_computation.25 | convolution fusion | flops 402948096 | bytes 3802116 | tf_op jit(solution)/shard_map/dot_general | solution.py:105
  127.6 0.6 fusion.67
  128.3 2.4 %collective-permute-start.15 = (bf16[2,256,64]{2,1,0:T(8,128)(2,1)S(1)}, bf16[2,256,64]{2,1,0:T(8,128)(2,1)S(1)}, u32[]{:S(2)}, u32[]{:S(2)}) collective-permute-start(bf16[2,256,64]{2,1,0:T(8,128)(2,1)S(1)} %pad_maximum_fusion.7), channel_id=1, source_target_pairs={{0,1},{1,2},{2,3},{4,5},{5,6},{6,7},{8,9},{9,10},{10,11},{12,13},{... | collective-permute-start | bytes 196616 | tf_op jit(solution)/shard_map/ppermute | solution.py:19
  130.8 3.0 %collective-permute-start.16 = (bf16[2,256,64]{2,1,0:T(8,128)(2,1)S(1)}, bf16[2,256,64]{2,1,0:T(8,128)(2,1)}, u32[]{:S(2)}, u32[]{:S(2)}) collective-permute-start(bf16[2,256,64]{2,1,0:T(8,128)(2,1)S(1)} %pad_maximum_fusion.7), channel_id=1, source_target_pairs={{0,9},{1,10},{2,11},{4,13},{5,14},{6,15},{8,1},{9,2},{10,3},{12,5}... | collective-permute-start | bytes 196616 | tf_op jit(solution)/shard_map/ppermute | solution.py:130
  133.8 1.8 %collective-permute-start.17 = (bf16[2,256,64]{2,1,0:T(8,128)(2,1)S(1)}, bf16[2,256,64]{2,1,0:T(8,128)(2,1)}, u32[]{:S(2)}, u32[]{:S(2)}) collective-permute-start(bf16[2,256,64]{2,1,0:T(8,128)(2,1)S(1)} %pad_maximum_fusion.7), channel_id=1, source_target_pairs={{0,8},{4,12},{8,0},{12,4},{16,24},{20,28},{24,16},{28,20},{1,9},{5... | collective-permute-start | bytes 196616 | tf_op jit(solution)/shard_map/ppermute | solution.py:121
  136.0 1.6 scatter_fusion
  137.6 0.7 copy.44
  138.3 3.3 %all-to-all-start = ((bf16[4,16,2,512]{3,1,2,0:T(8,128)(2,1)}), bf16[4,16,2,512]{3,1,2,0:T(8,128)(2,1)S(1)}, u32[]{:S(2)}, u32[]{:S(2)}) async-start(bf16[4,16,2,512]{3,1,2,0:T(8,128)(2,1)} %copy.44), calls=%async_computation | async-start | bytes 262144 | tf_op jit(solution)/shard_map/all_to_all | solution.py:187
  141.7 3.1 %fusion.43 = (bf16[256,256]{1,0:T(8,128)(2,1)S(1)}, bf16[256,256]{1,0:T(8,128)(2,1)S(1)}) fusion(f32[256,384]{1,0:T(8,128)S(1)} %fusion.18, f32[256,1]{1,0:T(8,128)S(1)} %copy-done.7, f32[256,255]{1,0:T(8,128)S(1)} %copy-done.4, f32[256,255]{1,0:T(8,128)S(1)} %copy-done.3, f32[256,1]{1,0:T(8,128)S(1)} %copy-done.6, f32[256]{0:T(256)} %multiply_power_fusion, ...), kind=kLoop, calls=%fused_computation.55 | loop fusion | flops 1310720 | bytes 1838336 | tf_op jit(solution)/shard_map/convert_element_type | solution.py:116
  144.8 1.1 maximum_select_fusion.4
  146.0 1.1 maximum_select_fusion.3
  147.2 2.4 %fusion.81 = (f32[1024]{0:T(1024)S(1)}, f32[1024,1024]{0,1:T(8,128)S(1)}) fusion(s32[1024]{0:T(1024)S(1)} %bitcast.96, pred[1024]{0:T(1024)(128)(4,1)} %broadcast_compare_fusion, s32[1024]{0:T(1024)S(1)} %bitcast.93, s32[1024]{0:T(1024)S(1)} %pad_add_fusion, bf16[1024,128]{1,0:T(8,128)(2,1)S(1)} %bitcast.88, bf16[1024,128]{1,0:T(8,128)(2,1)S(1)} %bitcast.92), kind=kOutput, calls=%fused_computation.154 | convolution fusion | flops 275774464 | bytes 4736000 | tf_op jit(solution)/shard_map/dot_general | solution.py:148
  149.6 2.1 %fusion.1 = f32[1024]{0:T(1024)S(1)} fusion(f32[1024]{0:T(1024)S(1)} %get-tuple-element.48, f32[1024,1024]{0,1:T(8,128)S(1)} %get-tuple-element.49, s32[1024]{0:T(1024)S(1)} %bitcast.97, pred[1024]{0:T(1024)(128)(4,1)S(1)} %copy-done.14, s32[1024]{0:T(1024)S(1)} %bitcast.94, s32[1024]{0:T(1024)S(1)} %pad_add_fusion), kind=kLoop, calls=%fused_computation.6 | loop fusion | flops 8387584 | bytes 4215808 | tf_op jit(solution)/shard_map/reduce_sum | solution.py:159
  151.7 2.3 %fusion.14 = bf16[1024,128]{1,0:T(8,128)(2,1)S(1)} fusion(bf16[1024,128]{1,0:T(8,128)(2,1)S(1)} %bitcast.91, f32[1024]{0:T(1024)S(1)} %get-tuple-element.48, f32[1024]{0:T(1024)S(1)} %fusion.1, pred[1024]{0:T(1024)(128)(4,1)S(1)} %copy-done.21, f32[1024,1024]{0,1:T(8,128)S(1)} %get-tuple-element.49, s32[1024]{0:T(1024)S(1)} %bitcast.98, ...), kind=kOutput, calls=%fused_computation.17 | convolution fusion | flops 277217280 | bytes 4741120 | tf_op jit(solution)/shard_map/dot_general | solution.py:161
  154.0 0.7 copy.54
  155.1 0.9 copy.46
  156.0 0.9 copy.47
  (122 shorter events, 8.7 us)
Async XLA Ops:
  7.2 9.6 %copy-start.9 = (bf16[2048,32]{0,1:T(8,128)(2,1)S(1)}, bf16[2048,32]{0,1:T(8,128)(2,1)}, u32[]{:S(2)}) copy-start(bf16[2048,32]{0,1:T(8,128)(2,1)} %param.11) | copy-start | bytes 393220
  7.2 9.6 %copy-start.8 = (bf16[2048,32]{0,1:T(8,128)(2,1)S(1)}, bf16[2048,32]{0,1:T(8,128)(2,1)}, u32[]{:S(2)}) copy-start(bf16[2048,32]{0,1:T(8,128)(2,1)} %param.12) | copy-start | bytes 393220
  7.2 10.0 %copy-start.15 = (s32[32,1]{0,1:T(1,128)S(1)}, s32[32,1]{0,1:T(1,128)}, u32[]{:S(2)}) copy-start(s32[32,1]{0,1:T(1,128)} %param.15) | copy-start | bytes 388
  7.2 10.9 %copy-start.11 = (s32[512]{0:T(512)S(1)}, s32[512]{0:T(512)}, u32[]{:S(2)}) copy-start(s32[512]{0:T(512)} %param.13) | copy-start | bytes 6148
  7.2 10.9 %copy-start.16 = (s32[512]{0:T(512)S(1)}, s32[512]{0:T(512)}, u32[]{:S(2)}) copy-start(s32[512]{0:T(512)} %param.14) | copy-start | bytes 6148
  7.2 85.6 %all-gather.3.cloned.1.call-start = ((), (), s32[]{:S(2)}) async-start(), calls=%async_computation.1 | async-start | bytes 4718592 | tf_op jit(solution)/shard_map/all_gather | solution.py:99
  10.7 107.9 %all-gather.5.cloned.1.call-start = ((), (), s32[]{:S(2)}) async-start(), calls=%async_computation.2 | async-start | bytes 4718592 | tf_op jit(solution)/shard_map/all_gather | solution.py:99
  11.5 14.3 %collective-permute-start.10 = (f32[512]{0:T(512)S(1)}, f32[512]{0:T(512)S(1)}, u32[]{:S(2)}, u32[]{:S(2)}) collective-permute-start(f32[512]{0:T(512)S(1)} %get-tuple-element.16), channel_id=1, source_target_pairs={{0,24},{4,28},{8,16},{12,20},{16,8},{20,12},{24,0},{28,4},{1,25},{... | collective-permute-start | bytes 6152 | tf_op jit(solution)/shard_map/ppermute | solution.py:84
  16.6 9.1 %collective-permute-start.11 = (f32[512]{0:T(512)S(1)}, f32[512]{0:T(512)S(1)}, u32[]{:S(2)}, u32[]{:S(2)}) collective-permute-start(f32[512]{0:T(512)S(1)} %get-tuple-element.16), channel_id=1, source_target_pairs={{0,28},{4,24},{8,20},{12,16},{16,12},{20,8},{24,4},{28,0},{1,29},{... | collective-permute-start | bytes 6152 | tf_op jit(solution)/shard_map/ppermute | solution.py:84
  16.6 10.8 %collective-permute-start.5 = (f32[512]{0:T(512)S(1)}, f32[512]{0:T(512)S(1)}, u32[]{:S(2)}, u32[]{:S(2)}) collective-permute-start(f32[512]{0:T(512)S(1)} %get-tuple-element.16), channel_id=1, source_target_pairs={{0,4},{4,0},{8,12},{12,8},{16,20},{20,16},{24,28},{28,24},{1,5},{5... | collective-permute-start | bytes 6152 | tf_op jit(solution)/shard_map/ppermute | solution.py:84
  16.8 1.9 %collective-permute-start.1 = (bf16[2,2048,32]{1,2,0:T(8,128)(2,1)S(1)}, bf16[2,2048,32]{1,2,0:T(8,128)(2,1)S(1)}, u32[]{:S(2)}, u32[]{:S(2)}) collective-permute-start(bf16[2,2048,32]{1,2,0:T(8,128)(2,1)S(1)} %pad_maximum_fusion.2), channel_id=1, source_target_pairs={{0,4},{4,0},{8,12},{12,8},{16,20},{20,16},{24,28},{28,24},{1,5},{5... | collective-permute-start | bytes 786440 | tf_op jit(solution)/shard_map/ppermute | solution.py:67
  21.1 73.8 %collective-permute-start.4 = (bf16[2048,384]{1,0:T(8,128)(2,1)S(1)}, bf16[2048,384]{1,0:T(8,128)(2,1)S(1)}, u32[]{:S(2)}, u32[]{:S(2)}) collective-permute-start(bf16[2048,384]{1,0:T(8,128)(2,1)S(1)} %pad_maximum_fusion), channel_id=1, source_target_pairs={{0,3},{1,2},{2,1},{3,0},{4,7},{5,6},{6,5},{7,4},{8,11},{9,10},{10,... | collective-permute-start | bytes 4718600 | tf_op jit(solution)/shard_map/ppermute | solution.py:73
  24.1 72.7 %collective-permute-start.2 = (bf16[2048,384]{1,0:T(8,128)(2,1)S(1)}, bf16[2048,384]{1,0:T(8,128)(2,1)}, u32[]{:S(2)}, u32[]{:S(2)}) collective-permute-start(bf16[2048,384]{1,0:T(8,128)(2,1)S(1)} %pad_maximum_fusion), channel_id=1, source_target_pairs={{0,1},{1,0},{2,3},{3,2},{4,5},{5,4},{6,7},{7,6},{8,9},{9,8},{10,11... | collective-permute-start | bytes 4718600 | tf_op jit(solution)/shard_map/ppermute | solution.py:73
  25.8 4.6 %collective-permute-start.6 = (f32[512]{0:T(512)S(1)}, f32[512]{0:T(512)S(1)}, u32[]{:S(2)}, u32[]{:S(2)}) collective-permute-start(f32[512]{0:T(512)S(1)} %get-tuple-element.16), channel_id=1, source_target_pairs={{0,8},{4,12},{8,0},{12,4},{16,24},{20,28},{24,16},{28,20},{1,9},{5... | collective-permute-start | bytes 6152 | tf_op jit(solution)/shard_map/ppermute | solution.py:84
  25.8 5.0 %collective-permute-start.7 = (f32[512]{0:T(512)S(1)}, f32[512]{0:T(512)S(1)}, u32[]{:S(2)}, u32[]{:S(2)}) collective-permute-start(f32[512]{0:T(512)S(1)} %get-tuple-element.16), channel_id=1, source_target_pairs={{0,12},{4,8},{8,4},{12,0},{16,28},{20,24},{24,20},{28,16},{1,13},{... | collective-permute-start | bytes 6152 | tf_op jit(solution)/shard_map/ppermute | solution.py:84
  27.4 7.3 %collective-permute-start.8 = (f32[512]{0:T(512)S(1)}, f32[512]{0:T(512)S(1)}, u32[]{:S(2)}, u32[]{:S(2)}) collective-permute-start(f32[512]{0:T(512)S(1)} %get-tuple-element.16), channel_id=1, source_target_pairs={{0,16},{4,20},{8,24},{12,28},{16,0},{20,4},{24,8},{28,12},{1,17},{... | collective-permute-start | bytes 6152 | tf_op jit(solution)/shard_map/ppermute | solution.py:84
  30.4 4.4 %collective-permute-start.9 = (f32[512]{0:T(512)S(1)}, f32[512]{0:T(512)S(1)}, u32[]{:S(2)}, u32[]{:S(2)}) collective-permute-start(f32[512]{0:T(512)S(1)} %get-tuple-element.16), channel_id=1, source_target_pairs={{0,20},{4,16},{8,28},{12,24},{16,4},{20,0},{24,12},{28,8},{1,21},{... | collective-permute-start | bytes 6152 | tf_op jit(solution)/shard_map/ppermute | solution.py:84
  30.7 60.8 %collective-permute-start = (s32[512]{0:T(512)S(1)}, s32[512]{0:T(512)S(1)}, u32[]{:S(2)}, u32[]{:S(2)}) collective-permute-start(s32[512]{0:T(512)S(1)} %broadcast_add_fusion), channel_id=1, source_target_pairs={{0,1},{1,2},{2,3},{4,5},{5,6},{6,7},{8,9},{9,10},{10,11},{12,13},{... | collective-permute-start | bytes 6152 | tf_op jit(solution)/shard_map/ppermute | solution.py:19
  35.4 63.6 %collective-permute-start.3 = (bf16[2048,384]{1,0:T(8,128)(2,1)S(1)}, bf16[2048,384]{1,0:T(8,128)(2,1)}, u32[]{:S(2)}, u32[]{:S(2)}) collective-permute-start(bf16[2048,384]{1,0:T(8,128)(2,1)S(1)} %pad_maximum_fusion), channel_id=1, source_target_pairs={{0,2},{1,3},{2,0},{3,1},{4,6},{5,7},{6,4},{7,5},{8,10},{9,11},{10,... | collective-permute-start | bytes 4718600 | tf_op jit(solution)/shard_map/ppermute | solution.py:73
  92.8 4.1 %copy-start.1 = (bf16[256,8192]{1,0:T(8,128)(2,1)S(1)}, bf16[256,8192]{1,0:T(8,128)(2,1)}, u32[]{:S(2)}) copy-start(bf16[256,8192]{1,0:T(8,128)(2,1)} %all-gather.3.cloned.1.call-done) | copy-start | bytes 12582916
  92.8 6.2 %copy-start.13 = (f32[256]{0:T(256)S(1)}, f32[256]{0:T(256)}, u32[]{:S(2)}) copy-start(f32[256]{0:T(256)} %get-tuple-element.45) | copy-start | bytes 3076
  96.8 5.3 %copy-start.10 = (f32[256]{0:T(256)S(1)}, f32[256]{0:T(256)}, u32[]{:S(2)}) copy-start(f32[256]{0:T(256)} %get-tuple-element.43) | copy-start | bytes 3076
  96.9 5.3 %copy-start.17 = (pred[64]{0:T(512)(128)(4,1)S(1)}, pred[64]{0:T(512)(128)(4,1)}, u32[]{:S(2)}) copy-start(pred[64]{0:T(512)(128)(4,1)} %fusion.78) | copy-start | bytes 196
  96.9 5.3 %copy-start.19 = (f32[64]{0:T(128)S(1)}, f32[64]{0:T(128)}, u32[]{:S(2)}) copy-start(f32[64]{0:T(128)} %multiply_power_fusion.1) | copy-start | bytes 772
  102.8 14.9 %collective-permute-start.12 = (bf16[2,256,64]{2,1,0:T(8,128)(2,1)S(1)}, bf16[2,256,64]{2,1,0:T(8,128)(2,1)S(1)}, u32[]{:S(2)}, u32[]{:S(2)}) collective-permute-start(bf16[2,256,64]{2,1,0:T(8,128)(2,1)S(1)} %pad_maximum_fusion.6), channel_id=1, source_target_pairs={{0,1},{1,2},{2,3},{4,5},{5,6},{6,7},{8,9},{9,10},{10,11},{12,13},{... | collective-permute-start | bytes 196616 | tf_op jit(solution)/shard_map/ppermute | solution.py:19
  107.3 10.4 %collective-permute-start.13 = (bf16[2,256,64]{2,1,0:T(8,128)(2,1)S(1)}, bf16[2,256,64]{2,1,0:T(8,128)(2,1)S(1)}, u32[]{:S(2)}, u32[]{:S(2)}) collective-permute-start(bf16[2,256,64]{2,1,0:T(8,128)(2,1)S(1)} %pad_maximum_fusion.6), channel_id=1, source_target_pairs={{0,9},{1,10},{2,11},{4,13},{5,14},{6,15},{8,1},{9,2},{10,3},{12,5}... | collective-permute-start | bytes 196616 | tf_op jit(solution)/shard_map/ppermute | solution.py:130
  109.8 7.8 %collective-permute-start.14 = (bf16[2,256,64]{2,1,0:T(8,128)(2,1)S(1)}, bf16[2,256,64]{2,1,0:T(8,128)(2,1)S(1)}, u32[]{:S(2)}, u32[]{:S(2)}) collective-permute-start(bf16[2,256,64]{2,1,0:T(8,128)(2,1)S(1)} %pad_maximum_fusion.6), channel_id=1, source_target_pairs={{0,8},{4,12},{8,0},{12,4},{16,24},{20,28},{24,16},{28,20},{1,9},{5... | collective-permute-start | bytes 196616 | tf_op jit(solution)/shard_map/ppermute | solution.py:121
  118.6 4.0 %copy-start = (bf16[256,8192]{1,0:T(8,128)(2,1)S(1)}, bf16[256,8192]{1,0:T(8,128)(2,1)}, u32[]{:S(2)}) copy-start(bf16[256,8192]{1,0:T(8,128)(2,1)} %all-gather.5.cloned.1.call-done) | copy-start | bytes 12582916
  118.6 6.2 %copy-start.12 = (f32[256]{0:T(256)S(1)}, f32[256]{0:T(256)}, u32[]{:S(2)}) copy-start(f32[256]{0:T(256)} %get-tuple-element.44) | copy-start | bytes 3076
  122.7 4.9 %copy-start.18 = (pred[64]{0:T(512)(128)(4,1)S(1)}, pred[64]{0:T(512)(128)(4,1)}, u32[]{:S(2)}) copy-start(pred[64]{0:T(512)(128)(4,1)} %fusion.78) | copy-start | bytes 196
  122.7 4.9 %copy-start.20 = (f32[64]{0:T(128)S(1)}, f32[64]{0:T(128)}, u32[]{:S(2)}) copy-start(f32[64]{0:T(128)} %multiply_power_fusion.1) | copy-start | bytes 772
  124.8 10.8 %copy-start.5 = (bf16[2,256,32]{2,1,0:T(8,128)(2,1)S(1)}, bf16[2,256,32]{2,1,0:T(8,128)(2,1)}, u32[]{:S(2)}) copy-start(bf16[2,256,32]{2,1,0:T(8,128)(2,1)} %fusion.53) | copy-start | bytes 98308
  124.8 16.8 %copy-start.3 = (f32[256,255]{1,0:T(8,128)S(1)}, f32[256,255]{1,0:T(8,128)}, u32[]{:S(2)}) copy-start(f32[256,255]{1,0:T(8,128)} %get-tuple-element.30) | copy-start | bytes 783364
  124.8 16.8 %copy-start.4 = (f32[256,255]{1,0:T(8,128)S(1)}, f32[256,255]{1,0:T(8,128)}, u32[]{:S(2)}) copy-start(f32[256,255]{1,0:T(8,128)} %get-tuple-element.31) | copy-start | bytes 783364
  124.8 16.8 %copy-start.6 = (f32[256,1]{1,0:T(8,128)S(1)}, f32[256,1]{1,0:T(8,128)}, u32[]{:S(2)}) copy-start(f32[256,1]{1,0:T(8,128)} %get-tuple-element.26) | copy-start | bytes 3076
  124.9 16.8 %copy-start.7 = (f32[256,1]{1,0:T(8,128)S(1)}, f32[256,1]{1,0:T(8,128)}, u32[]{:S(2)}) copy-start(f32[256,1]{1,0:T(8,128)} %get-tuple-element.29) | copy-start | bytes 3076
  127.4 19.7 %copy-start.2 = (bf16[2,512,128]{2,1,0:T(8,128)(2,1)S(1)}, bf16[2,512,128]{2,1,0:T(8,128)(2,1)}, u32[]{:S(2)}) copy-start(bf16[2,512,128]{2,1,0:T(8,128)(2,1)} %pad_maximum_fusion.3) | copy-start | bytes 786436
  128.3 17.6 %collective-permute-start.15 = (bf16[2,256,64]{2,1,0:T(8,128)(2,1)S(1)}, bf16[2,256,64]{2,1,0:T(8,128)(2,1)S(1)}, u32[]{:S(2)}, u32[]{:S(2)}) collective-permute-start(bf16[2,256,64]{2,1,0:T(8,128)(2,1)S(1)} %pad_maximum_fusion.7), channel_id=1, source_target_pairs={{0,1},{1,2},{2,3},{4,5},{5,6},{6,7},{8,9},{9,10},{10,11},{12,13},{... | collective-permute-start | bytes 196616 | tf_op jit(solution)/shard_map/ppermute | solution.py:19
  130.8 15.2 %collective-permute-start.16 = (bf16[2,256,64]{2,1,0:T(8,128)(2,1)S(1)}, bf16[2,256,64]{2,1,0:T(8,128)(2,1)}, u32[]{:S(2)}, u32[]{:S(2)}) collective-permute-start(bf16[2,256,64]{2,1,0:T(8,128)(2,1)S(1)} %pad_maximum_fusion.7), channel_id=1, source_target_pairs={{0,9},{1,10},{2,11},{4,13},{5,14},{6,15},{8,1},{9,2},{10,3},{12,5}... | collective-permute-start | bytes 196616 | tf_op jit(solution)/shard_map/ppermute | solution.py:130
  133.8 11.1 %collective-permute-start.17 = (bf16[2,256,64]{2,1,0:T(8,128)(2,1)S(1)}, bf16[2,256,64]{2,1,0:T(8,128)(2,1)}, u32[]{:S(2)}, u32[]{:S(2)}) collective-permute-start(bf16[2,256,64]{2,1,0:T(8,128)(2,1)S(1)} %pad_maximum_fusion.7), channel_id=1, source_target_pairs={{0,8},{4,12},{8,0},{12,4},{16,24},{20,28},{24,16},{28,20},{1,9},{5... | collective-permute-start | bytes 196616 | tf_op jit(solution)/shard_map/ppermute | solution.py:121
  138.3 16.5 %all-to-all-start = ((bf16[4,16,2,512]{3,1,2,0:T(8,128)(2,1)}), bf16[4,16,2,512]{3,1,2,0:T(8,128)(2,1)S(1)}, u32[]{:S(2)}, u32[]{:S(2)}) async-start(bf16[4,16,2,512]{3,1,2,0:T(8,128)(2,1)} %copy.44), calls=%async_computation | async-start | bytes 262144 | tf_op jit(solution)/shard_map/all_to_all | solution.py:187
  147.2 2.4 %copy-start.14 = (pred[1024]{0:T(1024)(128)(4,1)S(1)}, pred[1024]{0:T(1024)(128)(4,1)}, u32[]{:S(2)}) copy-start(pred[1024]{0:T(1024)(128)(4,1)} %broadcast_compare_fusion) | copy-start | bytes 3076
  147.2 4.5 %copy-start.21 = (pred[1024]{0:T(1024)(128)(4,1)S(1)}, pred[1024]{0:T(1024)(128)(4,1)}, u32[]{:S(2)}) copy-start(pred[1024]{0:T(1024)(128)(4,1)} %ge.25) | copy-start | bytes 3076
Sparse Core Ops, SparseCore 0:
  10.9 49.9 all-gather.2
  62.5 45.8 all-gather.4

commit v7 on v5

--- a/solution.py
+++ b/solution.py
@@ -87,11 +87,12 @@
         mark_list.insert(0, shifted(marks, "gy", shift_by))
     scaling = 1.0 / jnp.sqrt(squares / D + EPSILON)
     query_cols = head_local * HD
-    halves = 2
-    half_rows = token_count // halves
+    first_rows = token_count * 3 // 4
+    cuts = [(0, first_rows), (first_rows, token_count)]
     query_halves, kv_halves, head_halves = [], [], []
-    for h in range(halves):
-        rows_of = slice(h * half_rows, (h + 1) * half_rows)
+    for begin, finish in cuts:
+        rows_of = slice(begin, finish)
+        half_rows = finish - begin
         normed = lax.all_gather(local_normed[rows_of], "gx", axis=1, tiled=True)
         if head_halves:
             normed, head_halves[-1] = lax.optimization_barrier((normed, head_halves[-1]))
@@ -123,7 +124,7 @@
     own_kv = jnp.concatenate(kv_halves, axis=1)
     key_piece = own_kv[0]
     value_piece = own_kv[1]
-    window_kv = jnp.stack(head_halves, axis=2).reshape(2, (span_count + 1) * token_count, HD)
+    window_kv = jnp.concatenate(head_halves, axis=2).reshape(2, (span_count + 1) * token_count, HD)
     window_keys = window_kv[0]
     window_values = window_kv[1]
     window_marks = jnp.concatenate(mark_list, axis=0)

time: 152 us -> 152 us (level)
  matrix products: 14.8 us -> 17.8 us
    ppermute x3, waiting for transfers between devices: 1.56 us -> 41.6 us  [shifted(): return lax.ppermute(value, axis, pairs)]
    all_gather x2, waiting for transfers between devices: 24.1 us -> 2.71 us  [shards(): normed = lax.all_gather(local_normed[rows_of], 'gx', axis=1, tiled=True)]
    ppermute x3, waiting for transfers between devices: 20 us -> 0.01 us  [shards(): lax.ppermute(local_weights, 'gy', partner_route(gy_count, gy_count, k))]
    ppermute x4, waiting for transfers between devices: 10.9 us -> 16.7 us  [shards(): theirs = lax.ppermute(held, 'gx', partner_route(gx_count, quarters, step))]
    all_to_all x1, waiting for transfers between devices: 3.91 us -> 0.01 us  [shards(): lax.all_to_all(send_kv, 'gy', split_axis=0, concat_axis=0, tiled=True)]
    dot_general x8, matrix products: 10.9 us -> 13.7 us  [shards(): part = jnp.dot(rows, block, preferred_element_type=jnp.float32)]
    concatenate x6, local copies, waits for them, and re-layouts: 2.76 us -> 1.08 us  [joined(): jnp.concatenate([mine, theirs], axis=-1)]
    select_n x5 -> x6, other arithmetic: 3.33 us -> 1.75 us  [joined(): jnp.where(mine_first, jnp.concatenate([mine, theirs], axis=-1), jnp.conca...]
  transfers between devices with their start and end apart: 20 -> 20, of which waited for: 9 -> 11; matrix products, arithmetic and copies ran while one was open for 16% -> 15% of each run, Pallas kernels for 0% -> 0%
where the time goes in v7:
time: 152 us; the launch traced here: 151 us
  waiting for transfers between devices  64.2 us (42%)
  starting transfers between devices  28.8 us (19%)
  matrix products  17.8 us (12%)
  between operations  14.8 us (10%)
  local copies, waits for them, and re-layouts  12.7 us (8%)
  other arithmetic  12.7 us (8%)
    ppermute x3, waiting for transfers between devices, shifted(): return lax.ppermute(value, axis, pairs)  41.6 us
    ppermute x4, waiting for transfers between devices, shards(): theirs = lax.ppermute(held, 'gx', partner_route(gx_count, quarters, step))  16.7 us
    dot_general x8, matrix products, shards(): part = jnp.dot(rows, block, preferred_element_type=jnp.float32)  13.7 us
    ppermute x7, starting transfers between devices, shards(): lax.ppermute(local_squares, 'gx', partner_route(gx_count, gx_count, k))  9.88 us
    ppermute x3, starting transfers between devices, shifted(): return lax.ppermute(value, axis, pairs)  9.6 us
    all_to_all x1, starting transfers between devices, shards(): lax.all_to_all(send_kv, 'gy', split_axis=0, concat_axis=0, tiled=True)  3.82 us
    ppermute x3, starting transfers between devices, shards(): lax.ppermute(local_weights, 'gy', partner_route(gy_count, gy_count, k))  3.64 us
    unnamed x38, local copies, waits for them, and re-layouts  3.52 us
  transfers between devices with their start and end apart: 20, of which 11 were waited for; matrix products, arithmetic and copies ran while one was open for 15% of the time, Pallas kernels for 0%

profile of v7, /device:TPU:0, one launch (start us, length us, event | category | flops | bytes accessed | tf_op | source)
XLA Modules:
  0.0 151.0 jit_solution(683487202247644687)
XLA Ops:
  7.2 0.8 dynamic-slice_convert_fusion
  8.0 1.6 %fusion.4 = (f32[512]{0:T(512)S(1)}, bf16[512,1024]{1,0:T(8,128)(2,1)S(1)}) fusion(bf16[512,1024]{1,0:T(8,128)(2,1)} %param.8, f32[1024]{0:T(1024)S(1)} %dynamic-slice_convert_fusion), kind=kLoop, calls=%fused_computation.11 | loop fusion | flops 2620928 | bytes 2103296 | tf_op jit(solution)/shard_map/reduce_sum | solution.py:77
  9.6 1.0 slice.166
  11.3 2.7 %collective-permute-start.5 = (f32[512]{0:T(512)S(1)}, f32[512]{0:T(512)}, u32[]{:S(2)}, u32[]{:S(2)}) collective-permute-start(f32[512]{0:T(512)S(1)} %get-tuple-element.13), channel_id=1, source_target_pairs={{0,8},{4,12},{8,0},{12,4},{16,24},{20,28},{24,16},{28,20},{1,9},{5... | collective-permute-start | bytes 6152 | tf_op jit(solution)/shard_map/ppermute | solution.py:80
  14.0 0.6 copy.24
  14.6 1.2 pad_maximum_fusion
  15.9 1.7 %collective-permute-start.2 = (bf16[2048,320]{0,1:T(8,128)(2,1)}, bf16[2048,320]{0,1:T(8,128)(2,1)}, u32[]{:S(2)}, u32[]{:S(2)}) collective-permute-start(bf16[2048,320]{0,1:T(8,128)(2,1)} %pad_maximum_fusion), channel_id=1, source_target_pairs={{0,2},{1,3},{2,0},{3,1},{4,6},{5,7},{6,4},{7,5},{8,10},{9,11},{10,... | collective-permute-start | bytes 3932168 | tf_op jit(solution)/shard_map/ppermute | solution.py:69
  17.5 1.4 collective-permute-start.3
  19.0 0.7 slice.172
  19.8 0.7 slice_convert_fusion.3
  21.4 2.7 %collective-permute-start.7 = (f32[512]{0:T(512)S(1)}, f32[512]{0:T(512)S(1)}, u32[]{:S(2)}, u32[]{:S(2)}) collective-permute-start(f32[512]{0:T(512)S(1)} %get-tuple-element.13), channel_id=1, source_target_pairs={{0,16},{4,20},{8,24},{12,28},{16,0},{20,4},{24,8},{28,12},{1,17},{... | collective-permute-start | bytes 6152 | tf_op jit(solution)/shard_map/ppermute | solution.py:80
  24.7 1.4 collective-permute-done.7
  26.1 3.6 %collective-permute-start.9 = (f32[512]{0:T(512)S(1)}, f32[512]{0:T(512)S(1)}, u32[]{:S(2)}, u32[]{:S(2)}) collective-permute-start(f32[512]{0:T(512)S(1)} %get-tuple-element.13), channel_id=1, source_target_pairs={{0,24},{4,28},{8,16},{12,20},{16,8},{20,12},{24,0},{28,4},{1,25},{... | collective-permute-start | bytes 6152 | tf_op jit(solution)/shard_map/ppermute | solution.py:80
  30.0 1.5 collective-permute-done.9
  31.5 2.2 %collective-permute-start = (s32[512]{0:T(512)S(1)}, s32[512]{0:T(512)S(1)}, u32[]{:S(2)}, u32[]{:S(2)}) collective-permute-start(s32[512]{0:T(512)S(1)} %broadcast_add_fusion), channel_id=1, source_target_pairs={{0,1},{1,2},{2,3},{4,5},{5,6},{6,7},{8,9},{9,10},{10,11},{12,13},{... | collective-permute-start | bytes 6152 | tf_op jit(solution)/shard_map/ppermute | solution.py:19
  34.7 0.7 stack.53
  35.4 0.6 gather_fusion
  36.0 39.7 %collective-permute-done = s32[512]{0:T(512)S(1)} collective-permute-done((s32[512]{0:T(512)S(1)}, s32[512]{0:T(512)S(1)}, u32[]{:S(2)}, u32[]{:S(2)}) %collective-permute-start) | collective-permute-done | bytes 2080 | tf_op jit(solution)/shard_map/ppermute | solution.py:19
  75.8 2.7 %all-gather.3.cloned.1.call-done = bf16[384,8192]{1,0:T(8,128)(2,1)} async-done(((bf16[384,1024]{1,0:T(8,128)(2,1)}), bf16[384,8192]{1,0:T(8,128)(2,1)}) %all-gather.3.cloned.1.call-update) | async-done | bytes 6291472 | tf_op jit(solution)/shard_map/all_gather | solution.py:96
  78.5 2.4 %fusion.14 = f32[384,320]{0,1:T(8,128)S(1)} fusion(bf16[384,8192]{1,0:T(8,128)(2,1)} %all-gather.3.cloned.1.call-done, s32[]{:T(128)S(6)} %select_n.211, bf16[2048,32]{0,1:T(8,128)(2,1)S(1)} %copy-done.2, bf16[2048,32]{0,1:T(8,128)(2,1)} %param.11, bf16[2048,256]{0,1:T(8,128)(2,1)S(1)} %copy.24), kind=kOutput, calls=%fused_computation.20 | convolution fusion | flops 507248640 | bytes 3375108 | tf_op jit(solution)/shard_map/dot_general | solution.py:102
  80.9 0.9 copy-done.14
  81.8 2.2 %fusion.10 = f32[384,320]{0,1:T(8,128)S(1)} fusion(bf16[2048,320]{0,1:T(8,128)(2,1)} %collective-permute-done.2, bf16[384,8192]{1,0:T(8,128)(2,1)S(1)} %copy-done.14, s32[]{:T(128)S(6)} %select_n.213), kind=kOutput, calls=%fused_computation.16 | convolution fusion | flops 503316480 | bytes 3375108 | tf_op jit(solution)/shard_map/dot_general | solution.py:102
  84.0 0.9 fusion.8
  84.9 2.3 %fusion.28 = f32[384,320]{0,1:T(8,128)S(1)} fusion(f32[384,320]{0,1:T(8,128)S(1)} %fusion.8, f32[384,320]{0,1:T(8,128)S(1)} %fusion.10, f32[384,320]{0,1:T(8,128)S(1)} %fusion.14, bf16[2048,320]{0,1:T(8,128)(2,1)} %collective-permute-done.1, bf16[384,8192]{1,0:T(8,128)(2,1)S(1)} %copy-done.14, s32[]{:T(128)S(6)} %select_n.212, f32[384]{0:T(512)S(1)} %bitcast.107), kind=kOutput, calls=%fused_computation.27 | convolution fusion | flops 503808000 | bytes 4851716 | tf_op jit(solution)/shard_map/dot_general | solution.py:102
  87.5 3.3 %collective-permute-start.11 = (bf16[2,384,32]{1,2,0:T(8,128)(2,1)S(1)}, bf16[2,384,32]{1,2,0:T(8,128)(2,1)S(1)}, u32[]{:S(2)}, u32[]{:S(2)}) collective-permute-start(bf16[2,384,32]{1,2,0:T(8,128)(2,1)S(1)} %pad_maximum_fusion.3), channel_id=1, source_target_pairs={{0,1},{1,2},{2,3},{4,5},{5,6},{6,7},{8,9},{9,10},{10,11},{12,13},{... | collective-permute-start | bytes 147464 | tf_op jit(solution)/shard_map/ppermute | solution.py:19
  91.4 1.2 collective-permute-done.11
  92.7 1.2 collective-permute-done.12
  94.1 1.9 %fusion.49 = bf16[384,256]{0,1:T(8,128)(2,1)S(1)} fusion(f32[384,320]{0,1:T(8,128)S(1)} %fusion.28, f32[384,1]{0,1:T(1,128)S(1)} %get-tuple-element.22, f32[384,255]{0,1:T(8,128)S(1)} %get-tuple-element.24, f32[384,255]{0,1:T(8,128)S(1)} %get-tuple-element.23, f32[384,1]{0,1:T(1,128)S(1)} %get-tuple-element.19, f32[256]{0:T(256)S(1)} %multiply_power_fusion, ...), kind=kLoop, calls=%fused_computation.49 | loop fusion | flops 983040 | bytes 1379072 | tf_op jit(solution)/shard_map/convert_element_type | solution.py:110
  96.5 14.1 %collective-permute-done.13 = bf16[2,768,64]{1,2,0:T(8,128)(2,1)} collective-permute-done((bf16[2,768,64]{1,2,0:T(8,128)(2,1)S(1)}, bf16[2,768,64]{1,2,0:T(8,128)(2,1)}, u32[]{:S(2)}, u32[]{:S(2)}) %collective-permute-start.13) | collective-permute-done | bytes 196640 | tf_op jit(solution)/shard_map/ppermute | solution.py:119
  110.6 1.0 concatenate.122
  111.6 0.9 broadcast_select_fusion
  112.5 1.7 %fusion.45 = f32[128,320]{0,1:T(8,128)S(1)} fusion(bf16[128,8192]{1,0:T(8,128)(2,1)} %all-gather.5.cloned.1.call-done, s32[]{:T(128)S(6)} %select_n.211, bf16[2048,32]{0,1:T(8,128)(2,1)S(1)} %copy-done.2, bf16[2048,32]{0,1:T(8,128)(2,1)} %param.11, bf16[2048,256]{0,1:T(8,128)(2,1)S(1)} %copy.24), kind=kOutput, calls=%fused_computation.45 | convolution fusion | flops 171704320 | bytes 1998852 | tf_op jit(solution)/shard_map/dot_general | solution.py:102
  114.8 1.8 %convolution_add_fusion.1 = f32[128,320]{0,1:T(8,128)S(1)} fusion(f32[128,320]{0,1:T(8,128)S(1)} %fusion.45, bf16[2048,320]{0,1:T(8,128)(2,1)} %collective-permute-done.1, bf16[128,8192]{1,0:T(8,128)(2,1)S(1)} %copy-done, s32[]{:T(128)S(6)} %select_n.212), kind=kOutput, calls=%fused_computation.31 | convolution fusion | flops 167813120 | bytes 2162692 | tf_op jit(solution)/shard_map/dot_general | solution.py:102
  116.7 1.9 %fusion.38 = f32[128,320]{0,1:T(8,128)S(1)} fusion(f32[128,320]{0,1:T(8,128)S(1)} %fusion.41, f32[128,320]{0,1:T(8,128)S(1)} %convolution_add_fusion.1, bf16[2048,320]{0,1:T(8,128)(2,1)} %collective-permute-done.2, bf16[128,8192]{1,0:T(8,128)(2,1)S(1)} %copy-done, s32[]{:T(128)S(6)} %select_n.213, f32[128]{0:T(128)S(1)} %copy-done.13), kind=kOutput, calls=%fused_computation.33 | convolution fusion | flops 167895040 | bytes 2327044 | tf_op jit(solution)/shard_map/dot_general | solution.py:102
  119.4 1.5 scatter_fusion
  120.9 0.7 copy.29
  121.5 3.8 %all-to-all-start = ((bf16[4,16,2,512]{3,1,2,0:T(8,128)(2,1)}), bf16[4,16,2,512]{3,1,2,0:T(8,128)(2,1)S(1)}, u32[]{:S(2)}, u32[]{:S(2)}) async-start(bf16[4,16,2,512]{3,1,2,0:T(8,128)(2,1)} %copy.29), calls=%async_computation | async-start | bytes 262144 | tf_op jit(solution)/shard_map/all_to_all | solution.py:176
  125.4 4.1 %collective-permute-start.14 = (bf16[2,128,32]{1,2,0:T(8,128)(2,1)S(1)}, bf16[2,128,32]{1,2,0:T(8,128)(2,1)S(1)}, u32[]{:S(2)}, u32[]{:S(2)}) collective-permute-start(bf16[2,128,32]{1,2,0:T(8,128)(2,1)S(1)} %pad_maximum_fusion.4), channel_id=1, source_target_pairs={{0,1},{1,2},{2,3},{4,5},{5,6},{6,7},{8,9},{9,10},{10,11},{12,13},{... | collective-permute-start | bytes 49160 | tf_op jit(solution)/shard_map/ppermute | solution.py:19
  129.5 0.6 fusion.57
  130.1 0.7 collective-permute-done.14
  131.0 1.0 collective-permute-done.15
  131.9 1.6 %collective-permute-start.16 = (bf16[2,256,64]{1,2,0:T(8,128)(2,1)S(1)}, bf16[2,256,64]{1,2,0:T(8,128)(2,1)S(1)}, u32[]{:S(2)}, u32[]{:S(2)}) collective-permute-start(bf16[2,256,64]{1,2,0:T(8,128)(2,1)S(1)} %maximum_select_fusion.1), channel_id=1, source_target_pairs={{0,8},{4,12},{8,0},{12,4},{16,24},{20,28},{24,16},{28,20},{1,9},{5... | collective-permute-start | bytes 196616 | tf_op jit(solution)/shard_map/ppermute | solution.py:119
  134.0 0.9 copy.31
  134.9 0.9 copy.32
  137.2 1.8 %fusion.91 = (f32[1024]{0:T(1024)S(1)}, f32[1024,1024]{0,1:T(8,128)S(1)}) fusion(s32[1024]{0:T(1024)S(1)} %bitcast.97, pred[1024]{0:T(1024)(128)(4,1)S(1)} %broadcast_compare_fusion, s32[1024]{0:T(1024)S(1)} %bitcast.94, s32[1024]{0:T(1024)S(1)} %pad_add_fusion, bf16[1024,128]{1,0:T(8,128)(2,1)S(1)} %bitcast.89, bf16[1024,128]{0,1:T(8,128)(2,1)S(1)} %bitcast.93), kind=kOutput, calls=%fused_computation.147 | convolution fusion | flops 275774464 | bytes 4736000 | tf_op jit(solution)/shard_map/dot_general | solution.py:137
  139.0 2.1 %fusion.1 = f32[1024]{0:T(1024)S(1)} fusion(f32[1024]{0:T(1024)S(1)} %get-tuple-element.35, f32[1024,1024]{0,1:T(8,128)S(1)} %get-tuple-element.36, s32[1024]{0:T(1024)S(1)} %bitcast.98, pred[1024]{0:T(1024)(128)(4,1)S(1)} %broadcast_compare_fusion, s32[1024]{0:T(1024)S(1)} %bitcast.95, s32[1024]{0:T(1024)S(1)} %pad_add_fusion), kind=kLoop, calls=%fused_computation.6 | loop fusion | flops 8387584 | bytes 4215808 | tf_op jit(solution)/shard_map/reduce_sum | solution.py:148
  141.1 2.3 %fusion.34 = bf16[1024,128]{1,0:T(8,128)(2,1)S(1)} fusion(bf16[1024,128]{0,1:T(8,128)(2,1)S(1)} %bitcast.90, f32[1024]{0:T(1024)S(1)} %get-tuple-element.35, f32[1024]{0:T(1024)S(1)} %fusion.1, pred[1024]{0:T(1024)(128)(4,1)S(1)} %copy-done.11, f32[1024,1024]{0,1:T(8,128)S(1)} %get-tuple-element.36, s32[1024]{0:T(1024)S(1)} %bitcast.99, ...), kind=kOutput, calls=%fused_computation.29 | convolution fusion | flops 277217280 | bytes 4741120 | tf_op jit(solution)/shard_map/dot_general | solution.py:150
  143.5 0.7 copy.39
  (115 shorter events, 8.5 us)
Async XLA Ops:
  7.2 6.8 %copy-start.1 = (bf16[2048,256]{1,0:T(8,128)(2,1)S(1)}, bf16[2048,256]{1,0:T(8,128)(2,1)}, u32[]{:S(2)}) copy-start(bf16[2048,256]{1,0:T(8,128)(2,1)} %param.10) | copy-start | bytes 3145732
  7.2 71.3 %all-gather.3.cloned.1.call-start = ((), (), s32[]{:S(2)}) async-start(), calls=%async_computation.1 | async-start | bytes 7077888 | tf_op jit(solution)/shard_map/all_gather | solution.py:96
  9.6 5.0 %copy-start.2 = (bf16[2048,32]{0,1:T(8,128)(2,1)S(1)}, bf16[2048,32]{0,1:T(8,128)(2,1)}, u32[]{:S(2)}) copy-start(bf16[2048,32]{0,1:T(8,128)(2,1)} %param.12) | copy-start | bytes 393220
  9.6 5.0 %copy-start.3 = (bf16[2048,32]{0,1:T(8,128)(2,1)S(1)}, bf16[2048,32]{0,1:T(8,128)(2,1)}, u32[]{:S(2)}) copy-start(bf16[2048,32]{0,1:T(8,128)(2,1)} %param.11) | copy-start | bytes 393220
  10.7 101.8 %all-gather.5.cloned.1.call-start = ((), (), s32[]{:S(2)}) async-start(), calls=%async_computation.2 | async-start | bytes 2359296 | tf_op jit(solution)/shard_map/all_gather | solution.py:96
  10.7 9.0 %copy-start.10 = (s32[512]{0:T(512)S(1)}, s32[512]{0:T(512)}, u32[]{:S(2)}) copy-start(s32[512]{0:T(512)} %param.14) | copy-start | bytes 6148
  10.7 9.7 %copy-start.4 = (s32[512]{0:T(512)S(1)}, s32[512]{0:T(512)}, u32[]{:S(2)}) copy-start(s32[512]{0:T(512)} %param.13) | copy-start | bytes 6148
  10.7 9.8 %copy-start.9 = (s32[32,1]{0,1:T(1,128)S(1)}, s32[32,1]{0,1:T(1,128)}, u32[]{:S(2)}) copy-start(s32[32,1]{0,1:T(1,128)} %param.15) | copy-start | bytes 388
  10.7 10.7 %collective-permute-start.4 = (f32[512]{0:T(512)S(1)}, f32[512]{0:T(512)}, u32[]{:S(2)}, u32[]{:S(2)}) collective-permute-start(f32[512]{0:T(512)S(1)} %get-tuple-element.13), channel_id=1, source_target_pairs={{0,4},{4,0},{8,12},{12,8},{16,20},{20,16},{24,28},{28,24},{1,5},{5... | collective-permute-start | bytes 6152 | tf_op jit(solution)/shard_map/ppermute | solution.py:80
  11.3 12.8 %collective-permute-start.5 = (f32[512]{0:T(512)S(1)}, f32[512]{0:T(512)}, u32[]{:S(2)}, u32[]{:S(2)}) collective-permute-start(f32[512]{0:T(512)S(1)} %get-tuple-element.13), channel_id=1, source_target_pairs={{0,8},{4,12},{8,0},{12,4},{16,24},{20,28},{24,16},{28,20},{1,9},{5... | collective-permute-start | bytes 6152 | tf_op jit(solution)/shard_map/ppermute | solution.py:80
  13.9 10.7 %collective-permute-start.6 = (f32[512]{0:T(512)S(1)}, f32[512]{0:T(512)}, u32[]{:S(2)}, u32[]{:S(2)}) collective-permute-start(f32[512]{0:T(512)S(1)} %get-tuple-element.13), channel_id=1, source_target_pairs={{0,12},{4,8},{8,4},{12,0},{16,28},{20,24},{24,20},{28,16},{1,13},{... | collective-permute-start | bytes 6152 | tf_op jit(solution)/shard_map/ppermute | solution.py:80
  15.9 65.1 %collective-permute-start.2 = (bf16[2048,320]{0,1:T(8,128)(2,1)}, bf16[2048,320]{0,1:T(8,128)(2,1)}, u32[]{:S(2)}, u32[]{:S(2)}) collective-permute-start(bf16[2048,320]{0,1:T(8,128)(2,1)} %pad_maximum_fusion), channel_id=1, source_target_pairs={{0,2},{1,3},{2,0},{3,1},{4,6},{5,7},{6,4},{7,5},{8,10},{9,11},{10,... | collective-permute-start | bytes 3932168 | tf_op jit(solution)/shard_map/ppermute | solution.py:69
  17.5 66.4 %collective-permute-start.3 = (bf16[2048,320]{0,1:T(8,128)(2,1)}, bf16[2048,320]{0,1:T(8,128)(2,1)S(1)}, u32[]{:S(2)}, u32[]{:S(2)}) collective-permute-start(bf16[2048,320]{0,1:T(8,128)(2,1)} %pad_maximum_fusion), channel_id=1, source_target_pairs={{0,3},{1,2},{2,1},{3,0},{4,7},{5,6},{6,5},{7,4},{8,11},{9,10},{10,... | collective-permute-start | bytes 3932168 | tf_op jit(solution)/shard_map/ppermute | solution.py:69
  21.4 65.8 %copy-start.5 = (pred[32]{0:T(512)(128)(4,1)}, pred[32]{0:T(512)(128)(4,1)S(1)}, u32[]{:S(2)}) copy-start(pred[32]{0:T(512)(128)(4,1)S(1)} %fusion.88) | copy-start | bytes 100
  21.4 4.6 %collective-permute-start.7 = (f32[512]{0:T(512)S(1)}, f32[512]{0:T(512)S(1)}, u32[]{:S(2)}, u32[]{:S(2)}) collective-permute-start(f32[512]{0:T(512)S(1)} %get-tuple-element.13), channel_id=1, source_target_pairs={{0,16},{4,20},{8,24},{12,28},{16,0},{20,4},{24,8},{28,12},{1,17},{... | collective-permute-start | bytes 6152 | tf_op jit(solution)/shard_map/ppermute | solution.py:80
  24.1 60.8 %collective-permute-start.1 = (bf16[2048,320]{0,1:T(8,128)(2,1)}, bf16[2048,320]{0,1:T(8,128)(2,1)}, u32[]{:S(2)}, u32[]{:S(2)}) collective-permute-start(bf16[2048,320]{0,1:T(8,128)(2,1)} %pad_maximum_fusion), channel_id=1, source_target_pairs={{0,1},{1,0},{2,3},{3,2},{4,5},{5,4},{6,7},{7,6},{8,9},{9,8},{10,11... | collective-permute-start | bytes 3932168 | tf_op jit(solution)/shard_map/ppermute | solution.py:69
  24.6 5.1 %collective-permute-start.8 = (f32[512]{0:T(512)S(1)}, f32[512]{0:T(512)S(1)}, u32[]{:S(2)}, u32[]{:S(2)}) collective-permute-start(f32[512]{0:T(512)S(1)} %get-tuple-element.13), channel_id=1, source_target_pairs={{0,20},{4,16},{8,28},{12,24},{16,4},{20,0},{24,12},{28,8},{1,21},{... | collective-permute-start | bytes 6152 | tf_op jit(solution)/shard_map/ppermute | solution.py:80
  26.1 5.5 %collective-permute-start.9 = (f32[512]{0:T(512)S(1)}, f32[512]{0:T(512)S(1)}, u32[]{:S(2)}, u32[]{:S(2)}) collective-permute-start(f32[512]{0:T(512)S(1)} %get-tuple-element.13), channel_id=1, source_target_pairs={{0,24},{4,28},{8,16},{12,20},{16,8},{20,12},{24,0},{28,4},{1,25},{... | collective-permute-start | bytes 6152 | tf_op jit(solution)/shard_map/ppermute | solution.py:80
  29.7 57.6 %copy-start.7 = (f32[32]{0:T(128)}, f32[32]{0:T(128)S(1)}, u32[]{:S(2)}) copy-start(f32[32]{0:T(128)S(1)} %multiply_power_fusion.1) | copy-start | bytes 388
  29.7 5.0 %collective-permute-start.10 = (f32[512]{0:T(512)S(1)}, f32[512]{0:T(512)S(1)}, u32[]{:S(2)}, u32[]{:S(2)}) collective-permute-start(f32[512]{0:T(512)S(1)} %get-tuple-element.13), channel_id=1, source_target_pairs={{0,28},{4,24},{8,20},{12,16},{16,12},{20,8},{24,4},{28,0},{1,29},{... | collective-permute-start | bytes 6152 | tf_op jit(solution)/shard_map/ppermute | solution.py:80
  31.5 44.2 %collective-permute-start = (s32[512]{0:T(512)S(1)}, s32[512]{0:T(512)S(1)}, u32[]{:S(2)}, u32[]{:S(2)}) collective-permute-start(s32[512]{0:T(512)S(1)} %broadcast_add_fusion), channel_id=1, source_target_pairs={{0,1},{1,2},{2,3},{4,5},{5,6},{6,7},{8,9},{9,10},{10,11},{12,13},{... | collective-permute-start | bytes 6152 | tf_op jit(solution)/shard_map/ppermute | solution.py:19
  78.5 3.3 %copy-start.14 = (bf16[384,8192]{1,0:T(8,128)(2,1)S(1)}, bf16[384,8192]{1,0:T(8,128)(2,1)}, u32[]{:S(2)}) copy-start(bf16[384,8192]{1,0:T(8,128)(2,1)} %all-gather.3.cloned.1.call-done) | copy-start | bytes 18874372
  87.5 5.0 %collective-permute-start.11 = (bf16[2,384,32]{1,2,0:T(8,128)(2,1)S(1)}, bf16[2,384,32]{1,2,0:T(8,128)(2,1)S(1)}, u32[]{:S(2)}, u32[]{:S(2)}) collective-permute-start(bf16[2,384,32]{1,2,0:T(8,128)(2,1)S(1)} %pad_maximum_fusion.3), channel_id=1, source_target_pairs={{0,1},{1,2},{2,3},{4,5},{5,6},{6,7},{8,9},{9,10},{10,11},{12,13},{... | collective-permute-start | bytes 147464 | tf_op jit(solution)/shard_map/ppermute | solution.py:19
  92.6 1.4 collective-permute-start.12
  94.0 16.6 %collective-permute-start.13 = (bf16[2,768,64]{1,2,0:T(8,128)(2,1)S(1)}, bf16[2,768,64]{1,2,0:T(8,128)(2,1)}, u32[]{:S(2)}, u32[]{:S(2)}) collective-permute-start(bf16[2,768,64]{1,2,0:T(8,128)(2,1)S(1)} %maximum_select_fusion), channel_id=1, source_target_pairs={{0,8},{4,12},{8,0},{12,4},{16,24},{20,28},{24,16},{28,20},{1,9},{5... | collective-permute-start | bytes 589832 | tf_op jit(solution)/shard_map/ppermute | solution.py:119
  112.5 1.8 %copy-start = (bf16[128,8192]{1,0:T(8,128)(2,1)S(1)}, bf16[128,8192]{1,0:T(8,128)(2,1)}, u32[]{:S(2)}) copy-start(bf16[128,8192]{1,0:T(8,128)(2,1)} %all-gather.5.cloned.1.call-done) | copy-start | bytes 6291460
  114.3 2.4 %copy-start.13 = (f32[128]{0:T(128)S(1)}, f32[128]{0:T(128)}, u32[]{:S(2)}) copy-start(f32[128]{0:T(128)} %slice.147) | copy-start | bytes 1540
  114.8 3.8 %copy-start.6 = (pred[32]{0:T(512)(128)(4,1)S(1)}, pred[32]{0:T(512)(128)(4,1)}, u32[]{:S(2)}) copy-start(pred[32]{0:T(512)(128)(4,1)} %copy-done.5) | copy-start | bytes 100
  114.8 3.8 %copy-start.8 = (f32[32]{0:T(128)S(1)}, f32[32]{0:T(128)}, u32[]{:S(2)}) copy-start(f32[32]{0:T(128)} %copy-done.7) | copy-start | bytes 388
  114.8 4.6 %copy-start.12 = (s32[32]{0:T(128)S(1)}, s32[32]{0:T(128)}, u32[]{:S(2)}) copy-start(s32[32]{0:T(128)} %fusion.90) | copy-start | bytes 388
  121.5 12.1 %all-to-all-start = ((bf16[4,16,2,512]{3,1,2,0:T(8,128)(2,1)}), bf16[4,16,2,512]{3,1,2,0:T(8,128)(2,1)S(1)}, u32[]{:S(2)}, u32[]{:S(2)}) async-start(bf16[4,16,2,512]{3,1,2,0:T(8,128)(2,1)} %copy.29), calls=%async_computation | async-start | bytes 262144 | tf_op jit(solution)/shard_map/all_to_all | solution.py:176
  125.4 5.3 %collective-permute-start.14 = (bf16[2,128,32]{1,2,0:T(8,128)(2,1)S(1)}, bf16[2,128,32]{1,2,0:T(8,128)(2,1)S(1)}, u32[]{:S(2)}, u32[]{:S(2)}) collective-permute-start(bf16[2,128,32]{1,2,0:T(8,128)(2,1)S(1)} %pad_maximum_fusion.4), channel_id=1, source_target_pairs={{0,1},{1,2},{2,3},{4,5},{5,6},{6,7},{8,9},{9,10},{10,11},{12,13},{... | collective-permute-start | bytes 49160 | tf_op jit(solution)/shard_map/ppermute | solution.py:19
  130.7 1.2 collective-permute-start.15
  131.9 4.3 %collective-permute-start.16 = (bf16[2,256,64]{1,2,0:T(8,128)(2,1)S(1)}, bf16[2,256,64]{1,2,0:T(8,128)(2,1)S(1)}, u32[]{:S(2)}, u32[]{:S(2)}) collective-permute-start(bf16[2,256,64]{1,2,0:T(8,128)(2,1)S(1)} %maximum_select_fusion.1), channel_id=1, source_target_pairs={{0,8},{4,12},{8,0},{12,4},{16,24},{20,28},{24,16},{28,20},{1,9},{5... | collective-permute-start | bytes 196616 | tf_op jit(solution)/shard_map/ppermute | solution.py:119
  139.0 2.1 %copy-start.11 = (pred[1024]{0:T(1024)(128)(4,1)S(1)}, pred[1024]{0:T(1024)(128)(4,1)}, u32[]{:S(2)}) copy-start(pred[1024]{0:T(1024)(128)(4,1)} %ge.25) | copy-start | bytes 3076
Sparse Core Ops, SparseCore 0:
  10.8 67.6 all-gather.2
  80.7 31.5 all-gather.4

commit v8 on v6

--- a/solution.py
+++ b/solution.py
@@ -91,7 +91,7 @@
         mark_list.insert(0, shifted(marks, "gy", shift_by))
     scaling = 1.0 / jnp.sqrt(squares / D + EPSILON)
     query_cols = head_local * HD
-    halves = 2
+    halves = 1
     half_rows = token_count // halves
     query_halves, kv_halves, head_halves = [], [], []
     for h in range(halves):

time: 164 us -> 140 us (0.85)
  other arithmetic: 19.2 us -> 9.41 us
  starting transfers between devices: 37 us -> 27.6 us
  matrix products: 21.3 us -> 13.7 us
  waiting for transfers between devices: 60.2 us -> 67.7 us
  local copies, waits for them, and re-layouts: 11.4 us -> 7.17 us
    dot_general x8 -> x4, matrix products: 16.6 us -> 11 us  [shards(): part = jnp.dot(rows, block, preferred_element_type=jnp.float32)]
    all_gather x2 -> x1, waiting for transfers between devices: 0.01 us -> 4.98 us  [shards(): normed = lax.all_gather(local_normed[rows_of], 'gx', axis=1, tiled=True)]
    ppermute x7, waiting for transfers between devices: 0.02 us -> 4.78 us  [shards(): lax.ppermute(local_squares, 'gx', partner_route(gx_count, gx_count, k))]
    ppermute x3 -> x2, starting transfers between devices: 10.3 us -> 5.71 us  [shifted(): return lax.ppermute(value, axis, pairs)]
    ppermute x2 -> x1, starting transfers between devices: 4.14 us -> 0.07 us  [shards(): lax.ppermute(half_kv, 'gx', partner_route(gx_count, quarters, 2))]
    ppermute x2 -> x1, waiting for transfers between devices: 3.84 us -> 0.01 us  [shards(): lax.ppermute(half_kv, 'gx', partner_route(gx_count, quarters, 2))]
    select_n x5 -> x3, other arithmetic: 2.66 us -> 0.22 us  [joined(): jnp.where(mine_first, jnp.concatenate([mine, theirs], axis=-1), jnp.conca...]
    all_to_all x1, waiting for transfers between devices: 0.01 us -> 2.01 us  [shards(): lax.all_to_all(send_kv, 'gy', split_axis=0, concat_axis=0, tiled=True)]
  transfers between devices with their start and end apart: 21 -> 17, of which waited for: 2 -> 7; matrix products, arithmetic and copies ran while one was open for 22% -> 14% of each run, Pallas kernels for 0% -> 0%
where the time goes in v8:
time: 140 us
  waiting for transfers between devices  67.7 us (48%)
  starting transfers between devices  27.6 us (20%)
  between operations  14.6 us (10%)
  matrix products  13.7 us (10%)
  other arithmetic  9.41 us (7%)
  local copies, waits for them, and re-layouts  7.17 us (5%)
    ppermute x2, waiting for transfers between devices, shifted(): return lax.ppermute(value, axis, pairs)  55.1 us
    dot_general x4, matrix products, shards(): part = jnp.dot(rows, block, preferred_element_type=jnp.float32)  11 us
    ppermute x7, starting transfers between devices, shards(): lax.ppermute(local_squares, 'gx', partner_route(gx_count, gx_count, k))  9.36 us
    ppermute x2, starting transfers between devices, shifted(): return lax.ppermute(value, axis, pairs)  5.71 us
    all_gather x1, waiting for transfers between devices, shards(): normed = lax.all_gather(local_normed[rows_of], 'gx', axis=1, tiled=True)  4.98 us
    ppermute x1, starting transfers between devices, shards(): other = lax.ppermute(half_kv, ('gx', 'gy'), route)  4.81 us
    ppermute x7, waiting for transfers between devices, shards(): lax.ppermute(local_squares, 'gx', partner_route(gx_count, gx_count, k))  4.78 us
    ppermute x3, starting transfers between devices, shards(): lax.ppermute(local_weights, 'gy', partner_route(gy_count, gy_count, k))  3.68 us
  transfers between devices with their start and end apart: 17, of which 7 were waited for; matrix products, arithmetic and copies ran while one was open for 14% of the time, Pallas kernels for 0%

profile of v8, /device:TPU:0, one launch (start us, length us, event | category | flops | bytes accessed | tf_op | source)
XLA Modules:
  0.0 140.1 jit_solution(8520841914466015234)
XLA Ops:
  7.3 0.7 dynamic-slice_convert_fusion
  8.0 2.5 %fusion.4 = (f32[512]{0:T(512)S(1)}, bf16[512,1024]{1,0:T(8,128)(2,1)}) fusion(bf16[512,1024]{1,0:T(8,128)(2,1)} %param.8, f32[1024]{0:T(1024)S(1)} %dynamic-slice_convert_fusion), kind=kLoop, calls=%fused_computation.11 | loop fusion | flops 2620928 | bytes 2103296 | tf_op jit(solution)/shard_map/reduce_sum | solution.py:81
  10.5 5.1 %collective-permute-start.10 = (f32[512]{0:T(512)S(1)}, f32[512]{0:T(512)S(1)}, u32[]{:S(2)}, u32[]{:S(2)}) collective-permute-start(f32[512]{0:T(512)S(1)} %get-tuple-element.9), channel_id=1, source_target_pairs={{0,24},{4,28},{8,16},{12,20},{16,8},{20,12},{24,0},{28,4},{1,25},{... | collective-permute-start | bytes 6152 | tf_op jit(solution)/shard_map/ppermute | solution.py:84
  15.7 0.2 collective-permute-start.5
  15.9 0.4 collective-permute-start.1
  16.4 0.2 select_reduce_fusion
  16.7 0.8 collective-permute-done.1
  17.5 0.1 maximum_select_fusion
  17.6 0.3 copy.24
  17.9 0.3 copy.25
  18.2 1.6 %pad_maximum_fusion = bf16[2048,384]{1,0:T(8,128)(2,1)S(1)} fusion(bf16[2048,64]{1,0:T(8,128)(2,1)S(1)} %copy.25, bf16[2048,64]{1,0:T(8,128)(2,1)S(1)} %copy.24, bf16[2048,256]{1,0:T(8,128)(2,1)} %param.10), kind=kLoop, calls=%fused_computation.22 | loop fusion | flops 4718592 | bytes 3145728 | tf_op jit(solution)/shard_map/concatenate | solution.py:69
  19.8 1.7 %collective-permute-start.3 = (bf16[2048,384]{1,0:T(8,128)(2,1)S(1)}, bf16[2048,384]{1,0:T(8,128)(2,1)}, u32[]{:S(2)}, u32[]{:S(2)}) collective-permute-start(bf16[2048,384]{1,0:T(8,128)(2,1)S(1)} %pad_maximum_fusion), channel_id=1, source_target_pairs={{0,2},{1,3},{2,0},{3,1},{4,6},{5,7},{6,4},{7,5},{8,10},{9,11},{10,... | collective-permute-start | bytes 4718600 | tf_op jit(solution)/shard_map/ppermute | solution.py:73
  21.5 1.5 %collective-permute-start.4 = (bf16[2048,384]{1,0:T(8,128)(2,1)S(1)}, bf16[2048,384]{1,0:T(8,128)(2,1)}, u32[]{:S(2)}, u32[]{:S(2)}) collective-permute-start(bf16[2048,384]{1,0:T(8,128)(2,1)S(1)} %pad_maximum_fusion), channel_id=1, source_target_pairs={{0,3},{1,2},{2,1},{3,0},{4,7},{5,6},{6,5},{7,4},{8,11},{9,10},{10,... | collective-permute-start | bytes 4718600 | tf_op jit(solution)/shard_map/ppermute | solution.py:73
  23.1 0.5 collective-permute-start.2
  23.6 0.8 collective-permute-start.7
  24.4 2.3 %collective-permute-done.6 = f32[512]{0:T(512)S(1)} collective-permute-done((f32[512]{0:T(512)S(1)}, f32[512]{0:T(512)S(1)}, u32[]{:S(2)}, u32[]{:S(2)}) %collective-permute-start.6) | collective-permute-done | bytes 2080 | tf_op jit(solution)/shard_map/ppermute | solution.py:84
  26.7 2.1 %collective-permute-start.8 = (f32[512]{0:T(512)S(1)}, f32[512]{0:T(512)S(1)}, u32[]{:S(2)}, u32[]{:S(2)}) collective-permute-start(f32[512]{0:T(512)S(1)} %get-tuple-element.9), channel_id=1, source_target_pairs={{0,16},{4,20},{8,24},{12,28},{16,0},{20,4},{24,8},{28,12},{1,17},{... | collective-permute-start | bytes 6152 | tf_op jit(solution)/shard_map/ppermute | solution.py:84
  28.9 1.0 collective-permute-start.9
  29.9 1.3 collective-permute-done.8
  31.3 2.3 %collective-permute-start = (s32[512]{0:T(512)S(1)}, s32[512]{0:T(512)S(1)}, u32[]{:S(2)}, u32[]{:S(2)}) collective-permute-start(s32[512]{0:T(512)S(1)} %broadcast_add_fusion), channel_id=1, source_target_pairs={{0,1},{1,2},{2,3},{4,5},{5,6},{6,7},{8,9},{9,10},{10,11},{12,13},{... | collective-permute-start | bytes 6152 | tf_op jit(solution)/shard_map/ppermute | solution.py:19
  33.7 1.1 collective-permute-done.9
  34.9 0.6 gather_fusion
  35.5 55.1 %collective-permute-done = s32[512]{0:T(512)S(1)} collective-permute-done((s32[512]{0:T(512)S(1)}, s32[512]{0:T(512)S(1)}, u32[]{:S(2)}, u32[]{:S(2)}) %collective-permute-start) | collective-permute-done | bytes 2080 | tf_op jit(solution)/shard_map/ppermute | solution.py:19
  90.5 0.1 select_reduce_fusion.1
  90.6 5.0 %all-gather.2.cloned.1.call-done = bf16[512,8192]{1,0:T(8,128)(2,1)} async-done(((bf16[512,1024]{1,0:T(8,128)(2,1)}), bf16[512,8192]{1,0:T(8,128)(2,1)}) %all-gather.2.cloned.1.call-update) | async-done | bytes 8388624 | tf_op jit(solution)/shard_map/all_gather | solution.py:99
  95.6 2.8 %fusion.14 = f32[512,384]{0,1:T(8,128)S(1)} fusion(bf16[2048,384]{1,0:T(8,128)(2,1)S(1)} %pad_maximum_fusion, bf16[512,8192]{1,0:T(8,128)(2,1)} %all-gather.2.cloned.1.call-done, s32[]{:T(128)S(6)} %select_n.156), kind=kOutput, calls=%fused_computation.20 | convolution fusion | flops 805306368 | bytes 4456452 | tf_op jit(solution)/shard_map/dot_general | solution.py:105
  98.4 3.3 %fusion.10 = f32[512,384]{0,1:T(8,128)S(1)} fusion(bf16[2048,384]{1,0:T(8,128)(2,1)} %collective-permute-done.3, bf16[512,8192]{1,0:T(8,128)(2,1)} %all-gather.2.cloned.1.call-done, s32[]{:T(128)S(6)} %select_n.162), kind=kOutput, calls=%fused_computation.16 | convolution fusion | flops 805306368 | bytes 4456452 | tf_op jit(solution)/shard_map/dot_general | solution.py:105
  101.7 2.5 %fusion.8 = f32[512,384]{0,1:T(8,128)S(1)} fusion(bf16[2048,384]{1,0:T(8,128)(2,1)} %collective-permute-done.4, bf16[512,8192]{1,0:T(8,128)(2,1)S(1)} %copy-done, s32[]{:T(128)S(6)} %select_n.163), kind=kOutput, calls=%fused_computation.14 | convolution fusion | flops 805306368 | bytes 4456452 | tf_op jit(solution)/shard_map/dot_general | solution.py:105
  104.2 2.5 %fusion.25 = f32[512,384]{0,1:T(8,128)S(1)} fusion(f32[512,384]{0,1:T(8,128)S(1)} %fusion.8, f32[512,384]{0,1:T(8,128)S(1)} %fusion.10, f32[512,384]{0,1:T(8,128)S(1)} %fusion.14, bf16[2048,384]{1,0:T(8,128)(2,1)} %collective-permute-done.2, bf16[512,8192]{1,0:T(8,128)(2,1)S(1)} %copy-done, s32[]{:T(128)S(6)} %select_n.161, f32[512]{0:T(512)S(1)} %add_rsqrt_fusion), kind=kOutput, calls=%fused_computation.26 | convolution fusion | flops 806092800 | bytes 6817796 | tf_op jit(solution)/shard_map/dot_general | solution.py:105
  106.8 0.6 fusion.62
  107.5 3.4 %collective-permute-start.12 = (bf16[2,512,64]{1,2,0:T(8,128)(2,1)S(1)}, bf16[2,512,64]{1,2,0:T(8,128)(2,1)S(1)}, u32[]{:S(2)}, u32[]{:S(2)}) collective-permute-start(bf16[2,512,64]{1,2,0:T(8,128)(2,1)S(1)} %pad_maximum_fusion.3), channel_id=1, source_target_pairs={{0,1},{1,2},{2,3},{4,5},{5,6},{6,7},{8,9},{9,10},{10,11},{12,13},{... | collective-permute-start | bytes 393224 | tf_op jit(solution)/shard_map/ppermute | solution.py:19
  110.9 4.8 %collective-permute-start.13 = (bf16[2,512,64]{1,2,0:T(8,128)(2,1)S(1)}, bf16[2,512,64]{1,2,0:T(8,128)(2,1)S(1)}, u32[]{:S(2)}, u32[]{:S(2)}) collective-permute-start(bf16[2,512,64]{1,2,0:T(8,128)(2,1)S(1)} %pad_maximum_fusion.3), channel_id=1, source_target_pairs={{0,9},{1,10},{2,11},{4,13},{5,14},{6,15},{8,1},{9,2},{10,3},{12,5}... | collective-permute-start | bytes 393224 | tf_op jit(solution)/shard_map/ppermute | solution.py:130
  115.7 0.1 fusion.76
  115.8 0.2 copy.28
  116.0 0.2 reshape.180
  116.4 1.5 %scatter_fusion = bf16[64,2,512]{2,1,0:T(2,128)(2,1)S(1)} fusion(bf16[64,2,512]{2,1,0:T(2,128)(2,1)S(1)} %broadcast_in_dim.68, s32[32]{0:T(128)S(1)} %fusion.71, bf16[32,2,512]{2,1,0:T(2,128)(2,1)S(1)} %copy.29), kind=kCustom, calls=%fused_computation.1 | custom fusion | bytes 196736 | tf_op jit(solution)/shard_map/scatter | solution.py:184
  117.9 0.7 copy.30
  118.5 3.5 %all-to-all-start = ((bf16[4,16,2,512]{3,1,2,0:T(8,128)(2,1)}), bf16[4,16,2,512]{3,1,2,0:T(8,128)(2,1)S(1)}, u32[]{:S(2)}, u32[]{:S(2)}) async-start(bf16[4,16,2,512]{3,1,2,0:T(8,128)(2,1)} %copy.30), calls=%async_computation | async-start | bytes 262144 | tf_op jit(solution)/shard_map/all_to_all | solution.py:187
  122.0 2.6 %fusion.41 = bf16[512,256]{0,1:T(8,128)(2,1)S(1)} fusion(f32[512,384]{0,1:T(8,128)S(1)} %fusion.25, f32[512,1]{0,1:T(1,128)S(1)} %get-tuple-element.16, f32[512,255]{0,1:T(8,128)S(1)} %get-tuple-element.18, f32[512,255]{0,1:T(8,128)S(1)} %get-tuple-element.17, f32[512,1]{0,1:T(1,128)S(1)} %get-tuple-element.15, f32[256]{0:T(256)S(1)} %multiply_power_fusion, ...), kind=kLoop, calls=%fused_computation.36 | loop fusion | flops 1310720 | bytes 1838336 | tf_op jit(solution)/shard_map/convert_element_type | solution.py:116
  124.7 0.2 copy.26
  124.8 2.0 %all-to-all-done = bf16[4,16,2,512]{3,1,2,0:T(8,128)(2,1)S(1)} async-done(((bf16[4,16,2,512]{3,1,2,0:T(8,128)(2,1)}), bf16[4,16,2,512]{3,1,2,0:T(8,128)(2,1)S(1)}, u32[]{:S(2)}, u32[]{:S(2)}) %all-to-all-start) | async-done | bytes 131104 | tf_op jit(solution)/shard_map/all_to_all | solution.py:187
  126.9 0.3 reshape.182
  127.2 0.9 copy.32
  128.1 0.9 copy.33
  129.2 1.7 %fusion.77 = (f32[1024]{0:T(1024)S(1)}, f32[1024,1024]{0,1:T(8,128)S(1)}) fusion(bf16[1024,128]{1,0:T(8,128)(2,1)S(1)} %bitcast.76, bf16[2,512,128]{1,2,0:T(8,128)(2,1)S(1)} %maximum_select_fusion.1, bf16[2,512,128]{1,2,0:T(8,128)(2,1)S(1)} %maximum_select_fusion.2, s32[1024]{0:T(1024)S(1)} %bitcast.81, pred[1024]{0:T(1024)(128)(4,1)S(1)} %broadcast_compare_fusion, ...), kind=kOutput, calls=%fused_computation.117 | convolution fusion | flops 276298752 | bytes 4998144 | tf_op jit(solution)/shard_map/dot_general | solution.py:148
  130.9 0.6 fusion.1
  131.6 0.9 fusion.34
  132.5 0.7 copy.38
  (63 shorter events, 1.0 us)
Async XLA Ops:
  7.2 8.7 %copy-start.2 = (bf16[2048,32]{0,1:T(8,128)(2,1)S(1)}, bf16[2048,32]{0,1:T(8,128)(2,1)}, u32[]{:S(2)}) copy-start(bf16[2048,32]{0,1:T(8,128)(2,1)} %param.11) | copy-start | bytes 393220
  7.2 8.7 %copy-start.1 = (bf16[2048,32]{0,1:T(8,128)(2,1)S(1)}, bf16[2048,32]{0,1:T(8,128)(2,1)}, u32[]{:S(2)}) copy-start(bf16[2048,32]{0,1:T(8,128)(2,1)} %param.12) | copy-start | bytes 393220
  7.2 9.1 %copy-start.4 = (s32[32,1]{0,1:T(1,128)S(1)}, s32[32,1]{0,1:T(1,128)}, u32[]{:S(2)}) copy-start(s32[32,1]{0,1:T(1,128)} %param.15) | copy-start | bytes 388
  7.2 9.4 %copy-start.3 = (s32[512]{0:T(512)S(1)}, s32[512]{0:T(512)}, u32[]{:S(2)}) copy-start(s32[512]{0:T(512)} %param.13) | copy-start | bytes 6148
  7.2 88.4 %all-gather.2.cloned.1.call-start = ((), (), s32[]{:S(2)}) async-start(), calls=%async_computation.1 | async-start | bytes 9437184 | tf_op jit(solution)/shard_map/all_gather | solution.py:99
  10.5 12.5 %collective-permute-start.10 = (f32[512]{0:T(512)S(1)}, f32[512]{0:T(512)S(1)}, u32[]{:S(2)}, u32[]{:S(2)}) collective-permute-start(f32[512]{0:T(512)S(1)} %get-tuple-element.9), channel_id=1, source_target_pairs={{0,24},{4,28},{8,16},{12,20},{16,8},{20,12},{24,0},{28,4},{1,25},{... | collective-permute-start | bytes 6152 | tf_op jit(solution)/shard_map/ppermute | solution.py:84
  15.7 7.5 %collective-permute-start.11 = (f32[512]{0:T(512)S(1)}, f32[512]{0:T(512)S(1)}, u32[]{:S(2)}, u32[]{:S(2)}) collective-permute-start(f32[512]{0:T(512)S(1)} %get-tuple-element.9), channel_id=1, source_target_pairs={{0,28},{4,24},{8,20},{12,16},{16,12},{20,8},{24,4},{28,0},{1,29},{... | collective-permute-start | bytes 6152 | tf_op jit(solution)/shard_map/ppermute | solution.py:84
  15.7 7.9 %collective-permute-start.5 = (f32[512]{0:T(512)S(1)}, f32[512]{0:T(512)S(1)}, u32[]{:S(2)}, u32[]{:S(2)}) collective-permute-start(f32[512]{0:T(512)S(1)} %get-tuple-element.9), channel_id=1, source_target_pairs={{0,4},{4,0},{8,12},{12,8},{16,20},{20,16},{24,28},{28,24},{1,5},{5... | collective-permute-start | bytes 6152 | tf_op jit(solution)/shard_map/ppermute | solution.py:84
  15.9 1.6 %collective-permute-start.1 = (bf16[2,2048,32]{1,2,0:T(8,128)(2,1)S(1)}, bf16[2,2048,32]{1,2,0:T(8,128)(2,1)S(1)}, u32[]{:S(2)}, u32[]{:S(2)}) collective-permute-start(bf16[2,2048,32]{1,2,0:T(8,128)(2,1)S(1)} %pad_maximum_fusion.2), channel_id=1, source_target_pairs={{0,4},{4,0},{8,12},{12,8},{16,20},{20,16},{24,28},{28,24},{1,5},{5... | collective-permute-start | bytes 786440 | tf_op jit(solution)/shard_map/ppermute | solution.py:67
  17.9 15.7 %copy-start.5 = (s32[512]{0:T(512)S(1)}, s32[512]{0:T(512)}, u32[]{:S(2)}) copy-start(s32[512]{0:T(512)} %param.14) | copy-start | bytes 6148
  19.8 78.6 %collective-permute-start.3 = (bf16[2048,384]{1,0:T(8,128)(2,1)S(1)}, bf16[2048,384]{1,0:T(8,128)(2,1)}, u32[]{:S(2)}, u32[]{:S(2)}) collective-permute-start(bf16[2048,384]{1,0:T(8,128)(2,1)S(1)} %pad_maximum_fusion), channel_id=1, source_target_pairs={{0,2},{1,3},{2,0},{3,1},{4,6},{5,7},{6,4},{7,5},{8,10},{9,11},{10,... | collective-permute-start | bytes 4718600 | tf_op jit(solution)/shard_map/ppermute | solution.py:73
  21.5 80.2 %collective-permute-start.4 = (bf16[2048,384]{1,0:T(8,128)(2,1)S(1)}, bf16[2048,384]{1,0:T(8,128)(2,1)}, u32[]{:S(2)}, u32[]{:S(2)}) collective-permute-start(bf16[2048,384]{1,0:T(8,128)(2,1)S(1)} %pad_maximum_fusion), channel_id=1, source_target_pairs={{0,3},{1,2},{2,1},{3,0},{4,7},{5,6},{6,5},{7,4},{8,11},{9,10},{10,... | collective-permute-start | bytes 4718600 | tf_op jit(solution)/shard_map/ppermute | solution.py:73
  23.0 3.7 %collective-permute-start.6 = (f32[512]{0:T(512)S(1)}, f32[512]{0:T(512)S(1)}, u32[]{:S(2)}, u32[]{:S(2)}) collective-permute-start(f32[512]{0:T(512)S(1)} %get-tuple-element.9), channel_id=1, source_target_pairs={{0,8},{4,12},{8,0},{12,4},{16,24},{20,28},{24,16},{28,20},{1,9},{5... | collective-permute-start | bytes 6152 | tf_op jit(solution)/shard_map/ppermute | solution.py:84
  23.1 81.1 %collective-permute-start.2 = (bf16[2048,384]{1,0:T(8,128)(2,1)S(1)}, bf16[2048,384]{1,0:T(8,128)(2,1)}, u32[]{:S(2)}, u32[]{:S(2)}) collective-permute-start(bf16[2048,384]{1,0:T(8,128)(2,1)S(1)} %pad_maximum_fusion), channel_id=1, source_target_pairs={{0,1},{1,0},{2,3},{3,2},{4,5},{5,4},{6,7},{7,6},{8,9},{9,8},{10,11... | collective-permute-start | bytes 4718600 | tf_op jit(solution)/shard_map/ppermute | solution.py:73
  23.6 5.3 %collective-permute-start.7 = (f32[512]{0:T(512)S(1)}, f32[512]{0:T(512)S(1)}, u32[]{:S(2)}, u32[]{:S(2)}) collective-permute-start(f32[512]{0:T(512)S(1)} %get-tuple-element.9), channel_id=1, source_target_pairs={{0,12},{4,8},{8,4},{12,0},{16,28},{20,24},{24,20},{28,16},{1,13},{... | collective-permute-start | bytes 6152 | tf_op jit(solution)/shard_map/ppermute | solution.py:84
  26.7 4.5 %collective-permute-start.8 = (f32[512]{0:T(512)S(1)}, f32[512]{0:T(512)S(1)}, u32[]{:S(2)}, u32[]{:S(2)}) collective-permute-start(f32[512]{0:T(512)S(1)} %get-tuple-element.9), channel_id=1, source_target_pairs={{0,16},{4,20},{8,24},{12,28},{16,0},{20,4},{24,8},{28,12},{1,17},{... | collective-permute-start | bytes 6152 | tf_op jit(solution)/shard_map/ppermute | solution.py:84
  28.9 6.0 %collective-permute-start.9 = (f32[512]{0:T(512)S(1)}, f32[512]{0:T(512)S(1)}, u32[]{:S(2)}, u32[]{:S(2)}) collective-permute-start(f32[512]{0:T(512)S(1)} %get-tuple-element.9), channel_id=1, source_target_pairs={{0,20},{4,16},{8,28},{12,24},{16,4},{20,0},{24,12},{28,8},{1,21},{... | collective-permute-start | bytes 6152 | tf_op jit(solution)/shard_map/ppermute | solution.py:84
  31.3 59.3 %collective-permute-start = (s32[512]{0:T(512)S(1)}, s32[512]{0:T(512)S(1)}, u32[]{:S(2)}, u32[]{:S(2)}) collective-permute-start(s32[512]{0:T(512)S(1)} %broadcast_add_fusion), channel_id=1, source_target_pairs={{0,1},{1,2},{2,3},{4,5},{5,6},{6,7},{8,9},{9,10},{10,11},{12,13},{... | collective-permute-start | bytes 6152 | tf_op jit(solution)/shard_map/ppermute | solution.py:19
  95.6 6.1 %copy-start = (bf16[512,8192]{1,0:T(8,128)(2,1)S(1)}, bf16[512,8192]{1,0:T(8,128)(2,1)}, u32[]{:S(2)}) copy-start(bf16[512,8192]{1,0:T(8,128)(2,1)} %all-gather.2.cloned.1.call-done) | copy-start | bytes 25165828
  107.4 21.7 %collective-permute-start.14 = (bf16[2,512,64]{1,2,0:T(8,128)(2,1)S(1)}, bf16[2,512,64]{1,2,0:T(8,128)(2,1)S(1)}, u32[]{:S(2)}, u32[]{:S(2)}) collective-permute-start(bf16[2,512,64]{1,2,0:T(8,128)(2,1)S(1)} %pad_maximum_fusion.3), channel_id=1, source_target_pairs={{0,8},{4,12},{8,0},{12,4},{16,24},{20,28},{24,16},{28,20},{1,9},{5... | collective-permute-start | bytes 393224 | tf_op jit(solution)/shard_map/ppermute | solution.py:121
  107.5 21.6 %collective-permute-start.12 = (bf16[2,512,64]{1,2,0:T(8,128)(2,1)S(1)}, bf16[2,512,64]{1,2,0:T(8,128)(2,1)S(1)}, u32[]{:S(2)}, u32[]{:S(2)}) collective-permute-start(bf16[2,512,64]{1,2,0:T(8,128)(2,1)S(1)} %pad_maximum_fusion.3), channel_id=1, source_target_pairs={{0,1},{1,2},{2,3},{4,5},{5,6},{6,7},{8,9},{9,10},{10,11},{12,13},{... | collective-permute-start | bytes 393224 | tf_op jit(solution)/shard_map/ppermute | solution.py:19
  110.9 18.3 %collective-permute-start.13 = (bf16[2,512,64]{1,2,0:T(8,128)(2,1)S(1)}, bf16[2,512,64]{1,2,0:T(8,128)(2,1)S(1)}, u32[]{:S(2)}, u32[]{:S(2)}) collective-permute-start(bf16[2,512,64]{1,2,0:T(8,128)(2,1)S(1)} %pad_maximum_fusion.3), channel_id=1, source_target_pairs={{0,9},{1,10},{2,11},{4,13},{5,14},{6,15},{8,1},{9,2},{10,3},{12,5}... | collective-permute-start | bytes 393224 | tf_op jit(solution)/shard_map/ppermute | solution.py:130
  118.5 8.3 %all-to-all-start = ((bf16[4,16,2,512]{3,1,2,0:T(8,128)(2,1)}), bf16[4,16,2,512]{3,1,2,0:T(8,128)(2,1)S(1)}, u32[]{:S(2)}, u32[]{:S(2)}) async-start(bf16[4,16,2,512]{3,1,2,0:T(8,128)(2,1)} %copy.30), calls=%async_computation | async-start | bytes 262144 | tf_op jit(solution)/shard_map/all_to_all | solution.py:187
Sparse Core Ops, SparseCore 0:
  10.7 84.9 all-gather.1

commit v9 on v8

--- a/solution.py
+++ b/solution.py
@@ -99,37 +99,43 @@
         normed = lax.all_gather(local_normed[rows_of], "gx", axis=1, tiled=True)
         if head_halves:
             normed, head_halves[-1] = lax.optimization_barrier((normed, head_halves[-1]))
-        products = None
+        query_cols = head_local * HD
+        kv_products = None
+        q_products = None
         for source, block in pieces:
             rows = lax.dynamic_slice_in_dim(normed, source * row_block, row_block, 1)
-            part = jnp.dot(rows, block, preferred_element_type=jnp.float32)
-            products = part if products is None else products + part
-        projected = products * scaling[rows_of, None]
+            kv_part = jnp.dot(rows, block[:, query_cols:], preferred_element_type=jnp.float32)
+            kv_products = kv_part if kv_products is None else kv_products + kv_part
         places = positions[rows_of]
-        key_half = rope(
-            projected[:, query_cols : query_cols + half_cols],
-            places,
-            half_cols,
-            (spot // 2) * quarter,
-        ).astype(jnp.bfloat16)
-        value_half = projected[:, query_cols + half_cols :].astype(jnp.bfloat16)
-        query_halves.append(rope(projected[:, :query_cols], places, HD, 0).astype(jnp.bfloat16))
+        kv_projected = kv_products * scaling[rows_of, None]
+        key_half = rope(kv_projected[:, :half_cols], places, half_cols, (spot // 2) * quarter)
+        key_half = key_half.astype(jnp.bfloat16)
+        value_half = kv_projected[:, half_cols:].astype(jnp.bfloat16)
         half_kv = jnp.stack([key_half, value_half])
-        kv_halves.append(lax.dynamic_slice_in_dim(half_kv, (spot % 2) * quarter, quarter, 2))
-        low_half = (spot // 2) % 2 == 0
-        window_list = [
-            joined(half_kv, lax.ppermute(half_kv, "gx", partner_route(gx_count, quarters, 2)), low_half)
-        ]
+        normed, half_kv = lax.optimization_barrier((normed, half_kv))
+        received = [lax.ppermute(half_kv, "gx", partner_route(gx_count, quarters, 2))]
         for shift_by in range(1, span_count + 1):
             route = []
             for i in range(gx_count):
                 peer = i - i % quarters + ((i % quarters) ^ 2)
                 for j in range(gy_count - shift_by):
                     route.append((i * gy_count + j, peer * gy_count + j + shift_by))
-            same = shifted(half_kv, "gy", shift_by)
-            other = lax.ppermute(half_kv, ("gx", "gy"), route)
+            received.append(shifted(half_kv, "gy", shift_by))
+            received.append(lax.ppermute(half_kv, ("gx", "gy"), route))
+        for source, block in pieces:
+            rows = lax.dynamic_slice_in_dim(normed, source * row_block, row_block, 1)
+            q_part = jnp.dot(rows, block[:, :query_cols], preferred_element_type=jnp.float32)
+            q_products = q_part if q_products is None else q_products + q_part
+        received, q_products = lax.optimization_barrier((received, q_products))
+        low_half = (spot // 2) % 2 == 0
+        window_list = [joined(half_kv, received[0], low_half)]
+        for shift_by in range(1, span_count + 1):
+            same, other = received[2 * shift_by - 1], received[2 * shift_by]
             window_list.insert(0, joined(same, other, low_half))
         held = jnp.concatenate(window_list, axis=1)
+        projected = q_products * scaling[rows_of, None]
+        query_halves.append(rope(projected, places, HD, 0).astype(jnp.bfloat16))
+        kv_halves.append(lax.dynamic_slice_in_dim(half_kv, (spot % 2) * quarter, quarter, 2))
         head_halves.append(held.reshape(2, span_count + 1, half_rows, HD))
     queries = jnp.concatenate(query_halves, axis=0)
     own_kv = jnp.concatenate(kv_halves, axis=1)

time: 140 us -> 146 us (1.043)
  matrix products: 13.7 us -> 21.1 us
  waiting for transfers between devices: 67.7 us -> 61.7 us
  starting transfers between devices: 27.6 us -> 31.6 us
    dot_general x4 -> x8, matrix products: 11 us -> 18.4 us  [the longest x4 9.98 us: shards(): jnp.dot(rows, block[:, query_cols:], preferred_element_type=jnp.float32)]
    ppermute x7, waiting for transfers between devices: 4.78 us -> 0.96 us  [shards(): lax.ppermute(local_squares, 'gx', partner_route(gx_count, gx_count, k))]
    ppermute x7, starting transfers between devices: 9.36 us -> 12.6 us  [shards(): lax.ppermute(local_squares, 'gx', partner_route(gx_count, gx_count, k))]
    ppermute x2, waiting for transfers between devices: 55.1 us -> 52.1 us  [shifted(): return lax.ppermute(value, axis, pairs)]
    all_gather x1, waiting for transfers between devices: 4.98 us -> 7.63 us  [shards(): normed = lax.all_gather(local_normed[rows_of], 'gx', axis=1, tiled=True)]
    convert_element_type x1 -> x0, other arithmetic: 2.61 us -> none  [shards(): rope(projected[:, :query_cols], places, HD, 0).astype(jnp.bfloat16)]
    reshape x0 -> x1, other arithmetic: none -> 2.52 us  [shards(): queries.reshape(token_count, head_local, HD).transpose(1, 0, 2)]
    all_to_all x1, waiting for transfers between devices: 2.01 us -> 0.01 us  [shards(): lax.all_to_all(send_kv, 'gy', split_axis=0, concat_axis=0, tiled=True)]
  transfers between devices with their start and end apart: 17 -> 17, of which waited for: 7 -> 5; matrix products, arithmetic and copies ran while one was open for 14% -> 17% of each run, Pallas kernels for 0% -> 0%
where the time goes in v9:
time: 146 us
  waiting for transfers between devices  61.7 us (42%)
  starting transfers between devices  31.6 us (22%)
  matrix products  21.1 us (14%)
  between operations  14.6 us (10%)
  other arithmetic  9.5 us (7%)
  local copies, waits for them, and re-layouts  7.26 us (5%)
    ppermute x2, waiting for transfers between devices, shifted(): return lax.ppermute(value, axis, pairs)  52.1 us
    ppermute x7, starting transfers between devices, shards(): lax.ppermute(local_squares, 'gx', partner_route(gx_count, gx_count, k))  12.6 us
    dot_general x4, matrix products, shards(): jnp.dot(rows, block[:, query_cols:], preferred_element_type=jnp.float32)  9.98 us
    dot_general x4, matrix products, shards(): jnp.dot(rows, block[:, :query_cols], preferred_element_type=jnp.float32)  8.46 us
    all_gather x1, waiting for transfers between devices, shards(): normed = lax.all_gather(local_normed[rows_of], 'gx', axis=1, tiled=True)  7.63 us
    ppermute x2, starting transfers between devices, shifted(): return lax.ppermute(value, axis, pairs)  6.77 us
    ppermute x1, starting transfers between devices, shards(): received.append(lax.ppermute(half_kv, ('gx', 'gy'), route))  4.81 us
    ppermute x3, starting transfers between devices, shards(): lax.ppermute(local_weights, 'gy', partner_route(gy_count, gy_count, k))  3.55 us
  transfers between devices with their start and end apart: 17, of which 5 were waited for; matrix products, arithmetic and copies ran while one was open for 17% of the time, Pallas kernels for 0%

profile of v9, /device:TPU:0, one launch (start us, length us, event | category | flops | bytes accessed | tf_op | source)
XLA Modules:
  0.0 145.8 jit_solution(3560195201385425089)
XLA Ops:
  7.3 0.7 dynamic-slice_convert_fusion
  8.0 2.5 %fusion.4 = (f32[512]{0:T(512)S(1)}, bf16[512,1024]{1,0:T(8,128)(2,1)}) fusion(bf16[512,1024]{1,0:T(8,128)(2,1)} %param.8, f32[1024]{0:T(1024)S(1)} %dynamic-slice_convert_fusion), kind=kLoop, calls=%fused_computation.11 | loop fusion | flops 2620928 | bytes 2103296 | tf_op jit(solution)/shard_map/reduce_sum | solution.py:81
  10.5 0.5 collective-permute-start.5
  11.0 2.6 %collective-permute-start.6 = (f32[512]{0:T(512)S(1)}, f32[512]{0:T(512)S(1)}, u32[]{:S(2)}, u32[]{:S(2)}) collective-permute-start(f32[512]{0:T(512)S(1)} %get-tuple-element.21), channel_id=1, source_target_pairs={{0,8},{4,12},{8,0},{12,4},{16,24},{20,28},{24,16},{28,20},{1,9},{5... | collective-permute-start | bytes 6152 | tf_op jit(solution)/shard_map/ppermute | solution.py:84
  13.7 0.2 collective-permute-start.1
  14.1 0.2 select_reduce_fusion
  14.4 0.9 collective-permute-done.1
  15.5 0.3 copy.25
  15.8 0.3 copy.24
  16.1 1.6 %pad_maximum_fusion = bf16[2048,384]{1,0:T(8,128)(2,1)S(1)} fusion(bf16[2048,64]{1,0:T(8,128)(2,1)S(1)} %copy.25, bf16[2048,64]{1,0:T(8,128)(2,1)S(1)} %copy.24, bf16[2048,256]{1,0:T(8,128)(2,1)} %param.10), kind=kLoop, calls=%fused_computation.30 | loop fusion | flops 4718592 | bytes 3145728 | tf_op jit(solution)/shard_map/concatenate | solution.py:69
  17.6 2.5 %collective-permute-start.4 = (bf16[2048,384]{1,0:T(8,128)(2,1)S(1)}, bf16[2048,384]{1,0:T(8,128)(2,1)}, u32[]{:S(2)}, u32[]{:S(2)}) collective-permute-start(bf16[2048,384]{1,0:T(8,128)(2,1)S(1)} %pad_maximum_fusion), channel_id=1, source_target_pairs={{0,3},{1,2},{2,1},{3,0},{4,7},{5,6},{6,5},{7,4},{8,11},{9,10},{10,... | collective-permute-start | bytes 4718600 | tf_op jit(solution)/shard_map/ppermute | solution.py:73
  20.1 0.5 collective-permute-start.3
  20.6 0.5 collective-permute-start.2
  21.3 2.7 %collective-permute-start.8 = (f32[512]{0:T(512)S(1)}, f32[512]{0:T(512)S(1)}, u32[]{:S(2)}, u32[]{:S(2)}) collective-permute-start(f32[512]{0:T(512)S(1)} %get-tuple-element.21), channel_id=1, source_target_pairs={{0,16},{4,20},{8,24},{12,28},{16,0},{20,4},{24,8},{28,12},{1,17},{... | collective-permute-start | bytes 6152 | tf_op jit(solution)/shard_map/ppermute | solution.py:84
  24.0 0.3 collective-permute-done.7
  24.3 1.9 %collective-permute-start.9 = (f32[512]{0:T(512)S(1)}, f32[512]{0:T(512)S(1)}, u32[]{:S(2)}, u32[]{:S(2)}) collective-permute-start(f32[512]{0:T(512)S(1)} %get-tuple-element.21), channel_id=1, source_target_pairs={{0,20},{4,16},{8,28},{12,24},{16,4},{20,0},{24,12},{28,8},{1,21},{... | collective-permute-start | bytes 6152 | tf_op jit(solution)/shard_map/ppermute | solution.py:84
  26.2 3.4 %collective-permute-start.10 = (f32[512]{0:T(512)S(1)}, f32[512]{0:T(512)S(1)}, u32[]{:S(2)}, u32[]{:S(2)}) collective-permute-start(f32[512]{0:T(512)S(1)} %get-tuple-element.21), channel_id=1, source_target_pairs={{0,24},{4,28},{8,16},{12,20},{16,8},{20,12},{24,0},{28,4},{1,25},{... | collective-permute-start | bytes 6152 | tf_op jit(solution)/shard_map/ppermute | solution.py:84
  29.6 1.4 collective-permute-start.11
  31.0 0.6 collective-permute-done.10
  31.7 3.4 %collective-permute-start = (s32[512]{0:T(512)S(1)}, s32[512]{0:T(512)S(1)}, u32[]{:S(2)}, u32[]{:S(2)}) collective-permute-start(s32[512]{0:T(512)S(1)} %broadcast_add_fusion), channel_id=1, source_target_pairs={{0,1},{1,2},{2,3},{4,5},{5,6},{6,7},{8,9},{9,10},{10,11},{12,13},{... | collective-permute-start | bytes 6152 | tf_op jit(solution)/shard_map/ppermute | solution.py:19
  35.2 0.6 gather_fusion
  35.8 52.1 %collective-permute-done = s32[512]{0:T(512)S(1)} collective-permute-done((s32[512]{0:T(512)S(1)}, s32[512]{0:T(512)S(1)}, u32[]{:S(2)}, u32[]{:S(2)}) %collective-permute-start) | collective-permute-done | bytes 2080 | tf_op jit(solution)/shard_map/ppermute | solution.py:19
  88.0 7.6 %all-gather.2.cloned.1.call-done = bf16[512,8192]{1,0:T(8,128)(2,1)} async-done(((bf16[512,1024]{1,0:T(8,128)(2,1)}), bf16[512,8192]{1,0:T(8,128)(2,1)}) %all-gather.2.cloned.1.call-update) | async-done | bytes 8388624 | tf_op jit(solution)/shard_map/all_gather | solution.py:99
  95.7 2.6 %fusion.22 = f32[512,128]{0,1:T(8,128)S(1)} fusion(bf16[512,8192]{1,0:T(8,128)(2,1)} %all-gather.2.cloned.1.call-done, s32[]{:T(128)S(6)} %select_n.161, bf16[2048,64]{0,1:T(8,128)(2,1)S(1)} %get-tuple-element.30, bf16[2048,64]{0,1:T(8,128)(2,1)S(1)} %get-tuple-element.29), kind=kOutput, calls=%fused_computation.28 | convolution fusion | flops 269484032 | bytes 2883588 | tf_op jit(solution)/shard_map/dot_general | solution.py:107
  98.2 2.9 %fusion.16 = f32[512,128]{0,1:T(8,128)S(1)} fusion(bf16[512,8192]{1,0:T(8,128)(2,1)} %all-gather.2.cloned.1.call-done, s32[]{:T(128)S(6)} %select_n.168, bf16[2048,384]{1,0:T(8,128)(2,1)} %collective-permute-done.4), kind=kOutput, calls=%fused_computation.22 | convolution fusion | flops 268435456 | bytes 2883588 | tf_op jit(solution)/shard_map/dot_general | solution.py:107
  101.2 2.5 %fusion.18 = f32[512,128]{0,1:T(8,128)S(1)} fusion(bf16[512,8192]{1,0:T(8,128)(2,1)} %all-gather.2.cloned.1.call-done, s32[]{:T(128)S(6)} %select_n.167, bf16[2048,384]{1,0:T(8,128)(2,1)} %collective-permute-done.3), kind=kOutput, calls=%fused_computation.24 | convolution fusion | flops 268435456 | bytes 2883588 | tf_op jit(solution)/shard_map/dot_general | solution.py:107
  103.7 2.0 %fusion.51 = f32[512,128]{0,1:T(8,128)S(1)} fusion(f32[512,128]{0,1:T(8,128)S(1)} %fusion.16, f32[512,128]{0,1:T(8,128)S(1)} %fusion.18, f32[512,128]{0,1:T(8,128)S(1)} %fusion.22, bf16[512,8192]{1,0:T(8,128)(2,1)S(1)} %copy-done, s32[]{:T(128)S(6)} %select_n.166, bf16[2048,384]{1,0:T(8,128)(2,1)} %collective-permute-done.2, f32[512]{0:T(512)S(1)} %add_rsqrt_fusion), kind=kOutput, calls=%fused_computation.40 | convolution fusion | flops 268697600 | bytes 3672068 | tf_op jit(solution)/shard_map/dot_general | solution.py:107
  105.8 0.6 fusion.88
  106.5 3.4 %collective-permute-start.13 = (bf16[2,512,64]{1,2,0:T(8,128)(2,1)S(1)}, bf16[2,512,64]{1,2,0:T(8,128)(2,1)S(1)}, u32[]{:S(2)}, u32[]{:S(2)}) collective-permute-start(bf16[2,512,64]{1,2,0:T(8,128)(2,1)S(1)} %pad_maximum_fusion.3), channel_id=1, source_target_pairs={{0,1},{1,2},{2,3},{4,5},{5,6},{6,7},{8,9},{9,10},{10,11},{12,13},{... | collective-permute-start | bytes 393224 | tf_op jit(solution)/shard_map/ppermute | solution.py:19
  109.9 4.8 %collective-permute-start.14 = (bf16[2,512,64]{1,2,0:T(8,128)(2,1)S(1)}, bf16[2,512,64]{1,2,0:T(8,128)(2,1)S(1)}, u32[]{:S(2)}, u32[]{:S(2)}) collective-permute-start(bf16[2,512,64]{1,2,0:T(8,128)(2,1)S(1)} %pad_maximum_fusion.3), channel_id=1, source_target_pairs={{0,9},{1,10},{2,11},{4,13},{5,14},{6,15},{8,1},{9,2},{10,3},{12,5}... | collective-permute-start | bytes 393224 | tf_op jit(solution)/shard_map/ppermute | solution.py:124
  114.7 0.7 fusion.14
  115.6 0.2 reshape.180
  116.0 1.5 %scatter_fusion = bf16[64,2,512]{2,1,0:T(2,128)(2,1)S(1)} fusion(bf16[64,2,512]{2,1,0:T(2,128)(2,1)S(1)} %broadcast_in_dim.69, s32[32]{0:T(128)S(1)} %fusion.101, bf16[32,2,512]{2,1,0:T(2,128)(2,1)S(1)} %copy.29), kind=kCustom, calls=%fused_computation.1 | custom fusion | bytes 196736 | tf_op jit(solution)/shard_map/scatter | solution.py:190
  117.5 0.7 copy.30
  118.2 3.5 %all-to-all-start = ((bf16[4,16,2,512]{3,1,2,0:T(8,128)(2,1)}), bf16[4,16,2,512]{3,1,2,0:T(8,128)(2,1)S(1)}, u32[]{:S(2)}, u32[]{:S(2)}) async-start(bf16[4,16,2,512]{3,1,2,0:T(8,128)(2,1)} %copy.30), calls=%async_computation | async-start | bytes 262144 | tf_op jit(solution)/shard_map/all_to_all | solution.py:193
  121.7 2.6 %fusion.8 = f32[512,256]{1,0:T(8,128)S(1)} fusion(bf16[512,8192]{1,0:T(8,128)(2,1)} %all-gather.2.cloned.1.call-done, s32[]{:T(128)S(6)} %select_n.168, bf16[2048,384]{1,0:T(8,128)(2,1)} %collective-permute-done.4), kind=kOutput, calls=%fused_computation.14 | convolution fusion | flops 536870912 | bytes 3670020 | tf_op jit(solution)/shard_map/dot_general | solution.py:127
  124.3 2.6 %fusion.10 = f32[512,256]{1,0:T(8,128)S(1)} fusion(bf16[512,8192]{1,0:T(8,128)(2,1)} %all-gather.2.cloned.1.call-done, s32[]{:T(128)S(6)} %select_n.167, bf16[2048,384]{1,0:T(8,128)(2,1)} %collective-permute-done.3), kind=kOutput, calls=%fused_computation.16 | convolution fusion | flops 536870912 | bytes 3670020 | tf_op jit(solution)/shard_map/dot_general | solution.py:127
  126.9 2.6 %fusion.30 = f32[512,256]{1,0:T(8,128)S(1)} fusion(f32[512,256]{1,0:T(8,128)S(1)} %fusion.8, f32[512,256]{1,0:T(8,128)S(1)} %fusion.10, f32[512,256]{1,0:T(8,128)S(1)} %fusion.14, bf16[512,8192]{1,0:T(8,128)(2,1)} %all-gather.2.cloned.1.call-done, s32[]{:T(128)S(6)} %select_n.166, bf16[2048,384]{1,0:T(8,128)(2,1)} %collective-permute-done.2), kind=kOutput, calls=%fused_computation.33 | convolution fusion | flops 537264128 | bytes 5242884 | tf_op jit(solution)/shard_map/dot_general | solution.py:127
  129.5 0.3 reshape.182
  129.8 0.9 copy.32
  130.7 0.9 copy.33
  131.8 0.2 fusion.105
  132.1 0.2 maximum_select_fusion.1
  132.3 2.5 %copy_bitcast_fusion.1 = bf16[512,2,128]{2,0,1:T(8,128)(2,1)S(1)} fusion(f32[512,255]{1,0:T(8,128)S(1)} %get-tuple-element.26, f32[512,1]{1,0:T(8,128)S(1)} %get-tuple-element.28, f32[512,1]{1,0:T(8,128)S(1)} %get-tuple-element.27, f32[512,255]{1,0:T(8,128)S(1)} %get-tuple-element.25, f32[256]{0:T(256)S(1)} %multiply_power_fusion, ...), kind=kLoop, calls=%fused_computation.66 | loop fusion | flops 1441792 | bytes 1840384 | tf_op jit(solution)/shard_map/reshape | solution.py:150
  134.9 1.8 %fusion.109 = (f32[1024]{0:T(1024)S(1)}, f32[1024,1024]{0,1:T(8,128)S(1)}) fusion(bf16[1024,128]{1,0:T(8,128)(2,1)S(1)} %bitcast.75, bf16[2,512,128]{1,2,0:T(8,128)(2,1)S(1)} %get-tuple-element.37, bf16[2,512,128]{1,2,0:T(8,128)(2,1)S(1)} %get-tuple-element.38, s32[1024]{0:T(1024)S(1)} %bitcast.80, pred[1024]{0:T(1024)(128)(4,1)S(1)} %broadcast_compare_fusion, ...), kind=kOutput, calls=%fused_computation.144 | convolution fusion | flops 276298752 | bytes 4998144 | tf_op jit(solution)/shard_map/dot_general | solution.py:154
  136.6 0.6 fusion.1
  137.3 0.9 fusion.39
  138.2 0.7 copy.40
  (69 shorter events, 1.5 us)
Async XLA Ops:
  7.2 6.5 %copy-start.2 = (bf16[2048,32]{0,1:T(8,128)(2,1)S(1)}, bf16[2048,32]{0,1:T(8,128)(2,1)}, u32[]{:S(2)}) copy-start(bf16[2048,32]{0,1:T(8,128)(2,1)} %param.12) | copy-start | bytes 393220
  7.2 6.5 %copy-start.3 = (bf16[2048,32]{0,1:T(8,128)(2,1)S(1)}, bf16[2048,32]{0,1:T(8,128)(2,1)}, u32[]{:S(2)}) copy-start(bf16[2048,32]{0,1:T(8,128)(2,1)} %param.11) | copy-start | bytes 393220
  7.2 6.8 %copy-start.5 = (s32[32,1]{0,1:T(1,128)S(1)}, s32[32,1]{0,1:T(1,128)}, u32[]{:S(2)}) copy-start(s32[32,1]{0,1:T(1,128)} %param.15) | copy-start | bytes 388
  7.2 7.1 %copy-start.4 = (s32[512]{0:T(512)S(1)}, s32[512]{0:T(512)}, u32[]{:S(2)}) copy-start(s32[512]{0:T(512)} %param.13) | copy-start | bytes 6148
  7.2 88.4 %all-gather.2.cloned.1.call-start = ((), (), s32[]{:S(2)}) async-start(), calls=%async_computation.1 | async-start | bytes 9437184 | tf_op jit(solution)/shard_map/all_gather | solution.py:99
  10.5 10.7 %collective-permute-start.5 = (f32[512]{0:T(512)S(1)}, f32[512]{0:T(512)S(1)}, u32[]{:S(2)}, u32[]{:S(2)}) collective-permute-start(f32[512]{0:T(512)S(1)} %get-tuple-element.21), channel_id=1, source_target_pairs={{0,4},{4,0},{8,12},{12,8},{16,20},{20,16},{24,28},{28,24},{1,5},{5... | collective-permute-start | bytes 6152 | tf_op jit(solution)/shard_map/ppermute | solution.py:84
  11.0 10.2 %collective-permute-start.6 = (f32[512]{0:T(512)S(1)}, f32[512]{0:T(512)S(1)}, u32[]{:S(2)}, u32[]{:S(2)}) collective-permute-start(f32[512]{0:T(512)S(1)} %get-tuple-element.21), channel_id=1, source_target_pairs={{0,8},{4,12},{8,0},{12,4},{16,24},{20,28},{24,16},{28,20},{1,9},{5... | collective-permute-start | bytes 6152 | tf_op jit(solution)/shard_map/ppermute | solution.py:84
  13.7 1.6 %collective-permute-start.1 = (bf16[2,2048,32]{1,2,0:T(8,128)(2,1)S(1)}, bf16[2,2048,32]{1,2,0:T(8,128)(2,1)S(1)}, u32[]{:S(2)}, u32[]{:S(2)}) collective-permute-start(bf16[2,2048,32]{1,2,0:T(8,128)(2,1)S(1)} %pad_maximum_fusion.2), channel_id=1, source_target_pairs={{0,4},{4,0},{8,12},{12,8},{16,20},{20,16},{24,28},{28,24},{1,5},{5... | collective-permute-start | bytes 786440 | tf_op jit(solution)/shard_map/ppermute | solution.py:67
  15.8 19.3 %copy-start.6 = (s32[512]{0:T(512)S(1)}, s32[512]{0:T(512)}, u32[]{:S(2)}) copy-start(s32[512]{0:T(512)} %param.14) | copy-start | bytes 6148
  17.6 80.6 %collective-permute-start.4 = (bf16[2048,384]{1,0:T(8,128)(2,1)S(1)}, bf16[2048,384]{1,0:T(8,128)(2,1)}, u32[]{:S(2)}, u32[]{:S(2)}) collective-permute-start(bf16[2048,384]{1,0:T(8,128)(2,1)S(1)} %pad_maximum_fusion), channel_id=1, source_target_pairs={{0,3},{1,2},{2,1},{3,0},{4,7},{5,6},{6,5},{7,4},{8,11},{9,10},{10,... | collective-permute-start | bytes 4718600 | tf_op jit(solution)/shard_map/ppermute | solution.py:73
  20.1 81.0 %collective-permute-start.3 = (bf16[2048,384]{1,0:T(8,128)(2,1)S(1)}, bf16[2048,384]{1,0:T(8,128)(2,1)}, u32[]{:S(2)}, u32[]{:S(2)}) collective-permute-start(bf16[2048,384]{1,0:T(8,128)(2,1)S(1)} %pad_maximum_fusion), channel_id=1, source_target_pairs={{0,2},{1,3},{2,0},{3,1},{4,6},{5,7},{6,4},{7,5},{8,10},{9,11},{10,... | collective-permute-start | bytes 4718600 | tf_op jit(solution)/shard_map/ppermute | solution.py:73
  20.6 83.1 %collective-permute-start.2 = (bf16[2048,384]{1,0:T(8,128)(2,1)S(1)}, bf16[2048,384]{1,0:T(8,128)(2,1)}, u32[]{:S(2)}, u32[]{:S(2)}) collective-permute-start(bf16[2048,384]{1,0:T(8,128)(2,1)S(1)} %pad_maximum_fusion), channel_id=1, source_target_pairs={{0,1},{1,0},{2,3},{3,2},{4,5},{5,4},{6,7},{7,6},{8,9},{9,8},{10,11... | collective-permute-start | bytes 4718600 | tf_op jit(solution)/shard_map/ppermute | solution.py:73
  21.2 3.1 %collective-permute-start.7 = (f32[512]{0:T(512)S(1)}, f32[512]{0:T(512)S(1)}, u32[]{:S(2)}, u32[]{:S(2)}) collective-permute-start(f32[512]{0:T(512)S(1)} %get-tuple-element.21), channel_id=1, source_target_pairs={{0,12},{4,8},{8,4},{12,0},{16,28},{20,24},{24,20},{28,16},{1,13},{... | collective-permute-start | bytes 6152 | tf_op jit(solution)/shard_map/ppermute | solution.py:84
  21.3 4.9 %collective-permute-start.8 = (f32[512]{0:T(512)S(1)}, f32[512]{0:T(512)S(1)}, u32[]{:S(2)}, u32[]{:S(2)}) collective-permute-start(f32[512]{0:T(512)S(1)} %get-tuple-element.21), channel_id=1, source_target_pairs={{0,16},{4,20},{8,24},{12,28},{16,0},{20,4},{24,8},{28,12},{1,17},{... | collective-permute-start | bytes 6152 | tf_op jit(solution)/shard_map/ppermute | solution.py:84
  24.3 5.3 %collective-permute-start.9 = (f32[512]{0:T(512)S(1)}, f32[512]{0:T(512)S(1)}, u32[]{:S(2)}, u32[]{:S(2)}) collective-permute-start(f32[512]{0:T(512)S(1)} %get-tuple-element.21), channel_id=1, source_target_pairs={{0,20},{4,16},{8,28},{12,24},{16,4},{20,0},{24,12},{28,8},{1,21},{... | collective-permute-start | bytes 6152 | tf_op jit(solution)/shard_map/ppermute | solution.py:84
  26.2 5.5 %collective-permute-start.10 = (f32[512]{0:T(512)S(1)}, f32[512]{0:T(512)S(1)}, u32[]{:S(2)}, u32[]{:S(2)}) collective-permute-start(f32[512]{0:T(512)S(1)} %get-tuple-element.21), channel_id=1, source_target_pairs={{0,24},{4,28},{8,16},{12,20},{16,8},{20,12},{24,0},{28,4},{1,25},{... | collective-permute-start | bytes 6152 | tf_op jit(solution)/shard_map/ppermute | solution.py:84
  29.6 5.6 %collective-permute-start.11 = (f32[512]{0:T(512)S(1)}, f32[512]{0:T(512)S(1)}, u32[]{:S(2)}, u32[]{:S(2)}) collective-permute-start(f32[512]{0:T(512)S(1)} %get-tuple-element.21), channel_id=1, source_target_pairs={{0,28},{4,24},{8,20},{12,16},{16,12},{20,8},{24,4},{28,0},{1,29},{... | collective-permute-start | bytes 6152 | tf_op jit(solution)/shard_map/ppermute | solution.py:84
  31.7 56.2 %collective-permute-start = (s32[512]{0:T(512)S(1)}, s32[512]{0:T(512)S(1)}, u32[]{:S(2)}, u32[]{:S(2)}) collective-permute-start(s32[512]{0:T(512)S(1)} %broadcast_add_fusion), channel_id=1, source_target_pairs={{0,1},{1,2},{2,3},{4,5},{5,6},{6,7},{8,9},{9,10},{10,11},{12,13},{... | collective-permute-start | bytes 6152 | tf_op jit(solution)/shard_map/ppermute | solution.py:19
  95.7 8.1 %copy-start = (bf16[512,8192]{1,0:T(8,128)(2,1)S(1)}, bf16[512,8192]{1,0:T(8,128)(2,1)}, u32[]{:S(2)}) copy-start(bf16[512,8192]{1,0:T(8,128)(2,1)} %all-gather.2.cloned.1.call-done) | copy-start | bytes 25165828
  103.7 11.0 %copy-start.1 = (bf16[2048,256]{1,0:T(8,128)(2,1)S(1)}, bf16[2048,256]{1,0:T(8,128)(2,1)}, u32[]{:S(2)}) copy-start(bf16[2048,256]{1,0:T(8,128)(2,1)} %param.10) | copy-start | bytes 3145732
  106.4 25.3 %collective-permute-start.12 = (bf16[2,512,64]{1,2,0:T(8,128)(2,1)S(1)}, bf16[2,512,64]{1,2,0:T(8,128)(2,1)S(1)}, u32[]{:S(2)}, u32[]{:S(2)}) collective-permute-start(bf16[2,512,64]{1,2,0:T(8,128)(2,1)S(1)} %pad_maximum_fusion.3), channel_id=1, source_target_pairs={{0,8},{4,12},{8,0},{12,4},{16,24},{20,28},{24,16},{28,20},{1,9},{5... | collective-permute-start | bytes 393224 | tf_op jit(solution)/shard_map/ppermute | solution.py:116
  106.5 25.2 %collective-permute-start.13 = (bf16[2,512,64]{1,2,0:T(8,128)(2,1)S(1)}, bf16[2,512,64]{1,2,0:T(8,128)(2,1)S(1)}, u32[]{:S(2)}, u32[]{:S(2)}) collective-permute-start(bf16[2,512,64]{1,2,0:T(8,128)(2,1)S(1)} %pad_maximum_fusion.3), channel_id=1, source_target_pairs={{0,1},{1,2},{2,3},{4,5},{5,6},{6,7},{8,9},{9,10},{10,11},{12,13},{... | collective-permute-start | bytes 393224 | tf_op jit(solution)/shard_map/ppermute | solution.py:19
  109.9 21.8 %collective-permute-start.14 = (bf16[2,512,64]{1,2,0:T(8,128)(2,1)S(1)}, bf16[2,512,64]{1,2,0:T(8,128)(2,1)S(1)}, u32[]{:S(2)}, u32[]{:S(2)}) collective-permute-start(bf16[2,512,64]{1,2,0:T(8,128)(2,1)S(1)} %pad_maximum_fusion.3), channel_id=1, source_target_pairs={{0,9},{1,10},{2,11},{4,13},{5,14},{6,15},{8,1},{9,2},{10,3},{12,5}... | collective-permute-start | bytes 393224 | tf_op jit(solution)/shard_map/ppermute | solution.py:124
  118.2 11.3 %all-to-all-start = ((bf16[4,16,2,512]{3,1,2,0:T(8,128)(2,1)}), bf16[4,16,2,512]{3,1,2,0:T(8,128)(2,1)S(1)}, u32[]{:S(2)}, u32[]{:S(2)}) async-start(bf16[4,16,2,512]{3,1,2,0:T(8,128)(2,1)} %copy.30), calls=%async_computation | async-start | bytes 262144 | tf_op jit(solution)/shard_map/all_to_all | solution.py:193
Sparse Core Ops, SparseCore 0:
  10.6 84.9 all-gather.1

commit v10 on v8

--- a/solution.py
+++ b/solution.py
@@ -96,13 +96,16 @@
     query_halves, kv_halves, head_halves = [], [], []
     for h in range(halves):
         rows_of = slice(h * half_rows, (h + 1) * half_rows)
-        normed = lax.all_gather(local_normed[rows_of], "gx", axis=1, tiled=True)
+        normed = lax.all_gather(local_normed[rows_of], "gx", axis=0, tiled=False)
+        per_piece = row_block // feature_block
+        normed = normed.reshape(gx_count // per_piece, per_piece, half_rows, feature_block)
         if head_halves:
             normed, head_halves[-1] = lax.optimization_barrier((normed, head_halves[-1]))
         products = None
         for source, block in pieces:
-            rows = lax.dynamic_slice_in_dim(normed, source * row_block, row_block, 1)
-            part = jnp.dot(rows, block, preferred_element_type=jnp.float32)
+            rows = lax.dynamic_index_in_dim(normed, source, 0, keepdims=False)
+            weights_of = block.reshape(per_piece, feature_block, block.shape[1])
+            part = jnp.einsum("btd,bdc->tc", rows, weights_of, preferred_element_type=jnp.float32)
             products = part if products is None else products + part
         projected = products * scaling[rows_of, None]
         places = positions[rows_of]

time: 140 us -> 141 us (level)
  waiting for transfers between devices: 67.7 us -> 63.2 us
  local copies, waits for them, and re-layouts: 7.17 us -> 9.75 us
    ppermute x2, waiting for transfers between devices: 55.1 us -> 51.4 us  [shifted(): return lax.ppermute(value, axis, pairs)]
  transfers between devices with their start and end apart: 17 -> 17, of which waited for: 7 -> 6; matrix products, arithmetic and copies ran while one was open for 14% -> 16% of each run, Pallas kernels for 0% -> 0%
where the time goes in v10:
time: 141 us; the launch traced here: 140 us
  waiting for transfers between devices  63.2 us (45%)
  starting transfers between devices  28.5 us (20%)
  between operations  14.6 us (10%)
  matrix products  13.7 us (10%)
  other arithmetic  10.5 us (7%)
  local copies, waits for them, and re-layouts  9.75 us (7%)
    ppermute x2, waiting for transfers between devices, shifted(): return lax.ppermute(value, axis, pairs)  51.4 us
    dot_general x4, matrix products, shards(): jnp.einsum('btd,bdc->tc', rows, weights_of, preferred_element_type=jnp.fl...  11 us
    ppermute x7, starting transfers between devices, shards(): lax.ppermute(local_squares, 'gx', partner_route(gx_count, gx_count, k))  9.4 us
    ppermute x2, starting transfers between devices, shifted(): return lax.ppermute(value, axis, pairs)  6.78 us
    ppermute x7, waiting for transfers between devices, shards(): lax.ppermute(local_squares, 'gx', partner_route(gx_count, gx_count, k))  4.81 us
    ppermute x1, starting transfers between devices, shards(): other = lax.ppermute(half_kv, ('gx', 'gy'), route)  4.8 us
    all_gather x1, waiting for transfers between devices, shards(): normed = lax.all_gather(local_normed[rows_of], 'gx', axis=0, tiled=False)  4.52 us
    ppermute x3, starting transfers between devices, shards(): lax.ppermute(local_weights, 'gy', partner_route(gy_count, gy_count, k))  3.7 us
  transfers between devices with their start and end apart: 17, of which 6 were waited for; matrix products, arithmetic and copies ran while one was open for 16% of the time, Pallas kernels for 0%

profile of v10, /device:TPU:0, one launch (start us, length us, event | category | flops | bytes accessed | tf_op | source)
XLA Modules:
  0.0 140.2 jit_solution(9098048920851550044)
XLA Ops:
  7.3 0.7 dynamic-slice_convert_fusion
  8.0 2.5 %fusion.4 = (f32[512]{0:T(512)S(1)}, bf16[512,1024]{1,0:T(8,128)(2,1)}) fusion(bf16[512,1024]{1,0:T(8,128)(2,1)} %param.8, f32[1024]{0:T(1024)S(1)} %dynamic-slice_convert_fusion), kind=kLoop, calls=%fused_computation.11 | loop fusion | flops 2620928 | bytes 2103296 | tf_op jit(solution)/shard_map/reduce_sum | solution.py:81
  10.5 0.5 collective-permute-start.5
  11.1 2.6 %collective-permute-start.6 = (f32[512]{0:T(512)S(1)}, f32[512]{0:T(512)S(1)}, u32[]{:S(2)}, u32[]{:S(2)}) collective-permute-start(f32[512]{0:T(512)S(1)} %get-tuple-element.9), channel_id=1, source_target_pairs={{0,8},{4,12},{8,0},{12,4},{16,24},{20,28},{24,16},{28,20},{1,9},{5... | collective-permute-start | bytes 6152 | tf_op jit(solution)/shard_map/ppermute | solution.py:84
  13.8 0.2 collective-permute-start.1
  14.2 0.2 select_reduce_fusion
  14.4 0.5 copy.32
  15.0 0.5 collective-permute-done.1
  15.4 0.5 copy.33
  15.9 1.2 maximum_select_fusion
  17.1 0.3 fusion.98
  17.4 0.9 copy-done
  18.3 1.5 %pad_maximum_fusion = bf16[2048,384]{1,0:T(8,128)(2,1)} fusion(bf16[2048,64]{1,0:T(8,128)(2,1)S(1)} %get-tuple-element.13, bf16[2048,64]{1,0:T(8,128)(2,1)S(1)} %get-tuple-element.12, bf16[2048,256]{1,0:T(8,128)(2,1)S(1)} %copy-done), kind=kLoop, calls=%fused_computation.31 | loop fusion | flops 4718592 | bytes 3145728 | tf_op jit(solution)/shard_map/concatenate | solution.py:69
  19.9 2.6 %collective-permute-start.4 = (bf16[2048,384]{1,0:T(8,128)(2,1)}, bf16[2048,384]{1,0:T(8,128)(2,1)}, u32[]{:S(2)}, u32[]{:S(2)}) collective-permute-start(bf16[2048,384]{1,0:T(8,128)(2,1)} %pad_maximum_fusion), channel_id=1, source_target_pairs={{0,3},{1,2},{2,1},{3,0},{4,7},{5,6},{6,5},{7,4},{8,11},{9,10},{10,... | collective-permute-start | bytes 4718600 | tf_op jit(solution)/shard_map/ppermute | solution.py:73
  22.5 0.6 collective-permute-start.2
  23.1 2.7 %collective-permute-start.8 = (f32[512]{0:T(512)S(1)}, f32[512]{0:T(512)S(1)}, u32[]{:S(2)}, u32[]{:S(2)}) collective-permute-start(f32[512]{0:T(512)S(1)} %get-tuple-element.9), channel_id=1, source_target_pairs={{0,16},{4,20},{8,24},{12,28},{16,0},{20,4},{24,8},{28,12},{1,17},{... | collective-permute-start | bytes 6152 | tf_op jit(solution)/shard_map/ppermute | solution.py:84
  25.7 0.5 collective-permute-start.3
  26.3 2.8 %collective-permute-done.8 = f32[512]{0:T(512)S(1)} collective-permute-done((f32[512]{0:T(512)S(1)}, f32[512]{0:T(512)S(1)}, u32[]{:S(2)}, u32[]{:S(2)}) %collective-permute-start.8) | collective-permute-done | bytes 2080 | tf_op jit(solution)/shard_map/ppermute | solution.py:84
  29.1 2.2 %collective-permute-start.10 = (f32[512]{0:T(512)S(1)}, f32[512]{0:T(512)S(1)}, u32[]{:S(2)}, u32[]{:S(2)}) collective-permute-start(f32[512]{0:T(512)S(1)} %get-tuple-element.9), channel_id=1, source_target_pairs={{0,24},{4,28},{8,16},{12,20},{16,8},{20,12},{24,0},{28,4},{1,25},{... | collective-permute-start | bytes 6152 | tf_op jit(solution)/shard_map/ppermute | solution.py:84
  31.3 1.2 collective-permute-start.11
  32.6 2.0 %collective-permute-done.10 = f32[512]{0:T(512)S(1)} collective-permute-done((f32[512]{0:T(512)S(1)}, f32[512]{0:T(512)S(1)}, u32[]{:S(2)}, u32[]{:S(2)}) %collective-permute-start.10) | collective-permute-done | bytes 2080 | tf_op jit(solution)/shard_map/ppermute | solution.py:84
  34.6 3.4 %collective-permute-start = (s32[512]{0:T(512)S(1)}, s32[512]{0:T(512)S(1)}, u32[]{:S(2)}, u32[]{:S(2)}) collective-permute-start(s32[512]{0:T(512)S(1)} %broadcast_add_fusion), channel_id=1, source_target_pairs={{0,1},{1,2},{2,3},{4,5},{5,6},{6,7},{8,9},{9,10},{10,11},{12,13},{... | collective-permute-start | bytes 6152 | tf_op jit(solution)/shard_map/ppermute | solution.py:19
  38.0 0.5 copy.38
  38.7 0.6 gather_fusion
  39.3 51.4 %collective-permute-done = s32[512]{0:T(512)S(1)} collective-permute-done((s32[512]{0:T(512)S(1)}, s32[512]{0:T(512)S(1)}, u32[]{:S(2)}, u32[]{:S(2)}) %collective-permute-start) | collective-permute-done | bytes 2080 | tf_op jit(solution)/shard_map/ppermute | solution.py:19
  90.8 0.2 copy.39
  91.0 0.2 copy.40
  91.2 4.5 %all-gather.3.cloned.1.call-done = bf16[4096,1024]{1,0:T(8,128)(2,1)} async-done(((bf16[512,1024]{1,0:T(8,128)(2,1)}), bf16[4096,1024]{1,0:T(8,128)(2,1)}) %all-gather.3.cloned.1.call-update) | async-done | bytes 8388624 | tf_op jit(solution)/shard_map/all_gather | solution.py:99
  95.8 2.8 %fusion.25 = f32[512,384]{0,1:T(8,128)S(1)} fusion(bf16[2,1024,64]{1,2,0:T(8,128)(2,1)S(1)} %copy.40, bf16[2,1024,64]{1,2,0:T(8,128)(2,1)S(1)} %copy.39, bf16[2,1024,256]{1,2,0:T(8,128)(2,1)S(1)} %copy.38, bf16[4,2,512,1024]{3,2,1,0:T(8,128)(2,1)} %bitcast.142, s32[]{:T(128)S(6)} %select_n.157), kind=kOutput, calls=%fused_computation.32 | convolution fusion | flops 810024960 | bytes 4456452 | tf_op jit(solution)/shard_map/btd,bdc->tc/dot_general | solution.py:108
  98.6 3.2 %fusion.36 = f32[512,384]{0,1:T(8,128)S(1)} fusion(bf16[2,1024,384]{2,1,0:T(8,128)(2,1)} %bitcast.17, bf16[4,2,512,1024]{3,2,1,0:T(8,128)(2,1)} %bitcast.143, s32[]{:T(128)S(6)} %select_n.164), kind=kOutput, calls=%fused_computation.35 | convolution fusion | flops 805306368 | bytes 4456452 | tf_op jit(solution)/shard_map/btd,bdc->tc/dot_general | solution.py:108
  101.9 2.5 %fusion.42 = f32[512,384]{0,1:T(8,128)S(1)} fusion(f32[512,384]{0,1:T(8,128)S(1)} %fusion.25, bf16[2,1024,384]{2,1,0:T(8,128)(2,1)} %bitcast.11, bf16[4,2,512,1024]{3,2,1,0:T(8,128)(2,1)S(1)} %bitcast.144, s32[]{:T(128)S(6)} %select_n.162), kind=kOutput, calls=%fused_computation.37 | convolution fusion | flops 805502976 | bytes 5242884 | tf_op jit(solution)/shard_map/btd,bdc->tc/dot_general | solution.py:108
  104.3 2.5 %fusion.48 = f32[512,384]{0,1:T(8,128)S(1)} fusion(f32[512,384]{0,1:T(8,128)S(1)} %fusion.36, f32[512,384]{0,1:T(8,128)S(1)} %fusion.42, bf16[2,1024,384]{2,1,0:T(8,128)(2,1)} %bitcast.14, bf16[4,2,512,1024]{3,2,1,0:T(8,128)(2,1)S(1)} %bitcast.145, s32[]{:T(128)S(6)} %select_n.163, f32[512]{0:T(512)S(1)} %add_rsqrt_fusion), kind=kOutput, calls=%fused_computation.39 | convolution fusion | flops 805896192 | bytes 6031364 | tf_op jit(solution)/shard_map/btd,bdc->tc/dot_general | solution.py:108
  106.9 0.6 fusion.85
  107.6 3.4 %collective-permute-start.12 = (bf16[2,512,64]{1,2,0:T(8,128)(2,1)S(1)}, bf16[2,512,64]{1,2,0:T(8,128)(2,1)S(1)}, u32[]{:S(2)}, u32[]{:S(2)}) collective-permute-start(bf16[2,512,64]{1,2,0:T(8,128)(2,1)S(1)} %pad_maximum_fusion.3), channel_id=1, source_target_pairs={{0,1},{1,2},{2,3},{4,5},{5,6},{6,7},{8,9},{9,10},{10,11},{12,13},{... | collective-permute-start | bytes 393224 | tf_op jit(solution)/shard_map/ppermute | solution.py:19
  111.0 4.8 %collective-permute-start.13 = (bf16[2,512,64]{1,2,0:T(8,128)(2,1)S(1)}, bf16[2,512,64]{1,2,0:T(8,128)(2,1)S(1)}, u32[]{:S(2)}, u32[]{:S(2)}) collective-permute-start(bf16[2,512,64]{1,2,0:T(8,128)(2,1)S(1)} %pad_maximum_fusion.3), channel_id=1, source_target_pairs={{0,9},{1,10},{2,11},{4,13},{5,14},{6,15},{8,1},{9,2},{10,3},{12,5}... | collective-permute-start | bytes 393224 | tf_op jit(solution)/shard_map/ppermute | solution.py:133
  116.1 0.2 reshape.202
  116.5 1.5 %scatter_fusion = bf16[64,2,512]{2,1,0:T(2,128)(2,1)S(1)} fusion(bf16[64,2,512]{2,1,0:T(2,128)(2,1)S(1)} %broadcast_in_dim.68, s32[32]{0:T(128)S(1)} %fusion.94, bf16[32,2,512]{2,1,0:T(2,128)(2,1)S(1)} %copy.47), kind=kCustom, calls=%fused_computation.1 | custom fusion | bytes 196736 | tf_op jit(solution)/shard_map/scatter | solution.py:187
  118.0 0.7 copy.48
  118.7 3.5 %all-to-all-start = ((bf16[4,16,2,512]{3,1,2,0:T(8,128)(2,1)}), bf16[4,16,2,512]{3,1,2,0:T(8,128)(2,1)S(1)}, u32[]{:S(2)}, u32[]{:S(2)}) async-start(bf16[4,16,2,512]{3,1,2,0:T(8,128)(2,1)} %copy.48), calls=%async_computation | async-start | bytes 262144 | tf_op jit(solution)/shard_map/all_to_all | solution.py:190
  122.2 2.6 %fusion.64 = bf16[512,256]{0,1:T(8,128)(2,1)S(1)} fusion(f32[512,384]{0,1:T(8,128)S(1)} %fusion.48, f32[512,1]{0,1:T(1,128)S(1)} %get-tuple-element.20, f32[512,255]{0,1:T(8,128)S(1)} %get-tuple-element.22, f32[512,255]{0,1:T(8,128)S(1)} %get-tuple-element.21, f32[512,1]{0,1:T(1,128)S(1)} %get-tuple-element.19, f32[256]{0:T(256)S(1)} %multiply_power_fusion, ...), kind=kLoop, calls=%fused_computation.50 | loop fusion | flops 1310720 | bytes 1838336 | tf_op jit(solution)/shard_map/convert_element_type | solution.py:119
  125.0 2.0 %all-to-all-done = bf16[4,16,2,512]{3,1,2,0:T(8,128)(2,1)S(1)} async-done(((bf16[4,16,2,512]{3,1,2,0:T(8,128)(2,1)}), bf16[4,16,2,512]{3,1,2,0:T(8,128)(2,1)S(1)}, u32[]{:S(2)}, u32[]{:S(2)}) %all-to-all-start) | async-done | bytes 131104 | tf_op jit(solution)/shard_map/all_to_all | solution.py:190
  127.0 0.3 reshape.204
  127.3 0.9 copy.50
  128.3 0.9 copy.51
  129.3 1.8 %fusion.102 = (f32[1024]{0:T(1024)S(1)}, f32[1024,1024]{0,1:T(8,128)S(1)}) fusion(bf16[1024,128]{1,0:T(8,128)(2,1)S(1)} %bitcast.125, bf16[2,512,128]{1,2,0:T(8,128)(2,1)S(1)} %maximum_select_fusion.1, bf16[2,512,128]{1,2,0:T(8,128)(2,1)S(1)} %maximum_select_fusion.2, s32[1024]{0:T(1024)S(1)} %bitcast.132, pred[1024]{0:T(1024)(128)(4,1)S(1)} %broadcast_compare_fusion, ...), kind=kOutput, calls=%fused_computation.132 | convolution fusion | flops 276298752 | bytes 4998144 | tf_op jit(solution)/shard_map/dot_general | solution.py:151
  131.1 0.6 fusion.1
  131.7 0.9 fusion.57
  132.6 0.7 copy.63
  (68 shorter events, 1.6 us)
Async XLA Ops:
  7.2 6.6 %copy-start.2 = (bf16[2048,32]{0,1:T(8,128)(2,1)S(1)}, bf16[2048,32]{0,1:T(8,128)(2,1)}, u32[]{:S(2)}) copy-start(bf16[2048,32]{0,1:T(8,128)(2,1)} %param.11) | copy-start | bytes 393220
  7.2 6.6 %copy-start.1 = (bf16[2048,32]{0,1:T(8,128)(2,1)S(1)}, bf16[2048,32]{0,1:T(8,128)(2,1)}, u32[]{:S(2)}) copy-start(bf16[2048,32]{0,1:T(8,128)(2,1)} %param.12) | copy-start | bytes 393220
  7.2 6.8 %copy-start.4 = (s32[32,1]{0,1:T(1,128)S(1)}, s32[32,1]{0,1:T(1,128)}, u32[]{:S(2)}) copy-start(s32[32,1]{0,1:T(1,128)} %param.15) | copy-start | bytes 388
  7.2 7.2 %copy-start.3 = (s32[512]{0:T(512)S(1)}, s32[512]{0:T(512)}, u32[]{:S(2)}) copy-start(s32[512]{0:T(512)} %param.13) | copy-start | bytes 6148
  7.2 88.6 %all-gather.3.cloned.1.call-start = ((), (), s32[]{:S(2)}) async-start(), calls=%async_computation.1 | async-start | bytes 9437184 | tf_op jit(solution)/shard_map/all_gather | solution.py:99
  10.5 12.5 %collective-permute-start.5 = (f32[512]{0:T(512)S(1)}, f32[512]{0:T(512)S(1)}, u32[]{:S(2)}, u32[]{:S(2)}) collective-permute-start(f32[512]{0:T(512)S(1)} %get-tuple-element.9), channel_id=1, source_target_pairs={{0,4},{4,0},{8,12},{12,8},{16,20},{20,16},{24,28},{28,24},{1,5},{5... | collective-permute-start | bytes 6152 | tf_op jit(solution)/shard_map/ppermute | solution.py:84
  11.1 14.7 %collective-permute-start.6 = (f32[512]{0:T(512)S(1)}, f32[512]{0:T(512)S(1)}, u32[]{:S(2)}, u32[]{:S(2)}) collective-permute-start(f32[512]{0:T(512)S(1)} %get-tuple-element.9), channel_id=1, source_target_pairs={{0,8},{4,12},{8,0},{12,4},{16,24},{20,28},{24,16},{28,20},{1,9},{5... | collective-permute-start | bytes 6152 | tf_op jit(solution)/shard_map/ppermute | solution.py:84
  13.7 12.6 %collective-permute-start.7 = (f32[512]{0:T(512)S(1)}, f32[512]{0:T(512)S(1)}, u32[]{:S(2)}, u32[]{:S(2)}) collective-permute-start(f32[512]{0:T(512)S(1)} %get-tuple-element.9), channel_id=1, source_target_pairs={{0,12},{4,8},{8,4},{12,0},{16,28},{20,24},{24,20},{28,16},{1,13},{... | collective-permute-start | bytes 6152 | tf_op jit(solution)/shard_map/ppermute | solution.py:84
  13.8 1.6 %collective-permute-start.1 = (bf16[2,2048,32]{1,2,0:T(8,128)(2,1)S(1)}, bf16[2,2048,32]{1,2,0:T(8,128)(2,1)S(1)}, u32[]{:S(2)}, u32[]{:S(2)}) collective-permute-start(bf16[2,2048,32]{1,2,0:T(8,128)(2,1)S(1)} %pad_maximum_fusion.2), channel_id=1, source_target_pairs={{0,4},{4,0},{8,12},{12,8},{16,20},{20,16},{24,28},{28,24},{1,5},{5... | collective-permute-start | bytes 786440 | tf_op jit(solution)/shard_map/ppermute | solution.py:67
  17.1 1.2 copy-start
  18.3 20.2 %copy-start.5 = (s32[512]{0:T(512)S(1)}, s32[512]{0:T(512)}, u32[]{:S(2)}) copy-start(s32[512]{0:T(512)} %param.14) | copy-start | bytes 6148
  19.9 78.8 %collective-permute-start.4 = (bf16[2048,384]{1,0:T(8,128)(2,1)}, bf16[2048,384]{1,0:T(8,128)(2,1)}, u32[]{:S(2)}, u32[]{:S(2)}) collective-permute-start(bf16[2048,384]{1,0:T(8,128)(2,1)} %pad_maximum_fusion), channel_id=1, source_target_pairs={{0,3},{1,2},{2,1},{3,0},{4,7},{5,6},{6,5},{7,4},{8,11},{9,10},{10,... | collective-permute-start | bytes 4718600 | tf_op jit(solution)/shard_map/ppermute | solution.py:73
  22.5 79.4 %collective-permute-start.2 = (bf16[2048,384]{1,0:T(8,128)(2,1)}, bf16[2048,384]{1,0:T(8,128)(2,1)}, u32[]{:S(2)}, u32[]{:S(2)}) collective-permute-start(bf16[2048,384]{1,0:T(8,128)(2,1)} %pad_maximum_fusion), channel_id=1, source_target_pairs={{0,1},{1,0},{2,3},{3,2},{4,5},{5,4},{6,7},{7,6},{8,9},{9,8},{10,11... | collective-permute-start | bytes 4718600 | tf_op jit(solution)/shard_map/ppermute | solution.py:73
  23.1 6.0 %collective-permute-start.8 = (f32[512]{0:T(512)S(1)}, f32[512]{0:T(512)S(1)}, u32[]{:S(2)}, u32[]{:S(2)}) collective-permute-start(f32[512]{0:T(512)S(1)} %get-tuple-element.9), channel_id=1, source_target_pairs={{0,16},{4,20},{8,24},{12,28},{16,0},{20,4},{24,8},{28,12},{1,17},{... | collective-permute-start | bytes 6152 | tf_op jit(solution)/shard_map/ppermute | solution.py:84
  25.7 78.6 %collective-permute-start.3 = (bf16[2048,384]{1,0:T(8,128)(2,1)}, bf16[2048,384]{1,0:T(8,128)(2,1)}, u32[]{:S(2)}, u32[]{:S(2)}) collective-permute-start(bf16[2048,384]{1,0:T(8,128)(2,1)} %pad_maximum_fusion), channel_id=1, source_target_pairs={{0,2},{1,3},{2,0},{3,1},{4,6},{5,7},{6,4},{7,5},{8,10},{9,11},{10,... | collective-permute-start | bytes 4718600 | tf_op jit(solution)/shard_map/ppermute | solution.py:73
  26.3 5.1 %collective-permute-start.9 = (f32[512]{0:T(512)S(1)}, f32[512]{0:T(512)S(1)}, u32[]{:S(2)}, u32[]{:S(2)}) collective-permute-start(f32[512]{0:T(512)S(1)} %get-tuple-element.9), channel_id=1, source_target_pairs={{0,20},{4,16},{8,28},{12,24},{16,4},{20,0},{24,12},{28,8},{1,21},{... | collective-permute-start | bytes 6152 | tf_op jit(solution)/shard_map/ppermute | solution.py:84
  29.1 5.5 %collective-permute-start.10 = (f32[512]{0:T(512)S(1)}, f32[512]{0:T(512)S(1)}, u32[]{:S(2)}, u32[]{:S(2)}) collective-permute-start(f32[512]{0:T(512)S(1)} %get-tuple-element.9), channel_id=1, source_target_pairs={{0,24},{4,28},{8,16},{12,20},{16,8},{20,12},{24,0},{28,4},{1,25},{... | collective-permute-start | bytes 6152 | tf_op jit(solution)/shard_map/ppermute | solution.py:84
  31.3 7.3 %collective-permute-start.11 = (f32[512]{0:T(512)S(1)}, f32[512]{0:T(512)S(1)}, u32[]{:S(2)}, u32[]{:S(2)}) collective-permute-start(f32[512]{0:T(512)S(1)} %get-tuple-element.9), channel_id=1, source_target_pairs={{0,28},{4,24},{8,20},{12,16},{16,12},{20,8},{24,4},{28,0},{1,29},{... | collective-permute-start | bytes 6152 | tf_op jit(solution)/shard_map/ppermute | solution.py:84
  34.6 56.1 %collective-permute-start = (s32[512]{0:T(512)S(1)}, s32[512]{0:T(512)S(1)}, u32[]{:S(2)}, u32[]{:S(2)}) collective-permute-start(s32[512]{0:T(512)S(1)} %broadcast_add_fusion), channel_id=1, source_target_pairs={{0,1},{1,2},{2,3},{4,5},{5,6},{6,7},{8,9},{9,10},{10,11},{12,13},{... | collective-permute-start | bytes 6152 | tf_op jit(solution)/shard_map/ppermute | solution.py:19
  95.8 6.1 %copy-start.6 = (bf16[4096,1024]{1,0:T(8,128)(2,1)S(1)}, bf16[4096,1024]{1,0:T(8,128)(2,1)}, u32[]{:S(2)}) copy-start(bf16[4096,1024]{1,0:T(8,128)(2,1)} %all-gather.3.cloned.1.call-done) | copy-start | bytes 25165828
  107.5 21.7 %collective-permute-start.14 = (bf16[2,512,64]{1,2,0:T(8,128)(2,1)S(1)}, bf16[2,512,64]{1,2,0:T(8,128)(2,1)S(1)}, u32[]{:S(2)}, u32[]{:S(2)}) collective-permute-start(bf16[2,512,64]{1,2,0:T(8,128)(2,1)S(1)} %pad_maximum_fusion.3), channel_id=1, source_target_pairs={{0,8},{4,12},{8,0},{12,4},{16,24},{20,28},{24,16},{28,20},{1,9},{5... | collective-permute-start | bytes 393224 | tf_op jit(solution)/shard_map/ppermute | solution.py:124
  107.6 21.7 %collective-permute-start.12 = (bf16[2,512,64]{1,2,0:T(8,128)(2,1)S(1)}, bf16[2,512,64]{1,2,0:T(8,128)(2,1)S(1)}, u32[]{:S(2)}, u32[]{:S(2)}) collective-permute-start(bf16[2,512,64]{1,2,0:T(8,128)(2,1)S(1)} %pad_maximum_fusion.3), channel_id=1, source_target_pairs={{0,1},{1,2},{2,3},{4,5},{5,6},{6,7},{8,9},{9,10},{10,11},{12,13},{... | collective-permute-start | bytes 393224 | tf_op jit(solution)/shard_map/ppermute | solution.py:19
  111.0 18.3 %collective-permute-start.13 = (bf16[2,512,64]{1,2,0:T(8,128)(2,1)S(1)}, bf16[2,512,64]{1,2,0:T(8,128)(2,1)S(1)}, u32[]{:S(2)}, u32[]{:S(2)}) collective-permute-start(bf16[2,512,64]{1,2,0:T(8,128)(2,1)S(1)} %pad_maximum_fusion.3), channel_id=1, source_target_pairs={{0,9},{1,10},{2,11},{4,13},{5,14},{6,15},{8,1},{9,2},{10,3},{12,5}... | collective-permute-start | bytes 393224 | tf_op jit(solution)/shard_map/ppermute | solution.py:133
  118.7 8.3 %all-to-all-start = ((bf16[4,16,2,512]{3,1,2,0:T(8,128)(2,1)}), bf16[4,16,2,512]{3,1,2,0:T(8,128)(2,1)S(1)}, u32[]{:S(2)}, u32[]{:S(2)}) async-start(bf16[4,16,2,512]{3,1,2,0:T(8,128)(2,1)} %copy.48), calls=%async_computation | async-start | bytes 262144 | tf_op jit(solution)/shard_map/all_to_all | solution.py:190
Sparse Core Ops, SparseCore 0:
  10.7 85.0 all-gather.2

commit v11 on v10

--- a/solution.py
+++ b/solution.py
@@ -78,6 +78,7 @@
     feature_block = tokens_in.shape[1]
     local_gain = lax.dynamic_slice_in_dim(norm_gain, my_gx * feature_block, feature_block, 0)
     local_normed = (local_float * local_gain.astype(jnp.float32)[None, :]).astype(jnp.bfloat16)
+    local_normed, local_float = lax.optimization_barrier((local_normed, local_float))
     local_squares = jnp.sum(local_float * local_float, axis=1)
     square_parts = [local_squares]
     for k in range(1, gx_count):

time: 141 us -> 141 us (level)
    convert_element_type x0 -> x2, other arithmetic: none -> 2.76 us  [the longest x1 1.54 us: shards(): local_float = tokens_in.astype(jnp.float32)]
    reduce_sum x1, other arithmetic: 2.5 us -> 0.21 us  [shards(): local_squares = jnp.sum(local_float * local_float, axis=1)]
where the time goes in v11:
time: 141 us; the launch traced here: 140 us
  waiting for transfers between devices  63 us (45%)
  starting transfers between devices  28.5 us (20%)
  between operations  14.6 us (10%)
  matrix products  13.7 us (10%)
  other arithmetic  10.9 us (8%)
  local copies, waits for them, and re-layouts  9.77 us (7%)
    ppermute x2, waiting for transfers between devices, shifted(): return lax.ppermute(value, axis, pairs)  51.6 us
    dot_general x4, matrix products, shards(): jnp.einsum('btd,bdc->tc', rows, weights_of, preferred_element_type=jnp.fl...  11 us
    ppermute x7, starting transfers between devices, shards(): lax.ppermute(local_squares, 'gx', partner_route(gx_count, gx_count, k))  9.39 us
    ppermute x2, starting transfers between devices, shifted(): return lax.ppermute(value, axis, pairs)  6.78 us
    ppermute x1, starting transfers between devices, shards(): other = lax.ppermute(half_kv, ('gx', 'gy'), route)  4.79 us
    ppermute x7, waiting for transfers between devices, shards(): lax.ppermute(local_squares, 'gx', partner_route(gx_count, gx_count, k))  4.6 us
    all_gather x1, waiting for transfers between devices, shards(): normed = lax.all_gather(local_normed[rows_of], 'gx', axis=0, tiled=False)  4.32 us
    ppermute x3, starting transfers between devices, shards(): lax.ppermute(local_weights, 'gy', partner_route(gy_count, gy_count, k))  3.7 us
  transfers between devices with their start and end apart: 17, of which 6 were waited for; matrix products, arithmetic and copies ran while one was open for 16% of the time, Pallas kernels for 0%

profile of v11, /device:TPU:0, one launch (start us, length us, event | category | flops | bytes accessed | tf_op | source)
XLA Modules:
  0.0 140.4 jit_solution(7090310521009069844)
XLA Ops:
  7.2 1.5 %convert_element_type.52 = f32[512,1024]{1,0:T(8,128)S(1)} convert(bf16[512,1024]{1,0:T(8,128)(2,1)} %param.8) | non-fusion elementwise | flops 524288 | bytes 3145728 | tf_op jit(solution)/shard_map/convert_element_type | solution.py:76
  8.8 0.7 dynamic-slice_convert_fusion
  9.5 1.2 multiply_convert_fusion
  10.7 0.2 multiply_reduce_fusion
  10.9 0.5 collective-permute-start.5
  11.4 2.6 %collective-permute-start.6 = (f32[512]{0:T(512)S(1)}, f32[512]{0:T(512)S(1)}, u32[]{:S(2)}, u32[]{:S(2)}) collective-permute-start(f32[512]{0:T(512)S(1)} %multiply_reduce_fusion), channel_id=1, source_target_pairs={{0,8},{4,12},{8,0},{12,4},{16,24},{20,28},{24,16},{28,20},{1,9},{5... | collective-permute-start | bytes 6152 | tf_op jit(solution)/shard_map/ppermute | solution.py:85
  14.2 0.2 collective-permute-start.1
  14.8 0.5 copy.32
  15.4 0.5 collective-permute-done.1
  15.8 0.5 copy.33
  16.3 1.2 maximum_select_fusion
  17.5 0.3 fusion.96
  17.8 0.9 copy-done.1
  18.7 1.5 %pad_maximum_fusion = bf16[2048,384]{1,0:T(8,128)(2,1)} fusion(bf16[2048,64]{1,0:T(8,128)(2,1)S(1)} %get-tuple-element.15, bf16[2048,64]{1,0:T(8,128)(2,1)S(1)} %get-tuple-element.14, bf16[2048,256]{1,0:T(8,128)(2,1)S(1)} %copy-done.1), kind=kLoop, calls=%fused_computation.29 | loop fusion | flops 4718592 | bytes 3145728 | tf_op jit(solution)/shard_map/concatenate | solution.py:69
  20.2 2.6 %collective-permute-start.4 = (bf16[2048,384]{1,0:T(8,128)(2,1)}, bf16[2048,384]{1,0:T(8,128)(2,1)}, u32[]{:S(2)}, u32[]{:S(2)}) collective-permute-start(bf16[2048,384]{1,0:T(8,128)(2,1)} %pad_maximum_fusion), channel_id=1, source_target_pairs={{0,3},{1,2},{2,1},{3,0},{4,7},{5,6},{6,5},{7,4},{8,11},{9,10},{10,... | collective-permute-start | bytes 4718600 | tf_op jit(solution)/shard_map/ppermute | solution.py:73
  22.9 0.6 collective-permute-start.2
  23.5 2.7 %collective-permute-start.8 = (f32[512]{0:T(512)S(1)}, f32[512]{0:T(512)S(1)}, u32[]{:S(2)}, u32[]{:S(2)}) collective-permute-start(f32[512]{0:T(512)S(1)} %multiply_reduce_fusion), channel_id=1, source_target_pairs={{0,16},{4,20},{8,24},{12,28},{16,0},{20,4},{24,8},{28,12},{1,17},{... | collective-permute-start | bytes 6152 | tf_op jit(solution)/shard_map/ppermute | solution.py:85
  26.1 0.5 collective-permute-start.3
  26.7 2.6 %collective-permute-done.8 = f32[512]{0:T(512)S(1)} collective-permute-done((f32[512]{0:T(512)S(1)}, f32[512]{0:T(512)S(1)}, u32[]{:S(2)}, u32[]{:S(2)}) %collective-permute-start.8) | collective-permute-done | bytes 2080 | tf_op jit(solution)/shard_map/ppermute | solution.py:85
  29.3 2.4 %collective-permute-start.10 = (f32[512]{0:T(512)S(1)}, f32[512]{0:T(512)S(1)}, u32[]{:S(2)}, u32[]{:S(2)}) collective-permute-start(f32[512]{0:T(512)S(1)} %multiply_reduce_fusion), channel_id=1, source_target_pairs={{0,24},{4,28},{8,16},{12,20},{16,8},{20,12},{24,0},{28,4},{1,25},{... | collective-permute-start | bytes 6152 | tf_op jit(solution)/shard_map/ppermute | solution.py:85
  31.7 1.0 collective-permute-start.11
  32.8 2.0 %collective-permute-done.10 = f32[512]{0:T(512)S(1)} collective-permute-done((f32[512]{0:T(512)S(1)}, f32[512]{0:T(512)S(1)}, u32[]{:S(2)}, u32[]{:S(2)}) %collective-permute-start.10) | collective-permute-done | bytes 2080 | tf_op jit(solution)/shard_map/ppermute | solution.py:85
  34.8 3.4 %collective-permute-start = (s32[512]{0:T(512)S(1)}, s32[512]{0:T(512)S(1)}, u32[]{:S(2)}, u32[]{:S(2)}) collective-permute-start(s32[512]{0:T(512)S(1)} %broadcast_add_fusion), channel_id=1, source_target_pairs={{0,1},{1,2},{2,3},{4,5},{5,6},{6,7},{8,9},{9,10},{10,11},{12,13},{... | collective-permute-start | bytes 6152 | tf_op jit(solution)/shard_map/ppermute | solution.py:19
  38.2 0.5 copy.38
  38.9 0.6 gather_fusion
  39.5 51.6 %collective-permute-done = s32[512]{0:T(512)S(1)} collective-permute-done((s32[512]{0:T(512)S(1)}, s32[512]{0:T(512)S(1)}, u32[]{:S(2)}, u32[]{:S(2)}) %collective-permute-start) | collective-permute-done | bytes 2080 | tf_op jit(solution)/shard_map/ppermute | solution.py:19
  91.2 0.2 copy.39
  91.6 4.3 %all-gather.3.cloned.1.call-done = bf16[4096,1024]{1,0:T(8,128)(2,1)} async-done(((bf16[512,1024]{1,0:T(8,128)(2,1)}), bf16[4096,1024]{1,0:T(8,128)(2,1)}) %all-gather.3.cloned.1.call-update) | async-done | bytes 8388624 | tf_op jit(solution)/shard_map/all_gather | solution.py:100
  95.9 2.8 %fusion.23 = f32[512,384]{0,1:T(8,128)S(1)} fusion(bf16[2,1024,64]{1,2,0:T(8,128)(2,1)S(1)} %copy.40, bf16[2,1024,64]{1,2,0:T(8,128)(2,1)S(1)} %copy.39, bf16[2,1024,256]{1,2,0:T(8,128)(2,1)S(1)} %copy.38, bf16[4,2,512,1024]{3,2,1,0:T(8,128)(2,1)} %bitcast.142, s32[]{:T(128)S(6)} %select_n.157), kind=kOutput, calls=%fused_computation.30 | convolution fusion | flops 810024960 | bytes 4456452 | tf_op jit(solution)/shard_map/btd,bdc->tc/dot_general | solution.py:109
  98.8 3.2 %fusion.34 = f32[512,384]{0,1:T(8,128)S(1)} fusion(bf16[2,1024,384]{2,1,0:T(8,128)(2,1)} %bitcast.17, bf16[4,2,512,1024]{3,2,1,0:T(8,128)(2,1)} %bitcast.143, s32[]{:T(128)S(6)} %select_n.164), kind=kOutput, calls=%fused_computation.33 | convolution fusion | flops 805306368 | bytes 4456452 | tf_op jit(solution)/shard_map/btd,bdc->tc/dot_general | solution.py:109
  102.0 2.5 %fusion.40 = f32[512,384]{0,1:T(8,128)S(1)} fusion(f32[512,384]{0,1:T(8,128)S(1)} %fusion.23, bf16[2,1024,384]{2,1,0:T(8,128)(2,1)} %bitcast.11, bf16[4,2,512,1024]{3,2,1,0:T(8,128)(2,1)S(1)} %bitcast.144, s32[]{:T(128)S(6)} %select_n.162), kind=kOutput, calls=%fused_computation.35 | convolution fusion | flops 805502976 | bytes 5242884 | tf_op jit(solution)/shard_map/btd,bdc->tc/dot_general | solution.py:109
  104.5 2.5 %fusion.46 = f32[512,384]{0,1:T(8,128)S(1)} fusion(f32[512,384]{0,1:T(8,128)S(1)} %fusion.34, f32[512,384]{0,1:T(8,128)S(1)} %fusion.40, bf16[2,1024,384]{2,1,0:T(8,128)(2,1)} %bitcast.14, bf16[4,2,512,1024]{3,2,1,0:T(8,128)(2,1)S(1)} %bitcast.145, s32[]{:T(128)S(6)} %select_n.163, f32[512]{0:T(512)S(1)} %add_rsqrt_fusion), kind=kOutput, calls=%fused_computation.37 | convolution fusion | flops 805896192 | bytes 6031364 | tf_op jit(solution)/shard_map/btd,bdc->tc/dot_general | solution.py:109
  107.1 0.6 fusion.83
  107.8 3.4 %collective-permute-start.12 = (bf16[2,512,64]{1,2,0:T(8,128)(2,1)S(1)}, bf16[2,512,64]{1,2,0:T(8,128)(2,1)S(1)}, u32[]{:S(2)}, u32[]{:S(2)}) collective-permute-start(bf16[2,512,64]{1,2,0:T(8,128)(2,1)S(1)} %pad_maximum_fusion.3), channel_id=1, source_target_pairs={{0,1},{1,2},{2,3},{4,5},{5,6},{6,7},{8,9},{9,10},{10,11},{12,13},{... | collective-permute-start | bytes 393224 | tf_op jit(solution)/shard_map/ppermute | solution.py:19
  111.2 4.8 %collective-permute-start.13 = (bf16[2,512,64]{1,2,0:T(8,128)(2,1)S(1)}, bf16[2,512,64]{1,2,0:T(8,128)(2,1)S(1)}, u32[]{:S(2)}, u32[]{:S(2)}) collective-permute-start(bf16[2,512,64]{1,2,0:T(8,128)(2,1)S(1)} %pad_maximum_fusion.3), channel_id=1, source_target_pairs={{0,9},{1,10},{2,11},{4,13},{5,14},{6,15},{8,1},{9,2},{10,3},{12,5}... | collective-permute-start | bytes 393224 | tf_op jit(solution)/shard_map/ppermute | solution.py:134
  116.3 0.2 reshape.202
  116.7 1.5 %scatter_fusion = bf16[64,2,512]{2,1,0:T(2,128)(2,1)S(1)} fusion(bf16[64,2,512]{2,1,0:T(2,128)(2,1)S(1)} %broadcast_in_dim.68, s32[32]{0:T(128)S(1)} %fusion.92, bf16[32,2,512]{2,1,0:T(2,128)(2,1)S(1)} %copy.47), kind=kCustom, calls=%fused_computation.1 | custom fusion | bytes 196736 | tf_op jit(solution)/shard_map/scatter | solution.py:188
  118.2 0.7 copy.48
  118.9 3.5 %all-to-all-start = ((bf16[4,16,2,512]{3,1,2,0:T(8,128)(2,1)}), bf16[4,16,2,512]{3,1,2,0:T(8,128)(2,1)S(1)}, u32[]{:S(2)}, u32[]{:S(2)}) async-start(bf16[4,16,2,512]{3,1,2,0:T(8,128)(2,1)} %copy.48), calls=%async_computation | async-start | bytes 262144 | tf_op jit(solution)/shard_map/all_to_all | solution.py:191
  122.4 2.6 %fusion.62 = bf16[512,256]{0,1:T(8,128)(2,1)S(1)} fusion(f32[512,384]{0,1:T(8,128)S(1)} %fusion.46, f32[512,1]{0,1:T(1,128)S(1)} %get-tuple-element.22, f32[512,255]{0,1:T(8,128)S(1)} %get-tuple-element.24, f32[512,255]{0,1:T(8,128)S(1)} %get-tuple-element.23, f32[512,1]{0,1:T(1,128)S(1)} %get-tuple-element.21, f32[256]{0:T(256)S(1)} %multiply_power_fusion, ...), kind=kLoop, calls=%fused_computation.48 | loop fusion | flops 1310720 | bytes 1838336 | tf_op jit(solution)/shard_map/convert_element_type | solution.py:120
  125.2 2.0 %all-to-all-done = bf16[4,16,2,512]{3,1,2,0:T(8,128)(2,1)S(1)} async-done(((bf16[4,16,2,512]{3,1,2,0:T(8,128)(2,1)}), bf16[4,16,2,512]{3,1,2,0:T(8,128)(2,1)S(1)}, u32[]{:S(2)}, u32[]{:S(2)}) %all-to-all-start) | async-done | bytes 131104 | tf_op jit(solution)/shard_map/all_to_all | solution.py:191
  127.2 0.3 reshape.204
  127.5 0.9 copy.50
  128.4 0.9 copy.51
  129.5 1.7 %fusion.100 = (f32[1024]{0:T(1024)S(1)}, f32[1024,1024]{0,1:T(8,128)S(1)}) fusion(bf16[1024,128]{1,0:T(8,128)(2,1)S(1)} %bitcast.125, bf16[2,512,128]{1,2,0:T(8,128)(2,1)S(1)} %maximum_select_fusion.1, bf16[2,512,128]{1,2,0:T(8,128)(2,1)S(1)} %maximum_select_fusion.2, s32[1024]{0:T(1024)S(1)} %bitcast.132, pred[1024]{0:T(1024)(128)(4,1)S(1)} %broadcast_compare_fusion, ...), kind=kOutput, calls=%fused_computation.130 | convolution fusion | flops 276298752 | bytes 4998144 | tf_op jit(solution)/shard_map/dot_general | solution.py:152
  131.3 0.6 fusion.1
  131.9 0.9 fusion.55
  132.8 0.7 copy.63
  (72 shorter events, 1.9 us)
Async XLA Ops:
  7.2 2.3 %copy-start = (bf16[512,1024]{1,0:T(8,128)(2,1)S(1)}, bf16[512,1024]{1,0:T(8,128)(2,1)}, u32[]{:S(2)}) copy-start(bf16[512,1024]{1,0:T(8,128)(2,1)} %param.8) | copy-start | bytes 3145732
  7.2 88.8 %all-gather.3.cloned.1.call-start = ((), (), s32[]{:S(2)}) async-start(), calls=%async_computation.1 | async-start | bytes 9437184 | tf_op jit(solution)/shard_map/all_gather | solution.py:100
  10.7 3.5 %copy-start.2 = (bf16[2048,32]{0,1:T(8,128)(2,1)S(1)}, bf16[2048,32]{0,1:T(8,128)(2,1)}, u32[]{:S(2)}) copy-start(bf16[2048,32]{0,1:T(8,128)(2,1)} %param.12) | copy-start | bytes 393220
  10.7 3.5 %copy-start.3 = (bf16[2048,32]{0,1:T(8,128)(2,1)S(1)}, bf16[2048,32]{0,1:T(8,128)(2,1)}, u32[]{:S(2)}) copy-start(bf16[2048,32]{0,1:T(8,128)(2,1)} %param.11) | copy-start | bytes 393220
  10.7 3.7 %copy-start.5 = (s32[32,1]{0,1:T(1,128)S(1)}, s32[32,1]{0,1:T(1,128)}, u32[]{:S(2)}) copy-start(s32[32,1]{0,1:T(1,128)} %param.15) | copy-start | bytes 388
  10.7 4.1 %copy-start.4 = (s32[512]{0:T(512)S(1)}, s32[512]{0:T(512)}, u32[]{:S(2)}) copy-start(s32[512]{0:T(512)} %param.13) | copy-start | bytes 6148
  10.9 12.5 %collective-permute-start.5 = (f32[512]{0:T(512)S(1)}, f32[512]{0:T(512)S(1)}, u32[]{:S(2)}, u32[]{:S(2)}) collective-permute-start(f32[512]{0:T(512)S(1)} %multiply_reduce_fusion), channel_id=1, source_target_pairs={{0,4},{4,0},{8,12},{12,8},{16,20},{20,16},{24,28},{28,24},{1,5},{5... | collective-permute-start | bytes 6152 | tf_op jit(solution)/shard_map/ppermute | solution.py:85
  11.4 14.7 %collective-permute-start.6 = (f32[512]{0:T(512)S(1)}, f32[512]{0:T(512)S(1)}, u32[]{:S(2)}, u32[]{:S(2)}) collective-permute-start(f32[512]{0:T(512)S(1)} %multiply_reduce_fusion), channel_id=1, source_target_pairs={{0,8},{4,12},{8,0},{12,4},{16,24},{20,28},{24,16},{28,20},{1,9},{5... | collective-permute-start | bytes 6152 | tf_op jit(solution)/shard_map/ppermute | solution.py:85
  14.1 12.6 %collective-permute-start.7 = (f32[512]{0:T(512)S(1)}, f32[512]{0:T(512)S(1)}, u32[]{:S(2)}, u32[]{:S(2)}) collective-permute-start(f32[512]{0:T(512)S(1)} %multiply_reduce_fusion), channel_id=1, source_target_pairs={{0,12},{4,8},{8,4},{12,0},{16,28},{20,24},{24,20},{28,16},{1,13},{... | collective-permute-start | bytes 6152 | tf_op jit(solution)/shard_map/ppermute | solution.py:85
  14.2 1.6 %collective-permute-start.1 = (bf16[2,2048,32]{1,2,0:T(8,128)(2,1)S(1)}, bf16[2,2048,32]{1,2,0:T(8,128)(2,1)S(1)}, u32[]{:S(2)}, u32[]{:S(2)}) collective-permute-start(bf16[2,2048,32]{1,2,0:T(8,128)(2,1)S(1)} %pad_maximum_fusion.2), channel_id=1, source_target_pairs={{0,4},{4,0},{8,12},{12,8},{16,20},{20,16},{24,28},{28,24},{1,5},{5... | collective-permute-start | bytes 786440 | tf_op jit(solution)/shard_map/ppermute | solution.py:67
  17.5 1.2 copy-start.1
  18.7 20.0 %copy-start.6 = (s32[512]{0:T(512)S(1)}, s32[512]{0:T(512)}, u32[]{:S(2)}) copy-start(s32[512]{0:T(512)} %param.14) | copy-start | bytes 6148
  20.2 78.5 %collective-permute-start.4 = (bf16[2048,384]{1,0:T(8,128)(2,1)}, bf16[2048,384]{1,0:T(8,128)(2,1)}, u32[]{:S(2)}, u32[]{:S(2)}) collective-permute-start(bf16[2048,384]{1,0:T(8,128)(2,1)} %pad_maximum_fusion), channel_id=1, source_target_pairs={{0,3},{1,2},{2,1},{3,0},{4,7},{5,6},{6,5},{7,4},{8,11},{9,10},{10,... | collective-permute-start | bytes 4718600 | tf_op jit(solution)/shard_map/ppermute | solution.py:73
  22.9 79.2 %collective-permute-start.2 = (bf16[2048,384]{1,0:T(8,128)(2,1)}, bf16[2048,384]{1,0:T(8,128)(2,1)}, u32[]{:S(2)}, u32[]{:S(2)}) collective-permute-start(bf16[2048,384]{1,0:T(8,128)(2,1)} %pad_maximum_fusion), channel_id=1, source_target_pairs={{0,1},{1,0},{2,3},{3,2},{4,5},{5,4},{6,7},{7,6},{8,9},{9,8},{10,11... | collective-permute-start | bytes 4718600 | tf_op jit(solution)/shard_map/ppermute | solution.py:73
  23.5 5.8 %collective-permute-start.8 = (f32[512]{0:T(512)S(1)}, f32[512]{0:T(512)S(1)}, u32[]{:S(2)}, u32[]{:S(2)}) collective-permute-start(f32[512]{0:T(512)S(1)} %multiply_reduce_fusion), channel_id=1, source_target_pairs={{0,16},{4,20},{8,24},{12,28},{16,0},{20,4},{24,8},{28,12},{1,17},{... | collective-permute-start | bytes 6152 | tf_op jit(solution)/shard_map/ppermute | solution.py:85
  26.1 78.4 %collective-permute-start.3 = (bf16[2048,384]{1,0:T(8,128)(2,1)}, bf16[2048,384]{1,0:T(8,128)(2,1)}, u32[]{:S(2)}, u32[]{:S(2)}) collective-permute-start(bf16[2048,384]{1,0:T(8,128)(2,1)} %pad_maximum_fusion), channel_id=1, source_target_pairs={{0,2},{1,3},{2,0},{3,1},{4,6},{5,7},{6,4},{7,5},{8,10},{9,11},{10,... | collective-permute-start | bytes 4718600 | tf_op jit(solution)/shard_map/ppermute | solution.py:73
  26.7 5.1 %collective-permute-start.9 = (f32[512]{0:T(512)S(1)}, f32[512]{0:T(512)S(1)}, u32[]{:S(2)}, u32[]{:S(2)}) collective-permute-start(f32[512]{0:T(512)S(1)} %multiply_reduce_fusion), channel_id=1, source_target_pairs={{0,20},{4,16},{8,28},{12,24},{16,4},{20,0},{24,12},{28,8},{1,21},{... | collective-permute-start | bytes 6152 | tf_op jit(solution)/shard_map/ppermute | solution.py:85
  29.3 5.5 %collective-permute-start.10 = (f32[512]{0:T(512)S(1)}, f32[512]{0:T(512)S(1)}, u32[]{:S(2)}, u32[]{:S(2)}) collective-permute-start(f32[512]{0:T(512)S(1)} %multiply_reduce_fusion), channel_id=1, source_target_pairs={{0,24},{4,28},{8,16},{12,20},{16,8},{20,12},{24,0},{28,4},{1,25},{... | collective-permute-start | bytes 6152 | tf_op jit(solution)/shard_map/ppermute | solution.py:85
  31.7 7.1 %collective-permute-start.11 = (f32[512]{0:T(512)S(1)}, f32[512]{0:T(512)S(1)}, u32[]{:S(2)}, u32[]{:S(2)}) collective-permute-start(f32[512]{0:T(512)S(1)} %multiply_reduce_fusion), channel_id=1, source_target_pairs={{0,28},{4,24},{8,20},{12,16},{16,12},{20,8},{24,4},{28,0},{1,29},{... | collective-permute-start | bytes 6152 | tf_op jit(solution)/shard_map/ppermute | solution.py:85
  34.8 56.3 %collective-permute-start = (s32[512]{0:T(512)S(1)}, s32[512]{0:T(512)S(1)}, u32[]{:S(2)}, u32[]{:S(2)}) collective-permute-start(s32[512]{0:T(512)S(1)} %broadcast_add_fusion), channel_id=1, source_target_pairs={{0,1},{1,2},{2,3},{4,5},{5,6},{6,7},{8,9},{9,10},{10,11},{12,13},{... | collective-permute-start | bytes 6152 | tf_op jit(solution)/shard_map/ppermute | solution.py:19
  95.9 6.1 %copy-start.7 = (bf16[4096,1024]{1,0:T(8,128)(2,1)S(1)}, bf16[4096,1024]{1,0:T(8,128)(2,1)}, u32[]{:S(2)}) copy-start(bf16[4096,1024]{1,0:T(8,128)(2,1)} %all-gather.3.cloned.1.call-done) | copy-start | bytes 25165828
  107.7 21.7 %collective-permute-start.14 = (bf16[2,512,64]{1,2,0:T(8,128)(2,1)S(1)}, bf16[2,512,64]{1,2,0:T(8,128)(2,1)S(1)}, u32[]{:S(2)}, u32[]{:S(2)}) collective-permute-start(bf16[2,512,64]{1,2,0:T(8,128)(2,1)S(1)} %pad_maximum_fusion.3), channel_id=1, source_target_pairs={{0,8},{4,12},{8,0},{12,4},{16,24},{20,28},{24,16},{28,20},{1,9},{5... | collective-permute-start | bytes 393224 | tf_op jit(solution)/shard_map/ppermute | solution.py:125
  107.8 21.7 %collective-permute-start.12 = (bf16[2,512,64]{1,2,0:T(8,128)(2,1)S(1)}, bf16[2,512,64]{1,2,0:T(8,128)(2,1)S(1)}, u32[]{:S(2)}, u32[]{:S(2)}) collective-permute-start(bf16[2,512,64]{1,2,0:T(8,128)(2,1)S(1)} %pad_maximum_fusion.3), channel_id=1, source_target_pairs={{0,1},{1,2},{2,3},{4,5},{5,6},{6,7},{8,9},{9,10},{10,11},{12,13},{... | collective-permute-start | bytes 393224 | tf_op jit(solution)/shard_map/ppermute | solution.py:19
  111.2 18.2 %collective-permute-start.13 = (bf16[2,512,64]{1,2,0:T(8,128)(2,1)S(1)}, bf16[2,512,64]{1,2,0:T(8,128)(2,1)S(1)}, u32[]{:S(2)}, u32[]{:S(2)}) collective-permute-start(bf16[2,512,64]{1,2,0:T(8,128)(2,1)S(1)} %pad_maximum_fusion.3), channel_id=1, source_target_pairs={{0,9},{1,10},{2,11},{4,13},{5,14},{6,15},{8,1},{9,2},{10,3},{12,5}... | collective-permute-start | bytes 393224 | tf_op jit(solution)/shard_map/ppermute | solution.py:134
  118.9 8.3 %all-to-all-start = ((bf16[4,16,2,512]{3,1,2,0:T(8,128)(2,1)}), bf16[4,16,2,512]{3,1,2,0:T(8,128)(2,1)S(1)}, u32[]{:S(2)}, u32[]{:S(2)}) async-start(bf16[4,16,2,512]{3,1,2,0:T(8,128)(2,1)} %copy.48), calls=%async_computation | async-start | bytes 262144 | tf_op jit(solution)/shard_map/all_to_all | solution.py:191
Sparse Core Ops, SparseCore 0:
  10.8 85.0 all-gather.2

commit v12 on v10

--- a/solution.py
+++ b/solution.py
@@ -187,7 +187,8 @@
         .set(kv_pages)
     )
     send_kv = send_kv.reshape(owner_count, capacity, 2, PAGE * quarter)
-    got_kv = lax.all_to_all(send_kv, "gy", split_axis=0, concat_axis=0, tiled=True)
+    gathered = lax.all_gather(send_kv, "gy", axis=0, tiled=False)
+    got_kv = lax.dynamic_index_in_dim(gathered, my_gy, 1, keepdims=False)
     got_kv = got_kv.reshape(owner_count * capacity, 2, PAGE, quarter)
     key_cache = got_kv[:, 0]
     value_cache = got_kv[:, 1]

time: 141 us -> 145 us (1.028)
  blocking collectives: 0 us -> 10.6 us
  starting transfers between devices: 28.5 us -> 25 us
  waiting for transfers between devices: 63.2 us -> 61.4 us
    all_gather x0 -> x1, blocking collectives: none -> 10.6 us  [shards(): gathered = lax.all_gather(send_kv, 'gy', axis=0, tiled=False)]
    all_to_all x1 -> x0, starting transfers between devices: 3.51 us -> none  [shards(): lax.all_to_all(send_kv, 'gy', split_axis=0, concat_axis=0, tiled=True)]
    all_to_all x1 -> x0, waiting for transfers between devices: 2 us -> none  [shards(): lax.all_to_all(send_kv, 'gy', split_axis=0, concat_axis=0, tiled=True)]
  transfers between devices with their start and end apart: 17 -> 16, of which waited for: 6 -> 5; matrix products, arithmetic and copies ran while one was open for 16% -> 15% of each run, Pallas kernels for 0% -> 0%
where the time goes in v12:
time: 145 us
  waiting for transfers between devices  61.4 us (42%)
  starting transfers between devices  25 us (17%)
  between operations  14.6 us (10%)
  matrix products  13.7 us (9%)
  blocking collectives  10.6 us (7%)
  other arithmetic  10.4 us (7%)
  local copies, waits for them, and re-layouts  9.03 us (6%)
    ppermute x2, waiting for transfers between devices, shifted(): return lax.ppermute(value, axis, pairs)  51.4 us
    dot_general x4, matrix products, shards(): jnp.einsum('btd,bdc->tc', rows, weights_of, preferred_element_type=jnp.fl...  11 us
    all_gather x1, blocking collectives, shards(): gathered = lax.all_gather(send_kv, 'gy', axis=0, tiled=False)  10.6 us
    ppermute x7, starting transfers between devices, shards(): lax.ppermute(local_squares, 'gx', partner_route(gx_count, gx_count, k))  9.4 us
    ppermute x2, starting transfers between devices, shifted(): return lax.ppermute(value, axis, pairs)  6.75 us
    ppermute x7, waiting for transfers between devices, shards(): lax.ppermute(local_squares, 'gx', partner_route(gx_count, gx_count, k))  4.92 us
    ppermute x1, starting transfers between devices, shards(): other = lax.ppermute(half_kv, ('gx', 'gy'), route)  4.8 us
    all_gather x1, waiting for transfers between devices, shards(): normed = lax.all_gather(local_normed[rows_of], 'gx', axis=0, tiled=False)  4.57 us
  transfers between devices with their start and end apart: 16, of which 5 were waited for; matrix products, arithmetic and copies ran while one was open for 15% of the time, Pallas kernels for 0%

profile of v12, /device:TPU:0, one launch (start us, length us, event | category | flops | bytes accessed | tf_op | source)
XLA Modules:
  0.0 144.7 jit_solution(4417472422182035257)
XLA Ops:
  7.3 0.7 dynamic-slice_convert_fusion
  8.0 2.5 %fusion.4 = (f32[512]{0:T(512)S(1)}, bf16[512,1024]{1,0:T(8,128)(2,1)}) fusion(bf16[512,1024]{1,0:T(8,128)(2,1)} %param.8, f32[1024]{0:T(1024)S(1)} %dynamic-slice_convert_fusion), kind=kLoop, calls=%fused_computation.11 | loop fusion | flops 2620928 | bytes 2103296 | tf_op jit(solution)/shard_map/reduce_sum | solution.py:81
  10.5 0.5 collective-permute-start.5
  11.1 2.6 %collective-permute-start.6 = (f32[512]{0:T(512)S(1)}, f32[512]{0:T(512)S(1)}, u32[]{:S(2)}, u32[]{:S(2)}) collective-permute-start(f32[512]{0:T(512)S(1)} %get-tuple-element.9), channel_id=1, source_target_pairs={{0,8},{4,12},{8,0},{12,4},{16,24},{20,28},{24,16},{28,20},{1,9},{5... | collective-permute-start | bytes 6152 | tf_op jit(solution)/shard_map/ppermute | solution.py:84
  13.8 0.2 collective-permute-start.1
  14.2 0.2 select_reduce_fusion
  14.4 0.5 copy.32
  14.9 0.5 collective-permute-done.1
  15.4 0.5 copy.33
  15.9 1.2 maximum_select_fusion
  17.1 0.3 fusion.98
  17.4 0.9 copy-done
  18.3 1.5 %pad_maximum_fusion = bf16[2048,384]{1,0:T(8,128)(2,1)} fusion(bf16[2048,64]{1,0:T(8,128)(2,1)S(1)} %get-tuple-element.13, bf16[2048,64]{1,0:T(8,128)(2,1)S(1)} %get-tuple-element.12, bf16[2048,256]{1,0:T(8,128)(2,1)S(1)} %copy-done), kind=kLoop, calls=%fused_computation.31 | loop fusion | flops 4718592 | bytes 3145728 | tf_op jit(solution)/shard_map/concatenate | solution.py:69
  19.8 2.6 %collective-permute-start.4 = (bf16[2048,384]{1,0:T(8,128)(2,1)}, bf16[2048,384]{1,0:T(8,128)(2,1)}, u32[]{:S(2)}, u32[]{:S(2)}) collective-permute-start(bf16[2048,384]{1,0:T(8,128)(2,1)} %pad_maximum_fusion), channel_id=1, source_target_pairs={{0,3},{1,2},{2,1},{3,0},{4,7},{5,6},{6,5},{7,4},{8,11},{9,10},{10,... | collective-permute-start | bytes 4718600 | tf_op jit(solution)/shard_map/ppermute | solution.py:73
  22.4 0.6 collective-permute-start.2
  23.0 2.7 %collective-permute-start.8 = (f32[512]{0:T(512)S(1)}, f32[512]{0:T(512)S(1)}, u32[]{:S(2)}, u32[]{:S(2)}) collective-permute-start(f32[512]{0:T(512)S(1)} %get-tuple-element.9), channel_id=1, source_target_pairs={{0,16},{4,20},{8,24},{12,28},{16,0},{20,4},{24,8},{28,12},{1,17},{... | collective-permute-start | bytes 6152 | tf_op jit(solution)/shard_map/ppermute | solution.py:84
  25.7 0.5 collective-permute-start.3
  26.3 2.8 %collective-permute-done.8 = f32[512]{0:T(512)S(1)} collective-permute-done((f32[512]{0:T(512)S(1)}, f32[512]{0:T(512)S(1)}, u32[]{:S(2)}, u32[]{:S(2)}) %collective-permute-start.8) | collective-permute-done | bytes 2080 | tf_op jit(solution)/shard_map/ppermute | solution.py:84
  29.1 2.1 %collective-permute-start.10 = (f32[512]{0:T(512)S(1)}, f32[512]{0:T(512)S(1)}, u32[]{:S(2)}, u32[]{:S(2)}) collective-permute-start(f32[512]{0:T(512)S(1)} %get-tuple-element.9), channel_id=1, source_target_pairs={{0,24},{4,28},{8,16},{12,20},{16,8},{20,12},{24,0},{28,4},{1,25},{... | collective-permute-start | bytes 6152 | tf_op jit(solution)/shard_map/ppermute | solution.py:84
  31.3 1.3 collective-permute-start.11
  32.6 2.1 %collective-permute-done.10 = f32[512]{0:T(512)S(1)} collective-permute-done((f32[512]{0:T(512)S(1)}, f32[512]{0:T(512)S(1)}, u32[]{:S(2)}, u32[]{:S(2)}) %collective-permute-start.10) | collective-permute-done | bytes 2080 | tf_op jit(solution)/shard_map/ppermute | solution.py:84
  34.7 3.3 %collective-permute-start = (s32[512]{0:T(512)S(1)}, s32[512]{0:T(512)S(1)}, u32[]{:S(2)}, u32[]{:S(2)}) collective-permute-start(s32[512]{0:T(512)S(1)} %broadcast_add_fusion), channel_id=1, source_target_pairs={{0,1},{1,2},{2,3},{4,5},{5,6},{6,7},{8,9},{9,10},{10,11},{12,13},{... | collective-permute-start | bytes 6152 | tf_op jit(solution)/shard_map/ppermute | solution.py:19
  38.0 0.5 copy.38
  38.7 0.6 gather_fusion
  39.3 51.4 %collective-permute-done = s32[512]{0:T(512)S(1)} collective-permute-done((s32[512]{0:T(512)S(1)}, s32[512]{0:T(512)S(1)}, u32[]{:S(2)}, u32[]{:S(2)}) %collective-permute-start) | collective-permute-done | bytes 2080 | tf_op jit(solution)/shard_map/ppermute | solution.py:19
  90.8 0.2 copy.39
  91.0 0.2 copy.40
  91.2 4.6 %all-gather.3.cloned.1.call-done = bf16[4096,1024]{1,0:T(8,128)(2,1)} async-done(((bf16[512,1024]{1,0:T(8,128)(2,1)}), bf16[4096,1024]{1,0:T(8,128)(2,1)}) %all-gather.3.cloned.1.call-update) | async-done | bytes 8388624 | tf_op jit(solution)/shard_map/all_gather | solution.py:99
  95.8 2.8 %fusion.25 = f32[512,384]{0,1:T(8,128)S(1)} fusion(bf16[2,1024,64]{1,2,0:T(8,128)(2,1)S(1)} %copy.40, bf16[2,1024,64]{1,2,0:T(8,128)(2,1)S(1)} %copy.39, bf16[2,1024,256]{1,2,0:T(8,128)(2,1)S(1)} %copy.38, bf16[4,2,512,1024]{3,2,1,0:T(8,128)(2,1)} %bitcast.142, s32[]{:T(128)S(6)} %select_n.159), kind=kOutput, calls=%fused_computation.32 | convolution fusion | flops 810024960 | bytes 4456452 | tf_op jit(solution)/shard_map/btd,bdc->tc/dot_general | solution.py:108
  98.6 3.2 %fusion.36 = f32[512,384]{0,1:T(8,128)S(1)} fusion(bf16[2,1024,384]{2,1,0:T(8,128)(2,1)} %bitcast.17, bf16[4,2,512,1024]{3,2,1,0:T(8,128)(2,1)} %bitcast.143, s32[]{:T(128)S(6)} %select_n.166), kind=kOutput, calls=%fused_computation.35 | convolution fusion | flops 805306368 | bytes 4456452 | tf_op jit(solution)/shard_map/btd,bdc->tc/dot_general | solution.py:108
  101.9 2.5 %fusion.42 = f32[512,384]{0,1:T(8,128)S(1)} fusion(f32[512,384]{0,1:T(8,128)S(1)} %fusion.25, bf16[2,1024,384]{2,1,0:T(8,128)(2,1)} %bitcast.11, bf16[4,2,512,1024]{3,2,1,0:T(8,128)(2,1)S(1)} %bitcast.144, s32[]{:T(128)S(6)} %select_n.164), kind=kOutput, calls=%fused_computation.37 | convolution fusion | flops 805502976 | bytes 5242884 | tf_op jit(solution)/shard_map/btd,bdc->tc/dot_general | solution.py:108
  104.3 2.5 %fusion.48 = f32[512,384]{0,1:T(8,128)S(1)} fusion(f32[512,384]{0,1:T(8,128)S(1)} %fusion.36, f32[512,384]{0,1:T(8,128)S(1)} %fusion.42, bf16[2,1024,384]{2,1,0:T(8,128)(2,1)} %bitcast.14, bf16[4,2,512,1024]{3,2,1,0:T(8,128)(2,1)S(1)} %bitcast.145, s32[]{:T(128)S(6)} %select_n.165, f32[512]{0:T(512)S(1)} %add_rsqrt_fusion), kind=kOutput, calls=%fused_computation.39 | convolution fusion | flops 805896192 | bytes 6031364 | tf_op jit(solution)/shard_map/btd,bdc->tc/dot_general | solution.py:108
  106.9 0.6 fusion.85
  107.6 3.4 %collective-permute-start.12 = (bf16[2,512,64]{1,2,0:T(8,128)(2,1)S(1)}, bf16[2,512,64]{1,2,0:T(8,128)(2,1)S(1)}, u32[]{:S(2)}, u32[]{:S(2)}) collective-permute-start(bf16[2,512,64]{1,2,0:T(8,128)(2,1)S(1)} %pad_maximum_fusion.3), channel_id=1, source_target_pairs={{0,1},{1,2},{2,3},{4,5},{5,6},{6,7},{8,9},{9,10},{10,11},{12,13},{... | collective-permute-start | bytes 393224 | tf_op jit(solution)/shard_map/ppermute | solution.py:19
  111.0 4.8 %collective-permute-start.13 = (bf16[2,512,64]{1,2,0:T(8,128)(2,1)S(1)}, bf16[2,512,64]{1,2,0:T(8,128)(2,1)S(1)}, u32[]{:S(2)}, u32[]{:S(2)}) collective-permute-start(bf16[2,512,64]{1,2,0:T(8,128)(2,1)S(1)} %pad_maximum_fusion.3), channel_id=1, source_target_pairs={{0,9},{1,10},{2,11},{4,13},{5,14},{6,15},{8,1},{9,2},{10,3},{12,5}... | collective-permute-start | bytes 393224 | tf_op jit(solution)/shard_map/ppermute | solution.py:133
  116.0 0.2 copy.46
  116.1 0.2 reshape.200
  116.5 1.5 %scatter_fusion = bf16[64,2,512]{2,1,0:T(2,128)(2,1)S(1)} fusion(bf16[64,2,512]{2,1,0:T(2,128)(2,1)S(1)} %broadcast_in_dim.68, s32[32]{0:T(128)S(1)} %fusion.94, bf16[32,2,512]{2,1,0:T(2,128)(2,1)S(1)} %copy.47), kind=kCustom, calls=%fused_computation.1 | custom fusion | bytes 196736 | tf_op jit(solution)/shard_map/scatter | solution.py:187
  118.0 10.6 %all_gather.11 = bf16[4,4,16,2,512]{4,2,0,3,1:T(8,128)(2,1)S(1)} all-gather(bf16[1,4,16,2,512]{4,2,0,3,1:T(8,128)(2,1)S(1)} %copy.48), channel_id=1, replica_groups=mesh['gx'=8,'gy'=4] {'gy'}, dimensions={0}, use_global_device_ids=true | all-gather | bytes 655360 | tf_op jit(solution)/shard_map/all_gather | solution.py:190
  128.6 0.3 reshape.201
  128.9 2.6 %fusion.64 = bf16[512,256]{0,1:T(8,128)(2,1)S(1)} fusion(f32[512,384]{0,1:T(8,128)S(1)} %fusion.48, f32[512,1]{0,1:T(1,128)S(1)} %get-tuple-element.20, f32[512,255]{0,1:T(8,128)S(1)} %get-tuple-element.22, f32[512,255]{0,1:T(8,128)S(1)} %get-tuple-element.21, f32[512,1]{0,1:T(1,128)S(1)} %get-tuple-element.19, f32[256]{0:T(256)S(1)} %multiply_power_fusion, ...), kind=kLoop, calls=%fused_computation.50 | loop fusion | flops 1310720 | bytes 1838336 | tf_op jit(solution)/shard_map/convert_element_type | solution.py:119
  131.6 0.9 copy.49
  132.5 0.9 copy.50
  133.4 0.2 copy.44
  133.8 1.7 %fusion.102 = (f32[1024]{0:T(1024)S(1)}, f32[1024,1024]{0,1:T(8,128)S(1)}) fusion(bf16[1024,128]{1,0:T(8,128)(2,1)S(1)} %bitcast.125, bf16[2,512,128]{1,2,0:T(8,128)(2,1)S(1)} %maximum_select_fusion.1, bf16[2,512,128]{1,2,0:T(8,128)(2,1)S(1)} %maximum_select_fusion.2, s32[1024]{0:T(1024)S(1)} %bitcast.132, pred[1024]{0:T(1024)(128)(4,1)S(1)} %broadcast_compare_fusion, ...), kind=kOutput, calls=%fused_computation.133 | convolution fusion | flops 276298752 | bytes 4998144 | tf_op jit(solution)/shard_map/dot_general | solution.py:151
  135.5 0.6 fusion.1
  136.1 0.9 fusion.57
  137.1 0.7 copy.62
  (67 shorter events, 1.2 us)
Async XLA Ops:
  7.2 6.6 %copy-start.2 = (bf16[2048,32]{0,1:T(8,128)(2,1)S(1)}, bf16[2048,32]{0,1:T(8,128)(2,1)}, u32[]{:S(2)}) copy-start(bf16[2048,32]{0,1:T(8,128)(2,1)} %param.11) | copy-start | bytes 393220
  7.2 6.6 %copy-start.1 = (bf16[2048,32]{0,1:T(8,128)(2,1)S(1)}, bf16[2048,32]{0,1:T(8,128)(2,1)}, u32[]{:S(2)}) copy-start(bf16[2048,32]{0,1:T(8,128)(2,1)} %param.12) | copy-start | bytes 393220
  7.2 6.8 %copy-start.4 = (s32[32,1]{0,1:T(1,128)S(1)}, s32[32,1]{0,1:T(1,128)}, u32[]{:S(2)}) copy-start(s32[32,1]{0,1:T(1,128)} %param.15) | copy-start | bytes 388
  7.2 7.2 %copy-start.3 = (s32[512]{0:T(512)S(1)}, s32[512]{0:T(512)}, u32[]{:S(2)}) copy-start(s32[512]{0:T(512)} %param.13) | copy-start | bytes 6148
  7.2 88.5 %all-gather.3.cloned.1.call-start = ((), (), s32[]{:S(2)}) async-start(), calls=%async_computation | async-start | bytes 9437184 | tf_op jit(solution)/shard_map/all_gather | solution.py:99
  10.5 12.5 %collective-permute-start.5 = (f32[512]{0:T(512)S(1)}, f32[512]{0:T(512)S(1)}, u32[]{:S(2)}, u32[]{:S(2)}) collective-permute-start(f32[512]{0:T(512)S(1)} %get-tuple-element.9), channel_id=1, source_target_pairs={{0,4},{4,0},{8,12},{12,8},{16,20},{20,16},{24,28},{28,24},{1,5},{5... | collective-permute-start | bytes 6152 | tf_op jit(solution)/shard_map/ppermute | solution.py:84
  11.1 14.6 %collective-permute-start.6 = (f32[512]{0:T(512)S(1)}, f32[512]{0:T(512)S(1)}, u32[]{:S(2)}, u32[]{:S(2)}) collective-permute-start(f32[512]{0:T(512)S(1)} %get-tuple-element.9), channel_id=1, source_target_pairs={{0,8},{4,12},{8,0},{12,4},{16,24},{20,28},{24,16},{28,20},{1,9},{5... | collective-permute-start | bytes 6152 | tf_op jit(solution)/shard_map/ppermute | solution.py:84
  13.7 12.5 %collective-permute-start.7 = (f32[512]{0:T(512)S(1)}, f32[512]{0:T(512)S(1)}, u32[]{:S(2)}, u32[]{:S(2)}) collective-permute-start(f32[512]{0:T(512)S(1)} %get-tuple-element.9), channel_id=1, source_target_pairs={{0,12},{4,8},{8,4},{12,0},{16,28},{20,24},{24,20},{28,16},{1,13},{... | collective-permute-start | bytes 6152 | tf_op jit(solution)/shard_map/ppermute | solution.py:84
  13.8 1.6 %collective-permute-start.1 = (bf16[2,2048,32]{1,2,0:T(8,128)(2,1)S(1)}, bf16[2,2048,32]{1,2,0:T(8,128)(2,1)S(1)}, u32[]{:S(2)}, u32[]{:S(2)}) collective-permute-start(bf16[2,2048,32]{1,2,0:T(8,128)(2,1)S(1)} %pad_maximum_fusion.2), channel_id=1, source_target_pairs={{0,4},{4,0},{8,12},{12,8},{16,20},{20,16},{24,28},{28,24},{1,5},{5... | collective-permute-start | bytes 786440 | tf_op jit(solution)/shard_map/ppermute | solution.py:67
  17.1 1.2 copy-start
  18.3 20.3 %copy-start.5 = (s32[512]{0:T(512)S(1)}, s32[512]{0:T(512)}, u32[]{:S(2)}) copy-start(s32[512]{0:T(512)} %param.14) | copy-start | bytes 6148
  19.8 78.8 %collective-permute-start.4 = (bf16[2048,384]{1,0:T(8,128)(2,1)}, bf16[2048,384]{1,0:T(8,128)(2,1)}, u32[]{:S(2)}, u32[]{:S(2)}) collective-permute-start(bf16[2048,384]{1,0:T(8,128)(2,1)} %pad_maximum_fusion), channel_id=1, source_target_pairs={{0,3},{1,2},{2,1},{3,0},{4,7},{5,6},{6,5},{7,4},{8,11},{9,10},{10,... | collective-permute-start | bytes 4718600 | tf_op jit(solution)/shard_map/ppermute | solution.py:73
  22.4 79.4 %collective-permute-start.2 = (bf16[2048,384]{1,0:T(8,128)(2,1)}, bf16[2048,384]{1,0:T(8,128)(2,1)}, u32[]{:S(2)}, u32[]{:S(2)}) collective-permute-start(bf16[2048,384]{1,0:T(8,128)(2,1)} %pad_maximum_fusion), channel_id=1, source_target_pairs={{0,1},{1,0},{2,3},{3,2},{4,5},{5,4},{6,7},{7,6},{8,9},{9,8},{10,11... | collective-permute-start | bytes 4718600 | tf_op jit(solution)/shard_map/ppermute | solution.py:73
  23.0 6.1 %collective-permute-start.8 = (f32[512]{0:T(512)S(1)}, f32[512]{0:T(512)S(1)}, u32[]{:S(2)}, u32[]{:S(2)}) collective-permute-start(f32[512]{0:T(512)S(1)} %get-tuple-element.9), channel_id=1, source_target_pairs={{0,16},{4,20},{8,24},{12,28},{16,0},{20,4},{24,8},{28,12},{1,17},{... | collective-permute-start | bytes 6152 | tf_op jit(solution)/shard_map/ppermute | solution.py:84
  25.7 78.6 %collective-permute-start.3 = (bf16[2048,384]{1,0:T(8,128)(2,1)}, bf16[2048,384]{1,0:T(8,128)(2,1)}, u32[]{:S(2)}, u32[]{:S(2)}) collective-permute-start(bf16[2048,384]{1,0:T(8,128)(2,1)} %pad_maximum_fusion), channel_id=1, source_target_pairs={{0,2},{1,3},{2,0},{3,1},{4,6},{5,7},{6,4},{7,5},{8,10},{9,11},{10,... | collective-permute-start | bytes 4718600 | tf_op jit(solution)/shard_map/ppermute | solution.py:73
  26.2 5.1 %collective-permute-start.9 = (f32[512]{0:T(512)S(1)}, f32[512]{0:T(512)S(1)}, u32[]{:S(2)}, u32[]{:S(2)}) collective-permute-start(f32[512]{0:T(512)S(1)} %get-tuple-element.9), channel_id=1, source_target_pairs={{0,20},{4,16},{8,28},{12,24},{16,4},{20,0},{24,12},{28,8},{1,21},{... | collective-permute-start | bytes 6152 | tf_op jit(solution)/shard_map/ppermute | solution.py:84
  29.1 5.5 %collective-permute-start.10 = (f32[512]{0:T(512)S(1)}, f32[512]{0:T(512)S(1)}, u32[]{:S(2)}, u32[]{:S(2)}) collective-permute-start(f32[512]{0:T(512)S(1)} %get-tuple-element.9), channel_id=1, source_target_pairs={{0,24},{4,28},{8,16},{12,20},{16,8},{20,12},{24,0},{28,4},{1,25},{... | collective-permute-start | bytes 6152 | tf_op jit(solution)/shard_map/ppermute | solution.py:84
  31.3 7.4 %collective-permute-start.11 = (f32[512]{0:T(512)S(1)}, f32[512]{0:T(512)S(1)}, u32[]{:S(2)}, u32[]{:S(2)}) collective-permute-start(f32[512]{0:T(512)S(1)} %get-tuple-element.9), channel_id=1, source_target_pairs={{0,28},{4,24},{8,20},{12,16},{16,12},{20,8},{24,4},{28,0},{1,29},{... | collective-permute-start | bytes 6152 | tf_op jit(solution)/shard_map/ppermute | solution.py:84
  34.7 56.0 %collective-permute-start = (s32[512]{0:T(512)S(1)}, s32[512]{0:T(512)S(1)}, u32[]{:S(2)}, u32[]{:S(2)}) collective-permute-start(s32[512]{0:T(512)S(1)} %broadcast_add_fusion), channel_id=1, source_target_pairs={{0,1},{1,2},{2,3},{4,5},{5,6},{6,7},{8,9},{9,10},{10,11},{12,13},{... | collective-permute-start | bytes 6152 | tf_op jit(solution)/shard_map/ppermute | solution.py:19
  95.7 6.1 %copy-start.6 = (bf16[4096,1024]{1,0:T(8,128)(2,1)S(1)}, bf16[4096,1024]{1,0:T(8,128)(2,1)}, u32[]{:S(2)}) copy-start(bf16[4096,1024]{1,0:T(8,128)(2,1)} %all-gather.3.cloned.1.call-done) | copy-start | bytes 25165828
  107.5 26.1 %collective-permute-start.14 = (bf16[2,512,64]{1,2,0:T(8,128)(2,1)S(1)}, bf16[2,512,64]{1,2,0:T(8,128)(2,1)S(1)}, u32[]{:S(2)}, u32[]{:S(2)}) collective-permute-start(bf16[2,512,64]{1,2,0:T(8,128)(2,1)S(1)} %pad_maximum_fusion.3), channel_id=1, source_target_pairs={{0,8},{4,12},{8,0},{12,4},{16,24},{20,28},{24,16},{28,20},{1,9},{5... | collective-permute-start | bytes 393224 | tf_op jit(solution)/shard_map/ppermute | solution.py:124
  107.6 26.1 %collective-permute-start.12 = (bf16[2,512,64]{1,2,0:T(8,128)(2,1)S(1)}, bf16[2,512,64]{1,2,0:T(8,128)(2,1)S(1)}, u32[]{:S(2)}, u32[]{:S(2)}) collective-permute-start(bf16[2,512,64]{1,2,0:T(8,128)(2,1)S(1)} %pad_maximum_fusion.3), channel_id=1, source_target_pairs={{0,1},{1,2},{2,3},{4,5},{5,6},{6,7},{8,9},{9,10},{10,11},{12,13},{... | collective-permute-start | bytes 393224 | tf_op jit(solution)/shard_map/ppermute | solution.py:19
  111.0 22.7 %collective-permute-start.13 = (bf16[2,512,64]{1,2,0:T(8,128)(2,1)S(1)}, bf16[2,512,64]{1,2,0:T(8,128)(2,1)S(1)}, u32[]{:S(2)}, u32[]{:S(2)}) collective-permute-start(bf16[2,512,64]{1,2,0:T(8,128)(2,1)S(1)} %pad_maximum_fusion.3), channel_id=1, source_target_pairs={{0,9},{1,10},{2,11},{4,13},{5,14},{6,15},{8,1},{9,2},{10,3},{12,5}... | collective-permute-start | bytes 393224 | tf_op jit(solution)/shard_map/ppermute | solution.py:133
Sparse Core Ops, SparseCore 0:
  10.7 85.0 all-gather.2

commit v13 on v10

--- a/solution.py
+++ b/solution.py
@@ -188,6 +188,7 @@
     )
     send_kv = send_kv.reshape(owner_count, capacity, 2, PAGE * quarter)
     got_kv = lax.all_to_all(send_kv, "gy", split_axis=0, concat_axis=0, tiled=True)
+    got_kv, context = lax.optimization_barrier((got_kv, context))
     got_kv = got_kv.reshape(owner_count * capacity, 2, PAGE, quarter)
     key_cache = got_kv[:, 0]
     value_cache = got_kv[:, 1]

time: 141 us -> 139 us (0.986)
  transfers between devices with their start and end apart: 17 -> 17, of which waited for: 6 -> 6; matrix products, arithmetic and copies ran while one was open for 16% -> 18% of each run, Pallas kernels for 0% -> 0%
where the time goes in v13:
time: 139 us
  waiting for transfers between devices  61.9 us (45%)
  starting transfers between devices  28.5 us (21%)
  between operations  14.6 us (11%)
  matrix products  13.6 us (10%)
  other arithmetic  10.5 us (8%)
  local copies, waits for them, and re-layouts  9.69 us (7%)
    ppermute x2, waiting for transfers between devices, shifted(): return lax.ppermute(value, axis, pairs)  51.4 us
    dot_general x4, matrix products, shards(): jnp.einsum('btd,bdc->tc', rows, weights_of, preferred_element_type=jnp.fl...  11 us
    ppermute x7, starting transfers between devices, shards(): lax.ppermute(local_squares, 'gx', partner_route(gx_count, gx_count, k))  9.4 us
    ppermute x2, starting transfers between devices, shifted(): return lax.ppermute(value, axis, pairs)  6.78 us
    ppermute x7, waiting for transfers between devices, shards(): lax.ppermute(local_squares, 'gx', partner_route(gx_count, gx_count, k))  4.84 us
    ppermute x1, starting transfers between devices, shards(): other = lax.ppermute(half_kv, ('gx', 'gy'), route)  4.8 us
    all_gather x1, waiting for transfers between devices, shards(): normed = lax.all_gather(local_normed[rows_of], 'gx', axis=0, tiled=False)  4.55 us
    ppermute x3, starting transfers between devices, shards(): lax.ppermute(local_weights, 'gy', partner_route(gy_count, gy_count, k))  3.7 us
  transfers between devices with their start and end apart: 17, of which 6 were waited for; matrix products, arithmetic and copies ran while one was open for 18% of the time, Pallas kernels for 0%

profile of v13, /device:TPU:0, one launch (start us, length us, event | category | flops | bytes accessed | tf_op | source)
XLA Modules:
  0.0 138.8 jit_solution(12607465129213450215)
XLA Ops:
  7.3 0.7 dynamic-slice_convert_fusion
  8.0 2.5 %fusion.4 = (f32[512]{0:T(512)S(1)}, bf16[512,1024]{1,0:T(8,128)(2,1)}) fusion(bf16[512,1024]{1,0:T(8,128)(2,1)} %param.8, f32[1024]{0:T(1024)S(1)} %dynamic-slice_convert_fusion), kind=kLoop, calls=%fused_computation.11 | loop fusion | flops 2620928 | bytes 2103296 | tf_op jit(solution)/shard_map/reduce_sum | solution.py:81
  10.5 0.5 collective-permute-start.4
  11.1 2.6 %collective-permute-start.5 = (f32[512]{0:T(512)S(1)}, f32[512]{0:T(512)S(1)}, u32[]{:S(2)}, u32[]{:S(2)}) collective-permute-start(f32[512]{0:T(512)S(1)} %get-tuple-element.13), channel_id=1, source_target_pairs={{0,8},{4,12},{8,0},{12,4},{16,24},{20,28},{24,16},{28,20},{1,9},{5... | collective-permute-start | bytes 6152 | tf_op jit(solution)/shard_map/ppermute | solution.py:84
  13.8 0.2 collective-permute-start
  14.2 0.2 select_reduce_fusion.1
  14.4 0.5 copy.32
  14.9 0.5 collective-permute-done
  15.4 0.5 copy.33
  15.9 1.2 maximum_select_fusion
  17.1 0.3 fusion.98
  17.3 0.9 copy-done
  18.3 1.5 %pad_maximum_fusion = bf16[2048,384]{1,0:T(8,128)(2,1)} fusion(bf16[2048,64]{1,0:T(8,128)(2,1)S(1)} %get-tuple-element.17, bf16[2048,64]{1,0:T(8,128)(2,1)S(1)} %get-tuple-element.16, bf16[2048,256]{1,0:T(8,128)(2,1)S(1)} %copy-done), kind=kLoop, calls=%fused_computation.31 | loop fusion | flops 4718592 | bytes 3145728 | tf_op jit(solution)/shard_map/concatenate | solution.py:69
  19.8 2.6 %collective-permute-start.3 = (bf16[2048,384]{1,0:T(8,128)(2,1)}, bf16[2048,384]{1,0:T(8,128)(2,1)}, u32[]{:S(2)}, u32[]{:S(2)}) collective-permute-start(bf16[2048,384]{1,0:T(8,128)(2,1)} %pad_maximum_fusion), channel_id=1, source_target_pairs={{0,3},{1,2},{2,1},{3,0},{4,7},{5,6},{6,5},{7,4},{8,11},{9,10},{10,... | collective-permute-start | bytes 4718600 | tf_op jit(solution)/shard_map/ppermute | solution.py:73
  22.4 0.6 collective-permute-start.1
  23.1 2.7 %collective-permute-start.7 = (f32[512]{0:T(512)S(1)}, f32[512]{0:T(512)S(1)}, u32[]{:S(2)}, u32[]{:S(2)}) collective-permute-start(f32[512]{0:T(512)S(1)} %get-tuple-element.13), channel_id=1, source_target_pairs={{0,16},{4,20},{8,24},{12,28},{16,0},{20,4},{24,8},{28,12},{1,17},{... | collective-permute-start | bytes 6152 | tf_op jit(solution)/shard_map/ppermute | solution.py:84
  25.7 0.5 collective-permute-start.2
  26.3 2.8 %collective-permute-done.7 = f32[512]{0:T(512)S(1)} collective-permute-done((f32[512]{0:T(512)S(1)}, f32[512]{0:T(512)S(1)}, u32[]{:S(2)}, u32[]{:S(2)}) %collective-permute-start.7) | collective-permute-done | bytes 2080 | tf_op jit(solution)/shard_map/ppermute | solution.py:84
  29.1 2.2 %collective-permute-start.9 = (f32[512]{0:T(512)S(1)}, f32[512]{0:T(512)S(1)}, u32[]{:S(2)}, u32[]{:S(2)}) collective-permute-start(f32[512]{0:T(512)S(1)} %get-tuple-element.13), channel_id=1, source_target_pairs={{0,24},{4,28},{8,16},{12,20},{16,8},{20,12},{24,0},{28,4},{1,25},{... | collective-permute-start | bytes 6152 | tf_op jit(solution)/shard_map/ppermute | solution.py:84
  31.3 1.3 collective-permute-start.10
  32.6 2.0 %collective-permute-done.9 = f32[512]{0:T(512)S(1)} collective-permute-done((f32[512]{0:T(512)S(1)}, f32[512]{0:T(512)S(1)}, u32[]{:S(2)}, u32[]{:S(2)}) %collective-permute-start.9) | collective-permute-done | bytes 2080 | tf_op jit(solution)/shard_map/ppermute | solution.py:84
  34.6 3.4 %collective-permute-start.11 = (s32[512]{0:T(512)S(1)}, s32[512]{0:T(512)S(1)}, u32[]{:S(2)}, u32[]{:S(2)}) collective-permute-start(s32[512]{0:T(512)S(1)} %broadcast_add_fusion), channel_id=1, source_target_pairs={{0,1},{1,2},{2,3},{4,5},{5,6},{6,7},{8,9},{9,10},{10,11},{12,13},{... | collective-permute-start | bytes 6152 | tf_op jit(solution)/shard_map/ppermute | solution.py:19
  38.0 0.5 copy.38
  38.7 0.6 gather_fusion
  39.3 51.4 %collective-permute-done.11 = s32[512]{0:T(512)S(1)} collective-permute-done((s32[512]{0:T(512)S(1)}, s32[512]{0:T(512)S(1)}, u32[]{:S(2)}, u32[]{:S(2)}) %collective-permute-start.11) | collective-permute-done | bytes 2080 | tf_op jit(solution)/shard_map/ppermute | solution.py:19
  90.8 0.2 copy.39
  91.0 0.2 copy.40
  91.2 4.5 %all-gather.3.cloned.1.call-done = bf16[4096,1024]{1,0:T(8,128)(2,1)} async-done(((bf16[512,1024]{1,0:T(8,128)(2,1)}), bf16[4096,1024]{1,0:T(8,128)(2,1)}) %all-gather.3.cloned.1.call-update) | async-done | bytes 8388624 | tf_op jit(solution)/shard_map/all_gather | solution.py:99
  95.8 2.8 %fusion.25 = f32[512,384]{0,1:T(8,128)S(1)} fusion(bf16[2,1024,64]{1,2,0:T(8,128)(2,1)S(1)} %copy.40, bf16[2,1024,64]{1,2,0:T(8,128)(2,1)S(1)} %copy.39, bf16[2,1024,256]{1,2,0:T(8,128)(2,1)S(1)} %copy.38, bf16[4,2,512,1024]{3,2,1,0:T(8,128)(2,1)} %bitcast.142, s32[]{:T(128)S(6)} %select_n.158), kind=kOutput, calls=%fused_computation.32 | convolution fusion | flops 810024960 | bytes 4456452 | tf_op jit(solution)/shard_map/btd,bdc->tc/dot_general | solution.py:108
  98.6 3.3 %fusion.36 = f32[512,384]{0,1:T(8,128)S(1)} fusion(bf16[2,1024,384]{2,1,0:T(8,128)(2,1)} %bitcast.20, bf16[4,2,512,1024]{3,2,1,0:T(8,128)(2,1)} %bitcast.143, s32[]{:T(128)S(6)} %select_n.165), kind=kOutput, calls=%fused_computation.35 | convolution fusion | flops 805306368 | bytes 4456452 | tf_op jit(solution)/shard_map/btd,bdc->tc/dot_general | solution.py:108
  101.9 2.5 %fusion.42 = f32[512,384]{0,1:T(8,128)S(1)} fusion(f32[512,384]{0,1:T(8,128)S(1)} %fusion.25, bf16[2,1024,384]{2,1,0:T(8,128)(2,1)} %bitcast.14, bf16[4,2,512,1024]{3,2,1,0:T(8,128)(2,1)S(1)} %bitcast.144, s32[]{:T(128)S(6)} %select_n.163), kind=kOutput, calls=%fused_computation.37 | convolution fusion | flops 805502976 | bytes 5242884 | tf_op jit(solution)/shard_map/btd,bdc->tc/dot_general | solution.py:108
  104.3 2.5 %fusion.48 = f32[512,384]{0,1:T(8,128)S(1)} fusion(f32[512,384]{0,1:T(8,128)S(1)} %fusion.36, f32[512,384]{0,1:T(8,128)S(1)} %fusion.42, bf16[2,1024,384]{2,1,0:T(8,128)(2,1)} %bitcast.17, bf16[4,2,512,1024]{3,2,1,0:T(8,128)(2,1)S(1)} %bitcast.145, s32[]{:T(128)S(6)} %select_n.164, f32[512]{0:T(512)S(1)} %add_rsqrt_fusion), kind=kOutput, calls=%fused_computation.39 | convolution fusion | flops 805896192 | bytes 6031364 | tf_op jit(solution)/shard_map/btd,bdc->tc/dot_general | solution.py:108
  106.9 0.6 fusion.85
  107.6 3.4 %collective-permute-start.12 = (bf16[2,512,64]{1,2,0:T(8,128)(2,1)S(1)}, bf16[2,512,64]{1,2,0:T(8,128)(2,1)S(1)}, u32[]{:S(2)}, u32[]{:S(2)}) collective-permute-start(bf16[2,512,64]{1,2,0:T(8,128)(2,1)S(1)} %pad_maximum_fusion.3), channel_id=1, source_target_pairs={{0,1},{1,2},{2,3},{4,5},{5,6},{6,7},{8,9},{9,10},{10,11},{12,13},{... | collective-permute-start | bytes 393224 | tf_op jit(solution)/shard_map/ppermute | solution.py:19
  111.0 4.8 %collective-permute-start.13 = (bf16[2,512,64]{1,2,0:T(8,128)(2,1)S(1)}, bf16[2,512,64]{1,2,0:T(8,128)(2,1)S(1)}, u32[]{:S(2)}, u32[]{:S(2)}) collective-permute-start(bf16[2,512,64]{1,2,0:T(8,128)(2,1)S(1)} %pad_maximum_fusion.3), channel_id=1, source_target_pairs={{0,9},{1,10},{2,11},{4,13},{5,14},{6,15},{8,1},{9,2},{10,3},{12,5}... | collective-permute-start | bytes 393224 | tf_op jit(solution)/shard_map/ppermute | solution.py:133
  115.9 2.6 %fusion.64 = bf16[512,256]{0,1:T(8,128)(2,1)S(1)} fusion(f32[512,384]{0,1:T(8,128)S(1)} %fusion.48, f32[512,1]{0,1:T(1,128)S(1)} %get-tuple-element.20, f32[512,255]{0,1:T(8,128)S(1)} %get-tuple-element.24, f32[512,255]{0,1:T(8,128)S(1)} %get-tuple-element.23, f32[512,1]{0,1:T(1,128)S(1)} %get-tuple-element.19, f32[256]{0:T(256)S(1)} %multiply_power_fusion, ...), kind=kLoop, calls=%fused_computation.50 | loop fusion | flops 1310720 | bytes 1838336 | tf_op jit(solution)/shard_map/convert_element_type | solution.py:119
  118.9 0.2 reshape.200
  119.3 1.5 %scatter_fusion = bf16[64,2,512]{2,1,0:T(2,128)(2,1)S(1)} fusion(bf16[64,2,512]{2,1,0:T(2,128)(2,1)S(1)} %broadcast_in_dim.44, s32[32]{0:T(128)S(1)} %fusion.93, bf16[32,2,512]{2,1,0:T(2,128)(2,1)S(1)} %copy.45), kind=kCustom, calls=%fused_computation.1 | custom fusion | bytes 196736 | tf_op jit(solution)/shard_map/scatter | solution.py:187
  120.8 0.7 copy.46
  121.5 3.5 %all-to-all-start = ((bf16[4,16,2,512]{3,1,2,0:T(8,128)(2,1)}), bf16[4,16,2,512]{3,1,2,0:T(8,128)(2,1)S(1)}, u32[]{:S(2)}, u32[]{:S(2)}) async-start(bf16[4,16,2,512]{3,1,2,0:T(8,128)(2,1)} %copy.46), calls=%async_computation | async-start | bytes 262144 | tf_op jit(solution)/shard_map/all_to_all | solution.py:190
  125.1 1.8 %fusion.102 = (f32[1024]{0:T(1024)S(1)}, f32[1024,1024]{0,1:T(8,128)S(1)}) fusion(bf16[1024,128]{1,0:T(8,128)(2,1)S(1)} %bitcast.125, bf16[2,512,128]{1,2,0:T(8,128)(2,1)S(1)} %maximum_select_fusion.1, bf16[2,512,128]{1,2,0:T(8,128)(2,1)S(1)} %maximum_select_fusion.2, s32[1024]{0:T(1024)S(1)} %bitcast.132, pred[1024]{0:T(1024)(128)(4,1)S(1)} %broadcast_compare_fusion, ...), kind=kOutput, calls=%fused_computation.132 | convolution fusion | flops 276298752 | bytes 4998144 | tf_op jit(solution)/shard_map/dot_general | solution.py:151
  126.9 0.6 fusion.1
  127.5 0.9 fusion.57
  128.4 0.7 copy.63
  129.2 0.6 all-to-all-done
  129.8 0.3 reshape.204
  130.1 0.9 copy.50
  131.0 0.9 copy.51
  (68 shorter events, 1.6 us)
Async XLA Ops:
  7.2 6.6 %copy-start.2 = (bf16[2048,32]{0,1:T(8,128)(2,1)S(1)}, bf16[2048,32]{0,1:T(8,128)(2,1)}, u32[]{:S(2)}) copy-start(bf16[2048,32]{0,1:T(8,128)(2,1)} %param.11) | copy-start | bytes 393220
  7.2 6.6 %copy-start.1 = (bf16[2048,32]{0,1:T(8,128)(2,1)S(1)}, bf16[2048,32]{0,1:T(8,128)(2,1)}, u32[]{:S(2)}) copy-start(bf16[2048,32]{0,1:T(8,128)(2,1)} %param.12) | copy-start | bytes 393220
  7.2 6.8 %copy-start.4 = (s32[32,1]{0,1:T(1,128)S(1)}, s32[32,1]{0,1:T(1,128)}, u32[]{:S(2)}) copy-start(s32[32,1]{0,1:T(1,128)} %param.15) | copy-start | bytes 388
  7.2 7.2 %copy-start.3 = (s32[512]{0:T(512)S(1)}, s32[512]{0:T(512)}, u32[]{:S(2)}) copy-start(s32[512]{0:T(512)} %param.13) | copy-start | bytes 6148
  7.2 88.6 %all-gather.3.cloned.1.call-start = ((), (), s32[]{:S(2)}) async-start(), calls=%async_computation.1 | async-start | bytes 9437184 | tf_op jit(solution)/shard_map/all_gather | solution.py:99
  10.5 12.5 %collective-permute-start.4 = (f32[512]{0:T(512)S(1)}, f32[512]{0:T(512)S(1)}, u32[]{:S(2)}, u32[]{:S(2)}) collective-permute-start(f32[512]{0:T(512)S(1)} %get-tuple-element.13), channel_id=1, source_target_pairs={{0,4},{4,0},{8,12},{12,8},{16,20},{20,16},{24,28},{28,24},{1,5},{5... | collective-permute-start | bytes 6152 | tf_op jit(solution)/shard_map/ppermute | solution.py:84
  11.1 14.7 %collective-permute-start.5 = (f32[512]{0:T(512)S(1)}, f32[512]{0:T(512)S(1)}, u32[]{:S(2)}, u32[]{:S(2)}) collective-permute-start(f32[512]{0:T(512)S(1)} %get-tuple-element.13), channel_id=1, source_target_pairs={{0,8},{4,12},{8,0},{12,4},{16,24},{20,28},{24,16},{28,20},{1,9},{5... | collective-permute-start | bytes 6152 | tf_op jit(solution)/shard_map/ppermute | solution.py:84
  13.7 12.5 %collective-permute-start.6 = (f32[512]{0:T(512)S(1)}, f32[512]{0:T(512)S(1)}, u32[]{:S(2)}, u32[]{:S(2)}) collective-permute-start(f32[512]{0:T(512)S(1)} %get-tuple-element.13), channel_id=1, source_target_pairs={{0,12},{4,8},{8,4},{12,0},{16,28},{20,24},{24,20},{28,16},{1,13},{... | collective-permute-start | bytes 6152 | tf_op jit(solution)/shard_map/ppermute | solution.py:84
  13.8 1.6 %collective-permute-start = (bf16[2,2048,32]{1,2,0:T(8,128)(2,1)S(1)}, bf16[2,2048,32]{1,2,0:T(8,128)(2,1)S(1)}, u32[]{:S(2)}, u32[]{:S(2)}) collective-permute-start(bf16[2,2048,32]{1,2,0:T(8,128)(2,1)S(1)} %pad_maximum_fusion.2), channel_id=1, source_target_pairs={{0,4},{4,0},{8,12},{12,8},{16,20},{20,16},{24,28},{28,24},{1,5},{5... | collective-permute-start | bytes 786440 | tf_op jit(solution)/shard_map/ppermute | solution.py:67
  17.1 1.2 copy-start
  18.3 20.3 %copy-start.5 = (s32[512]{0:T(512)S(1)}, s32[512]{0:T(512)}, u32[]{:S(2)}) copy-start(s32[512]{0:T(512)} %param.14) | copy-start | bytes 6148
  19.8 78.7 %collective-permute-start.3 = (bf16[2048,384]{1,0:T(8,128)(2,1)}, bf16[2048,384]{1,0:T(8,128)(2,1)}, u32[]{:S(2)}, u32[]{:S(2)}) collective-permute-start(bf16[2048,384]{1,0:T(8,128)(2,1)} %pad_maximum_fusion), channel_id=1, source_target_pairs={{0,3},{1,2},{2,1},{3,0},{4,7},{5,6},{6,5},{7,4},{8,11},{9,10},{10,... | collective-permute-start | bytes 4718600 | tf_op jit(solution)/shard_map/ppermute | solution.py:73
  22.4 79.4 %collective-permute-start.1 = (bf16[2048,384]{1,0:T(8,128)(2,1)}, bf16[2048,384]{1,0:T(8,128)(2,1)}, u32[]{:S(2)}, u32[]{:S(2)}) collective-permute-start(bf16[2048,384]{1,0:T(8,128)(2,1)} %pad_maximum_fusion), channel_id=1, source_target_pairs={{0,1},{1,0},{2,3},{3,2},{4,5},{5,4},{6,7},{7,6},{8,9},{9,8},{10,11... | collective-permute-start | bytes 4718600 | tf_op jit(solution)/shard_map/ppermute | solution.py:73
  23.1 6.1 %collective-permute-start.7 = (f32[512]{0:T(512)S(1)}, f32[512]{0:T(512)S(1)}, u32[]{:S(2)}, u32[]{:S(2)}) collective-permute-start(f32[512]{0:T(512)S(1)} %get-tuple-element.13), channel_id=1, source_target_pairs={{0,16},{4,20},{8,24},{12,28},{16,0},{20,4},{24,8},{28,12},{1,17},{... | collective-permute-start | bytes 6152 | tf_op jit(solution)/shard_map/ppermute | solution.py:84
  25.7 78.6 %collective-permute-start.2 = (bf16[2048,384]{1,0:T(8,128)(2,1)}, bf16[2048,384]{1,0:T(8,128)(2,1)}, u32[]{:S(2)}, u32[]{:S(2)}) collective-permute-start(bf16[2048,384]{1,0:T(8,128)(2,1)} %pad_maximum_fusion), channel_id=1, source_target_pairs={{0,2},{1,3},{2,0},{3,1},{4,6},{5,7},{6,4},{7,5},{8,10},{9,11},{10,... | collective-permute-start | bytes 4718600 | tf_op jit(solution)/shard_map/ppermute | solution.py:73
  26.2 5.1 %collective-permute-start.8 = (f32[512]{0:T(512)S(1)}, f32[512]{0:T(512)S(1)}, u32[]{:S(2)}, u32[]{:S(2)}) collective-permute-start(f32[512]{0:T(512)S(1)} %get-tuple-element.13), channel_id=1, source_target_pairs={{0,20},{4,16},{8,28},{12,24},{16,4},{20,0},{24,12},{28,8},{1,21},{... | collective-permute-start | bytes 6152 | tf_op jit(solution)/shard_map/ppermute | solution.py:84
  29.1 5.5 %collective-permute-start.9 = (f32[512]{0:T(512)S(1)}, f32[512]{0:T(512)S(1)}, u32[]{:S(2)}, u32[]{:S(2)}) collective-permute-start(f32[512]{0:T(512)S(1)} %get-tuple-element.13), channel_id=1, source_target_pairs={{0,24},{4,28},{8,16},{12,20},{16,8},{20,12},{24,0},{28,4},{1,25},{... | collective-permute-start | bytes 6152 | tf_op jit(solution)/shard_map/ppermute | solution.py:84
  31.3 7.3 %collective-permute-start.10 = (f32[512]{0:T(512)S(1)}, f32[512]{0:T(512)S(1)}, u32[]{:S(2)}, u32[]{:S(2)}) collective-permute-start(f32[512]{0:T(512)S(1)} %get-tuple-element.13), channel_id=1, source_target_pairs={{0,28},{4,24},{8,20},{12,16},{16,12},{20,8},{24,4},{28,0},{1,29},{... | collective-permute-start | bytes 6152 | tf_op jit(solution)/shard_map/ppermute | solution.py:84
  34.6 56.1 %collective-permute-start.11 = (s32[512]{0:T(512)S(1)}, s32[512]{0:T(512)S(1)}, u32[]{:S(2)}, u32[]{:S(2)}) collective-permute-start(s32[512]{0:T(512)S(1)} %broadcast_add_fusion), channel_id=1, source_target_pairs={{0,1},{1,2},{2,3},{4,5},{5,6},{6,7},{8,9},{9,10},{10,11},{12,13},{... | collective-permute-start | bytes 6152 | tf_op jit(solution)/shard_map/ppermute | solution.py:19
  95.8 6.1 %copy-start.6 = (bf16[4096,1024]{1,0:T(8,128)(2,1)S(1)}, bf16[4096,1024]{1,0:T(8,128)(2,1)}, u32[]{:S(2)}) copy-start(bf16[4096,1024]{1,0:T(8,128)(2,1)} %all-gather.3.cloned.1.call-done) | copy-start | bytes 25165828
  107.5 17.5 %collective-permute-start.14 = (bf16[2,512,64]{1,2,0:T(8,128)(2,1)S(1)}, bf16[2,512,64]{1,2,0:T(8,128)(2,1)S(1)}, u32[]{:S(2)}, u32[]{:S(2)}) collective-permute-start(bf16[2,512,64]{1,2,0:T(8,128)(2,1)S(1)} %pad_maximum_fusion.3), channel_id=1, source_target_pairs={{0,8},{4,12},{8,0},{12,4},{16,24},{20,28},{24,16},{28,20},{1,9},{5... | collective-permute-start | bytes 393224 | tf_op jit(solution)/shard_map/ppermute | solution.py:124
  107.6 17.5 %collective-permute-start.12 = (bf16[2,512,64]{1,2,0:T(8,128)(2,1)S(1)}, bf16[2,512,64]{1,2,0:T(8,128)(2,1)S(1)}, u32[]{:S(2)}, u32[]{:S(2)}) collective-permute-start(bf16[2,512,64]{1,2,0:T(8,128)(2,1)S(1)} %pad_maximum_fusion.3), channel_id=1, source_target_pairs={{0,1},{1,2},{2,3},{4,5},{5,6},{6,7},{8,9},{9,10},{10,11},{12,13},{... | collective-permute-start | bytes 393224 | tf_op jit(solution)/shard_map/ppermute | solution.py:19
  111.0 14.1 %collective-permute-start.13 = (bf16[2,512,64]{1,2,0:T(8,128)(2,1)S(1)}, bf16[2,512,64]{1,2,0:T(8,128)(2,1)S(1)}, u32[]{:S(2)}, u32[]{:S(2)}) collective-permute-start(bf16[2,512,64]{1,2,0:T(8,128)(2,1)S(1)} %pad_maximum_fusion.3), channel_id=1, source_target_pairs={{0,9},{1,10},{2,11},{4,13},{5,14},{6,15},{8,1},{9,2},{10,3},{12,5}... | collective-permute-start | bytes 393224 | tf_op jit(solution)/shard_map/ppermute | solution.py:133
  121.5 8.3 %all-to-all-start = ((bf16[4,16,2,512]{3,1,2,0:T(8,128)(2,1)}), bf16[4,16,2,512]{3,1,2,0:T(8,128)(2,1)S(1)}, u32[]{:S(2)}, u32[]{:S(2)}) async-start(bf16[4,16,2,512]{3,1,2,0:T(8,128)(2,1)} %copy.46), calls=%async_computation | async-start | bytes 262144 | tf_op jit(solution)/shard_map/all_to_all | solution.py:190
Sparse Core Ops, SparseCore 0:
  10.7 85.0 all-gather.2

commit v14 on v13

--- a/solution.py
+++ b/solution.py
@@ -78,6 +78,7 @@
     feature_block = tokens_in.shape[1]
     local_gain = lax.dynamic_slice_in_dim(norm_gain, my_gx * feature_block, feature_block, 0)
     local_normed = (local_float * local_gain.astype(jnp.float32)[None, :]).astype(jnp.bfloat16)
+    local_normed, local_float = lax.optimization_barrier((local_normed, local_float))
     local_squares = jnp.sum(local_float * local_float, axis=1)
     square_parts = [local_squares]
     for k in range(1, gx_count):

time: 139 us -> 139 us (level)
    convert_element_type x0 -> x2, other arithmetic: none -> 2.76 us  [the longest x1 1.54 us: shards(): local_float = tokens_in.astype(jnp.float32)]
    reduce_sum x1, other arithmetic: 2.5 us -> 0.21 us  [shards(): local_squares = jnp.sum(local_float * local_float, axis=1)]
    unnamed x19 -> x21, local copies, waits for them, and re-layouts: 2.8 us -> 2.81 us
where the time goes in v14:
time: 139 us
  waiting for transfers between devices  61.7 us (44%)
  starting transfers between devices  28.5 us (21%)
  between operations  14.6 us (11%)
  matrix products  13.6 us (10%)
  other arithmetic  10.9 us (8%)
  local copies, waits for them, and re-layouts  9.7 us (7%)
    ppermute x2, waiting for transfers between devices, shifted(): return lax.ppermute(value, axis, pairs)  51.6 us
    dot_general x4, matrix products, shards(): jnp.einsum('btd,bdc->tc', rows, weights_of, preferred_element_type=jnp.fl...  11 us
    ppermute x7, starting transfers between devices, shards(): lax.ppermute(local_squares, 'gx', partner_route(gx_count, gx_count, k))  9.39 us
    ppermute x2, starting transfers between devices, shifted(): return lax.ppermute(value, axis, pairs)  6.79 us
    ppermute x1, starting transfers between devices, shards(): other = lax.ppermute(half_kv, ('gx', 'gy'), route)  4.79 us
    ppermute x7, waiting for transfers between devices, shards(): lax.ppermute(local_squares, 'gx', partner_route(gx_count, gx_count, k))  4.63 us
    all_gather x1, waiting for transfers between devices, shards(): normed = lax.all_gather(local_normed[rows_of], 'gx', axis=0, tiled=False)  4.34 us
    ppermute x3, starting transfers between devices, shards(): lax.ppermute(local_weights, 'gy', partner_route(gy_count, gy_count, k))  3.7 us
  transfers between devices with their start and end apart: 17, of which 6 were waited for; matrix products, arithmetic and copies ran while one was open for 18% of the time, Pallas kernels for 0%

profile of v14, /device:TPU:0, one launch (start us, length us, event | category | flops | bytes accessed | tf_op | source)
XLA Modules:
  0.0 139.0 jit_solution(13499212338271112836)
XLA Ops:
  7.2 1.5 %convert_element_type.53 = f32[512,1024]{1,0:T(8,128)S(1)} convert(bf16[512,1024]{1,0:T(8,128)(2,1)} %param.8) | non-fusion elementwise | flops 524288 | bytes 3145728 | tf_op jit(solution)/shard_map/convert_element_type | solution.py:76
  8.8 0.7 dynamic-slice_convert_fusion
  9.5 1.2 multiply_convert_fusion
  10.7 0.2 multiply_reduce_fusion
  10.9 0.5 collective-permute-start.4
  11.4 2.6 %collective-permute-start.5 = (f32[512]{0:T(512)S(1)}, f32[512]{0:T(512)S(1)}, u32[]{:S(2)}, u32[]{:S(2)}) collective-permute-start(f32[512]{0:T(512)S(1)} %multiply_reduce_fusion), channel_id=1, source_target_pairs={{0,8},{4,12},{8,0},{12,4},{16,24},{20,28},{24,16},{28,20},{1,9},{5... | collective-permute-start | bytes 6152 | tf_op jit(solution)/shard_map/ppermute | solution.py:85
  14.2 0.2 collective-permute-start
  14.8 0.5 copy.32
  15.3 0.5 collective-permute-done
  15.8 0.5 copy.33
  16.3 1.2 maximum_select_fusion
  17.5 0.3 fusion.96
  17.7 0.9 copy-done.1
  18.7 1.5 %pad_maximum_fusion = bf16[2048,384]{1,0:T(8,128)(2,1)} fusion(bf16[2048,64]{1,0:T(8,128)(2,1)S(1)} %get-tuple-element.19, bf16[2048,64]{1,0:T(8,128)(2,1)S(1)} %get-tuple-element.18, bf16[2048,256]{1,0:T(8,128)(2,1)S(1)} %copy-done.1), kind=kLoop, calls=%fused_computation.29 | loop fusion | flops 4718592 | bytes 3145728 | tf_op jit(solution)/shard_map/concatenate | solution.py:69
  20.2 2.6 %collective-permute-start.3 = (bf16[2048,384]{1,0:T(8,128)(2,1)}, bf16[2048,384]{1,0:T(8,128)(2,1)}, u32[]{:S(2)}, u32[]{:S(2)}) collective-permute-start(bf16[2048,384]{1,0:T(8,128)(2,1)} %pad_maximum_fusion), channel_id=1, source_target_pairs={{0,3},{1,2},{2,1},{3,0},{4,7},{5,6},{6,5},{7,4},{8,11},{9,10},{10,... | collective-permute-start | bytes 4718600 | tf_op jit(solution)/shard_map/ppermute | solution.py:73
  22.8 0.6 collective-permute-start.1
  23.4 2.7 %collective-permute-start.7 = (f32[512]{0:T(512)S(1)}, f32[512]{0:T(512)S(1)}, u32[]{:S(2)}, u32[]{:S(2)}) collective-permute-start(f32[512]{0:T(512)S(1)} %multiply_reduce_fusion), channel_id=1, source_target_pairs={{0,16},{4,20},{8,24},{12,28},{16,0},{20,4},{24,8},{28,12},{1,17},{... | collective-permute-start | bytes 6152 | tf_op jit(solution)/shard_map/ppermute | solution.py:85
  26.1 0.5 collective-permute-start.2
  26.7 2.6 %collective-permute-done.7 = f32[512]{0:T(512)S(1)} collective-permute-done((f32[512]{0:T(512)S(1)}, f32[512]{0:T(512)S(1)}, u32[]{:S(2)}, u32[]{:S(2)}) %collective-permute-start.7) | collective-permute-done | bytes 2080 | tf_op jit(solution)/shard_map/ppermute | solution.py:85
  29.3 2.4 %collective-permute-start.9 = (f32[512]{0:T(512)S(1)}, f32[512]{0:T(512)S(1)}, u32[]{:S(2)}, u32[]{:S(2)}) collective-permute-start(f32[512]{0:T(512)S(1)} %multiply_reduce_fusion), channel_id=1, source_target_pairs={{0,24},{4,28},{8,16},{12,20},{16,8},{20,12},{24,0},{28,4},{1,25},{... | collective-permute-start | bytes 6152 | tf_op jit(solution)/shard_map/ppermute | solution.py:85
  31.7 1.1 collective-permute-start.10
  32.8 2.0 %collective-permute-done.9 = f32[512]{0:T(512)S(1)} collective-permute-done((f32[512]{0:T(512)S(1)}, f32[512]{0:T(512)S(1)}, u32[]{:S(2)}, u32[]{:S(2)}) %collective-permute-start.9) | collective-permute-done | bytes 2080 | tf_op jit(solution)/shard_map/ppermute | solution.py:85
  34.8 3.4 %collective-permute-start.11 = (s32[512]{0:T(512)S(1)}, s32[512]{0:T(512)S(1)}, u32[]{:S(2)}, u32[]{:S(2)}) collective-permute-start(s32[512]{0:T(512)S(1)} %broadcast_add_fusion), channel_id=1, source_target_pairs={{0,1},{1,2},{2,3},{4,5},{5,6},{6,7},{8,9},{9,10},{10,11},{12,13},{... | collective-permute-start | bytes 6152 | tf_op jit(solution)/shard_map/ppermute | solution.py:19
  38.2 0.5 copy.38
  38.9 0.6 gather_fusion
  39.4 51.6 %collective-permute-done.11 = s32[512]{0:T(512)S(1)} collective-permute-done((s32[512]{0:T(512)S(1)}, s32[512]{0:T(512)S(1)}, u32[]{:S(2)}, u32[]{:S(2)}) %collective-permute-start.11) | collective-permute-done | bytes 2080 | tf_op jit(solution)/shard_map/ppermute | solution.py:19
  91.4 0.2 copy.40
  91.6 4.3 %all-gather.3.cloned.1.call-done = bf16[4096,1024]{1,0:T(8,128)(2,1)} async-done(((bf16[512,1024]{1,0:T(8,128)(2,1)}), bf16[4096,1024]{1,0:T(8,128)(2,1)}) %all-gather.3.cloned.1.call-update) | async-done | bytes 8388624 | tf_op jit(solution)/shard_map/all_gather | solution.py:100
  95.9 2.8 %fusion.23 = f32[512,384]{0,1:T(8,128)S(1)} fusion(bf16[2,1024,64]{1,2,0:T(8,128)(2,1)S(1)} %copy.40, bf16[2,1024,64]{1,2,0:T(8,128)(2,1)S(1)} %copy.39, bf16[2,1024,256]{1,2,0:T(8,128)(2,1)S(1)} %copy.38, bf16[4,2,512,1024]{3,2,1,0:T(8,128)(2,1)} %bitcast.142, s32[]{:T(128)S(6)} %select_n.158), kind=kOutput, calls=%fused_computation.30 | convolution fusion | flops 810024960 | bytes 4456452 | tf_op jit(solution)/shard_map/btd,bdc->tc/dot_general | solution.py:109
  98.7 3.3 %fusion.34 = f32[512,384]{0,1:T(8,128)S(1)} fusion(bf16[2,1024,384]{2,1,0:T(8,128)(2,1)} %bitcast.20, bf16[4,2,512,1024]{3,2,1,0:T(8,128)(2,1)} %bitcast.143, s32[]{:T(128)S(6)} %select_n.165), kind=kOutput, calls=%fused_computation.33 | convolution fusion | flops 805306368 | bytes 4456452 | tf_op jit(solution)/shard_map/btd,bdc->tc/dot_general | solution.py:109
  102.0 2.5 %fusion.40 = f32[512,384]{0,1:T(8,128)S(1)} fusion(f32[512,384]{0,1:T(8,128)S(1)} %fusion.23, bf16[2,1024,384]{2,1,0:T(8,128)(2,1)} %bitcast.14, bf16[4,2,512,1024]{3,2,1,0:T(8,128)(2,1)S(1)} %bitcast.144, s32[]{:T(128)S(6)} %select_n.163), kind=kOutput, calls=%fused_computation.35 | convolution fusion | flops 805502976 | bytes 5242884 | tf_op jit(solution)/shard_map/btd,bdc->tc/dot_general | solution.py:109
  104.5 2.5 %fusion.46 = f32[512,384]{0,1:T(8,128)S(1)} fusion(f32[512,384]{0,1:T(8,128)S(1)} %fusion.34, f32[512,384]{0,1:T(8,128)S(1)} %fusion.40, bf16[2,1024,384]{2,1,0:T(8,128)(2,1)} %bitcast.17, bf16[4,2,512,1024]{3,2,1,0:T(8,128)(2,1)S(1)} %bitcast.145, s32[]{:T(128)S(6)} %select_n.164, f32[512]{0:T(512)S(1)} %add_rsqrt_fusion), kind=kOutput, calls=%fused_computation.37 | convolution fusion | flops 805896192 | bytes 6031364 | tf_op jit(solution)/shard_map/btd,bdc->tc/dot_general | solution.py:109
  107.0 0.6 fusion.83
  107.7 3.4 %collective-permute-start.12 = (bf16[2,512,64]{1,2,0:T(8,128)(2,1)S(1)}, bf16[2,512,64]{1,2,0:T(8,128)(2,1)S(1)}, u32[]{:S(2)}, u32[]{:S(2)}) collective-permute-start(bf16[2,512,64]{1,2,0:T(8,128)(2,1)S(1)} %pad_maximum_fusion.3), channel_id=1, source_target_pairs={{0,1},{1,2},{2,3},{4,5},{5,6},{6,7},{8,9},{9,10},{10,11},{12,13},{... | collective-permute-start | bytes 393224 | tf_op jit(solution)/shard_map/ppermute | solution.py:19
  111.2 4.8 %collective-permute-start.13 = (bf16[2,512,64]{1,2,0:T(8,128)(2,1)S(1)}, bf16[2,512,64]{1,2,0:T(8,128)(2,1)S(1)}, u32[]{:S(2)}, u32[]{:S(2)}) collective-permute-start(bf16[2,512,64]{1,2,0:T(8,128)(2,1)S(1)} %pad_maximum_fusion.3), channel_id=1, source_target_pairs={{0,9},{1,10},{2,11},{4,13},{5,14},{6,15},{8,1},{9,2},{10,3},{12,5}... | collective-permute-start | bytes 393224 | tf_op jit(solution)/shard_map/ppermute | solution.py:134
  116.1 2.6 %fusion.62 = bf16[512,256]{0,1:T(8,128)(2,1)S(1)} fusion(f32[512,384]{0,1:T(8,128)S(1)} %fusion.46, f32[512,1]{0,1:T(1,128)S(1)} %get-tuple-element.22, f32[512,255]{0,1:T(8,128)S(1)} %get-tuple-element.26, f32[512,255]{0,1:T(8,128)S(1)} %get-tuple-element.25, f32[512,1]{0,1:T(1,128)S(1)} %get-tuple-element.21, f32[256]{0:T(256)S(1)} %multiply_power_fusion, ...), kind=kLoop, calls=%fused_computation.48 | loop fusion | flops 1310720 | bytes 1838336 | tf_op jit(solution)/shard_map/convert_element_type | solution.py:120
  119.1 0.2 reshape.200
  119.5 1.5 %scatter_fusion = bf16[64,2,512]{2,1,0:T(2,128)(2,1)S(1)} fusion(bf16[64,2,512]{2,1,0:T(2,128)(2,1)S(1)} %broadcast_in_dim.44, s32[32]{0:T(128)S(1)} %fusion.91, bf16[32,2,512]{2,1,0:T(2,128)(2,1)S(1)} %copy.45), kind=kCustom, calls=%fused_computation.1 | custom fusion | bytes 196736 | tf_op jit(solution)/shard_map/scatter | solution.py:188
  121.0 0.7 copy.46
  121.6 3.5 %all-to-all-start = ((bf16[4,16,2,512]{3,1,2,0:T(8,128)(2,1)}), bf16[4,16,2,512]{3,1,2,0:T(8,128)(2,1)S(1)}, u32[]{:S(2)}, u32[]{:S(2)}) async-start(bf16[4,16,2,512]{3,1,2,0:T(8,128)(2,1)} %copy.46), calls=%async_computation | async-start | bytes 262144 | tf_op jit(solution)/shard_map/all_to_all | solution.py:191
  125.3 1.8 %fusion.100 = (f32[1024]{0:T(1024)S(1)}, f32[1024,1024]{0,1:T(8,128)S(1)}) fusion(bf16[1024,128]{1,0:T(8,128)(2,1)S(1)} %bitcast.125, bf16[2,512,128]{1,2,0:T(8,128)(2,1)S(1)} %maximum_select_fusion.1, bf16[2,512,128]{1,2,0:T(8,128)(2,1)S(1)} %maximum_select_fusion.2, s32[1024]{0:T(1024)S(1)} %bitcast.132, pred[1024]{0:T(1024)(128)(4,1)S(1)} %broadcast_compare_fusion, ...), kind=kOutput, calls=%fused_computation.130 | convolution fusion | flops 276298752 | bytes 4998144 | tf_op jit(solution)/shard_map/dot_general | solution.py:152
  127.1 0.6 fusion.1
  127.7 0.9 fusion.55
  128.6 0.7 copy.63
  129.4 0.6 all-to-all-done
  130.0 0.3 reshape.204
  130.3 0.9 copy.50
  131.2 0.9 copy.51
  (72 shorter events, 1.9 us)
Async XLA Ops:
  7.2 2.3 %copy-start = (bf16[512,1024]{1,0:T(8,128)(2,1)S(1)}, bf16[512,1024]{1,0:T(8,128)(2,1)}, u32[]{:S(2)}) copy-start(bf16[512,1024]{1,0:T(8,128)(2,1)} %param.8) | copy-start | bytes 3145732
  7.2 88.8 %all-gather.3.cloned.1.call-start = ((), (), s32[]{:S(2)}) async-start(), calls=%async_computation.1 | async-start | bytes 9437184 | tf_op jit(solution)/shard_map/all_gather | solution.py:100
  10.7 3.5 %copy-start.2 = (bf16[2048,32]{0,1:T(8,128)(2,1)S(1)}, bf16[2048,32]{0,1:T(8,128)(2,1)}, u32[]{:S(2)}) copy-start(bf16[2048,32]{0,1:T(8,128)(2,1)} %param.12) | copy-start | bytes 393220
  10.7 3.5 %copy-start.3 = (bf16[2048,32]{0,1:T(8,128)(2,1)S(1)}, bf16[2048,32]{0,1:T(8,128)(2,1)}, u32[]{:S(2)}) copy-start(bf16[2048,32]{0,1:T(8,128)(2,1)} %param.11) | copy-start | bytes 393220
  10.7 3.7 %copy-start.5 = (s32[32,1]{0,1:T(1,128)S(1)}, s32[32,1]{0,1:T(1,128)}, u32[]{:S(2)}) copy-start(s32[32,1]{0,1:T(1,128)} %param.15) | copy-start | bytes 388
  10.7 4.1 %copy-start.4 = (s32[512]{0:T(512)S(1)}, s32[512]{0:T(512)}, u32[]{:S(2)}) copy-start(s32[512]{0:T(512)} %param.13) | copy-start | bytes 6148
  10.9 12.5 %collective-permute-start.4 = (f32[512]{0:T(512)S(1)}, f32[512]{0:T(512)S(1)}, u32[]{:S(2)}, u32[]{:S(2)}) collective-permute-start(f32[512]{0:T(512)S(1)} %multiply_reduce_fusion), channel_id=1, source_target_pairs={{0,4},{4,0},{8,12},{12,8},{16,20},{20,16},{24,28},{28,24},{1,5},{5... | collective-permute-start | bytes 6152 | tf_op jit(solution)/shard_map/ppermute | solution.py:85
  11.4 14.7 %collective-permute-start.5 = (f32[512]{0:T(512)S(1)}, f32[512]{0:T(512)S(1)}, u32[]{:S(2)}, u32[]{:S(2)}) collective-permute-start(f32[512]{0:T(512)S(1)} %multiply_reduce_fusion), channel_id=1, source_target_pairs={{0,8},{4,12},{8,0},{12,4},{16,24},{20,28},{24,16},{28,20},{1,9},{5... | collective-permute-start | bytes 6152 | tf_op jit(solution)/shard_map/ppermute | solution.py:85
  14.1 12.5 %collective-permute-start.6 = (f32[512]{0:T(512)S(1)}, f32[512]{0:T(512)S(1)}, u32[]{:S(2)}, u32[]{:S(2)}) collective-permute-start(f32[512]{0:T(512)S(1)} %multiply_reduce_fusion), channel_id=1, source_target_pairs={{0,12},{4,8},{8,4},{12,0},{16,28},{20,24},{24,20},{28,16},{1,13},{... | collective-permute-start | bytes 6152 | tf_op jit(solution)/shard_map/ppermute | solution.py:85
  14.2 1.6 %collective-permute-start = (bf16[2,2048,32]{1,2,0:T(8,128)(2,1)S(1)}, bf16[2,2048,32]{1,2,0:T(8,128)(2,1)S(1)}, u32[]{:S(2)}, u32[]{:S(2)}) collective-permute-start(bf16[2,2048,32]{1,2,0:T(8,128)(2,1)S(1)} %pad_maximum_fusion.2), channel_id=1, source_target_pairs={{0,4},{4,0},{8,12},{12,8},{16,20},{20,16},{24,28},{28,24},{1,5},{5... | collective-permute-start | bytes 786440 | tf_op jit(solution)/shard_map/ppermute | solution.py:67
  17.4 1.2 copy-start.1
  18.7 20.1 %copy-start.6 = (s32[512]{0:T(512)S(1)}, s32[512]{0:T(512)}, u32[]{:S(2)}) copy-start(s32[512]{0:T(512)} %param.14) | copy-start | bytes 6148
  20.2 78.5 %collective-permute-start.3 = (bf16[2048,384]{1,0:T(8,128)(2,1)}, bf16[2048,384]{1,0:T(8,128)(2,1)}, u32[]{:S(2)}, u32[]{:S(2)}) collective-permute-start(bf16[2048,384]{1,0:T(8,128)(2,1)} %pad_maximum_fusion), channel_id=1, source_target_pairs={{0,3},{1,2},{2,1},{3,0},{4,7},{5,6},{6,5},{7,4},{8,11},{9,10},{10,... | collective-permute-start | bytes 4718600 | tf_op jit(solution)/shard_map/ppermute | solution.py:73
  22.8 79.2 %collective-permute-start.1 = (bf16[2048,384]{1,0:T(8,128)(2,1)}, bf16[2048,384]{1,0:T(8,128)(2,1)}, u32[]{:S(2)}, u32[]{:S(2)}) collective-permute-start(bf16[2048,384]{1,0:T(8,128)(2,1)} %pad_maximum_fusion), channel_id=1, source_target_pairs={{0,1},{1,0},{2,3},{3,2},{4,5},{5,4},{6,7},{7,6},{8,9},{9,8},{10,11... | collective-permute-start | bytes 4718600 | tf_op jit(solution)/shard_map/ppermute | solution.py:73
  23.4 5.8 %collective-permute-start.7 = (f32[512]{0:T(512)S(1)}, f32[512]{0:T(512)S(1)}, u32[]{:S(2)}, u32[]{:S(2)}) collective-permute-start(f32[512]{0:T(512)S(1)} %multiply_reduce_fusion), channel_id=1, source_target_pairs={{0,16},{4,20},{8,24},{12,28},{16,0},{20,4},{24,8},{28,12},{1,17},{... | collective-permute-start | bytes 6152 | tf_op jit(solution)/shard_map/ppermute | solution.py:85
  26.1 78.4 %collective-permute-start.2 = (bf16[2048,384]{1,0:T(8,128)(2,1)}, bf16[2048,384]{1,0:T(8,128)(2,1)}, u32[]{:S(2)}, u32[]{:S(2)}) collective-permute-start(bf16[2048,384]{1,0:T(8,128)(2,1)} %pad_maximum_fusion), channel_id=1, source_target_pairs={{0,2},{1,3},{2,0},{3,1},{4,6},{5,7},{6,4},{7,5},{8,10},{9,11},{10,... | collective-permute-start | bytes 4718600 | tf_op jit(solution)/shard_map/ppermute | solution.py:73
  26.6 5.1 %collective-permute-start.8 = (f32[512]{0:T(512)S(1)}, f32[512]{0:T(512)S(1)}, u32[]{:S(2)}, u32[]{:S(2)}) collective-permute-start(f32[512]{0:T(512)S(1)} %multiply_reduce_fusion), channel_id=1, source_target_pairs={{0,20},{4,16},{8,28},{12,24},{16,4},{20,0},{24,12},{28,8},{1,21},{... | collective-permute-start | bytes 6152 | tf_op jit(solution)/shard_map/ppermute | solution.py:85
  29.3 5.5 %collective-permute-start.9 = (f32[512]{0:T(512)S(1)}, f32[512]{0:T(512)S(1)}, u32[]{:S(2)}, u32[]{:S(2)}) collective-permute-start(f32[512]{0:T(512)S(1)} %multiply_reduce_fusion), channel_id=1, source_target_pairs={{0,24},{4,28},{8,16},{12,20},{16,8},{20,12},{24,0},{28,4},{1,25},{... | collective-permute-start | bytes 6152 | tf_op jit(solution)/shard_map/ppermute | solution.py:85
  31.7 7.1 %collective-permute-start.10 = (f32[512]{0:T(512)S(1)}, f32[512]{0:T(512)S(1)}, u32[]{:S(2)}, u32[]{:S(2)}) collective-permute-start(f32[512]{0:T(512)S(1)} %multiply_reduce_fusion), channel_id=1, source_target_pairs={{0,28},{4,24},{8,20},{12,16},{16,12},{20,8},{24,4},{28,0},{1,29},{... | collective-permute-start | bytes 6152 | tf_op jit(solution)/shard_map/ppermute | solution.py:85
  34.8 56.3 %collective-permute-start.11 = (s32[512]{0:T(512)S(1)}, s32[512]{0:T(512)S(1)}, u32[]{:S(2)}, u32[]{:S(2)}) collective-permute-start(s32[512]{0:T(512)S(1)} %broadcast_add_fusion), channel_id=1, source_target_pairs={{0,1},{1,2},{2,3},{4,5},{5,6},{6,7},{8,9},{9,10},{10,11},{12,13},{... | collective-permute-start | bytes 6152 | tf_op jit(solution)/shard_map/ppermute | solution.py:19
  95.9 6.1 %copy-start.7 = (bf16[4096,1024]{1,0:T(8,128)(2,1)S(1)}, bf16[4096,1024]{1,0:T(8,128)(2,1)}, u32[]{:S(2)}) copy-start(bf16[4096,1024]{1,0:T(8,128)(2,1)} %all-gather.3.cloned.1.call-done) | copy-start | bytes 25165828
  107.7 17.5 %collective-permute-start.14 = (bf16[2,512,64]{1,2,0:T(8,128)(2,1)S(1)}, bf16[2,512,64]{1,2,0:T(8,128)(2,1)S(1)}, u32[]{:S(2)}, u32[]{:S(2)}) collective-permute-start(bf16[2,512,64]{1,2,0:T(8,128)(2,1)S(1)} %pad_maximum_fusion.3), channel_id=1, source_target_pairs={{0,8},{4,12},{8,0},{12,4},{16,24},{20,28},{24,16},{28,20},{1,9},{5... | collective-permute-start | bytes 393224 | tf_op jit(solution)/shard_map/ppermute | solution.py:125
  107.7 17.5 %collective-permute-start.12 = (bf16[2,512,64]{1,2,0:T(8,128)(2,1)S(1)}, bf16[2,512,64]{1,2,0:T(8,128)(2,1)S(1)}, u32[]{:S(2)}, u32[]{:S(2)}) collective-permute-start(bf16[2,512,64]{1,2,0:T(8,128)(2,1)S(1)} %pad_maximum_fusion.3), channel_id=1, source_target_pairs={{0,1},{1,2},{2,3},{4,5},{5,6},{6,7},{8,9},{9,10},{10,11},{12,13},{... | collective-permute-start | bytes 393224 | tf_op jit(solution)/shard_map/ppermute | solution.py:19
  111.2 14.1 %collective-permute-start.13 = (bf16[2,512,64]{1,2,0:T(8,128)(2,1)S(1)}, bf16[2,512,64]{1,2,0:T(8,128)(2,1)S(1)}, u32[]{:S(2)}, u32[]{:S(2)}) collective-permute-start(bf16[2,512,64]{1,2,0:T(8,128)(2,1)S(1)} %pad_maximum_fusion.3), channel_id=1, source_target_pairs={{0,9},{1,10},{2,11},{4,13},{5,14},{6,15},{8,1},{9,2},{10,3},{12,5}... | collective-permute-start | bytes 393224 | tf_op jit(solution)/shard_map/ppermute | solution.py:134
  121.6 8.3 %all-to-all-start = ((bf16[4,16,2,512]{3,1,2,0:T(8,128)(2,1)}), bf16[4,16,2,512]{3,1,2,0:T(8,128)(2,1)S(1)}, u32[]{:S(2)}, u32[]{:S(2)}) async-start(bf16[4,16,2,512]{3,1,2,0:T(8,128)(2,1)} %copy.46), calls=%async_computation | async-start | bytes 262144 | tf_op jit(solution)/shard_map/all_to_all | solution.py:191
Sparse Core Ops, SparseCore 0:
  10.8 85.0 all-gather.2

commit v15 on v14

--- a/solution.py
+++ b/solution.py
@@ -121,18 +121,11 @@
         half_kv = jnp.stack([key_half, value_half])
         kv_halves.append(lax.dynamic_slice_in_dim(half_kv, (spot % 2) * quarter, quarter, 2))
         low_half = (spot // 2) % 2 == 0
-        window_list = [
-            joined(half_kv, lax.ppermute(half_kv, "gx", partner_route(gx_count, quarters, 2)), low_half)
-        ]
+        other_half = lax.ppermute(half_kv, "gx", partner_route(gx_count, quarters, 2))
+        head_now = joined(half_kv, other_half, low_half)
+        window_list = [head_now]
         for shift_by in range(1, span_count + 1):
-            route = []
-            for i in range(gx_count):
-                peer = i - i % quarters + ((i % quarters) ^ 2)
-                for j in range(gy_count - shift_by):
-                    route.append((i * gy_count + j, peer * gy_count + j + shift_by))
-            same = shifted(half_kv, "gy", shift_by)
-            other = lax.ppermute(half_kv, ("gx", "gy"), route)
-            window_list.insert(0, joined(same, other, low_half))
+            window_list.insert(0, shifted(head_now, "gy", shift_by))
         held = jnp.concatenate(window_list, axis=1)
         head_halves.append(held.reshape(2, span_count + 1, half_rows, HD))
     queries = jnp.concatenate(query_halves, axis=0)

time: 139 us -> 140 us (level)
  waiting for transfers between devices: 61.7 us -> 67.4 us
  starting transfers between devices: 28.5 us -> 23.7 us
    ppermute x1, waiting for transfers between devices: 0.01 us -> 5.55 us  [shards(): lax.ppermute(half_kv, 'gx', partner_route(gx_count, quarters, 2))]
    ppermute x1 -> x0, starting transfers between devices: 4.79 us -> none  [shards(): other = lax.ppermute(half_kv, ('gx', 'gy'), route)]
  transfers between devices with their start and end apart: 17 -> 16, of which waited for: 6 -> 7; matrix products, arithmetic and copies ran while one was open for 18% -> 17% of each run, Pallas kernels for 0% -> 0%
where the time goes in v15:
time: 140 us
  waiting for transfers between devices  67.4 us (48%)
  starting transfers between devices  23.7 us (17%)
  between operations  14.6 us (10%)
  matrix products  13.6 us (10%)
  other arithmetic  10.8 us (8%)
  local copies, waits for them, and re-layouts  9.73 us (7%)
    ppermute x2, waiting for transfers between devices, shifted(): return lax.ppermute(value, axis, pairs)  51.6 us
    dot_general x4, matrix products, shards(): jnp.einsum('btd,bdc->tc', rows, weights_of, preferred_element_type=jnp.fl...  11 us
    ppermute x7, starting transfers between devices, shards(): lax.ppermute(local_squares, 'gx', partner_route(gx_count, gx_count, k))  9.39 us
    ppermute x2, starting transfers between devices, shifted(): return lax.ppermute(value, axis, pairs)  6.79 us
    ppermute x1, waiting for transfers between devices, shards(): lax.ppermute(half_kv, 'gx', partner_route(gx_count, quarters, 2))  5.55 us
    ppermute x7, waiting for transfers between devices, shards(): lax.ppermute(local_squares, 'gx', partner_route(gx_count, gx_count, k))  4.64 us
    all_gather x1, waiting for transfers between devices, shards(): normed = lax.all_gather(local_normed[rows_of], 'gx', axis=0, tiled=False)  4.35 us
    ppermute x3, starting transfers between devices, shards(): lax.ppermute(local_weights, 'gy', partner_route(gy_count, gy_count, k))  3.7 us
  transfers between devices with their start and end apart: 16, of which 7 were waited for; matrix products, arithmetic and copies ran while one was open for 17% of the time, Pallas kernels for 0%

profile of v15, /device:TPU:0, one launch (start us, length us, event | category | flops | bytes accessed | tf_op | source)
XLA Modules:
  0.0 139.8 jit_solution(11057411894342322586)
XLA Ops:
  7.2 1.5 %convert_element_type.53 = f32[512,1024]{1,0:T(8,128)S(1)} convert(bf16[512,1024]{1,0:T(8,128)(2,1)} %param.8) | non-fusion elementwise | flops 524288 | bytes 3145728 | tf_op jit(solution)/shard_map/convert_element_type | solution.py:76
  8.8 0.7 dynamic-slice_convert_fusion
  9.5 1.2 multiply_convert_fusion
  10.7 0.2 multiply_reduce_fusion
  10.9 0.5 collective-permute-start.4
  11.4 2.6 %collective-permute-start.5 = (f32[512]{0:T(512)S(1)}, f32[512]{0:T(512)S(1)}, u32[]{:S(2)}, u32[]{:S(2)}) collective-permute-start(f32[512]{0:T(512)S(1)} %multiply_reduce_fusion), channel_id=1, source_target_pairs={{0,8},{4,12},{8,0},{12,4},{16,24},{20,28},{24,16},{28,20},{1,9},{5... | collective-permute-start | bytes 6152 | tf_op jit(solution)/shard_map/ppermute | solution.py:85
  14.8 0.5 copy.32
  15.3 0.5 collective-permute-done
  15.8 0.5 copy.33
  16.3 1.2 maximum_select_fusion
  17.5 0.3 fusion.93
  17.7 0.9 copy-done.1
  18.7 1.5 %pad_maximum_fusion = bf16[2048,384]{1,0:T(8,128)(2,1)} fusion(bf16[2048,64]{1,0:T(8,128)(2,1)S(1)} %get-tuple-element.19, bf16[2048,64]{1,0:T(8,128)(2,1)S(1)} %get-tuple-element.18, bf16[2048,256]{1,0:T(8,128)(2,1)S(1)} %copy-done.1), kind=kLoop, calls=%fused_computation.29 | loop fusion | flops 4718592 | bytes 3145728 | tf_op jit(solution)/shard_map/concatenate | solution.py:69
  20.2 2.6 %collective-permute-start.3 = (bf16[2048,384]{1,0:T(8,128)(2,1)}, bf16[2048,384]{1,0:T(8,128)(2,1)}, u32[]{:S(2)}, u32[]{:S(2)}) collective-permute-start(bf16[2048,384]{1,0:T(8,128)(2,1)} %pad_maximum_fusion), channel_id=1, source_target_pairs={{0,3},{1,2},{2,1},{3,0},{4,7},{5,6},{6,5},{7,4},{8,11},{9,10},{10,... | collective-permute-start | bytes 4718600 | tf_op jit(solution)/shard_map/ppermute | solution.py:73
  22.8 0.6 collective-permute-start.1
  23.4 2.7 %collective-permute-start.7 = (f32[512]{0:T(512)S(1)}, f32[512]{0:T(512)S(1)}, u32[]{:S(2)}, u32[]{:S(2)}) collective-permute-start(f32[512]{0:T(512)S(1)} %multiply_reduce_fusion), channel_id=1, source_target_pairs={{0,16},{4,20},{8,24},{12,28},{16,0},{20,4},{24,8},{28,12},{1,17},{... | collective-permute-start | bytes 6152 | tf_op jit(solution)/shard_map/ppermute | solution.py:85
  26.1 0.5 collective-permute-start.2
  26.7 2.6 %collective-permute-done.7 = f32[512]{0:T(512)S(1)} collective-permute-done((f32[512]{0:T(512)S(1)}, f32[512]{0:T(512)S(1)}, u32[]{:S(2)}, u32[]{:S(2)}) %collective-permute-start.7) | collective-permute-done | bytes 2080 | tf_op jit(solution)/shard_map/ppermute | solution.py:85
  29.3 2.3 %collective-permute-start.9 = (f32[512]{0:T(512)S(1)}, f32[512]{0:T(512)S(1)}, u32[]{:S(2)}, u32[]{:S(2)}) collective-permute-start(f32[512]{0:T(512)S(1)} %multiply_reduce_fusion), channel_id=1, source_target_pairs={{0,24},{4,28},{8,16},{12,20},{16,8},{20,12},{24,0},{28,4},{1,25},{... | collective-permute-start | bytes 6152 | tf_op jit(solution)/shard_map/ppermute | solution.py:85
  31.7 1.1 collective-permute-start.10
  32.8 2.0 %collective-permute-done.9 = f32[512]{0:T(512)S(1)} collective-permute-done((f32[512]{0:T(512)S(1)}, f32[512]{0:T(512)S(1)}, u32[]{:S(2)}, u32[]{:S(2)}) %collective-permute-start.9) | collective-permute-done | bytes 2080 | tf_op jit(solution)/shard_map/ppermute | solution.py:85
  34.8 3.4 %collective-permute-start.11 = (s32[512]{0:T(512)S(1)}, s32[512]{0:T(512)S(1)}, u32[]{:S(2)}, u32[]{:S(2)}) collective-permute-start(s32[512]{0:T(512)S(1)} %broadcast_add_fusion), channel_id=1, source_target_pairs={{0,1},{1,2},{2,3},{4,5},{5,6},{6,7},{8,9},{9,10},{10,11},{12,13},{... | collective-permute-start | bytes 6152 | tf_op jit(solution)/shard_map/ppermute | solution.py:19
  38.2 0.5 copy.38
  38.9 0.6 gather_fusion
  39.4 51.6 %collective-permute-done.11 = s32[512]{0:T(512)S(1)} collective-permute-done((s32[512]{0:T(512)S(1)}, s32[512]{0:T(512)S(1)}, u32[]{:S(2)}, u32[]{:S(2)}) %collective-permute-start.11) | collective-permute-done | bytes 2080 | tf_op jit(solution)/shard_map/ppermute | solution.py:19
  91.2 0.2 copy.39
  91.4 0.2 copy.40
  91.6 4.3 %all-gather.3.cloned.1.call-done = bf16[4096,1024]{1,0:T(8,128)(2,1)} async-done(((bf16[512,1024]{1,0:T(8,128)(2,1)}), bf16[4096,1024]{1,0:T(8,128)(2,1)}) %all-gather.3.cloned.1.call-update) | async-done | bytes 8388624 | tf_op jit(solution)/shard_map/all_gather | solution.py:100
  95.9 2.8 %fusion.23 = f32[512,384]{0,1:T(8,128)S(1)} fusion(bf16[2,1024,64]{1,2,0:T(8,128)(2,1)S(1)} %copy.40, bf16[2,1024,64]{1,2,0:T(8,128)(2,1)S(1)} %copy.39, bf16[2,1024,256]{1,2,0:T(8,128)(2,1)S(1)} %copy.38, bf16[4,2,512,1024]{3,2,1,0:T(8,128)(2,1)} %bitcast.140, s32[]{:T(128)S(6)} %select_n.154), kind=kOutput, calls=%fused_computation.30 | convolution fusion | flops 810024960 | bytes 4456452 | tf_op jit(solution)/shard_map/btd,bdc->tc/dot_general | solution.py:109
  98.7 3.3 %fusion.34 = f32[512,384]{0,1:T(8,128)S(1)} fusion(bf16[2,1024,384]{2,1,0:T(8,128)(2,1)} %bitcast.20, bf16[4,2,512,1024]{3,2,1,0:T(8,128)(2,1)} %bitcast.141, s32[]{:T(128)S(6)} %select_n.161), kind=kOutput, calls=%fused_computation.33 | convolution fusion | flops 805306368 | bytes 4456452 | tf_op jit(solution)/shard_map/btd,bdc->tc/dot_general | solution.py:109
  102.0 2.5 %fusion.40 = f32[512,384]{0,1:T(8,128)S(1)} fusion(f32[512,384]{0,1:T(8,128)S(1)} %fusion.23, bf16[2,1024,384]{2,1,0:T(8,128)(2,1)} %bitcast.14, bf16[4,2,512,1024]{3,2,1,0:T(8,128)(2,1)S(1)} %bitcast.142, s32[]{:T(128)S(6)} %select_n.159), kind=kOutput, calls=%fused_computation.35 | convolution fusion | flops 805502976 | bytes 5242884 | tf_op jit(solution)/shard_map/btd,bdc->tc/dot_general | solution.py:109
  104.5 2.5 %fusion.46 = f32[512,384]{0,1:T(8,128)S(1)} fusion(f32[512,384]{0,1:T(8,128)S(1)} %fusion.34, f32[512,384]{0,1:T(8,128)S(1)} %fusion.40, bf16[2,1024,384]{2,1,0:T(8,128)(2,1)} %bitcast.17, bf16[4,2,512,1024]{3,2,1,0:T(8,128)(2,1)S(1)} %bitcast.143, s32[]{:T(128)S(6)} %select_n.160, f32[512]{0:T(512)S(1)} %add_rsqrt_fusion), kind=kOutput, calls=%fused_computation.37 | convolution fusion | flops 805896192 | bytes 6031364 | tf_op jit(solution)/shard_map/btd,bdc->tc/dot_general | solution.py:109
  107.1 0.6 fusion.80
  107.8 5.5 %collective-permute-done.12 = bf16[2,512,64]{1,2,0:T(8,128)(2,1)S(1)} collective-permute-done((bf16[2,512,64]{1,2,0:T(8,128)(2,1)S(1)}, bf16[2,512,64]{1,2,0:T(8,128)(2,1)S(1)}, u32[]{:S(2)}, u32[]{:S(2)}) %collective-permute-start.12) | collective-permute-done | bytes 131104 | tf_op jit(solution)/shard_map/ppermute | solution.py:124
  113.4 3.4 %collective-permute-start.13 = (bf16[2,512,128]{1,2,0:T(8,128)(2,1)S(1)}, bf16[2,512,128]{1,2,0:T(8,128)(2,1)S(1)}, u32[]{:S(2)}, u32[]{:S(2)}) collective-permute-start(bf16[2,512,128]{1,2,0:T(8,128)(2,1)S(1)} %maximum_select_fusion.1), channel_id=1, source_target_pairs={{0,1},{1,2},{2,3},{4,5},{5,6},{6,7},{8,9},{9,10},{10,11},{12,13},{... | collective-permute-start | bytes 786440 | tf_op jit(solution)/shard_map/ppermute | solution.py:19
  116.9 2.6 %fusion.62 = bf16[512,256]{0,1:T(8,128)(2,1)S(1)} fusion(f32[512,384]{0,1:T(8,128)S(1)} %fusion.46, f32[512,1]{0,1:T(1,128)S(1)} %get-tuple-element.22, f32[512,255]{0,1:T(8,128)S(1)} %get-tuple-element.26, f32[512,255]{0,1:T(8,128)S(1)} %get-tuple-element.25, f32[512,1]{0,1:T(1,128)S(1)} %get-tuple-element.21, f32[256]{0:T(256)S(1)} %multiply_power_fusion, ...), kind=kLoop, calls=%fused_computation.48 | loop fusion | flops 1310720 | bytes 1838336 | tf_op jit(solution)/shard_map/convert_element_type | solution.py:120
  119.9 0.2 reshape.200
  120.3 1.5 %scatter_fusion = bf16[64,2,512]{2,1,0:T(2,128)(2,1)S(1)} fusion(bf16[64,2,512]{2,1,0:T(2,128)(2,1)S(1)} %broadcast_in_dim.44, s32[32]{0:T(128)S(1)} %fusion.88, bf16[32,2,512]{2,1,0:T(2,128)(2,1)S(1)} %copy.45), kind=kCustom, calls=%fused_computation.1 | custom fusion | bytes 196736 | tf_op jit(solution)/shard_map/scatter | solution.py:181
  121.8 0.7 copy.46
  122.5 3.5 %all-to-all-start = ((bf16[4,16,2,512]{3,1,2,0:T(8,128)(2,1)}), bf16[4,16,2,512]{3,1,2,0:T(8,128)(2,1)S(1)}, u32[]{:S(2)}, u32[]{:S(2)}) async-start(bf16[4,16,2,512]{3,1,2,0:T(8,128)(2,1)} %copy.46), calls=%async_computation | async-start | bytes 262144 | tf_op jit(solution)/shard_map/all_to_all | solution.py:184
  126.0 1.8 %fusion.97 = (f32[1024]{0:T(1024)S(1)}, f32[1024,1024]{0,1:T(8,128)S(1)}) fusion(bf16[1024,128]{1,0:T(8,128)(2,1)S(1)} %bitcast.123, bf16[2,512,128]{1,2,0:T(8,128)(2,1)S(1)} %collective-permute-done.13, bf16[2,512,128]{1,2,0:T(8,128)(2,1)S(1)} %maximum_select_fusion.1, s32[1024]{0:T(1024)S(1)} %bitcast.130, ...), kind=kOutput, calls=%fused_computation.128 | convolution fusion | flops 276298752 | bytes 4998144 | tf_op jit(solution)/shard_map/dot_general | solution.py:145
  127.8 0.6 fusion.1
  128.4 0.9 fusion.55
  129.3 0.7 copy.63
  130.1 0.7 all-to-all-done
  130.8 0.3 reshape.204
  131.2 0.9 copy.50
  132.1 0.9 copy.51
  (69 shorter events, 1.9 us)
Async XLA Ops:
  7.2 2.3 %copy-start = (bf16[512,1024]{1,0:T(8,128)(2,1)S(1)}, bf16[512,1024]{1,0:T(8,128)(2,1)}, u32[]{:S(2)}) copy-start(bf16[512,1024]{1,0:T(8,128)(2,1)} %param.8) | copy-start | bytes 3145732
  7.2 88.8 %all-gather.3.cloned.1.call-start = ((), (), s32[]{:S(2)}) async-start(), calls=%async_computation.1 | async-start | bytes 9437184 | tf_op jit(solution)/shard_map/all_gather | solution.py:100
  10.7 3.5 %copy-start.2 = (bf16[2048,32]{0,1:T(8,128)(2,1)S(1)}, bf16[2048,32]{0,1:T(8,128)(2,1)}, u32[]{:S(2)}) copy-start(bf16[2048,32]{0,1:T(8,128)(2,1)} %param.12) | copy-start | bytes 393220
  10.7 3.5 %copy-start.3 = (bf16[2048,32]{0,1:T(8,128)(2,1)S(1)}, bf16[2048,32]{0,1:T(8,128)(2,1)}, u32[]{:S(2)}) copy-start(bf16[2048,32]{0,1:T(8,128)(2,1)} %param.11) | copy-start | bytes 393220
  10.7 3.7 %copy-start.5 = (s32[32,1]{0,1:T(1,128)S(1)}, s32[32,1]{0,1:T(1,128)}, u32[]{:S(2)}) copy-start(s32[32,1]{0,1:T(1,128)} %param.15) | copy-start | bytes 388
  10.7 4.1 %copy-start.4 = (s32[512]{0:T(512)S(1)}, s32[512]{0:T(512)}, u32[]{:S(2)}) copy-start(s32[512]{0:T(512)} %param.13) | copy-start | bytes 6148
  10.9 12.5 %collective-permute-start.4 = (f32[512]{0:T(512)S(1)}, f32[512]{0:T(512)S(1)}, u32[]{:S(2)}, u32[]{:S(2)}) collective-permute-start(f32[512]{0:T(512)S(1)} %multiply_reduce_fusion), channel_id=1, source_target_pairs={{0,4},{4,0},{8,12},{12,8},{16,20},{20,16},{24,28},{28,24},{1,5},{5... | collective-permute-start | bytes 6152 | tf_op jit(solution)/shard_map/ppermute | solution.py:85
  11.4 14.6 %collective-permute-start.5 = (f32[512]{0:T(512)S(1)}, f32[512]{0:T(512)S(1)}, u32[]{:S(2)}, u32[]{:S(2)}) collective-permute-start(f32[512]{0:T(512)S(1)} %multiply_reduce_fusion), channel_id=1, source_target_pairs={{0,8},{4,12},{8,0},{12,4},{16,24},{20,28},{24,16},{28,20},{1,9},{5... | collective-permute-start | bytes 6152 | tf_op jit(solution)/shard_map/ppermute | solution.py:85
  14.1 12.5 %collective-permute-start.6 = (f32[512]{0:T(512)S(1)}, f32[512]{0:T(512)S(1)}, u32[]{:S(2)}, u32[]{:S(2)}) collective-permute-start(f32[512]{0:T(512)S(1)} %multiply_reduce_fusion), channel_id=1, source_target_pairs={{0,12},{4,8},{8,4},{12,0},{16,28},{20,24},{24,20},{28,16},{1,13},{... | collective-permute-start | bytes 6152 | tf_op jit(solution)/shard_map/ppermute | solution.py:85
  14.2 1.6 %collective-permute-start = (bf16[2,2048,32]{1,2,0:T(8,128)(2,1)S(1)}, bf16[2,2048,32]{1,2,0:T(8,128)(2,1)S(1)}, u32[]{:S(2)}, u32[]{:S(2)}) collective-permute-start(bf16[2,2048,32]{1,2,0:T(8,128)(2,1)S(1)} %pad_maximum_fusion.2), channel_id=1, source_target_pairs={{0,4},{4,0},{8,12},{12,8},{16,20},{20,16},{24,28},{28,24},{1,5},{5... | collective-permute-start | bytes 786440 | tf_op jit(solution)/shard_map/ppermute | solution.py:67
  17.4 1.2 copy-start.1
  18.7 20.1 %copy-start.6 = (s32[512]{0:T(512)S(1)}, s32[512]{0:T(512)}, u32[]{:S(2)}) copy-start(s32[512]{0:T(512)} %param.14) | copy-start | bytes 6148
  20.2 78.5 %collective-permute-start.3 = (bf16[2048,384]{1,0:T(8,128)(2,1)}, bf16[2048,384]{1,0:T(8,128)(2,1)}, u32[]{:S(2)}, u32[]{:S(2)}) collective-permute-start(bf16[2048,384]{1,0:T(8,128)(2,1)} %pad_maximum_fusion), channel_id=1, source_target_pairs={{0,3},{1,2},{2,1},{3,0},{4,7},{5,6},{6,5},{7,4},{8,11},{9,10},{10,... | collective-permute-start | bytes 4718600 | tf_op jit(solution)/shard_map/ppermute | solution.py:73
  22.8 79.2 %collective-permute-start.1 = (bf16[2048,384]{1,0:T(8,128)(2,1)}, bf16[2048,384]{1,0:T(8,128)(2,1)}, u32[]{:S(2)}, u32[]{:S(2)}) collective-permute-start(bf16[2048,384]{1,0:T(8,128)(2,1)} %pad_maximum_fusion), channel_id=1, source_target_pairs={{0,1},{1,0},{2,3},{3,2},{4,5},{5,4},{6,7},{7,6},{8,9},{9,8},{10,11... | collective-permute-start | bytes 4718600 | tf_op jit(solution)/shard_map/ppermute | solution.py:73
  23.4 5.9 %collective-permute-start.7 = (f32[512]{0:T(512)S(1)}, f32[512]{0:T(512)S(1)}, u32[]{:S(2)}, u32[]{:S(2)}) collective-permute-start(f32[512]{0:T(512)S(1)} %multiply_reduce_fusion), channel_id=1, source_target_pairs={{0,16},{4,20},{8,24},{12,28},{16,0},{20,4},{24,8},{28,12},{1,17},{... | collective-permute-start | bytes 6152 | tf_op jit(solution)/shard_map/ppermute | solution.py:85
  26.1 78.4 %collective-permute-start.2 = (bf16[2048,384]{1,0:T(8,128)(2,1)}, bf16[2048,384]{1,0:T(8,128)(2,1)}, u32[]{:S(2)}, u32[]{:S(2)}) collective-permute-start(bf16[2048,384]{1,0:T(8,128)(2,1)} %pad_maximum_fusion), channel_id=1, source_target_pairs={{0,2},{1,3},{2,0},{3,1},{4,6},{5,7},{6,4},{7,5},{8,10},{9,11},{10,... | collective-permute-start | bytes 4718600 | tf_op jit(solution)/shard_map/ppermute | solution.py:73
  26.6 5.1 %collective-permute-start.8 = (f32[512]{0:T(512)S(1)}, f32[512]{0:T(512)S(1)}, u32[]{:S(2)}, u32[]{:S(2)}) collective-permute-start(f32[512]{0:T(512)S(1)} %multiply_reduce_fusion), channel_id=1, source_target_pairs={{0,20},{4,16},{8,28},{12,24},{16,4},{20,0},{24,12},{28,8},{1,21},{... | collective-permute-start | bytes 6152 | tf_op jit(solution)/shard_map/ppermute | solution.py:85
  29.3 5.5 %collective-permute-start.9 = (f32[512]{0:T(512)S(1)}, f32[512]{0:T(512)S(1)}, u32[]{:S(2)}, u32[]{:S(2)}) collective-permute-start(f32[512]{0:T(512)S(1)} %multiply_reduce_fusion), channel_id=1, source_target_pairs={{0,24},{4,28},{8,16},{12,20},{16,8},{20,12},{24,0},{28,4},{1,25},{... | collective-permute-start | bytes 6152 | tf_op jit(solution)/shard_map/ppermute | solution.py:85
  31.7 7.1 %collective-permute-start.10 = (f32[512]{0:T(512)S(1)}, f32[512]{0:T(512)S(1)}, u32[]{:S(2)}, u32[]{:S(2)}) collective-permute-start(f32[512]{0:T(512)S(1)} %multiply_reduce_fusion), channel_id=1, source_target_pairs={{0,28},{4,24},{8,20},{12,16},{16,12},{20,8},{24,4},{28,0},{1,29},{... | collective-permute-start | bytes 6152 | tf_op jit(solution)/shard_map/ppermute | solution.py:85
  34.8 56.3 %collective-permute-start.11 = (s32[512]{0:T(512)S(1)}, s32[512]{0:T(512)S(1)}, u32[]{:S(2)}, u32[]{:S(2)}) collective-permute-start(s32[512]{0:T(512)S(1)} %broadcast_add_fusion), channel_id=1, source_target_pairs={{0,1},{1,2},{2,3},{4,5},{5,6},{6,7},{8,9},{9,10},{10,11},{12,13},{... | collective-permute-start | bytes 6152 | tf_op jit(solution)/shard_map/ppermute | solution.py:19
  95.9 6.1 %copy-start.7 = (bf16[4096,1024]{1,0:T(8,128)(2,1)S(1)}, bf16[4096,1024]{1,0:T(8,128)(2,1)}, u32[]{:S(2)}) copy-start(bf16[4096,1024]{1,0:T(8,128)(2,1)} %all-gather.3.cloned.1.call-done) | copy-start | bytes 25165828
  107.7 5.7 %collective-permute-start.12 = (bf16[2,512,64]{1,2,0:T(8,128)(2,1)S(1)}, bf16[2,512,64]{1,2,0:T(8,128)(2,1)S(1)}, u32[]{:S(2)}, u32[]{:S(2)}) collective-permute-start(bf16[2,512,64]{1,2,0:T(8,128)(2,1)S(1)} %pad_maximum_fusion.3), channel_id=1, source_target_pairs={{0,8},{4,12},{8,0},{12,4},{16,24},{20,28},{24,16},{28,20},{1,9},{5... | collective-permute-start | bytes 393224 | tf_op jit(solution)/shard_map/ppermute | solution.py:124
  113.4 12.6 %collective-permute-start.13 = (bf16[2,512,128]{1,2,0:T(8,128)(2,1)S(1)}, bf16[2,512,128]{1,2,0:T(8,128)(2,1)S(1)}, u32[]{:S(2)}, u32[]{:S(2)}) collective-permute-start(bf16[2,512,128]{1,2,0:T(8,128)(2,1)S(1)} %maximum_select_fusion.1), channel_id=1, source_target_pairs={{0,1},{1,2},{2,3},{4,5},{5,6},{6,7},{8,9},{9,10},{10,11},{12,13},{... | collective-permute-start | bytes 786440 | tf_op jit(solution)/shard_map/ppermute | solution.py:19
  122.5 8.3 %all-to-all-start = ((bf16[4,16,2,512]{3,1,2,0:T(8,128)(2,1)}), bf16[4,16,2,512]{3,1,2,0:T(8,128)(2,1)S(1)}, u32[]{:S(2)}, u32[]{:S(2)}) async-start(bf16[4,16,2,512]{3,1,2,0:T(8,128)(2,1)} %copy.46), calls=%async_computation | async-start | bytes 262144 | tf_op jit(solution)/shard_map/all_to_all | solution.py:184
Sparse Core Ops, SparseCore 0:
  10.8 85.0 all-gather.2

commit v16 on v14

--- a/solution.py
+++ b/solution.py
@@ -27,13 +27,17 @@
     return route
 
 
-def rope(matrix, places, width, first_pair):
-    cols = jnp.arange(matrix.shape[1], dtype=jnp.int32)
+def rope_tables(places, count, width, first_pair):
+    cols = jnp.arange(count, dtype=jnp.int32)
     pair_index = first_pair + (cols % width) // 2
     frequency = jnp.power(THETA, -(2.0 * pair_index.astype(jnp.float32)) / HD)
     angles = places.astype(jnp.float32)[:, None] * frequency[None, :]
-    cosine = jnp.cos(angles)
-    sine_of = jnp.sin(angles)
+    return lax.optimization_barrier((jnp.cos(angles), jnp.sin(angles)))
+
+
+def rope(matrix, tables):
+    cosine, sine_of = tables
+    cols = jnp.arange(matrix.shape[1], dtype=jnp.int32)
     following = jnp.roll(matrix, -1, axis=1)
     preceding = jnp.roll(matrix, 1, axis=1)
     even = (cols % 2 == 0)[None, :]
@@ -110,14 +114,12 @@
             products = part if products is None else products + part
         projected = products * scaling[rows_of, None]
         places = positions[rows_of]
-        key_half = rope(
-            projected[:, query_cols : query_cols + half_cols],
-            places,
-            half_cols,
-            (spot // 2) * quarter,
-        ).astype(jnp.bfloat16)
+        key_tables = rope_tables(places, half_cols, half_cols, (spot // 2) * quarter)
+        key_half = rope(projected[:, query_cols : query_cols + half_cols], key_tables)
+        key_half = key_half.astype(jnp.bfloat16)
         value_half = projected[:, query_cols + half_cols :].astype(jnp.bfloat16)
-        query_halves.append(rope(projected[:, :query_cols], places, HD, 0).astype(jnp.bfloat16))
+        query_tables = rope_tables(places, query_cols, HD, 0)
+        query_halves.append(rope(projected[:, :query_cols], query_tables).astype(jnp.bfloat16))
         half_kv = jnp.stack([key_half, value_half])
         kv_halves.append(lax.dynamic_slice_in_dim(half_kv, (spot % 2) * quarter, quarter, 2))
         low_half = (spot // 2) % 2 == 0

time: 139 us -> 137 us (0.986)
  waiting for transfers between devices: 61.7 us -> 56.7 us
  starting transfers between devices: 28.5 us -> 30.5 us
    ppermute x2, waiting for transfers between devices: 51.6 us -> 48.8 us  [shifted(): return lax.ppermute(value, axis, pairs)]
    sin x0 -> x2, other arithmetic: none -> 2.42 us  [rope_tables(): return lax.optimization_barrier((jnp.cos(angles), jnp.sin(angles)))]
    convert_element_type x2, other arithmetic: 2.63 us -> 0.24 us  [the longest x1 0.24 us: shards(): rope(projected[:, :query_cols], query_tables).astype(jnp.bfloat16)]
    ppermute x7, starting transfers between devices: 9.39 us -> 11.1 us  [shards(): lax.ppermute(local_squares, 'gx', partner_route(gx_count, gx_count, k))]
    ppermute x7, waiting for transfers between devices: 4.63 us -> 2.93 us  [shards(): lax.ppermute(local_squares, 'gx', partner_route(gx_count, gx_count, k))]
  transfers between devices with their start and end apart: 17 -> 17, of which waited for: 6 -> 5; matrix products, arithmetic and copies ran while one was open for 18% -> 19% of each run, Pallas kernels for 0% -> 0%
where the time goes in v16:
time: 137 us
  waiting for transfers between devices  56.7 us (41%)
  starting transfers between devices  30.5 us (22%)
  between operations  14.6 us (11%)
  matrix products  14 us (10%)
  local copies, waits for them, and re-layouts  10.5 us (8%)
  other arithmetic  10.4 us (8%)
    ppermute x2, waiting for transfers between devices, shifted(): return lax.ppermute(value, axis, pairs)  48.8 us
    dot_general x4, matrix products, shards(): jnp.einsum('btd,bdc->tc', rows, weights_of, preferred_element_type=jnp.fl...  11.3 us
    ppermute x7, starting transfers between devices, shards(): lax.ppermute(local_squares, 'gx', partner_route(gx_count, gx_count, k))  11.1 us
    ppermute x2, starting transfers between devices, shifted(): return lax.ppermute(value, axis, pairs)  6.77 us
    ppermute x1, starting transfers between devices, shards(): other = lax.ppermute(half_kv, ('gx', 'gy'), route)  4.99 us
    all_gather x1, waiting for transfers between devices, shards(): normed = lax.all_gather(local_normed[rows_of], 'gx', axis=0, tiled=False)  4.2 us
    ppermute x3, starting transfers between devices, shards(): lax.ppermute(local_weights, 'gy', partner_route(gy_count, gy_count, k))  3.91 us
    all_to_all x1, starting transfers between devices, shards(): lax.all_to_all(send_kv, 'gy', split_axis=0, concat_axis=0, tiled=True)  3.33 us
  transfers between devices with their start and end apart: 17, of which 5 were waited for; matrix products, arithmetic and copies ran while one was open for 19% of the time, Pallas kernels for 0%

profile of v16, /device:TPU:0, one launch (start us, length us, event | category | flops | bytes accessed | tf_op | source)
XLA Modules:
  0.0 136.6 jit_solution(15181319958376407113)
XLA Ops:
  7.2 1.5 %convert_element_type.53 = f32[512,1024]{1,0:T(8,128)S(1)} convert(bf16[512,1024]{1,0:T(8,128)(2,1)} %param.8) | non-fusion elementwise | flops 524288 | bytes 3145728 | tf_op jit(solution)/shard_map/convert_element_type | solution.py:80
  8.8 0.7 dynamic-slice_convert_fusion
  9.5 1.2 multiply_convert_fusion
  10.7 0.2 multiply_reduce_fusion
  10.9 0.5 collective-permute-start.4
  11.5 2.6 %collective-permute-start.5 = (f32[512]{0:T(512)S(1)}, f32[512]{0:T(512)S(1)}, u32[]{:S(2)}, u32[]{:S(2)}) collective-permute-start(f32[512]{0:T(512)S(1)} %multiply_reduce_fusion), channel_id=1, source_target_pairs={{0,8},{4,12},{8,0},{12,4},{16,24},{20,28},{24,16},{28,20},{1,9},{5... | collective-permute-start | bytes 6152 | tf_op jit(solution)/shard_map/ppermute | solution.py:89
  14.2 0.2 collective-permute-start
  14.9 0.5 copy.32
  15.4 0.5 multiply_sine_fusion.1
  15.9 0.5 copy.33
  16.4 1.2 maximum_select_fusion
  17.6 0.3 fusion.90
  17.9 0.9 copy-done.1
  18.8 1.5 %pad_maximum_fusion = bf16[2048,384]{1,0:T(8,128)(2,1)} fusion(bf16[2048,64]{1,0:T(8,128)(2,1)S(1)} %get-tuple-element.27, bf16[2048,64]{1,0:T(8,128)(2,1)S(1)} %get-tuple-element.26, bf16[2048,256]{1,0:T(8,128)(2,1)S(1)} %copy-done.1), kind=kLoop, calls=%fused_computation.29 | loop fusion | flops 4718592 | bytes 3145728 | tf_op jit(solution)/shard_map/concatenate | solution.py:73
  20.3 2.8 %collective-permute-start.3 = (bf16[2048,384]{1,0:T(8,128)(2,1)}, bf16[2048,384]{1,0:T(8,128)(2,1)}, u32[]{:S(2)}, u32[]{:S(2)}) collective-permute-start(bf16[2048,384]{1,0:T(8,128)(2,1)} %pad_maximum_fusion), channel_id=1, source_target_pairs={{0,3},{1,2},{2,1},{3,0},{4,7},{5,6},{6,5},{7,4},{8,11},{9,10},{10,... | collective-permute-start | bytes 4718600 | tf_op jit(solution)/shard_map/ppermute | solution.py:77
  23.1 1.9 %multiply_sine_fusion = (f32[512,256]{0,1:T(8,128)S(1)}, f32[512,256]{0,1:T(8,128)S(1)}) fusion(f32[256]{0:T(256)S(1)} %multiply_power_fusion, f32[512]{0:T(512)S(1)} %convert_element_type.56), kind=kLoop, calls=%fused_computation.42 | loop fusion | flops 131072 | bytes 1051648 | tf_op jit(solution)/shard_map/sin | solution.py:35
  25.0 0.6 collective-permute-start.1
  25.6 2.7 %collective-permute-start.7 = (f32[512]{0:T(512)S(1)}, f32[512]{0:T(512)S(1)}, u32[]{:S(2)}, u32[]{:S(2)}) collective-permute-start(f32[512]{0:T(512)S(1)} %multiply_reduce_fusion), channel_id=1, source_target_pairs={{0,16},{4,20},{8,24},{12,28},{16,0},{20,4},{24,8},{28,12},{1,17},{... | collective-permute-start | bytes 6152 | tf_op jit(solution)/shard_map/ppermute | solution.py:89
  28.3 0.5 collective-permute-start.2
  28.9 1.4 %collective-permute-done.7 = f32[512]{0:T(512)S(1)} collective-permute-done((f32[512]{0:T(512)S(1)}, f32[512]{0:T(512)S(1)}, u32[]{:S(2)}, u32[]{:S(2)}) %collective-permute-start.7) | collective-permute-done | bytes 2080 | tf_op jit(solution)/shard_map/ppermute | solution.py:89
  30.3 5.1 %collective-permute-start.9 = (f32[512]{0:T(512)S(1)}, f32[512]{0:T(512)S(1)}, u32[]{:S(2)}, u32[]{:S(2)}) collective-permute-start(f32[512]{0:T(512)S(1)} %multiply_reduce_fusion), channel_id=1, source_target_pairs={{0,24},{4,28},{8,16},{12,20},{16,8},{20,12},{24,0},{28,4},{1,25},{... | collective-permute-start | bytes 6152 | tf_op jit(solution)/shard_map/ppermute | solution.py:89
  35.5 1.5 %collective-permute-done.9 = f32[512]{0:T(512)S(1)} collective-permute-done((f32[512]{0:T(512)S(1)}, f32[512]{0:T(512)S(1)}, u32[]{:S(2)}, u32[]{:S(2)}) %collective-permute-start.9) | collective-permute-done | bytes 2080 | tf_op jit(solution)/shard_map/ppermute | solution.py:89
  37.0 3.4 %collective-permute-start.11 = (s32[512]{0:T(512)S(1)}, s32[512]{0:T(512)S(1)}, u32[]{:S(2)}, u32[]{:S(2)}) collective-permute-start(s32[512]{0:T(512)S(1)} %broadcast_add_fusion), channel_id=1, source_target_pairs={{0,1},{1,2},{2,3},{4,5},{5,6},{6,7},{8,9},{9,10},{10,11},{12,13},{... | collective-permute-start | bytes 6152 | tf_op jit(solution)/shard_map/ppermute | solution.py:19
  40.4 1.4 copy.38
  41.9 0.6 gather_fusion
  42.4 48.8 %collective-permute-done.11 = s32[512]{0:T(512)S(1)} collective-permute-done((s32[512]{0:T(512)S(1)}, s32[512]{0:T(512)S(1)}, u32[]{:S(2)}, u32[]{:S(2)}) %collective-permute-start.11) | collective-permute-done | bytes 2080 | tf_op jit(solution)/shard_map/ppermute | solution.py:19
  91.3 0.2 copy.39
  91.5 0.2 copy.40
  91.7 4.2 %all-gather.3.cloned.1.call-done = bf16[4096,1024]{1,0:T(8,128)(2,1)} async-done(((bf16[512,1024]{1,0:T(8,128)(2,1)}), bf16[4096,1024]{1,0:T(8,128)(2,1)}) %all-gather.3.cloned.1.call-update) | async-done | bytes 8388624 | tf_op jit(solution)/shard_map/all_gather | solution.py:104
  95.9 3.0 %fusion.23 = f32[512,384]{0,1:T(8,128)S(1)} fusion(bf16[2,1024,64]{1,2,0:T(8,128)(2,1)S(1)} %copy.40, bf16[2,1024,64]{1,2,0:T(8,128)(2,1)S(1)} %copy.39, bf16[2,1024,256]{1,2,0:T(8,128)(2,1)} %copy.38, bf16[4,2,512,1024]{3,2,1,0:T(8,128)(2,1)} %bitcast.142, s32[]{:T(128)S(6)} %select_n.158), kind=kOutput, calls=%fused_computation.30 | convolution fusion | flops 810024960 | bytes 4456452 | tf_op jit(solution)/shard_map/btd,bdc->tc/dot_general | solution.py:113
  99.0 3.4 %fusion.34 = f32[512,384]{0,1:T(8,128)S(1)} fusion(bf16[2,1024,384]{2,1,0:T(8,128)(2,1)} %bitcast.20, bf16[4,2,512,1024]{3,2,1,0:T(8,128)(2,1)} %bitcast.143, s32[]{:T(128)S(6)} %select_n.165), kind=kOutput, calls=%fused_computation.33 | convolution fusion | flops 805306368 | bytes 4456452 | tf_op jit(solution)/shard_map/btd,bdc->tc/dot_general | solution.py:113
  102.3 2.5 %fusion.40 = f32[512,384]{0,1:T(8,128)S(1)} fusion(f32[512,384]{0,1:T(8,128)S(1)} %fusion.23, bf16[2,1024,384]{2,1,0:T(8,128)(2,1)} %bitcast.14, bf16[4,2,512,1024]{3,2,1,0:T(8,128)(2,1)S(1)} %bitcast.144, s32[]{:T(128)S(6)} %select_n.163), kind=kOutput, calls=%fused_computation.35 | convolution fusion | flops 805502976 | bytes 5242884 | tf_op jit(solution)/shard_map/btd,bdc->tc/dot_general | solution.py:113
  104.8 2.5 %fusion.46 = f32[512,384]{0,1:T(8,128)S(1)} fusion(f32[512,384]{0,1:T(8,128)S(1)} %fusion.34, f32[512,384]{0,1:T(8,128)S(1)} %fusion.40, bf16[2,1024,384]{2,1,0:T(8,128)(2,1)} %bitcast.17, bf16[4,2,512,1024]{3,2,1,0:T(8,128)(2,1)S(1)} %bitcast.145, s32[]{:T(128)S(6)} %select_n.164, f32[512]{0:T(512)S(1)} %add_rsqrt_fusion), kind=kOutput, calls=%fused_computation.37 | convolution fusion | flops 805896192 | bytes 6031364 | tf_op jit(solution)/shard_map/btd,bdc->tc/dot_general | solution.py:113
  107.6 3.4 %collective-permute-start.12 = (bf16[2,512,64]{1,2,0:T(8,128)(2,1)S(1)}, bf16[2,512,64]{1,2,0:T(8,128)(2,1)S(1)}, u32[]{:S(2)}, u32[]{:S(2)}) collective-permute-start(bf16[2,512,64]{1,2,0:T(8,128)(2,1)S(1)} %pad_maximum_fusion.3), channel_id=1, source_target_pairs={{0,1},{1,2},{2,3},{4,5},{5,6},{6,7},{8,9},{9,10},{10,11},{12,13},{... | collective-permute-start | bytes 393224 | tf_op jit(solution)/shard_map/ppermute | solution.py:19
  111.0 5.0 %collective-permute-start.13 = (bf16[2,512,64]{1,2,0:T(8,128)(2,1)S(1)}, bf16[2,512,64]{1,2,0:T(8,128)(2,1)S(1)}, u32[]{:S(2)}, u32[]{:S(2)}) collective-permute-start(bf16[2,512,64]{1,2,0:T(8,128)(2,1)S(1)} %pad_maximum_fusion.3), channel_id=1, source_target_pairs={{0,9},{1,10},{2,11},{4,13},{5,14},{6,15},{8,1},{9,2},{10,3},{12,5}... | collective-permute-start | bytes 393224 | tf_op jit(solution)/shard_map/ppermute | solution.py:136
  116.1 0.2 fusion.60
  116.7 0.2 reshape.200
  117.1 1.5 %scatter_fusion = bf16[64,2,512]{2,1,0:T(2,128)(2,1)S(1)} fusion(bf16[64,2,512]{2,1,0:T(2,128)(2,1)S(1)} %broadcast_in_dim.44, s32[32]{0:T(128)S(1)} %fusion.85, bf16[32,2,512]{2,1,0:T(2,128)(2,1)S(1)} %copy.45), kind=kCustom, calls=%fused_computation.1 | custom fusion | bytes 196736 | tf_op jit(solution)/shard_map/scatter | solution.py:190
  118.6 0.7 copy.46
  119.3 3.3 %all-to-all-start = ((bf16[4,16,2,512]{3,1,2,0:T(8,128)(2,1)}), bf16[4,16,2,512]{3,1,2,0:T(8,128)(2,1)S(1)}, u32[]{:S(2)}, u32[]{:S(2)}) async-start(bf16[4,16,2,512]{3,1,2,0:T(8,128)(2,1)} %copy.46), calls=%async_computation | async-start | bytes 262144 | tf_op jit(solution)/shard_map/all_to_all | solution.py:193
  122.8 1.7 %fusion.94 = (f32[1024]{0:T(1024)S(1)}, f32[1024,1024]{0,1:T(8,128)S(1)}) fusion(bf16[1024,128]{1,0:T(8,128)(2,1)S(1)} %bitcast.125, bf16[2,512,128]{1,2,0:T(8,128)(2,1)S(1)} %maximum_select_fusion.1, bf16[2,512,128]{1,2,0:T(8,128)(2,1)S(1)} %maximum_select_fusion.2, s32[1024]{0:T(1024)S(1)} %bitcast.132, pred[1024]{0:T(1024)(128)(4,1)S(1)} %broadcast_compare_fusion, ...), kind=kOutput, calls=%fused_computation.130 | convolution fusion | flops 276298752 | bytes 4998144 | tf_op jit(solution)/shard_map/dot_general | solution.py:154
  124.5 0.6 fusion.1
  125.1 0.9 fusion.55
  126.1 0.7 copy.63
  126.8 0.8 all-to-all-done
  127.6 0.3 reshape.204
  127.9 0.9 copy.50
  128.9 0.9 copy.51
  (74 shorter events, 1.9 us)
Async XLA Ops:
  7.2 2.3 %copy-start = (bf16[512,1024]{1,0:T(8,128)(2,1)S(1)}, bf16[512,1024]{1,0:T(8,128)(2,1)}, u32[]{:S(2)}) copy-start(bf16[512,1024]{1,0:T(8,128)(2,1)} %param.8) | copy-start | bytes 3145732
  7.2 88.7 %all-gather.3.cloned.1.call-start = ((), (), s32[]{:S(2)}) async-start(), calls=%async_computation.1 | async-start | bytes 9437184 | tf_op jit(solution)/shard_map/all_gather | solution.py:104
  10.7 3.5 %copy-start.2 = (bf16[2048,32]{0,1:T(8,128)(2,1)S(1)}, bf16[2048,32]{0,1:T(8,128)(2,1)}, u32[]{:S(2)}) copy-start(bf16[2048,32]{0,1:T(8,128)(2,1)} %param.12) | copy-start | bytes 393220
  10.7 3.5 %copy-start.3 = (bf16[2048,32]{0,1:T(8,128)(2,1)S(1)}, bf16[2048,32]{0,1:T(8,128)(2,1)}, u32[]{:S(2)}) copy-start(bf16[2048,32]{0,1:T(8,128)(2,1)} %param.11) | copy-start | bytes 393220
  10.7 3.7 %copy-start.5 = (s32[32,1]{0,1:T(1,128)S(1)}, s32[32,1]{0,1:T(1,128)}, u32[]{:S(2)}) copy-start(s32[32,1]{0,1:T(1,128)} %param.15) | copy-start | bytes 388
  10.7 4.1 %copy-start.4 = (s32[512]{0:T(512)S(1)}, s32[512]{0:T(512)}, u32[]{:S(2)}) copy-start(s32[512]{0:T(512)} %param.13) | copy-start | bytes 6148
  10.7 4.6 %copy-start.6 = (s32[512]{0:T(512)S(1)}, s32[512]{0:T(512)}, u32[]{:S(2)}) copy-start(s32[512]{0:T(512)} %param.14) | copy-start | bytes 6148
  10.9 14.7 %collective-permute-start.4 = (f32[512]{0:T(512)S(1)}, f32[512]{0:T(512)S(1)}, u32[]{:S(2)}, u32[]{:S(2)}) collective-permute-start(f32[512]{0:T(512)S(1)} %multiply_reduce_fusion), channel_id=1, source_target_pairs={{0,4},{4,0},{8,12},{12,8},{16,20},{20,16},{24,28},{28,24},{1,5},{5... | collective-permute-start | bytes 6152 | tf_op jit(solution)/shard_map/ppermute | solution.py:89
  11.5 16.8 %collective-permute-start.5 = (f32[512]{0:T(512)S(1)}, f32[512]{0:T(512)S(1)}, u32[]{:S(2)}, u32[]{:S(2)}) collective-permute-start(f32[512]{0:T(512)S(1)} %multiply_reduce_fusion), channel_id=1, source_target_pairs={{0,8},{4,12},{8,0},{12,4},{16,24},{20,28},{24,16},{28,20},{1,9},{5... | collective-permute-start | bytes 6152 | tf_op jit(solution)/shard_map/ppermute | solution.py:89
  14.1 14.7 %collective-permute-start.6 = (f32[512]{0:T(512)S(1)}, f32[512]{0:T(512)S(1)}, u32[]{:S(2)}, u32[]{:S(2)}) collective-permute-start(f32[512]{0:T(512)S(1)} %multiply_reduce_fusion), channel_id=1, source_target_pairs={{0,12},{4,8},{8,4},{12,0},{16,28},{20,24},{24,20},{28,16},{1,13},{... | collective-permute-start | bytes 6152 | tf_op jit(solution)/shard_map/ppermute | solution.py:89
  14.2 1.7 %collective-permute-start = (bf16[2,2048,32]{1,2,0:T(8,128)(2,1)S(1)}, bf16[2,2048,32]{1,2,0:T(8,128)(2,1)S(1)}, u32[]{:S(2)}, u32[]{:S(2)}) collective-permute-start(bf16[2,2048,32]{1,2,0:T(8,128)(2,1)S(1)} %pad_maximum_fusion.2), channel_id=1, source_target_pairs={{0,4},{4,0},{8,12},{12,8},{16,20},{20,16},{24,28},{28,24},{1,5},{5... | collective-permute-start | bytes 786440 | tf_op jit(solution)/shard_map/ppermute | solution.py:71
  17.6 1.2 copy-start.1
  20.3 78.6 %collective-permute-start.3 = (bf16[2048,384]{1,0:T(8,128)(2,1)}, bf16[2048,384]{1,0:T(8,128)(2,1)}, u32[]{:S(2)}, u32[]{:S(2)}) collective-permute-start(bf16[2048,384]{1,0:T(8,128)(2,1)} %pad_maximum_fusion), channel_id=1, source_target_pairs={{0,3},{1,2},{2,1},{3,0},{4,7},{5,6},{6,5},{7,4},{8,11},{9,10},{10,... | collective-permute-start | bytes 4718600 | tf_op jit(solution)/shard_map/ppermute | solution.py:77
  25.0 77.3 %collective-permute-start.1 = (bf16[2048,384]{1,0:T(8,128)(2,1)}, bf16[2048,384]{1,0:T(8,128)(2,1)}, u32[]{:S(2)}, u32[]{:S(2)}) collective-permute-start(bf16[2048,384]{1,0:T(8,128)(2,1)} %pad_maximum_fusion), channel_id=1, source_target_pairs={{0,1},{1,0},{2,3},{3,2},{4,5},{5,4},{6,7},{7,6},{8,9},{9,8},{10,11... | collective-permute-start | bytes 4718600 | tf_op jit(solution)/shard_map/ppermute | solution.py:77
  25.6 4.6 %collective-permute-start.7 = (f32[512]{0:T(512)S(1)}, f32[512]{0:T(512)S(1)}, u32[]{:S(2)}, u32[]{:S(2)}) collective-permute-start(f32[512]{0:T(512)S(1)} %multiply_reduce_fusion), channel_id=1, source_target_pairs={{0,16},{4,20},{8,24},{12,28},{16,0},{20,4},{24,8},{28,12},{1,17},{... | collective-permute-start | bytes 6152 | tf_op jit(solution)/shard_map/ppermute | solution.py:89
  28.3 76.5 %collective-permute-start.2 = (bf16[2048,384]{1,0:T(8,128)(2,1)}, bf16[2048,384]{1,0:T(8,128)(2,1)}, u32[]{:S(2)}, u32[]{:S(2)}) collective-permute-start(bf16[2048,384]{1,0:T(8,128)(2,1)} %pad_maximum_fusion), channel_id=1, source_target_pairs={{0,2},{1,3},{2,0},{3,1},{4,6},{5,7},{6,4},{7,5},{8,10},{9,11},{10,... | collective-permute-start | bytes 4718600 | tf_op jit(solution)/shard_map/ppermute | solution.py:77
  28.8 6.6 %collective-permute-start.8 = (f32[512]{0:T(512)S(1)}, f32[512]{0:T(512)S(1)}, u32[]{:S(2)}, u32[]{:S(2)}) collective-permute-start(f32[512]{0:T(512)S(1)} %multiply_reduce_fusion), channel_id=1, source_target_pairs={{0,20},{4,16},{8,28},{12,24},{16,4},{20,0},{24,12},{28,8},{1,21},{... | collective-permute-start | bytes 6152 | tf_op jit(solution)/shard_map/ppermute | solution.py:89
  30.3 6.8 %collective-permute-start.9 = (f32[512]{0:T(512)S(1)}, f32[512]{0:T(512)S(1)}, u32[]{:S(2)}, u32[]{:S(2)}) collective-permute-start(f32[512]{0:T(512)S(1)} %multiply_reduce_fusion), channel_id=1, source_target_pairs={{0,24},{4,28},{8,16},{12,20},{16,8},{20,12},{24,0},{28,4},{1,25},{... | collective-permute-start | bytes 6152 | tf_op jit(solution)/shard_map/ppermute | solution.py:89
  35.4 6.4 %collective-permute-start.10 = (f32[512]{0:T(512)S(1)}, f32[512]{0:T(512)S(1)}, u32[]{:S(2)}, u32[]{:S(2)}) collective-permute-start(f32[512]{0:T(512)S(1)} %multiply_reduce_fusion), channel_id=1, source_target_pairs={{0,28},{4,24},{8,20},{12,16},{16,12},{20,8},{24,4},{28,0},{1,29},{... | collective-permute-start | bytes 6152 | tf_op jit(solution)/shard_map/ppermute | solution.py:89
  37.0 54.2 %collective-permute-start.11 = (s32[512]{0:T(512)S(1)}, s32[512]{0:T(512)S(1)}, u32[]{:S(2)}, u32[]{:S(2)}) collective-permute-start(s32[512]{0:T(512)S(1)} %broadcast_add_fusion), channel_id=1, source_target_pairs={{0,1},{1,2},{2,3},{4,5},{5,6},{6,7},{8,9},{9,10},{10,11},{12,13},{... | collective-permute-start | bytes 6152 | tf_op jit(solution)/shard_map/ppermute | solution.py:19
  95.9 6.4 %copy-start.7 = (bf16[4096,1024]{1,0:T(8,128)(2,1)S(1)}, bf16[4096,1024]{1,0:T(8,128)(2,1)}, u32[]{:S(2)}) copy-start(bf16[4096,1024]{1,0:T(8,128)(2,1)} %all-gather.3.cloned.1.call-done) | copy-start | bytes 25165828
  107.5 15.1 %collective-permute-start.14 = (bf16[2,512,64]{1,2,0:T(8,128)(2,1)S(1)}, bf16[2,512,64]{1,2,0:T(8,128)(2,1)S(1)}, u32[]{:S(2)}, u32[]{:S(2)}) collective-permute-start(bf16[2,512,64]{1,2,0:T(8,128)(2,1)S(1)} %pad_maximum_fusion.3), channel_id=1, source_target_pairs={{0,8},{4,12},{8,0},{12,4},{16,24},{20,28},{24,16},{28,20},{1,9},{5... | collective-permute-start | bytes 393224 | tf_op jit(solution)/shard_map/ppermute | solution.py:127
  107.6 15.1 %collective-permute-start.12 = (bf16[2,512,64]{1,2,0:T(8,128)(2,1)S(1)}, bf16[2,512,64]{1,2,0:T(8,128)(2,1)S(1)}, u32[]{:S(2)}, u32[]{:S(2)}) collective-permute-start(bf16[2,512,64]{1,2,0:T(8,128)(2,1)S(1)} %pad_maximum_fusion.3), channel_id=1, source_target_pairs={{0,1},{1,2},{2,3},{4,5},{5,6},{6,7},{8,9},{9,10},{10,11},{12,13},{... | collective-permute-start | bytes 393224 | tf_op jit(solution)/shard_map/ppermute | solution.py:19
  111.0 11.7 %collective-permute-start.13 = (bf16[2,512,64]{1,2,0:T(8,128)(2,1)S(1)}, bf16[2,512,64]{1,2,0:T(8,128)(2,1)S(1)}, u32[]{:S(2)}, u32[]{:S(2)}) collective-permute-start(bf16[2,512,64]{1,2,0:T(8,128)(2,1)S(1)} %pad_maximum_fusion.3), channel_id=1, source_target_pairs={{0,9},{1,10},{2,11},{4,13},{5,14},{6,15},{8,1},{9,2},{10,3},{12,5}... | collective-permute-start | bytes 393224 | tf_op jit(solution)/shard_map/ppermute | solution.py:136
  119.3 8.3 %all-to-all-start = ((bf16[4,16,2,512]{3,1,2,0:T(8,128)(2,1)}), bf16[4,16,2,512]{3,1,2,0:T(8,128)(2,1)S(1)}, u32[]{:S(2)}, u32[]{:S(2)}) async-start(bf16[4,16,2,512]{3,1,2,0:T(8,128)(2,1)} %copy.46), calls=%async_computation | async-start | bytes 262144 | tf_op jit(solution)/shard_map/all_to_all | solution.py:193
Sparse Core Ops, SparseCore 0:
  10.8 85.0 all-gather.2

commit v17 on v16

--- a/solution.py
+++ b/solution.py
@@ -159,6 +159,7 @@
     key_place = jnp.arange(window_keys.shape[0], dtype=jnp.int32)
     allowed = (window_marks[None, :] == query_marks[:, None] + 1) & (window_marks[None, :] > 0)
     allowed = allowed & (key_place[None, :] <= query_place[:, None] + reach_rows)
+    allowed = lax.optimization_barrier(allowed)
     masked = jnp.where(allowed, scores, MASKED)
     highest = jnp.max(masked, axis=1, keepdims=True)
     exponent = jnp.exp(masked - highest)

time: 137 us -> 137 us (level)
  other arithmetic: 10.4 us -> 13.3 us
  starting transfers between devices: 30.5 us -> 29 us
    ppermute x2, waiting for transfers between devices: 48.8 us -> 0.01 us  [shifted(): return lax.ppermute(value, axis, pairs)]
    all_gather x1, waiting for transfers between devices: 4.2 us -> 52 us  [shards(): normed = lax.all_gather(local_normed[rows_of], 'gx', axis=0, tiled=False)]
    ppermute x7, starting transfers between devices: 11.1 us -> 9.45 us  [shards(): lax.ppermute(local_squares, 'gx', partner_route(gx_count, gx_count, k))]
    and x0 -> x1, other arithmetic: none -> 1.39 us  [shards(): allowed & (key_place[None, :] <= query_place[:, None] + reach_rows)]
    unnamed x21 -> x25, local copies, waits for them, and re-layouts: 2.81 us -> 1.91 us
  transfers between devices with their start and end apart: 17 -> 17, of which waited for: 5 -> 6; matrix products, arithmetic and copies ran while one was open for 19% -> 20% of each run, Pallas kernels for 0% -> 0%
where the time goes in v17:
time: 137 us
  waiting for transfers between devices  56.6 us (41%)
  starting transfers between devices  29 us (21%)
  between operations  14.7 us (11%)
  matrix products  13.5 us (10%)
  other arithmetic  13.3 us (10%)
  local copies, waits for them, and re-layouts  9.47 us (7%)
    all_gather x1, waiting for transfers between devices, shards(): normed = lax.all_gather(local_normed[rows_of], 'gx', axis=0, tiled=False)  52 us
    dot_general x4, matrix products, shards(): jnp.einsum('btd,bdc->tc', rows, weights_of, preferred_element_type=jnp.fl...  11.1 us
    ppermute x7, starting transfers between devices, shards(): lax.ppermute(local_squares, 'gx', partner_route(gx_count, gx_count, k))  9.45 us
    ppermute x2, starting transfers between devices, shifted(): return lax.ppermute(value, axis, pairs)  6.89 us
    ppermute x1, starting transfers between devices, shards(): other = lax.ppermute(half_kv, ('gx', 'gy'), route)  4.89 us
    ppermute x3, starting transfers between devices, shards(): lax.ppermute(local_weights, 'gy', partner_route(gy_count, gy_count, k))  4.14 us
    ppermute x7, waiting for transfers between devices, shards(): lax.ppermute(local_squares, 'gx', partner_route(gx_count, gx_count, k))  4.01 us
    sin x2, other arithmetic, rope_tables(): return lax.optimization_barrier((jnp.cos(angles), jnp.sin(angles)))  3.34 us
  transfers between devices with their start and end apart: 17, of which 6 were waited for; matrix products, arithmetic and copies ran while one was open for 20% of the time, Pallas kernels for 0%

profile of v17, /device:TPU:0, one launch (start us, length us, event | category | flops | bytes accessed | tf_op | source)
XLA Modules:
  0.0 136.5 jit_solution(7009157493826863472)
XLA Ops:
  7.2 1.5 %convert_element_type.53 = f32[512,1024]{1,0:T(8,128)S(1)} convert(bf16[512,1024]{1,0:T(8,128)(2,1)} %param.8) | non-fusion elementwise | flops 524288 | bytes 3145728 | tf_op jit(solution)/shard_map/convert_element_type | solution.py:80
  8.8 0.8 dynamic-slice_convert_fusion
  9.6 1.2 multiply_convert_fusion
  10.9 0.2 multiply_reduce_fusion
  11.1 0.5 collective-permute-start.4
  11.6 2.6 %collective-permute-start.5 = (f32[512]{0:T(512)S(1)}, f32[512]{0:T(512)S(1)}, u32[]{:S(2)}, u32[]{:S(2)}) collective-permute-start(f32[512]{0:T(512)S(1)} %multiply_reduce_fusion), channel_id=1, source_target_pairs={{0,8},{4,12},{8,0},{12,4},{16,24},{20,28},{24,16},{28,20},{1,9},{5... | collective-permute-start | bytes 6152 | tf_op jit(solution)/shard_map/ppermute | solution.py:89
  14.3 0.2 collective-permute-start
  14.5 3.4 %collective-permute-start.11 = (s32[512]{0:T(512)S(1)}, s32[512]{0:T(512)S(1)}, u32[]{:S(2)}, u32[]{:S(2)}) collective-permute-start(s32[512]{0:T(512)S(1)} %broadcast_add_fusion), channel_id=1, source_target_pairs={{0,1},{1,2},{2,3},{4,5},{5,6},{6,7},{8,9},{9,10},{10,11},{12,13},{... | collective-permute-start | bytes 6152 | tf_op jit(solution)/shard_map/ppermute | solution.py:19
  18.4 0.5 multiply_sine_fusion.1
  19.0 0.5 copy.32
  19.4 2.8 %multiply_sine_fusion = (f32[512,256]{0,1:T(8,128)}, f32[512,256]{0,1:T(8,128)}) fusion(f32[256]{0:T(256)S(1)} %multiply_power_fusion, f32[512]{0:T(512)S(1)} %convert_element_type.56), kind=kLoop, calls=%fused_computation.42 | loop fusion | flops 131072 | bytes 1051648 | tf_op jit(solution)/shard_map/sin | solution.py:35
  22.3 0.5 copy.33
  22.8 1.2 maximum_select_fusion
  23.9 0.3 fusion.90
  24.2 1.5 %pad_maximum_fusion = bf16[2048,384]{1,0:T(8,128)(2,1)} fusion(bf16[2048,64]{1,0:T(8,128)(2,1)S(1)} %get-tuple-element.27, bf16[2048,64]{1,0:T(8,128)(2,1)S(1)} %get-tuple-element.26, bf16[2048,256]{1,0:T(8,128)(2,1)S(1)} %copy-done.1), kind=kLoop, calls=%fused_computation.29 | loop fusion | flops 4718592 | bytes 3145728 | tf_op jit(solution)/shard_map/concatenate | solution.py:73
  25.7 0.3 collective-permute-start.3
  26.1 2.7 %collective-permute-start.1 = (bf16[2048,384]{1,0:T(8,128)(2,1)}, bf16[2048,384]{1,0:T(8,128)(2,1)}, u32[]{:S(2)}, u32[]{:S(2)}) collective-permute-start(bf16[2048,384]{1,0:T(8,128)(2,1)} %pad_maximum_fusion), channel_id=1, source_target_pairs={{0,1},{1,0},{2,3},{3,2},{4,5},{5,4},{6,7},{7,6},{8,9},{9,8},{10,11... | collective-permute-start | bytes 4718600 | tf_op jit(solution)/shard_map/ppermute | solution.py:77
  28.8 0.5 copy.38
  29.6 2.7 %collective-permute-start.7 = (f32[512]{0:T(512)S(1)}, f32[512]{0:T(512)S(1)}, u32[]{:S(2)}, u32[]{:S(2)}) collective-permute-start(f32[512]{0:T(512)S(1)} %multiply_reduce_fusion), channel_id=1, source_target_pairs={{0,16},{4,20},{8,24},{12,28},{16,0},{20,4},{24,8},{28,12},{1,17},{... | collective-permute-start | bytes 6152 | tf_op jit(solution)/shard_map/ppermute | solution.py:89
  32.6 1.1 collective-permute-start.2
  33.7 1.3 collective-permute-done.7
  35.1 2.3 %collective-permute-start.9 = (f32[512]{0:T(512)S(1)}, f32[512]{0:T(512)S(1)}, u32[]{:S(2)}, u32[]{:S(2)}) collective-permute-start(f32[512]{0:T(512)S(1)} %multiply_reduce_fusion), channel_id=1, source_target_pairs={{0,24},{4,28},{8,16},{12,20},{16,8},{20,12},{24,0},{28,4},{1,25},{... | collective-permute-start | bytes 6152 | tf_op jit(solution)/shard_map/ppermute | solution.py:89
  37.4 1.1 collective-permute-start.10
  38.5 1.4 %fusion = pred[1024,1024]{0,1:T(32,128)(4,1)S(1)} fusion(s32[1024]{0:T(1024)S(1)} %bitcast.129, s32[1024]{0:T(1024)S(1)} %bitcast.128, s32[1024]{0:T(1024)S(1)} %pad_add_fusion, pred[1024]{0:T(1024)(128)(4,1)S(1)} %broadcast_compare_fusion), kind=kLoop, calls=%fused_computation.5 | loop fusion | flops 4194304 | bytes 1061888 | tf_op jit(solution)/shard_map/and | solution.py:161
  39.9 0.7 collective-permute-done.9
  40.6 1.7 %collective-permute-done.10 = f32[512]{0:T(512)S(1)} collective-permute-done((f32[512]{0:T(512)S(1)}, f32[512]{0:T(512)S(1)}, u32[]{:S(2)}, u32[]{:S(2)}) %collective-permute-start.10) | collective-permute-done | bytes 2080 | tf_op jit(solution)/shard_map/ppermute | solution.py:89
  42.4 0.6 gather_fusion
  43.0 0.9 copy.39
  44.1 52.0 %all-gather.3.cloned.1.call-done = bf16[4096,1024]{1,0:T(8,128)(2,1)} async-done(((bf16[512,1024]{1,0:T(8,128)(2,1)}), bf16[4096,1024]{1,0:T(8,128)(2,1)}) %all-gather.3.cloned.1.call-update) | async-done | bytes 8388624 | tf_op jit(solution)/shard_map/all_gather | solution.py:104
  96.1 2.7 %fusion.23 = f32[512,384]{0,1:T(8,128)S(1)} fusion(bf16[2,1024,64]{1,2,0:T(8,128)(2,1)S(1)} %copy.40, bf16[2,1024,64]{1,2,0:T(8,128)(2,1)} %copy.39, bf16[2,1024,256]{1,2,0:T(8,128)(2,1)S(1)} %copy.38, bf16[4,2,512,1024]{3,2,1,0:T(8,128)(2,1)} %bitcast.140, s32[]{:T(128)S(6)} %select_n.158), kind=kOutput, calls=%fused_computation.30 | convolution fusion | flops 810024960 | bytes 4456452 | tf_op jit(solution)/shard_map/btd,bdc->tc/dot_general | solution.py:113
  98.9 3.4 %fusion.34 = f32[512,384]{0,1:T(8,128)S(1)} fusion(bf16[2,1024,384]{2,1,0:T(8,128)(2,1)} %bitcast.20, bf16[4,2,512,1024]{3,2,1,0:T(8,128)(2,1)} %bitcast.141, s32[]{:T(128)S(6)} %select_n.165), kind=kOutput, calls=%fused_computation.33 | convolution fusion | flops 805306368 | bytes 4456452 | tf_op jit(solution)/shard_map/btd,bdc->tc/dot_general | solution.py:113
  102.3 2.5 %fusion.40 = f32[512,384]{0,1:T(8,128)S(1)} fusion(f32[512,384]{0,1:T(8,128)S(1)} %fusion.23, bf16[2,1024,384]{2,1,0:T(8,128)(2,1)} %bitcast.14, bf16[4,2,512,1024]{3,2,1,0:T(8,128)(2,1)S(1)} %bitcast.142, s32[]{:T(128)S(6)} %select_n.163), kind=kOutput, calls=%fused_computation.35 | convolution fusion | flops 805502976 | bytes 5242884 | tf_op jit(solution)/shard_map/btd,bdc->tc/dot_general | solution.py:113
  104.8 2.5 %fusion.46 = f32[512,384]{0,1:T(8,128)S(1)} fusion(f32[512,384]{0,1:T(8,128)S(1)} %fusion.34, f32[512,384]{0,1:T(8,128)S(1)} %fusion.40, bf16[2,1024,384]{2,1,0:T(8,128)(2,1)} %bitcast.17, bf16[4,2,512,1024]{3,2,1,0:T(8,128)(2,1)S(1)} %bitcast.143, s32[]{:T(128)S(6)} %select_n.164, f32[512]{0:T(512)S(1)} %add_rsqrt_fusion), kind=kOutput, calls=%fused_computation.37 | convolution fusion | flops 805896192 | bytes 6031364 | tf_op jit(solution)/shard_map/btd,bdc->tc/dot_general | solution.py:113
  107.5 3.5 %collective-permute-start.12 = (bf16[2,512,64]{1,2,0:T(8,128)(2,1)S(1)}, bf16[2,512,64]{1,2,0:T(8,128)(2,1)S(1)}, u32[]{:S(2)}, u32[]{:S(2)}) collective-permute-start(bf16[2,512,64]{1,2,0:T(8,128)(2,1)S(1)} %pad_maximum_fusion.3), channel_id=1, source_target_pairs={{0,1},{1,2},{2,3},{4,5},{5,6},{6,7},{8,9},{9,10},{10,11},{12,13},{... | collective-permute-start | bytes 393224 | tf_op jit(solution)/shard_map/ppermute | solution.py:19
  111.0 4.9 %collective-permute-start.13 = (bf16[2,512,64]{1,2,0:T(8,128)(2,1)S(1)}, bf16[2,512,64]{1,2,0:T(8,128)(2,1)S(1)}, u32[]{:S(2)}, u32[]{:S(2)}) collective-permute-start(bf16[2,512,64]{1,2,0:T(8,128)(2,1)S(1)} %pad_maximum_fusion.3), channel_id=1, source_target_pairs={{0,9},{1,10},{2,11},{4,13},{5,14},{6,15},{8,1},{9,2},{10,3},{12,5}... | collective-permute-start | bytes 393224 | tf_op jit(solution)/shard_map/ppermute | solution.py:136
  116.0 0.2 fusion.60
  116.6 0.2 reshape.200
  117.0 1.5 %scatter_fusion = bf16[64,2,512]{2,1,0:T(2,128)(2,1)S(1)} fusion(bf16[64,2,512]{2,1,0:T(2,128)(2,1)S(1)} %broadcast_in_dim.44, s32[32]{0:T(128)S(1)} %fusion.83, bf16[32,2,512]{2,1,0:T(2,128)(2,1)S(1)} %copy.45), kind=kCustom, calls=%fused_computation.1 | custom fusion | bytes 196736 | tf_op jit(solution)/shard_map/scatter | solution.py:191
  118.5 0.7 copy.46
  119.2 3.3 %all-to-all-start = ((bf16[4,16,2,512]{3,1,2,0:T(8,128)(2,1)}), bf16[4,16,2,512]{3,1,2,0:T(8,128)(2,1)S(1)}, u32[]{:S(2)}, u32[]{:S(2)}) async-start(bf16[4,16,2,512]{3,1,2,0:T(8,128)(2,1)} %copy.46), calls=%async_computation | async-start | bytes 262144 | tf_op jit(solution)/shard_map/all_to_all | solution.py:194
  122.7 1.0 fusion.3
  123.7 1.1 fusion.1
  124.8 1.4 %fusion.55 = bf16[1024,128]{1,0:T(8,128)(2,1)S(1)} fusion(pred[1024,1024]{0,1:T(32,128)(4,1)S(1)} %fusion, f32[1024,1024]{0,1:T(8,128)S(1)} %get-tuple-element.44, f32[1024]{0:T(1024)S(1)} %get-tuple-element.43, bf16[2,512,128]{1,2,0:T(8,128)(2,1)S(1)} %maximum_select_fusion.2, bf16[2,512,128]{1,2,0:T(8,128)(2,1)S(1)} %maximum_select_fusion.1, ...), kind=kOutput, calls=%fused_computation.41 | convolution fusion | flops 273547264 | bytes 6038528 | tf_op jit(solution)/shard_map/dot_general | solution.py:168
  126.2 0.7 copy.63
  127.0 0.6 all-to-all-done
  127.5 0.3 reshape.204
  127.9 0.9 copy.50
  128.8 0.9 copy.51
  (79 shorter events, 2.3 us)
Async XLA Ops:
  7.2 2.5 %copy-start = (bf16[512,1024]{1,0:T(8,128)(2,1)S(1)}, bf16[512,1024]{1,0:T(8,128)(2,1)}, u32[]{:S(2)}) copy-start(bf16[512,1024]{1,0:T(8,128)(2,1)} %param.8) | copy-start | bytes 3145732
  7.2 88.9 %all-gather.3.cloned.1.call-start = ((), (), s32[]{:S(2)}) async-start(), calls=%async_computation.1 | async-start | bytes 9437184 | tf_op jit(solution)/shard_map/all_gather | solution.py:104
  8.8 5.5 %copy-start.4 = (bf16[2048,32]{0,1:T(8,128)(2,1)S(1)}, bf16[2048,32]{0,1:T(8,128)(2,1)}, u32[]{:S(2)}) copy-start(bf16[2048,32]{0,1:T(8,128)(2,1)} %param.12) | copy-start | bytes 393220
  8.8 5.5 %copy-start.5 = (bf16[2048,32]{0,1:T(8,128)(2,1)S(1)}, bf16[2048,32]{0,1:T(8,128)(2,1)}, u32[]{:S(2)}) copy-start(bf16[2048,32]{0,1:T(8,128)(2,1)} %param.11) | copy-start | bytes 393220
  8.8 5.7 %copy-start.6 = (s32[512]{0:T(512)S(1)}, s32[512]{0:T(512)}, u32[]{:S(2)}) copy-start(s32[512]{0:T(512)} %param.13) | copy-start | bytes 6148
  8.8 9.2 %copy-start.8 = (s32[512]{0:T(512)S(1)}, s32[512]{0:T(512)}, u32[]{:S(2)}) copy-start(s32[512]{0:T(512)} %param.14) | copy-start | bytes 6148
  8.8 9.2 %copy-start.7 = (s32[32,1]{0,1:T(1,128)S(1)}, s32[32,1]{0,1:T(1,128)}, u32[]{:S(2)}) copy-start(s32[32,1]{0,1:T(1,128)} %param.15) | copy-start | bytes 388
  11.1 18.5 %collective-permute-start.4 = (f32[512]{0:T(512)S(1)}, f32[512]{0:T(512)S(1)}, u32[]{:S(2)}, u32[]{:S(2)}) collective-permute-start(f32[512]{0:T(512)S(1)} %multiply_reduce_fusion), channel_id=1, source_target_pairs={{0,4},{4,0},{8,12},{12,8},{16,20},{20,16},{24,28},{28,24},{1,5},{5... | collective-permute-start | bytes 6152 | tf_op jit(solution)/shard_map/ppermute | solution.py:89
  11.6 20.7 %collective-permute-start.5 = (f32[512]{0:T(512)S(1)}, f32[512]{0:T(512)S(1)}, u32[]{:S(2)}, u32[]{:S(2)}) collective-permute-start(f32[512]{0:T(512)S(1)} %multiply_reduce_fusion), channel_id=1, source_target_pairs={{0,8},{4,12},{8,0},{12,4},{16,24},{20,28},{24,16},{28,20},{1,9},{5... | collective-permute-start | bytes 6152 | tf_op jit(solution)/shard_map/ppermute | solution.py:89
  14.3 8.0 %collective-permute-start = (bf16[2,2048,32]{1,2,0:T(8,128)(2,1)S(1)}, bf16[2,2048,32]{1,2,0:T(8,128)(2,1)S(1)}, u32[]{:S(2)}, u32[]{:S(2)}) collective-permute-start(bf16[2,2048,32]{1,2,0:T(8,128)(2,1)S(1)} %pad_maximum_fusion.2), channel_id=1, source_target_pairs={{0,4},{4,0},{8,12},{12,8},{16,20},{20,16},{24,28},{28,24},{1,5},{5... | collective-permute-start | bytes 786440 | tf_op jit(solution)/shard_map/ppermute | solution.py:71
  14.5 14.9 %collective-permute-start.11 = (s32[512]{0:T(512)S(1)}, s32[512]{0:T(512)S(1)}, u32[]{:S(2)}, u32[]{:S(2)}) collective-permute-start(s32[512]{0:T(512)S(1)} %broadcast_add_fusion), channel_id=1, source_target_pairs={{0,1},{1,2},{2,3},{4,5},{5,6},{6,7},{8,9},{9,10},{10,11},{12,13},{... | collective-permute-start | bytes 6152 | tf_op jit(solution)/shard_map/ppermute | solution.py:19
  22.7 1.5 %copy-start.1 = (bf16[2048,256]{1,0:T(8,128)(2,1)S(1)}, bf16[2048,256]{1,0:T(8,128)(2,1)}, u32[]{:S(2)}) copy-start(bf16[2048,256]{1,0:T(8,128)(2,1)} %param.10) | copy-start | bytes 3145732
  25.7 73.1 %collective-permute-start.3 = (bf16[2048,384]{1,0:T(8,128)(2,1)}, bf16[2048,384]{1,0:T(8,128)(2,1)}, u32[]{:S(2)}, u32[]{:S(2)}) collective-permute-start(bf16[2048,384]{1,0:T(8,128)(2,1)} %pad_maximum_fusion), channel_id=1, source_target_pairs={{0,3},{1,2},{2,1},{3,0},{4,7},{5,6},{6,5},{7,4},{8,11},{9,10},{10,... | collective-permute-start | bytes 4718600 | tf_op jit(solution)/shard_map/ppermute | solution.py:77
  26.1 76.2 %collective-permute-start.1 = (bf16[2048,384]{1,0:T(8,128)(2,1)}, bf16[2048,384]{1,0:T(8,128)(2,1)}, u32[]{:S(2)}, u32[]{:S(2)}) collective-permute-start(bf16[2048,384]{1,0:T(8,128)(2,1)} %pad_maximum_fusion), channel_id=1, source_target_pairs={{0,1},{1,0},{2,3},{3,2},{4,5},{5,4},{6,7},{7,6},{8,9},{9,8},{10,11... | collective-permute-start | bytes 4718600 | tf_op jit(solution)/shard_map/ppermute | solution.py:77
  29.5 3.1 %collective-permute-start.6 = (f32[512]{0:T(512)S(1)}, f32[512]{0:T(512)S(1)}, u32[]{:S(2)}, u32[]{:S(2)}) collective-permute-start(f32[512]{0:T(512)S(1)} %multiply_reduce_fusion), channel_id=1, source_target_pairs={{0,12},{4,8},{8,4},{12,0},{16,28},{20,24},{24,20},{28,16},{1,13},{... | collective-permute-start | bytes 6152 | tf_op jit(solution)/shard_map/ppermute | solution.py:89
  29.6 5.5 %collective-permute-start.7 = (f32[512]{0:T(512)S(1)}, f32[512]{0:T(512)S(1)}, u32[]{:S(2)}, u32[]{:S(2)}) collective-permute-start(f32[512]{0:T(512)S(1)} %multiply_reduce_fusion), channel_id=1, source_target_pairs={{0,16},{4,20},{8,24},{12,28},{16,0},{20,4},{24,8},{28,12},{1,17},{... | collective-permute-start | bytes 6152 | tf_op jit(solution)/shard_map/ppermute | solution.py:89
  32.3 5.1 %collective-permute-start.8 = (f32[512]{0:T(512)S(1)}, f32[512]{0:T(512)S(1)}, u32[]{:S(2)}, u32[]{:S(2)}) collective-permute-start(f32[512]{0:T(512)S(1)} %multiply_reduce_fusion), channel_id=1, source_target_pairs={{0,20},{4,16},{8,28},{12,24},{16,4},{20,0},{24,12},{28,8},{1,21},{... | collective-permute-start | bytes 6152 | tf_op jit(solution)/shard_map/ppermute | solution.py:89
  32.6 72.2 %collective-permute-start.2 = (bf16[2048,384]{1,0:T(8,128)(2,1)}, bf16[2048,384]{1,0:T(8,128)(2,1)}, u32[]{:S(2)}, u32[]{:S(2)}) collective-permute-start(bf16[2048,384]{1,0:T(8,128)(2,1)} %pad_maximum_fusion), channel_id=1, source_target_pairs={{0,2},{1,3},{2,0},{3,1},{4,6},{5,7},{6,4},{7,5},{8,10},{9,11},{10,... | collective-permute-start | bytes 4718600 | tf_op jit(solution)/shard_map/ppermute | solution.py:77
  35.1 5.5 %collective-permute-start.9 = (f32[512]{0:T(512)S(1)}, f32[512]{0:T(512)S(1)}, u32[]{:S(2)}, u32[]{:S(2)}) collective-permute-start(f32[512]{0:T(512)S(1)} %multiply_reduce_fusion), channel_id=1, source_target_pairs={{0,24},{4,28},{8,16},{12,20},{16,8},{20,12},{24,0},{28,4},{1,25},{... | collective-permute-start | bytes 6152 | tf_op jit(solution)/shard_map/ppermute | solution.py:89
  37.4 5.0 %collective-permute-start.10 = (f32[512]{0:T(512)S(1)}, f32[512]{0:T(512)S(1)}, u32[]{:S(2)}, u32[]{:S(2)}) collective-permute-start(f32[512]{0:T(512)S(1)} %multiply_reduce_fusion), channel_id=1, source_target_pairs={{0,28},{4,24},{8,20},{12,16},{16,12},{20,8},{24,4},{28,0},{1,29},{... | collective-permute-start | bytes 6152 | tf_op jit(solution)/shard_map/ppermute | solution.py:89
  96.1 6.2 %copy-start.9 = (bf16[4096,1024]{1,0:T(8,128)(2,1)S(1)}, bf16[4096,1024]{1,0:T(8,128)(2,1)}, u32[]{:S(2)}) copy-start(bf16[4096,1024]{1,0:T(8,128)(2,1)} %all-gather.3.cloned.1.call-done) | copy-start | bytes 25165828
  107.2 8.8 %copy-start.2 = (f32[512,256]{0,1:T(8,128)S(1)}, f32[512,256]{0,1:T(8,128)}, u32[]{:S(2)}) copy-start(f32[512,256]{0,1:T(8,128)} %get-tuple-element.16) | copy-start | bytes 1572868
  107.3 8.8 %copy-start.3 = (f32[512,256]{0,1:T(8,128)S(1)}, f32[512,256]{0,1:T(8,128)}, u32[]{:S(2)}) copy-start(f32[512,256]{0,1:T(8,128)} %get-tuple-element.15) | copy-start | bytes 1572868
  107.4 15.1 %collective-permute-start.14 = (bf16[2,512,64]{1,2,0:T(8,128)(2,1)S(1)}, bf16[2,512,64]{1,2,0:T(8,128)(2,1)S(1)}, u32[]{:S(2)}, u32[]{:S(2)}) collective-permute-start(bf16[2,512,64]{1,2,0:T(8,128)(2,1)S(1)} %pad_maximum_fusion.3), channel_id=1, source_target_pairs={{0,8},{4,12},{8,0},{12,4},{16,24},{20,28},{24,16},{28,20},{1,9},{5... | collective-permute-start | bytes 393224 | tf_op jit(solution)/shard_map/ppermute | solution.py:127
  107.5 15.1 %collective-permute-start.12 = (bf16[2,512,64]{1,2,0:T(8,128)(2,1)S(1)}, bf16[2,512,64]{1,2,0:T(8,128)(2,1)S(1)}, u32[]{:S(2)}, u32[]{:S(2)}) collective-permute-start(bf16[2,512,64]{1,2,0:T(8,128)(2,1)S(1)} %pad_maximum_fusion.3), channel_id=1, source_target_pairs={{0,1},{1,2},{2,3},{4,5},{5,6},{6,7},{8,9},{9,10},{10,11},{12,13},{... | collective-permute-start | bytes 393224 | tf_op jit(solution)/shard_map/ppermute | solution.py:19
  111.0 11.6 %collective-permute-start.13 = (bf16[2,512,64]{1,2,0:T(8,128)(2,1)S(1)}, bf16[2,512,64]{1,2,0:T(8,128)(2,1)S(1)}, u32[]{:S(2)}, u32[]{:S(2)}) collective-permute-start(bf16[2,512,64]{1,2,0:T(8,128)(2,1)S(1)} %pad_maximum_fusion.3), channel_id=1, source_target_pairs={{0,9},{1,10},{2,11},{4,13},{5,14},{6,15},{8,1},{9,2},{10,3},{12,5}... | collective-permute-start | bytes 393224 | tf_op jit(solution)/shard_map/ppermute | solution.py:136
  119.2 8.3 %all-to-all-start = ((bf16[4,16,2,512]{3,1,2,0:T(8,128)(2,1)}), bf16[4,16,2,512]{3,1,2,0:T(8,128)(2,1)S(1)}, u32[]{:S(2)}, u32[]{:S(2)}) async-start(bf16[4,16,2,512]{3,1,2,0:T(8,128)(2,1)} %copy.46), calls=%async_computation | async-start | bytes 262144 | tf_op jit(solution)/shard_map/all_to_all | solution.py:194
Sparse Core Ops, SparseCore 0:
  11.0 85.0 all-gather.2

commit v18 on v17

--- a/solution.py
+++ b/solution.py
@@ -185,11 +185,11 @@
     rank_in = jnp.sum(earlier * one_hot, axis=1)
     slot_of = owner_of * capacity + rank_in
     kv_pages = own_kv.reshape(2, page_rows, PAGE * quarter).transpose(1, 0, 2)
-    send_kv = (
-        jnp.zeros((owner_count * capacity, 2, PAGE * quarter), jnp.bfloat16)
-        .at[slot_of]
-        .set(kv_pages)
-    )
+    slot_ids = jnp.arange(owner_count * capacity, dtype=jnp.int32)
+    placing = (slot_ids[:, None] == slot_of[None, :]).astype(jnp.bfloat16)
+    send_kv = jnp.einsum(
+        "sp,pkc->skc", placing, kv_pages, preferred_element_type=jnp.float32
+    ).astype(jnp.bfloat16)
     send_kv = send_kv.reshape(owner_count, capacity, 2, PAGE * quarter)
     got_kv = lax.all_to_all(send_kv, "gy", split_axis=0, concat_axis=0, tiled=True)
     got_kv, context = lax.optimization_barrier((got_kv, context))

time: 137 us -> 146 us (1.066)
  other arithmetic: 13.3 us -> 20.7 us
  local copies, waits for them, and re-layouts: 9.47 us -> 12.6 us
  waiting for transfers between devices: 56.6 us -> 53.5 us
    all_gather x1, waiting for transfers between devices: 52 us -> 48.7 us  [shards(): normed = lax.all_gather(local_normed[rows_of], 'gx', axis=0, tiled=False)]
    select_n x3, other arithmetic: 1.27 us -> 3.38 us  [joined(): jnp.where(mine_first, jnp.concatenate([mine, theirs], axis=-1), jnp.conca...]
    convert_element_type x1, other arithmetic: 0.22 us -> 1.93 us  [shards(): rope(projected[:, :query_cols], query_tables).astype(jnp.bfloat16)]
    reshape x1, local copies, waits for them, and re-layouts: 0.23 us -> 1.82 us  [shards(): kv_pages = own_kv.reshape(2, page_rows, PAGE * quarter).transpose(1, 0, 2)]
    dynamic_slice x1, local copies, waits for them, and re-layouts: 0.17 us -> 1.68 us  [shards(): lax.dynamic_slice_in_dim(half_kv, spot % 2 * quarter, quarter, 2)]
    scatter x1 -> x0, local copies, waits for them, and re-layouts: 1.49 us -> none  [shards(): send_kv = jnp.zeros((owner_count * capacity, 2, PAGE * quarter), jnp.bflo...]
  transfers between devices with their start and end apart: 17 -> 17, of which waited for: 6 -> 5; matrix products, arithmetic and copies ran while one was open for 20% -> 27% of each run, Pallas kernels for 0% -> 0%
where the time goes in v18:
time: 146 us
  waiting for transfers between devices  53.5 us (37%)
  starting transfers between devices  29.9 us (20%)
  other arithmetic  20.7 us (14%)
  between operations  14.6 us (10%)
  matrix products  14.5 us (10%)
  local copies, waits for them, and re-layouts  12.6 us (9%)
    all_gather x1, waiting for transfers between devices, shards(): normed = lax.all_gather(local_normed[rows_of], 'gx', axis=0, tiled=False)  48.7 us
    dot_general x4, matrix products, shards(): jnp.einsum('btd,bdc->tc', rows, weights_of, preferred_element_type=jnp.fl...  11 us
    ppermute x7, starting transfers between devices, shards(): lax.ppermute(local_squares, 'gx', partner_route(gx_count, gx_count, k))  10.6 us
    ppermute x2, starting transfers between devices, shifted(): return lax.ppermute(value, axis, pairs)  7.35 us
    ppermute x1, starting transfers between devices, shards(): other = lax.ppermute(half_kv, ('gx', 'gy'), route)  4.92 us
    ppermute x7, waiting for transfers between devices, shards(): lax.ppermute(local_squares, 'gx', partner_route(gx_count, gx_count, k))  4.77 us
    sin x2, other arithmetic, rope_tables(): return lax.optimization_barrier((jnp.cos(angles), jnp.sin(angles)))  4 us
    ppermute x3, starting transfers between devices, shards(): lax.ppermute(local_weights, 'gy', partner_route(gy_count, gy_count, k))  3.46 us
  transfers between devices with their start and end apart: 17, of which 5 were waited for; matrix products, arithmetic and copies ran while one was open for 27% of the time, Pallas kernels for 0%

profile of v18, /device:TPU:0, one launch (start us, length us, event | category | flops | bytes accessed | tf_op | source)
XLA Modules:
  0.0 145.8 jit_solution(3042772819661681484)
XLA Ops:
  7.2 1.5 %convert_element_type.57 = f32[512,1024]{1,0:T(8,128)S(1)} convert(bf16[512,1024]{1,0:T(8,128)(2,1)} %param.8) | non-fusion elementwise | flops 524288 | bytes 3145728 | tf_op jit(solution)/shard_map/convert_element_type | solution.py:80
  8.8 0.8 dynamic-slice_convert_fusion
  9.6 1.2 multiply_convert_fusion
  11.1 0.5 collective-permute-start.4
  11.6 2.6 %collective-permute-start.5 = (f32[512]{0:T(512)S(1)}, f32[512]{0:T(512)S(1)}, u32[]{:S(2)}, u32[]{:S(2)}) collective-permute-start(f32[512]{0:T(512)S(1)} %multiply_reduce_fusion), channel_id=1, source_target_pairs={{0,8},{4,12},{8,0},{12,4},{16,24},{20,28},{24,16},{28,20},{1,9},{5... | collective-permute-start | bytes 6152 | tf_op jit(solution)/shard_map/ppermute | solution.py:89
  14.6 3.4 %collective-permute-start.11 = (s32[512]{0:T(512)S(1)}, s32[512]{0:T(512)S(1)}, u32[]{:S(2)}, u32[]{:S(2)}) collective-permute-start(s32[512]{0:T(512)S(1)} %broadcast_add_fusion), channel_id=1, source_target_pairs={{0,1},{1,2},{2,3},{4,5},{5,6},{6,7},{8,9},{9,10},{10,11},{12,13},{... | collective-permute-start | bytes 6152 | tf_op jit(solution)/shard_map/ppermute | solution.py:19
  18.4 1.2 multiply_sine_fusion.1
  19.6 0.5 fusion.86
  20.6 2.8 %multiply_sine_fusion = (f32[512,256]{0,1:T(8,128)}, f32[512,256]{0,1:T(8,128)}) fusion(f32[256]{0:T(256)S(1)} %multiply_power_fusion, f32[512]{0:T(512)S(1)} %convert_element_type.60), kind=kLoop, calls=%fused_computation.42 | loop fusion | flops 131072 | bytes 1051648 | tf_op jit(solution)/shard_map/sin | solution.py:35
  23.4 0.5 copy.31
  23.9 1.2 maximum_select_fusion
  25.4 1.5 %pad_maximum_fusion = bf16[2048,384]{1,0:T(8,128)(2,1)} fusion(bf16[2048,64]{1,0:T(8,128)(2,1)S(1)} %get-tuple-element.27, bf16[2048,64]{1,0:T(8,128)(2,1)S(1)} %get-tuple-element.26, bf16[2048,256]{1,0:T(8,128)(2,1)S(1)} %copy-done.1), kind=kLoop, calls=%fused_computation.28 | loop fusion | flops 4718592 | bytes 3145728 | tf_op jit(solution)/shard_map/concatenate | solution.py:73
  27.2 0.6 multiply_add_fusion
  27.8 2.6 %collective-permute-start.1 = (bf16[2048,384]{1,0:T(8,128)(2,1)}, bf16[2048,384]{1,0:T(8,128)(2,1)}, u32[]{:S(2)}, u32[]{:S(2)}) collective-permute-start(bf16[2048,384]{1,0:T(8,128)(2,1)} %pad_maximum_fusion), channel_id=1, source_target_pairs={{0,1},{1,0},{2,3},{3,2},{4,5},{5,4},{6,7},{7,6},{8,9},{9,8},{10,11... | collective-permute-start | bytes 4718600 | tf_op jit(solution)/shard_map/ppermute | solution.py:77
  30.5 0.6 fusion.85
  31.1 0.5 copy.36
  31.6 0.6 ge.26
  32.3 2.7 %collective-permute-start.7 = (f32[512]{0:T(512)S(1)}, f32[512]{0:T(512)S(1)}, u32[]{:S(2)}, u32[]{:S(2)}) collective-permute-start(f32[512]{0:T(512)S(1)} %multiply_reduce_fusion), channel_id=1, source_target_pairs={{0,16},{4,20},{8,24},{12,28},{16,0},{20,4},{24,8},{28,12},{1,17},{... | collective-permute-start | bytes 6152 | tf_op jit(solution)/shard_map/ppermute | solution.py:89
  35.8 1.1 collective-permute-done.7
  36.9 4.5 %collective-permute-start.9 = (f32[512]{0:T(512)S(1)}, f32[512]{0:T(512)S(1)}, u32[]{:S(2)}, u32[]{:S(2)}) collective-permute-start(f32[512]{0:T(512)S(1)} %multiply_reduce_fusion), channel_id=1, source_target_pairs={{0,24},{4,28},{8,16},{12,20},{16,8},{20,12},{24,0},{28,4},{1,25},{... | collective-permute-start | bytes 6152 | tf_op jit(solution)/shard_map/ppermute | solution.py:89
  41.4 1.4 fusion
  43.0 3.4 %collective-permute-done.10 = f32[512]{0:T(512)S(1)} collective-permute-done((f32[512]{0:T(512)S(1)}, f32[512]{0:T(512)S(1)}, u32[]{:S(2)}, u32[]{:S(2)}) %collective-permute-start.10) | collective-permute-done | bytes 2080 | tf_op jit(solution)/shard_map/ppermute | solution.py:89
  46.4 0.6 gather_fusion
  47.5 48.7 %all-gather.3.cloned.1.call-done = bf16[4096,1024]{1,0:T(8,128)(2,1)} async-done(((bf16[512,1024]{1,0:T(8,128)(2,1)}), bf16[4096,1024]{1,0:T(8,128)(2,1)}) %all-gather.3.cloned.1.call-update) | async-done | bytes 8388624 | tf_op jit(solution)/shard_map/all_gather | solution.py:104
  96.1 2.8 %fusion.23 = f32[512,384]{0,1:T(8,128)S(1)} fusion(bf16[2,1024,64]{1,2,0:T(8,128)(2,1)S(1)} %copy.38, bf16[2,1024,64]{1,2,0:T(8,128)(2,1)S(1)} %copy.37, bf16[2,1024,256]{1,2,0:T(8,128)(2,1)S(1)} %copy.36, bf16[4,2,512,1024]{3,2,1,0:T(8,128)(2,1)} %bitcast.139, s32[]{:T(128)S(6)} %select_n.153), kind=kOutput, calls=%fused_computation.29 | convolution fusion | flops 810024960 | bytes 4456452 | tf_op jit(solution)/shard_map/btd,bdc->tc/dot_general | solution.py:113
  98.9 3.3 %fusion.34 = f32[512,384]{0,1:T(8,128)S(1)} fusion(bf16[2,1024,384]{2,1,0:T(8,128)(2,1)} %bitcast.19, bf16[4,2,512,1024]{3,2,1,0:T(8,128)(2,1)} %bitcast.140, s32[]{:T(128)S(6)} %select_n.160), kind=kOutput, calls=%fused_computation.32 | convolution fusion | flops 805306368 | bytes 4456452 | tf_op jit(solution)/shard_map/btd,bdc->tc/dot_general | solution.py:113
  102.2 2.5 %fusion.40 = f32[512,384]{0,1:T(8,128)S(1)} fusion(f32[512,384]{0,1:T(8,128)S(1)} %fusion.23, bf16[2,1024,384]{2,1,0:T(8,128)(2,1)} %bitcast.13, bf16[4,2,512,1024]{3,2,1,0:T(8,128)(2,1)S(1)} %bitcast.141, s32[]{:T(128)S(6)} %select_n.158), kind=kOutput, calls=%fused_computation.34 | convolution fusion | flops 805502976 | bytes 5242884 | tf_op jit(solution)/shard_map/btd,bdc->tc/dot_general | solution.py:113
  104.7 2.5 %fusion.46 = f32[512,384]{0,1:T(8,128)S(1)} fusion(f32[512,384]{0,1:T(8,128)S(1)} %fusion.34, f32[512,384]{0,1:T(8,128)S(1)} %fusion.40, bf16[2,1024,384]{2,1,0:T(8,128)(2,1)} %bitcast.16, bf16[4,2,512,1024]{3,2,1,0:T(8,128)(2,1)S(1)} %bitcast.142, s32[]{:T(128)S(6)} %select_n.159, f32[512]{0:T(512)S(1)} %add_rsqrt_fusion), kind=kOutput, calls=%fused_computation.36 | convolution fusion | flops 805896192 | bytes 6031364 | tf_op jit(solution)/shard_map/btd,bdc->tc/dot_general | solution.py:113
  107.5 0.7 pad_maximum_fusion.3
  108.1 4.0 %collective-permute-start.12 = (bf16[2,512,64]{1,2,0:T(8,128)(2,1)}, bf16[2,512,64]{1,2,0:T(8,128)(2,1)}, u32[]{:S(2)}, u32[]{:S(2)}) collective-permute-start(bf16[2,512,64]{1,2,0:T(8,128)(2,1)} %pad_maximum_fusion.3), channel_id=1, source_target_pairs={{0,1},{1,2},{2,3},{4,5},{5,6},{6,7},{8,9},{9,10},{10,11},{12,13},{... | collective-permute-start | bytes 393224 | tf_op jit(solution)/shard_map/ppermute | solution.py:19
  112.1 4.9 %collective-permute-start.13 = (bf16[2,512,64]{1,2,0:T(8,128)(2,1)}, bf16[2,512,64]{1,2,0:T(8,128)(2,1)}, u32[]{:S(2)}, u32[]{:S(2)}) collective-permute-start(bf16[2,512,64]{1,2,0:T(8,128)(2,1)} %pad_maximum_fusion.3), channel_id=1, source_target_pairs={{0,9},{1,10},{2,11},{4,13},{5,14},{6,15},{8,1},{9,2},{10,3},{12,5}... | collective-permute-start | bytes 393224 | tf_op jit(solution)/shard_map/ppermute | solution.py:136
  117.0 0.9 fusion.95
  117.9 0.6 fusion.74
  118.6 1.7 %copy.42 = bf16[2,512,32]{2,1,0:T(8,128)(2,1)} copy(bf16[2,512,32]{1,2,0:T(8,128)(2,1)} %fusion.74) | data formatting | bytes 131072 | tf_op jit(solution)/shard_map/dynamic_slice | solution.py:124
  120.2 1.8 %reshape.207 = bf16[2,32,512]{2,1,0:T(8,128)(2,1)} reshape(bf16[2,512,32]{2,1,0:T(8,128)(2,1)} %copy.42) | data formatting | bytes 131072 | tf_op jit(solution)/shard_map/reshape | solution.py:187
  122.1 1.9 %fusion.60 = bf16[512,256]{0,1:T(8,128)(2,1)} fusion(f32[512,256]{0,1:T(8,128)S(1)} %copy-done.2, f32[512,1]{0,1:T(1,128)S(1)} %get-tuple-element.30, f32[512,255]{0,1:T(8,128)} %get-tuple-element.34, f32[512,256]{0,1:T(8,128)S(1)} %copy-done.3, f32[512,384]{0,1:T(8,128)S(1)} %fusion.46, f32[512,255]{0,1:T(8,128)S(1)} %get-tuple-element.33, ...), kind=kLoop, calls=%fused_computation.48 | loop fusion | flops 1179648 | bytes 2883840 | tf_op jit(solution)/shard_map/convert_element_type | solution.py:122
  124.0 1.1 convolution_convert_fusion
  125.1 1.1 copy.44
  126.3 0.7 copy.43
  126.9 3.3 %all-to-all-start = ((bf16[4,16,2,512]{3,1,2,0:T(8,128)(2,1)}), bf16[4,16,2,512]{3,1,2,0:T(8,128)(2,1)S(1)}, u32[]{:S(2)}, u32[]{:S(2)}) async-start(bf16[4,16,2,512]{3,1,2,0:T(8,128)(2,1)} %copy.43), calls=%async_computation | async-start | bytes 262144 | tf_op jit(solution)/shard_map/all_to_all | solution.py:194
  130.3 1.1 maximum_select_fusion.2
  131.4 1.2 maximum_select_fusion.1
  132.5 1.0 fusion.3
  133.5 1.1 fusion.1
  134.6 1.4 fusion.55
  136.1 0.7 copy.60
  137.2 0.9 copy.47
  138.1 0.9 copy.48
  (87 shorter events, 4.2 us)
Async XLA Ops:
  7.2 2.5 %copy-start = (bf16[512,1024]{1,0:T(8,128)(2,1)S(1)}, bf16[512,1024]{1,0:T(8,128)(2,1)}, u32[]{:S(2)}) copy-start(bf16[512,1024]{1,0:T(8,128)(2,1)} %param.8) | copy-start | bytes 3145732
  7.2 88.9 %all-gather.3.cloned.1.call-start = ((), (), s32[]{:S(2)}) async-start(), calls=%async_computation.1 | async-start | bytes 9437184 | tf_op jit(solution)/shard_map/all_gather | solution.py:104
  8.8 5.5 %copy-start.5 = (bf16[2048,32]{0,1:T(8,128)(2,1)S(1)}, bf16[2048,32]{0,1:T(8,128)(2,1)}, u32[]{:S(2)}) copy-start(bf16[2048,32]{0,1:T(8,128)(2,1)} %param.12) | copy-start | bytes 393220
  8.8 5.5 %copy-start.6 = (bf16[2048,32]{0,1:T(8,128)(2,1)S(1)}, bf16[2048,32]{0,1:T(8,128)(2,1)}, u32[]{:S(2)}) copy-start(bf16[2048,32]{0,1:T(8,128)(2,1)} %param.11) | copy-start | bytes 393220
  8.8 5.8 %copy-start.7 = (s32[512]{0:T(512)S(1)}, s32[512]{0:T(512)}, u32[]{:S(2)}) copy-start(s32[512]{0:T(512)} %param.13) | copy-start | bytes 6148
  8.8 9.2 %copy-start.9 = (s32[512]{0:T(512)S(1)}, s32[512]{0:T(512)}, u32[]{:S(2)}) copy-start(s32[512]{0:T(512)} %param.14) | copy-start | bytes 6148
  8.8 9.2 %copy-start.8 = (s32[32,1]{0,1:T(1,128)S(1)}, s32[32,1]{0,1:T(1,128)}, u32[]{:S(2)}) copy-start(s32[32,1]{0,1:T(1,128)} %param.15) | copy-start | bytes 388
  11.1 21.1 %collective-permute-start.4 = (f32[512]{0:T(512)S(1)}, f32[512]{0:T(512)S(1)}, u32[]{:S(2)}, u32[]{:S(2)}) collective-permute-start(f32[512]{0:T(512)S(1)} %multiply_reduce_fusion), channel_id=1, source_target_pairs={{0,4},{4,0},{8,12},{12,8},{16,20},{20,16},{24,28},{28,24},{1,5},{5... | collective-permute-start | bytes 6152 | tf_op jit(solution)/shard_map/ppermute | solution.py:89
  11.6 23.3 %collective-permute-start.5 = (f32[512]{0:T(512)S(1)}, f32[512]{0:T(512)S(1)}, u32[]{:S(2)}, u32[]{:S(2)}) collective-permute-start(f32[512]{0:T(512)S(1)} %multiply_reduce_fusion), channel_id=1, source_target_pairs={{0,8},{4,12},{8,0},{12,4},{16,24},{20,28},{24,16},{28,20},{1,9},{5... | collective-permute-start | bytes 6152 | tf_op jit(solution)/shard_map/ppermute | solution.py:89
  14.3 9.1 %collective-permute-start = (bf16[2,2048,32]{1,2,0:T(8,128)(2,1)S(1)}, bf16[2,2048,32]{1,2,0:T(8,128)(2,1)S(1)}, u32[]{:S(2)}, u32[]{:S(2)}) collective-permute-start(bf16[2,2048,32]{1,2,0:T(8,128)(2,1)S(1)} %pad_maximum_fusion.2), channel_id=1, source_target_pairs={{0,4},{4,0},{8,12},{12,8},{16,20},{20,16},{24,28},{28,24},{1,5},{5... | collective-permute-start | bytes 786440 | tf_op jit(solution)/shard_map/ppermute | solution.py:71
  14.6 17.7 %collective-permute-start.11 = (s32[512]{0:T(512)S(1)}, s32[512]{0:T(512)S(1)}, u32[]{:S(2)}, u32[]{:S(2)}) collective-permute-start(s32[512]{0:T(512)S(1)} %broadcast_add_fusion), channel_id=1, source_target_pairs={{0,1},{1,2},{2,3},{4,5},{5,6},{6,7},{8,9},{9,10},{10,11},{12,13},{... | collective-permute-start | bytes 6152 | tf_op jit(solution)/shard_map/ppermute | solution.py:19
  23.9 1.5 copy-start.1
  26.9 72.0 %collective-permute-start.3 = (bf16[2048,384]{1,0:T(8,128)(2,1)}, bf16[2048,384]{1,0:T(8,128)(2,1)}, u32[]{:S(2)}, u32[]{:S(2)}) collective-permute-start(bf16[2048,384]{1,0:T(8,128)(2,1)} %pad_maximum_fusion), channel_id=1, source_target_pairs={{0,3},{1,2},{2,1},{3,0},{4,7},{5,6},{6,5},{7,4},{8,11},{9,10},{10,... | collective-permute-start | bytes 4718600 | tf_op jit(solution)/shard_map/ppermute | solution.py:77
  27.8 74.4 %collective-permute-start.1 = (bf16[2048,384]{1,0:T(8,128)(2,1)}, bf16[2048,384]{1,0:T(8,128)(2,1)}, u32[]{:S(2)}, u32[]{:S(2)}) collective-permute-start(bf16[2048,384]{1,0:T(8,128)(2,1)} %pad_maximum_fusion), channel_id=1, source_target_pairs={{0,1},{1,0},{2,3},{3,2},{4,5},{5,4},{6,7},{7,6},{8,9},{9,8},{10,11... | collective-permute-start | bytes 4718600 | tf_op jit(solution)/shard_map/ppermute | solution.py:77
  32.2 3.1 %collective-permute-start.6 = (f32[512]{0:T(512)S(1)}, f32[512]{0:T(512)S(1)}, u32[]{:S(2)}, u32[]{:S(2)}) collective-permute-start(f32[512]{0:T(512)S(1)} %multiply_reduce_fusion), channel_id=1, source_target_pairs={{0,12},{4,8},{8,4},{12,0},{16,28},{20,24},{24,20},{28,16},{1,13},{... | collective-permute-start | bytes 6152 | tf_op jit(solution)/shard_map/ppermute | solution.py:89
  32.3 4.6 %collective-permute-start.7 = (f32[512]{0:T(512)S(1)}, f32[512]{0:T(512)S(1)}, u32[]{:S(2)}, u32[]{:S(2)}) collective-permute-start(f32[512]{0:T(512)S(1)} %multiply_reduce_fusion), channel_id=1, source_target_pairs={{0,16},{4,20},{8,24},{12,28},{16,0},{20,4},{24,8},{28,12},{1,17},{... | collective-permute-start | bytes 6152 | tf_op jit(solution)/shard_map/ppermute | solution.py:89
  34.9 6.4 %collective-permute-start.8 = (f32[512]{0:T(512)S(1)}, f32[512]{0:T(512)S(1)}, u32[]{:S(2)}, u32[]{:S(2)}) collective-permute-start(f32[512]{0:T(512)S(1)} %multiply_reduce_fusion), channel_id=1, source_target_pairs={{0,20},{4,16},{8,28},{12,24},{16,4},{20,0},{24,12},{28,8},{1,21},{... | collective-permute-start | bytes 6152 | tf_op jit(solution)/shard_map/ppermute | solution.py:89
  35.3 69.4 %collective-permute-start.2 = (bf16[2048,384]{1,0:T(8,128)(2,1)}, bf16[2048,384]{1,0:T(8,128)(2,1)}, u32[]{:S(2)}, u32[]{:S(2)}) collective-permute-start(bf16[2048,384]{1,0:T(8,128)(2,1)} %pad_maximum_fusion), channel_id=1, source_target_pairs={{0,2},{1,3},{2,0},{3,1},{4,6},{5,7},{6,4},{7,5},{8,10},{9,11},{10,... | collective-permute-start | bytes 4718600 | tf_op jit(solution)/shard_map/ppermute | solution.py:77
  36.9 6.1 %collective-permute-start.9 = (f32[512]{0:T(512)S(1)}, f32[512]{0:T(512)S(1)}, u32[]{:S(2)}, u32[]{:S(2)}) collective-permute-start(f32[512]{0:T(512)S(1)} %multiply_reduce_fusion), channel_id=1, source_target_pairs={{0,24},{4,28},{8,16},{12,20},{16,8},{20,12},{24,0},{28,4},{1,25},{... | collective-permute-start | bytes 6152 | tf_op jit(solution)/shard_map/ppermute | solution.py:89
  41.4 5.0 %collective-permute-start.10 = (f32[512]{0:T(512)S(1)}, f32[512]{0:T(512)S(1)}, u32[]{:S(2)}, u32[]{:S(2)}) collective-permute-start(f32[512]{0:T(512)S(1)} %multiply_reduce_fusion), channel_id=1, source_target_pairs={{0,28},{4,24},{8,20},{12,16},{16,12},{20,8},{24,4},{28,0},{1,29},{... | collective-permute-start | bytes 6152 | tf_op jit(solution)/shard_map/ppermute | solution.py:89
  96.1 6.1 %copy-start.14 = (bf16[4096,1024]{1,0:T(8,128)(2,1)S(1)}, bf16[4096,1024]{1,0:T(8,128)(2,1)}, u32[]{:S(2)}) copy-start(bf16[4096,1024]{1,0:T(8,128)(2,1)} %all-gather.3.cloned.1.call-done) | copy-start | bytes 25165828
  104.7 2.6 %copy-start.4 = (f32[512,64]{0,1:T(8,128)S(1)}, f32[512,64]{0,1:T(8,128)}, u32[]{:S(2)}) copy-start(f32[512,64]{0,1:T(8,128)} %get-tuple-element.13) | copy-start | bytes 393220
  104.7 2.6 %copy-start.11 = (pred[64]{0:T(512)(128)(4,1)S(1)}, pred[64]{0:T(512)(128)(4,1)}, u32[]{:S(2)}) copy-start(pred[64]{0:T(512)(128)(4,1)} %fusion.86) | copy-start | bytes 196
  107.2 14.8 %copy-start.2 = (f32[512,256]{0,1:T(8,128)S(1)}, f32[512,256]{0,1:T(8,128)}, u32[]{:S(2)}) copy-start(f32[512,256]{0,1:T(8,128)} %get-tuple-element.16) | copy-start | bytes 1572868
  107.3 14.8 %copy-start.3 = (f32[512,256]{0,1:T(8,128)S(1)}, f32[512,256]{0,1:T(8,128)}, u32[]{:S(2)}) copy-start(f32[512,256]{0,1:T(8,128)} %get-tuple-element.15) | copy-start | bytes 1572868
  107.3 14.8 %copy-start.13 = (pred[256]{0:T(512)(128)(4,1)S(1)}, pred[256]{0:T(512)(128)(4,1)}, u32[]{:S(2)}) copy-start(pred[256]{0:T(512)(128)(4,1)} %fusion.85) | copy-start | bytes 772
  107.4 16.6 %copy-start.12 = (s32[32]{0:T(128)S(1)}, s32[32]{0:T(128)}, u32[]{:S(2)}) copy-start(s32[32]{0:T(128)} %multiply_add_fusion) | copy-start | bytes 388
  108.1 22.1 %collective-permute-start.14 = (bf16[2,512,64]{1,2,0:T(8,128)(2,1)}, bf16[2,512,64]{1,2,0:T(8,128)(2,1)}, u32[]{:S(2)}, u32[]{:S(2)}) collective-permute-start(bf16[2,512,64]{1,2,0:T(8,128)(2,1)} %pad_maximum_fusion.3), channel_id=1, source_target_pairs={{0,8},{4,12},{8,0},{12,4},{16,24},{20,28},{24,16},{28,20},{1,9},{5... | collective-permute-start | bytes 393224 | tf_op jit(solution)/shard_map/ppermute | solution.py:127
  108.1 23.2 %collective-permute-start.12 = (bf16[2,512,64]{1,2,0:T(8,128)(2,1)}, bf16[2,512,64]{1,2,0:T(8,128)(2,1)}, u32[]{:S(2)}, u32[]{:S(2)}) collective-permute-start(bf16[2,512,64]{1,2,0:T(8,128)(2,1)} %pad_maximum_fusion.3), channel_id=1, source_target_pairs={{0,1},{1,2},{2,3},{4,5},{5,6},{6,7},{8,9},{9,10},{10,11},{12,13},{... | collective-permute-start | bytes 393224 | tf_op jit(solution)/shard_map/ppermute | solution.py:19
  112.1 19.3 %collective-permute-start.13 = (bf16[2,512,64]{1,2,0:T(8,128)(2,1)}, bf16[2,512,64]{1,2,0:T(8,128)(2,1)}, u32[]{:S(2)}, u32[]{:S(2)}) collective-permute-start(bf16[2,512,64]{1,2,0:T(8,128)(2,1)} %pad_maximum_fusion.3), channel_id=1, source_target_pairs={{0,9},{1,10},{2,11},{4,13},{5,14},{6,15},{8,1},{9,2},{10,3},{12,5}... | collective-permute-start | bytes 393224 | tf_op jit(solution)/shard_map/ppermute | solution.py:136
  126.9 9.9 %all-to-all-start = ((bf16[4,16,2,512]{3,1,2,0:T(8,128)(2,1)}), bf16[4,16,2,512]{3,1,2,0:T(8,128)(2,1)S(1)}, u32[]{:S(2)}, u32[]{:S(2)}) async-start(bf16[4,16,2,512]{3,1,2,0:T(8,128)(2,1)} %copy.43), calls=%async_computation | async-start | bytes 262144 | tf_op jit(solution)/shard_map/all_to_all | solution.py:194
  133.5 1.1 copy-start.10
Sparse Core Ops, SparseCore 0:
  11.0 85.0 all-gather.2

commit v19 on v17

--- a/solution.py
+++ b/solution.py
@@ -80,7 +80,8 @@
     local_float = tokens_in.astype(jnp.float32)
     my_gx = lax.axis_index("gx")
     feature_block = tokens_in.shape[1]
-    local_gain = lax.dynamic_slice_in_dim(norm_gain, my_gx * feature_block, feature_block, 0)
+    gain_rows = norm_gain.reshape(gx_count, feature_block)
+    local_gain = lax.dynamic_index_in_dim(gain_rows, my_gx, 0, keepdims=False)
     local_normed = (local_float * local_gain.astype(jnp.float32)[None, :]).astype(jnp.bfloat16)
     local_normed, local_float = lax.optimization_barrier((local_normed, local_float))
     local_squares = jnp.sum(local_float * local_float, axis=1)

time: 137 us -> 137 us (level)
  no operation moved by 1% of the time
where the time goes in v19:
time: 137 us
  waiting for transfers between devices  56.6 us (41%)
  starting transfers between devices  29 us (21%)
  between operations  14.7 us (11%)
  matrix products  13.5 us (10%)
  other arithmetic  12.4 us (9%)
  local copies, waits for them, and re-layouts  10.3 us (8%)
    all_gather x1, waiting for transfers between devices, shards(): normed = lax.all_gather(local_normed[rows_of], 'gx', axis=0, tiled=False)  52 us
    dot_general x4, matrix products, shards(): jnp.einsum('btd,bdc->tc', rows, weights_of, preferred_element_type=jnp.fl...  11.1 us
    ppermute x7, starting transfers between devices, shards(): lax.ppermute(local_squares, 'gx', partner_route(gx_count, gx_count, k))  9.45 us
    ppermute x2, starting transfers between devices, shifted(): return lax.ppermute(value, axis, pairs)  6.9 us
    ppermute x1, starting transfers between devices, shards(): other = lax.ppermute(half_kv, ('gx', 'gy'), route)  4.88 us
    ppermute x3, starting transfers between devices, shards(): lax.ppermute(local_weights, 'gy', partner_route(gy_count, gy_count, k))  4.14 us
    ppermute x7, waiting for transfers between devices, shards(): lax.ppermute(local_squares, 'gx', partner_route(gx_count, gx_count, k))  4.01 us
    sin x2, other arithmetic, rope_tables(): return lax.optimization_barrier((jnp.cos(angles), jnp.sin(angles)))  3.34 us
  transfers between devices with their start and end apart: 17, of which 6 were waited for; matrix products, arithmetic and copies ran while one was open for 20% of the time, Pallas kernels for 0%

profile of v19, /device:TPU:0, one launch (start us, length us, event | category | flops | bytes accessed | tf_op | source)
XLA Modules:
  0.0 136.5 jit_solution(537904704744254728)
XLA Ops:
  7.2 0.8 reshape.198
  8.0 1.5 %convert_element_type.52 = f32[512,1024]{1,0:T(8,128)S(1)} convert(bf16[512,1024]{1,0:T(8,128)(2,1)} %param.8) | non-fusion elementwise | flops 524288 | bytes 3145728 | tf_op jit(solution)/shard_map/convert_element_type | solution.py:80
  9.6 1.2 multiply_convert_fusion
  10.9 0.2 multiply_reduce_fusion
  11.1 0.5 collective-permute-start.4
  11.6 2.6 %collective-permute-start.5 = (f32[512]{0:T(512)S(1)}, f32[512]{0:T(512)S(1)}, u32[]{:S(2)}, u32[]{:S(2)}) collective-permute-start(f32[512]{0:T(512)S(1)} %multiply_reduce_fusion), channel_id=1, source_target_pairs={{0,8},{4,12},{8,0},{12,4},{16,24},{20,28},{24,16},{28,20},{1,9},{5... | collective-permute-start | bytes 6152 | tf_op jit(solution)/shard_map/ppermute | solution.py:90
  14.3 0.2 collective-permute-start
  14.5 3.4 %collective-permute-start.11 = (s32[512]{0:T(512)S(1)}, s32[512]{0:T(512)S(1)}, u32[]{:S(2)}, u32[]{:S(2)}) collective-permute-start(s32[512]{0:T(512)S(1)} %broadcast_add_fusion), channel_id=1, source_target_pairs={{0,1},{1,2},{2,3},{4,5},{5,6},{6,7},{8,9},{9,10},{10,11},{12,13},{... | collective-permute-start | bytes 6152 | tf_op jit(solution)/shard_map/ppermute | solution.py:19
  18.4 0.5 multiply_sine_fusion.1
  18.9 0.5 copy.32
  19.4 2.8 %multiply_sine_fusion = (f32[512,256]{0,1:T(8,128)}, f32[512,256]{0,1:T(8,128)}) fusion(f32[256]{0:T(256)S(1)} %multiply_power_fusion, f32[512]{0:T(512)S(1)} %convert_element_type.54), kind=kLoop, calls=%fused_computation.42 | loop fusion | flops 131072 | bytes 1051648 | tf_op jit(solution)/shard_map/sin | solution.py:35
  22.2 0.5 copy.33
  22.7 1.2 maximum_select_fusion
  23.9 0.3 fusion.90
  24.2 1.5 %pad_maximum_fusion = bf16[2048,384]{1,0:T(8,128)(2,1)} fusion(bf16[2048,64]{1,0:T(8,128)(2,1)S(1)} %get-tuple-element.27, bf16[2048,64]{1,0:T(8,128)(2,1)S(1)} %get-tuple-element.26, bf16[2048,256]{1,0:T(8,128)(2,1)S(1)} %copy-done.1), kind=kLoop, calls=%fused_computation.29 | loop fusion | flops 4718592 | bytes 3145728 | tf_op jit(solution)/shard_map/concatenate | solution.py:73
  25.7 0.3 collective-permute-start.3
  26.1 2.7 %collective-permute-start.1 = (bf16[2048,384]{1,0:T(8,128)(2,1)}, bf16[2048,384]{1,0:T(8,128)(2,1)}, u32[]{:S(2)}, u32[]{:S(2)}) collective-permute-start(bf16[2048,384]{1,0:T(8,128)(2,1)} %pad_maximum_fusion), channel_id=1, source_target_pairs={{0,1},{1,0},{2,3},{3,2},{4,5},{5,4},{6,7},{7,6},{8,9},{9,8},{10,11... | collective-permute-start | bytes 4718600 | tf_op jit(solution)/shard_map/ppermute | solution.py:77
  28.8 0.5 copy.38
  29.5 2.7 %collective-permute-start.7 = (f32[512]{0:T(512)S(1)}, f32[512]{0:T(512)S(1)}, u32[]{:S(2)}, u32[]{:S(2)}) collective-permute-start(f32[512]{0:T(512)S(1)} %multiply_reduce_fusion), channel_id=1, source_target_pairs={{0,16},{4,20},{8,24},{12,28},{16,0},{20,4},{24,8},{28,12},{1,17},{... | collective-permute-start | bytes 6152 | tf_op jit(solution)/shard_map/ppermute | solution.py:90
  32.6 1.1 collective-permute-start.2
  33.7 1.3 collective-permute-done.7
  35.0 2.3 %collective-permute-start.9 = (f32[512]{0:T(512)S(1)}, f32[512]{0:T(512)S(1)}, u32[]{:S(2)}, u32[]{:S(2)}) collective-permute-start(f32[512]{0:T(512)S(1)} %multiply_reduce_fusion), channel_id=1, source_target_pairs={{0,24},{4,28},{8,16},{12,20},{16,8},{20,12},{24,0},{28,4},{1,25},{... | collective-permute-start | bytes 6152 | tf_op jit(solution)/shard_map/ppermute | solution.py:90
  37.3 1.1 collective-permute-start.10
  38.4 1.4 %fusion = pred[1024,1024]{0,1:T(32,128)(4,1)S(1)} fusion(s32[1024]{0:T(1024)S(1)} %bitcast.130, s32[1024]{0:T(1024)S(1)} %bitcast.129, s32[1024]{0:T(1024)S(1)} %pad_add_fusion, pred[1024]{0:T(1024)(128)(4,1)S(1)} %broadcast_compare_fusion), kind=kLoop, calls=%fused_computation.5 | loop fusion | flops 4194304 | bytes 1061888 | tf_op jit(solution)/shard_map/and | solution.py:162
  39.8 0.7 collective-permute-done.9
  40.5 1.7 %collective-permute-done.10 = f32[512]{0:T(512)S(1)} collective-permute-done((f32[512]{0:T(512)S(1)}, f32[512]{0:T(512)S(1)}, u32[]{:S(2)}, u32[]{:S(2)}) %collective-permute-start.10) | collective-permute-done | bytes 2080 | tf_op jit(solution)/shard_map/ppermute | solution.py:90
  42.3 0.6 gather_fusion
  43.0 0.9 copy.39
  44.1 52.0 %all-gather.3.cloned.1.call-done = bf16[4096,1024]{1,0:T(8,128)(2,1)} async-done(((bf16[512,1024]{1,0:T(8,128)(2,1)}), bf16[4096,1024]{1,0:T(8,128)(2,1)}) %all-gather.3.cloned.1.call-update) | async-done | bytes 8388624 | tf_op jit(solution)/shard_map/all_gather | solution.py:105
  96.1 2.8 %fusion.23 = f32[512,384]{0,1:T(8,128)S(1)} fusion(bf16[2,1024,64]{1,2,0:T(8,128)(2,1)S(1)} %copy.40, bf16[2,1024,64]{1,2,0:T(8,128)(2,1)} %copy.39, bf16[2,1024,256]{1,2,0:T(8,128)(2,1)S(1)} %copy.38, bf16[4,2,512,1024]{3,2,1,0:T(8,128)(2,1)} %bitcast.142, s32[]{:T(128)S(6)} %select_n.159), kind=kOutput, calls=%fused_computation.30 | convolution fusion | flops 810024960 | bytes 4456452 | tf_op jit(solution)/shard_map/btd,bdc->tc/dot_general | solution.py:114
  98.8 3.4 %fusion.34 = f32[512,384]{0,1:T(8,128)S(1)} fusion(bf16[2,1024,384]{2,1,0:T(8,128)(2,1)} %bitcast.21, bf16[4,2,512,1024]{3,2,1,0:T(8,128)(2,1)} %bitcast.143, s32[]{:T(128)S(6)} %select_n.166), kind=kOutput, calls=%fused_computation.33 | convolution fusion | flops 805306368 | bytes 4456452 | tf_op jit(solution)/shard_map/btd,bdc->tc/dot_general | solution.py:114
  102.3 2.5 %fusion.40 = f32[512,384]{0,1:T(8,128)S(1)} fusion(f32[512,384]{0,1:T(8,128)S(1)} %fusion.23, bf16[2,1024,384]{2,1,0:T(8,128)(2,1)} %bitcast.15, bf16[4,2,512,1024]{3,2,1,0:T(8,128)(2,1)S(1)} %bitcast.144, s32[]{:T(128)S(6)} %select_n.164), kind=kOutput, calls=%fused_computation.35 | convolution fusion | flops 805502976 | bytes 5242884 | tf_op jit(solution)/shard_map/btd,bdc->tc/dot_general | solution.py:114
  104.7 2.5 %fusion.46 = f32[512,384]{0,1:T(8,128)S(1)} fusion(f32[512,384]{0,1:T(8,128)S(1)} %fusion.34, f32[512,384]{0,1:T(8,128)S(1)} %fusion.40, bf16[2,1024,384]{2,1,0:T(8,128)(2,1)} %bitcast.18, bf16[4,2,512,1024]{3,2,1,0:T(8,128)(2,1)S(1)} %bitcast.145, s32[]{:T(128)S(6)} %select_n.165, f32[512]{0:T(512)S(1)} %add_rsqrt_fusion), kind=kOutput, calls=%fused_computation.37 | convolution fusion | flops 805896192 | bytes 6031364 | tf_op jit(solution)/shard_map/btd,bdc->tc/dot_general | solution.py:114
  107.5 3.5 %collective-permute-start.12 = (bf16[2,512,64]{1,2,0:T(8,128)(2,1)S(1)}, bf16[2,512,64]{1,2,0:T(8,128)(2,1)S(1)}, u32[]{:S(2)}, u32[]{:S(2)}) collective-permute-start(bf16[2,512,64]{1,2,0:T(8,128)(2,1)S(1)} %pad_maximum_fusion.3), channel_id=1, source_target_pairs={{0,1},{1,2},{2,3},{4,5},{5,6},{6,7},{8,9},{9,10},{10,11},{12,13},{... | collective-permute-start | bytes 393224 | tf_op jit(solution)/shard_map/ppermute | solution.py:19
  111.0 4.9 %collective-permute-start.13 = (bf16[2,512,64]{1,2,0:T(8,128)(2,1)S(1)}, bf16[2,512,64]{1,2,0:T(8,128)(2,1)S(1)}, u32[]{:S(2)}, u32[]{:S(2)}) collective-permute-start(bf16[2,512,64]{1,2,0:T(8,128)(2,1)S(1)} %pad_maximum_fusion.3), channel_id=1, source_target_pairs={{0,9},{1,10},{2,11},{4,13},{5,14},{6,15},{8,1},{9,2},{10,3},{12,5}... | collective-permute-start | bytes 393224 | tf_op jit(solution)/shard_map/ppermute | solution.py:137
  116.0 0.2 fusion.60
  116.6 0.2 reshape.203
  117.0 1.5 %scatter_fusion = bf16[64,2,512]{2,1,0:T(2,128)(2,1)S(1)} fusion(bf16[64,2,512]{2,1,0:T(2,128)(2,1)S(1)} %broadcast_in_dim.44, s32[32]{0:T(128)S(1)} %fusion.83, bf16[32,2,512]{2,1,0:T(2,128)(2,1)S(1)} %copy.45), kind=kCustom, calls=%fused_computation.1 | custom fusion | bytes 196736 | tf_op jit(solution)/shard_map/scatter | solution.py:192
  118.5 0.7 copy.46
  119.2 3.3 %all-to-all-start = ((bf16[4,16,2,512]{3,1,2,0:T(8,128)(2,1)}), bf16[4,16,2,512]{3,1,2,0:T(8,128)(2,1)S(1)}, u32[]{:S(2)}, u32[]{:S(2)}) async-start(bf16[4,16,2,512]{3,1,2,0:T(8,128)(2,1)} %copy.46), calls=%async_computation | async-start | bytes 262144 | tf_op jit(solution)/shard_map/all_to_all | solution.py:195
  122.7 1.0 fusion.3
  123.6 1.1 fusion.1
  124.7 1.4 %fusion.55 = bf16[1024,128]{1,0:T(8,128)(2,1)S(1)} fusion(pred[1024,1024]{0,1:T(32,128)(4,1)S(1)} %fusion, f32[1024,1024]{0,1:T(8,128)S(1)} %get-tuple-element.44, f32[1024]{0:T(1024)S(1)} %get-tuple-element.43, bf16[2,512,128]{1,2,0:T(8,128)(2,1)S(1)} %maximum_select_fusion.2, bf16[2,512,128]{1,2,0:T(8,128)(2,1)S(1)} %maximum_select_fusion.1, ...), kind=kOutput, calls=%fused_computation.41 | convolution fusion | flops 273547264 | bytes 6038528 | tf_op jit(solution)/shard_map/dot_general | solution.py:169
  126.2 0.7 copy.63
  126.9 0.6 all-to-all-done
  127.5 0.3 reshape.207
  127.8 0.9 copy.50
  128.7 0.9 copy.51
  (80 shorter events, 2.3 us)
Async XLA Ops:
  7.2 2.4 %copy-start = (bf16[512,1024]{1,0:T(8,128)(2,1)S(1)}, bf16[512,1024]{1,0:T(8,128)(2,1)}, u32[]{:S(2)}) copy-start(bf16[512,1024]{1,0:T(8,128)(2,1)} %param.8) | copy-start | bytes 3145732
  7.2 88.9 %all-gather.3.cloned.1.call-start = ((), (), s32[]{:S(2)}) async-start(), calls=%async_computation.1 | async-start | bytes 9437184 | tf_op jit(solution)/shard_map/all_gather | solution.py:105
  9.5 4.7 %copy-start.4 = (bf16[2048,32]{0,1:T(8,128)(2,1)S(1)}, bf16[2048,32]{0,1:T(8,128)(2,1)}, u32[]{:S(2)}) copy-start(bf16[2048,32]{0,1:T(8,128)(2,1)} %param.12) | copy-start | bytes 393220
  9.5 4.7 %copy-start.5 = (bf16[2048,32]{0,1:T(8,128)(2,1)S(1)}, bf16[2048,32]{0,1:T(8,128)(2,1)}, u32[]{:S(2)}) copy-start(bf16[2048,32]{0,1:T(8,128)(2,1)} %param.11) | copy-start | bytes 393220
  9.5 5.0 %copy-start.6 = (s32[512]{0:T(512)S(1)}, s32[512]{0:T(512)}, u32[]{:S(2)}) copy-start(s32[512]{0:T(512)} %param.13) | copy-start | bytes 6148
  9.5 8.4 %copy-start.8 = (s32[512]{0:T(512)S(1)}, s32[512]{0:T(512)}, u32[]{:S(2)}) copy-start(s32[512]{0:T(512)} %param.14) | copy-start | bytes 6148
  9.6 8.4 %copy-start.7 = (s32[32,1]{0,1:T(1,128)S(1)}, s32[32,1]{0,1:T(1,128)}, u32[]{:S(2)}) copy-start(s32[32,1]{0,1:T(1,128)} %param.15) | copy-start | bytes 388
  11.1 18.5 %collective-permute-start.4 = (f32[512]{0:T(512)S(1)}, f32[512]{0:T(512)S(1)}, u32[]{:S(2)}, u32[]{:S(2)}) collective-permute-start(f32[512]{0:T(512)S(1)} %multiply_reduce_fusion), channel_id=1, source_target_pairs={{0,4},{4,0},{8,12},{12,8},{16,20},{20,16},{24,28},{28,24},{1,5},{5... | collective-permute-start | bytes 6152 | tf_op jit(solution)/shard_map/ppermute | solution.py:90
  11.6 20.7 %collective-permute-start.5 = (f32[512]{0:T(512)S(1)}, f32[512]{0:T(512)S(1)}, u32[]{:S(2)}, u32[]{:S(2)}) collective-permute-start(f32[512]{0:T(512)S(1)} %multiply_reduce_fusion), channel_id=1, source_target_pairs={{0,8},{4,12},{8,0},{12,4},{16,24},{20,28},{24,16},{28,20},{1,9},{5... | collective-permute-start | bytes 6152 | tf_op jit(solution)/shard_map/ppermute | solution.py:90
  14.3 8.0 %collective-permute-start = (bf16[2,2048,32]{1,2,0:T(8,128)(2,1)S(1)}, bf16[2,2048,32]{1,2,0:T(8,128)(2,1)S(1)}, u32[]{:S(2)}, u32[]{:S(2)}) collective-permute-start(bf16[2,2048,32]{1,2,0:T(8,128)(2,1)S(1)} %pad_maximum_fusion.2), channel_id=1, source_target_pairs={{0,4},{4,0},{8,12},{12,8},{16,20},{20,16},{24,28},{28,24},{1,5},{5... | collective-permute-start | bytes 786440 | tf_op jit(solution)/shard_map/ppermute | solution.py:71
  14.5 14.9 %collective-permute-start.11 = (s32[512]{0:T(512)S(1)}, s32[512]{0:T(512)S(1)}, u32[]{:S(2)}, u32[]{:S(2)}) collective-permute-start(s32[512]{0:T(512)S(1)} %broadcast_add_fusion), channel_id=1, source_target_pairs={{0,1},{1,2},{2,3},{4,5},{5,6},{6,7},{8,9},{9,10},{10,11},{12,13},{... | collective-permute-start | bytes 6152 | tf_op jit(solution)/shard_map/ppermute | solution.py:19
  22.7 1.5 %copy-start.1 = (bf16[2048,256]{1,0:T(8,128)(2,1)S(1)}, bf16[2048,256]{1,0:T(8,128)(2,1)}, u32[]{:S(2)}) copy-start(bf16[2048,256]{1,0:T(8,128)(2,1)} %param.10) | copy-start | bytes 3145732
  25.7 73.1 %collective-permute-start.3 = (bf16[2048,384]{1,0:T(8,128)(2,1)}, bf16[2048,384]{1,0:T(8,128)(2,1)}, u32[]{:S(2)}, u32[]{:S(2)}) collective-permute-start(bf16[2048,384]{1,0:T(8,128)(2,1)} %pad_maximum_fusion), channel_id=1, source_target_pairs={{0,3},{1,2},{2,1},{3,0},{4,7},{5,6},{6,5},{7,4},{8,11},{9,10},{10,... | collective-permute-start | bytes 4718600 | tf_op jit(solution)/shard_map/ppermute | solution.py:77
  26.1 76.2 %collective-permute-start.1 = (bf16[2048,384]{1,0:T(8,128)(2,1)}, bf16[2048,384]{1,0:T(8,128)(2,1)}, u32[]{:S(2)}, u32[]{:S(2)}) collective-permute-start(bf16[2048,384]{1,0:T(8,128)(2,1)} %pad_maximum_fusion), channel_id=1, source_target_pairs={{0,1},{1,0},{2,3},{3,2},{4,5},{5,4},{6,7},{7,6},{8,9},{9,8},{10,11... | collective-permute-start | bytes 4718600 | tf_op jit(solution)/shard_map/ppermute | solution.py:77
  29.4 3.1 %collective-permute-start.6 = (f32[512]{0:T(512)S(1)}, f32[512]{0:T(512)S(1)}, u32[]{:S(2)}, u32[]{:S(2)}) collective-permute-start(f32[512]{0:T(512)S(1)} %multiply_reduce_fusion), channel_id=1, source_target_pairs={{0,12},{4,8},{8,4},{12,0},{16,28},{20,24},{24,20},{28,16},{1,13},{... | collective-permute-start | bytes 6152 | tf_op jit(solution)/shard_map/ppermute | solution.py:90
  29.5 5.5 %collective-permute-start.7 = (f32[512]{0:T(512)S(1)}, f32[512]{0:T(512)S(1)}, u32[]{:S(2)}, u32[]{:S(2)}) collective-permute-start(f32[512]{0:T(512)S(1)} %multiply_reduce_fusion), channel_id=1, source_target_pairs={{0,16},{4,20},{8,24},{12,28},{16,0},{20,4},{24,8},{28,12},{1,17},{... | collective-permute-start | bytes 6152 | tf_op jit(solution)/shard_map/ppermute | solution.py:90
  32.2 5.1 %collective-permute-start.8 = (f32[512]{0:T(512)S(1)}, f32[512]{0:T(512)S(1)}, u32[]{:S(2)}, u32[]{:S(2)}) collective-permute-start(f32[512]{0:T(512)S(1)} %multiply_reduce_fusion), channel_id=1, source_target_pairs={{0,20},{4,16},{8,28},{12,24},{16,4},{20,0},{24,12},{28,8},{1,21},{... | collective-permute-start | bytes 6152 | tf_op jit(solution)/shard_map/ppermute | solution.py:90
  32.6 72.2 %collective-permute-start.2 = (bf16[2048,384]{1,0:T(8,128)(2,1)}, bf16[2048,384]{1,0:T(8,128)(2,1)}, u32[]{:S(2)}, u32[]{:S(2)}) collective-permute-start(bf16[2048,384]{1,0:T(8,128)(2,1)} %pad_maximum_fusion), channel_id=1, source_target_pairs={{0,2},{1,3},{2,0},{3,1},{4,6},{5,7},{6,4},{7,5},{8,10},{9,11},{10,... | collective-permute-start | bytes 4718600 | tf_op jit(solution)/shard_map/ppermute | solution.py:77
  35.0 5.5 %collective-permute-start.9 = (f32[512]{0:T(512)S(1)}, f32[512]{0:T(512)S(1)}, u32[]{:S(2)}, u32[]{:S(2)}) collective-permute-start(f32[512]{0:T(512)S(1)} %multiply_reduce_fusion), channel_id=1, source_target_pairs={{0,24},{4,28},{8,16},{12,20},{16,8},{20,12},{24,0},{28,4},{1,25},{... | collective-permute-start | bytes 6152 | tf_op jit(solution)/shard_map/ppermute | solution.py:90
  37.3 5.0 %collective-permute-start.10 = (f32[512]{0:T(512)S(1)}, f32[512]{0:T(512)S(1)}, u32[]{:S(2)}, u32[]{:S(2)}) collective-permute-start(f32[512]{0:T(512)S(1)} %multiply_reduce_fusion), channel_id=1, source_target_pairs={{0,28},{4,24},{8,20},{12,16},{16,12},{20,8},{24,4},{28,0},{1,29},{... | collective-permute-start | bytes 6152 | tf_op jit(solution)/shard_map/ppermute | solution.py:90
  96.1 6.2 %copy-start.9 = (bf16[4096,1024]{1,0:T(8,128)(2,1)S(1)}, bf16[4096,1024]{1,0:T(8,128)(2,1)}, u32[]{:S(2)}) copy-start(bf16[4096,1024]{1,0:T(8,128)(2,1)} %all-gather.3.cloned.1.call-done) | copy-start | bytes 25165828
  107.2 8.8 %copy-start.2 = (f32[512,256]{0,1:T(8,128)S(1)}, f32[512,256]{0,1:T(8,128)}, u32[]{:S(2)}) copy-start(f32[512,256]{0,1:T(8,128)} %get-tuple-element.16) | copy-start | bytes 1572868
  107.2 8.8 %copy-start.3 = (f32[512,256]{0,1:T(8,128)S(1)}, f32[512,256]{0,1:T(8,128)}, u32[]{:S(2)}) copy-start(f32[512,256]{0,1:T(8,128)} %get-tuple-element.15) | copy-start | bytes 1572868
  107.4 15.1 %collective-permute-start.14 = (bf16[2,512,64]{1,2,0:T(8,128)(2,1)S(1)}, bf16[2,512,64]{1,2,0:T(8,128)(2,1)S(1)}, u32[]{:S(2)}, u32[]{:S(2)}) collective-permute-start(bf16[2,512,64]{1,2,0:T(8,128)(2,1)S(1)} %pad_maximum_fusion.3), channel_id=1, source_target_pairs={{0,8},{4,12},{8,0},{12,4},{16,24},{20,28},{24,16},{28,20},{1,9},{5... | collective-permute-start | bytes 393224 | tf_op jit(solution)/shard_map/ppermute | solution.py:128
  107.5 15.1 %collective-permute-start.12 = (bf16[2,512,64]{1,2,0:T(8,128)(2,1)S(1)}, bf16[2,512,64]{1,2,0:T(8,128)(2,1)S(1)}, u32[]{:S(2)}, u32[]{:S(2)}) collective-permute-start(bf16[2,512,64]{1,2,0:T(8,128)(2,1)S(1)} %pad_maximum_fusion.3), channel_id=1, source_target_pairs={{0,1},{1,2},{2,3},{4,5},{5,6},{6,7},{8,9},{9,10},{10,11},{12,13},{... | collective-permute-start | bytes 393224 | tf_op jit(solution)/shard_map/ppermute | solution.py:19
  111.0 11.6 %collective-permute-start.13 = (bf16[2,512,64]{1,2,0:T(8,128)(2,1)S(1)}, bf16[2,512,64]{1,2,0:T(8,128)(2,1)S(1)}, u32[]{:S(2)}, u32[]{:S(2)}) collective-permute-start(bf16[2,512,64]{1,2,0:T(8,128)(2,1)S(1)} %pad_maximum_fusion.3), channel_id=1, source_target_pairs={{0,9},{1,10},{2,11},{4,13},{5,14},{6,15},{8,1},{9,2},{10,3},{12,5}... | collective-permute-start | bytes 393224 | tf_op jit(solution)/shard_map/ppermute | solution.py:137
  119.2 8.3 %all-to-all-start = ((bf16[4,16,2,512]{3,1,2,0:T(8,128)(2,1)}), bf16[4,16,2,512]{3,1,2,0:T(8,128)(2,1)S(1)}, u32[]{:S(2)}, u32[]{:S(2)}) async-start(bf16[4,16,2,512]{3,1,2,0:T(8,128)(2,1)} %copy.46), calls=%async_computation | async-start | bytes 262144 | tf_op jit(solution)/shard_map/all_to_all | solution.py:195
Sparse Core Ops, SparseCore 0:
  11.0 85.0 all-gather.2

commit v20 on v17

--- a/solution.py
+++ b/solution.py
@@ -143,17 +143,16 @@
     value_piece = own_kv[1]
     window_kv = jnp.stack(head_halves, axis=2).reshape(2, (span_count + 1) * token_count, HD)
     window_keys = window_kv[0]
+    window_rows = window_keys.shape[0]
     window_values = window_kv[1]
     window_marks = jnp.concatenate(mark_list, axis=0)
     reach_rows = span_count * token_count
-    query_rows = (
-        queries.reshape(token_count, head_local, HD)
-        .transpose(1, 0, 2)
-        .reshape(head_local * token_count, HD)
-    )
-    scores = lax.dot_general(
-        query_rows, window_keys, (((1,), (1,)), ((), ())), preferred_element_type=jnp.float32
-    ) * HD ** (-0.5)
+    scores = jnp.einsum(
+        "thd,ud->htu",
+        queries.reshape(token_count, head_local, HD),
+        window_keys,
+        preferred_element_type=jnp.float32,
+    ).reshape(head_local * token_count, window_rows) * HD ** (-0.5)
     query_marks = jnp.tile(segment_ids, head_local)
     query_place = jnp.tile(jnp.arange(token_count, dtype=jnp.int32), head_local)
     key_place = jnp.arange(window_keys.shape[0], dtype=jnp.int32)

time: 137 us -> 153 us (1.12)
  local copies, waits for them, and re-layouts: 9.47 us -> 22.2 us
  other arithmetic: 13.3 us -> 23.9 us
  waiting for transfers between devices: 56.6 us -> 46.1 us
  starting transfers between devices: 29 us -> 32.5 us
    all_gather x1, waiting for transfers between devices: 52 us -> 42.1 us  [shards(): normed = lax.all_gather(local_normed[rows_of], 'gx', axis=0, tiled=False)]
    scatter x1, local copies, waits for them, and re-layouts: 1.49 us -> 4.35 us  [shards(): send_kv = jnp.zeros((owner_count * capacity, 2, PAGE * quarter), jnp.bflo...]
    ppermute x7, starting transfers between devices: 9.45 us -> 11.8 us  [shards(): lax.ppermute(local_squares, 'gx', partner_route(gx_count, gx_count, k))]
    select_n x3, other arithmetic: 1.27 us -> 3.38 us  [joined(): jnp.where(mine_first, jnp.concatenate([mine, theirs], axis=-1), jnp.conca...]
    reshape x1, local copies, waits for them, and re-layouts: 0.23 us -> 1.82 us  [shards(): kv_pages = own_kv.reshape(2, page_rows, PAGE * quarter).transpose(1, 0, 2)]
  transfers between devices with their start and end apart: 17 -> 17, of which waited for: 6 -> 4; matrix products, arithmetic and copies ran while one was open for 20% -> 32% of each run, Pallas kernels for 0% -> 0%
where the time goes in v20:
time: 153 us; the launch traced here: 152 us
  waiting for transfers between devices  46.1 us (30%)
  starting transfers between devices  32.5 us (21%)
  other arithmetic  23.9 us (16%)
  local copies, waits for them, and re-layouts  22.2 us (15%)
  between operations  14.5 us (9%)
  matrix products  12.8 us (8%)
    all_gather x1, waiting for transfers between devices, shards(): normed = lax.all_gather(local_normed[rows_of], 'gx', axis=0, tiled=False)  42.1 us
    ppermute x7, starting transfers between devices, shards(): lax.ppermute(local_squares, 'gx', partner_route(gx_count, gx_count, k))  11.8 us
    dot_general x4, matrix products, shards(): jnp.einsum('btd,bdc->tc', rows, weights_of, preferred_element_type=jnp.fl...  11.3 us
    ppermute x2, starting transfers between devices, shifted(): return lax.ppermute(value, axis, pairs)  8.1 us
    ppermute x1, starting transfers between devices, shards(): other = lax.ppermute(half_kv, ('gx', 'gy'), route)  4.81 us
    scatter x1, local copies, waits for them, and re-layouts, shards(): send_kv = jnp.zeros((owner_count * capacity, 2, PAGE * quarter), jnp.bflo...  4.35 us
    ppermute x7, waiting for transfers between devices, shards(): lax.ppermute(local_squares, 'gx', partner_route(gx_count, gx_count, k))  3.96 us
    all_to_all x1, starting transfers between devices, shards(): lax.all_to_all(send_kv, 'gy', split_axis=0, concat_axis=0, tiled=True)  3.95 us
  transfers between devices with their start and end apart: 17, of which 4 were waited for; matrix products, arithmetic and copies ran while one was open for 32% of the time, Pallas kernels for 0%

profile of v20, /device:TPU:0, one launch (start us, length us, event | category | flops | bytes accessed | tf_op | source)
XLA Modules:
  0.0 151.9 jit_solution(1654885602986355973)
XLA Ops:
  7.2 1.5 %convert_element_type.53 = f32[512,1024]{1,0:T(8,128)S(1)} convert(bf16[512,1024]{1,0:T(8,128)(2,1)} %param.8) | non-fusion elementwise | flops 524288 | bytes 3145728 | tf_op jit(solution)/shard_map/convert_element_type | solution.py:80
  8.8 0.7 dynamic-slice_convert_fusion
  9.5 1.3 multiply_convert_fusion
  10.8 0.8 multiply_reduce_fusion
  12.0 2.6 %collective-permute-start.5 = (f32[512]{0:T(512)}, f32[512]{0:T(512)}, u32[]{:S(2)}, u32[]{:S(2)}) collective-permute-start(f32[512]{0:T(512)} %multiply_reduce_fusion), channel_id=1, source_target_pairs={{0,8},{4,12},{8,0},{12,4},{16,24},{20,28},{24,16},{28,20},{1,9},{5... | collective-permute-start | bytes 6152 | tf_op jit(solution)/shard_map/ppermute | solution.py:89
  14.9 4.0 %collective-permute-start.11 = (s32[512]{0:T(512)S(1)}, s32[512]{0:T(512)}, u32[]{:S(2)}, u32[]{:S(2)}) collective-permute-start(s32[512]{0:T(512)S(1)} %broadcast_add_fusion), channel_id=1, source_target_pairs={{0,1},{1,2},{2,3},{4,5},{5,6},{6,7},{8,9},{9,10},{10,11},{12,13},{... | collective-permute-start | bytes 6152 | tf_op jit(solution)/shard_map/ppermute | solution.py:19
  20.2 0.7 select_reduce_fusion.1
  21.5 1.2 multiply_sine_fusion.1
  23.8 1.9 %multiply_sine_fusion = (f32[512,256]{0,1:T(8,128)S(1)}, f32[512,256]{0,1:T(8,128)S(1)}) fusion(f32[256]{0:T(256)S(1)} %multiply_power_fusion, f32[512]{0:T(512)S(1)} %convert_element_type.56), kind=kLoop, calls=%fused_computation.42 | loop fusion | flops 131072 | bytes 1051648 | tf_op jit(solution)/shard_map/sin | solution.py:35
  26.1 1.2 maximum_select_fusion
  27.6 0.9 copy-done.1
  28.5 1.5 %pad_maximum_fusion = bf16[2048,384]{1,0:T(8,128)(2,1)} fusion(bf16[2048,64]{1,0:T(8,128)(2,1)S(1)} %get-tuple-element.29, bf16[2048,64]{1,0:T(8,128)(2,1)S(1)} %get-tuple-element.28, bf16[2048,256]{1,0:T(8,128)(2,1)S(1)} %copy-done.1), kind=kLoop, calls=%fused_computation.29 | loop fusion | flops 4718592 | bytes 3145728 | tf_op jit(solution)/shard_map/concatenate | solution.py:73
  30.6 2.5 %collective-permute-start.1 = (bf16[2048,384]{1,0:T(8,128)(2,1)}, bf16[2048,384]{1,0:T(8,128)(2,1)}, u32[]{:S(2)}, u32[]{:S(2)}) collective-permute-start(bf16[2048,384]{1,0:T(8,128)(2,1)} %pad_maximum_fusion), channel_id=1, source_target_pairs={{0,1},{1,0},{2,3},{3,2},{4,5},{5,4},{6,7},{7,6},{8,9},{9,8},{10,11... | collective-permute-start | bytes 4718600 | tf_op jit(solution)/shard_map/ppermute | solution.py:77
  33.6 1.3 copy.41
  35.5 0.7 pad_add_fusion
  36.2 2.7 %collective-permute-start.7 = (f32[512]{0:T(512)}, f32[512]{0:T(512)S(1)}, u32[]{:S(2)}, u32[]{:S(2)}) collective-permute-start(f32[512]{0:T(512)} %multiply_reduce_fusion), channel_id=1, source_target_pairs={{0,16},{4,20},{8,24},{12,28},{16,0},{20,4},{24,8},{28,12},{1,17},{... | collective-permute-start | bytes 6152 | tf_op jit(solution)/shard_map/ppermute | solution.py:89
  39.1 1.0 collective-permute-start.2
  40.1 0.7 broadcast_compare_fusion
  41.0 5.9 %collective-permute-start.9 = (f32[512]{0:T(512)}, f32[512]{0:T(512)S(1)}, u32[]{:S(2)}, u32[]{:S(2)}) collective-permute-start(f32[512]{0:T(512)} %multiply_reduce_fusion), channel_id=1, source_target_pairs={{0,24},{4,28},{8,16},{12,20},{16,8},{20,12},{24,0},{28,4},{1,25},{... | collective-permute-start | bytes 6152 | tf_op jit(solution)/shard_map/ppermute | solution.py:89
  46.9 1.4 fusion
  48.7 3.3 %collective-permute-done.10 = f32[512]{0:T(512)S(1)} collective-permute-done((f32[512]{0:T(512)}, f32[512]{0:T(512)S(1)}, u32[]{:S(2)}, u32[]{:S(2)}) %collective-permute-start.10) | collective-permute-done | bytes 2080 | tf_op jit(solution)/shard_map/ppermute | solution.py:89
  52.0 0.7 stack.56
  53.9 42.1 %all-gather.3.cloned.1.call-done = bf16[4096,1024]{1,0:T(8,128)(2,1)} async-done(((bf16[512,1024]{1,0:T(8,128)(2,1)}), bf16[4096,1024]{1,0:T(8,128)(2,1)}) %all-gather.3.cloned.1.call-update) | async-done | bytes 8388624 | tf_op jit(solution)/shard_map/all_gather | solution.py:104
  95.9 3.0 %fusion.21 = f32[512,384]{0,1:T(8,128)S(1)} fusion(bf16[2,1024,64]{1,2,0:T(8,128)(2,1)S(1)} %copy.43, bf16[2,1024,64]{1,2,0:T(8,128)(2,1)S(1)} %copy.42, bf16[2,1024,256]{1,2,0:T(8,128)(2,1)} %copy.41, bf16[4,2,512,1024]{3,2,1,0:T(8,128)(2,1)} %bitcast.144, s32[]{:T(128)S(6)} %select_n.158), kind=kOutput, calls=%fused_computation.30 | convolution fusion | flops 810024960 | bytes 4456452 | tf_op jit(solution)/shard_map/btd,bdc->tc/dot_general | solution.py:113
  99.0 3.4 %fusion.32 = f32[512,384]{0,1:T(8,128)S(1)} fusion(bf16[2,1024,384]{2,1,0:T(8,128)(2,1)} %bitcast.20, bf16[4,2,512,1024]{3,2,1,0:T(8,128)(2,1)} %bitcast.145, s32[]{:T(128)S(6)} %select_n.165), kind=kOutput, calls=%fused_computation.33 | convolution fusion | flops 805306368 | bytes 4456452 | tf_op jit(solution)/shard_map/btd,bdc->tc/dot_general | solution.py:113
  102.3 2.5 %fusion.38 = f32[512,384]{0,1:T(8,128)S(1)} fusion(f32[512,384]{0,1:T(8,128)S(1)} %fusion.21, bf16[2,1024,384]{2,1,0:T(8,128)(2,1)} %bitcast.14, bf16[4,2,512,1024]{3,2,1,0:T(8,128)(2,1)S(1)} %bitcast.146, s32[]{:T(128)S(6)} %select_n.163), kind=kOutput, calls=%fused_computation.35 | convolution fusion | flops 805502976 | bytes 5242884 | tf_op jit(solution)/shard_map/btd,bdc->tc/dot_general | solution.py:113
  104.9 2.5 %fusion.44 = f32[512,384]{0,1:T(8,128)S(1)} fusion(f32[512,384]{0,1:T(8,128)S(1)} %fusion.32, f32[512,384]{0,1:T(8,128)S(1)} %fusion.38, bf16[2,1024,384]{2,1,0:T(8,128)(2,1)} %bitcast.17, bf16[4,2,512,1024]{3,2,1,0:T(8,128)(2,1)S(1)} %bitcast.147, s32[]{:T(128)S(6)} %select_n.164, f32[512]{0:T(512)S(1)} %add_rsqrt_fusion), kind=kOutput, calls=%fused_computation.37 | convolution fusion | flops 805896192 | bytes 6031364 | tf_op jit(solution)/shard_map/btd,bdc->tc/dot_general | solution.py:113
  107.6 0.7 pad_maximum_fusion.3
  108.2 4.1 %collective-permute-start.12 = (bf16[2,512,64]{1,2,0:T(8,128)(2,1)}, bf16[2,512,64]{1,2,0:T(8,128)(2,1)}, u32[]{:S(2)}, u32[]{:S(2)}) collective-permute-start(bf16[2,512,64]{1,2,0:T(8,128)(2,1)} %pad_maximum_fusion.3), channel_id=1, source_target_pairs={{0,1},{1,2},{2,3},{4,5},{5,6},{6,7},{8,9},{9,10},{10,11},{12,13},{... | collective-permute-start | bytes 393224 | tf_op jit(solution)/shard_map/ppermute | solution.py:19
  112.4 4.8 %collective-permute-start.13 = (bf16[2,512,64]{1,2,0:T(8,128)(2,1)}, bf16[2,512,64]{1,2,0:T(8,128)(2,1)}, u32[]{:S(2)}, u32[]{:S(2)}) collective-permute-start(bf16[2,512,64]{1,2,0:T(8,128)(2,1)} %pad_maximum_fusion.3), channel_id=1, source_target_pairs={{0,9},{1,10},{2,11},{4,13},{5,14},{6,15},{8,1},{9,2},{10,3},{12,5}... | collective-permute-start | bytes 393224 | tf_op jit(solution)/shard_map/ppermute | solution.py:136
  117.2 0.9 fusion.80
  118.7 1.7 %copy.47 = bf16[2,512,32]{2,1,0:T(8,128)(2,1)} copy(bf16[2,512,32]{1,2,0:T(8,128)(2,1)} %fusion.64) | data formatting | bytes 131072 | tf_op jit(solution)/shard_map/dynamic_slice | solution.py:124
  120.4 1.8 %reshape.200 = bf16[2,32,512]{2,1,0:T(8,128)(2,1)} reshape(bf16[2,512,32]{2,1,0:T(8,128)(2,1)} %copy.47) | data formatting | bytes 131072 | tf_op jit(solution)/shard_map/reshape | solution.py:186
  122.2 1.5 %copy.48 = bf16[32,2,512]{2,1,0:T(2,128)(2,1)} copy(bf16[32,2,512]{2,0,1:T(8,128)(2,1)} %bitcast.130) | data formatting | bytes 131072 | tf_op jit(solution)/shard_map/transpose | solution.py:186
  123.7 0.7 broadcast_in_dim.44
  124.5 4.3 %scatter_fusion = bf16[64,2,512]{2,1,0:T(2,128)(2,1)} fusion(bf16[64,2,512]{2,1,0:T(2,128)(2,1)} %broadcast_in_dim.44, s32[32]{0:T(128)S(1)} %copy-done.13, bf16[32,2,512]{2,1,0:T(2,128)(2,1)} %copy.48), kind=kCustom, calls=%fused_computation.1 | custom fusion | bytes 196736 | tf_op jit(solution)/shard_map/scatter | solution.py:190
  128.8 1.6 %copy.49 = bf16[4,16,2,512]{3,1,2,0:T(8,128)(2,1)} copy(bf16[4,16,2,512]{3,2,1,0:T(2,128)(2,1)} %bitcast.129) | data formatting | bytes 262144 | tf_op jit(solution)/shard_map/reshape | solution.py:192
  130.4 3.9 %all-to-all-start = ((bf16[4,16,2,512]{3,1,2,0:T(8,128)(2,1)}), bf16[4,16,2,512]{3,1,2,0:T(8,128)(2,1)}, u32[]{:S(2)}, u32[]{:S(2)}) async-start(bf16[4,16,2,512]{3,1,2,0:T(8,128)(2,1)} %copy.49), calls=%async_computation | async-start | bytes 262144 | tf_op jit(solution)/shard_map/all_to_all | solution.py:193
  134.3 1.2 fusion.51
  135.6 1.1 maximum_select_fusion.2
  136.7 1.2 maximum_select_fusion.1
  137.8 0.8 convolution_multiply_fusion
  139.3 1.3 fusion.1
  140.5 0.7 fusion.48
  141.3 0.7 copy.70
  142.0 0.9 copy.53
  143.3 0.9 copy.54
  144.2 0.9 copy.55
  (95 shorter events, 9.8 us)
Async XLA Ops:
  7.2 2.3 %copy-start = (bf16[512,1024]{1,0:T(8,128)(2,1)S(1)}, bf16[512,1024]{1,0:T(8,128)(2,1)}, u32[]{:S(2)}) copy-start(bf16[512,1024]{1,0:T(8,128)(2,1)} %param.8) | copy-start | bytes 3145732
  7.2 88.8 %all-gather.3.cloned.1.call-start = ((), (), s32[]{:S(2)}) async-start(), calls=%async_computation.1 | async-start | bytes 9437184 | tf_op jit(solution)/shard_map/all_gather | solution.py:104
  10.7 3.9 %copy-start.3 = (bf16[2048,32]{0,1:T(8,128)(2,1)S(1)}, bf16[2048,32]{0,1:T(8,128)(2,1)}, u32[]{:S(2)}) copy-start(bf16[2048,32]{0,1:T(8,128)(2,1)} %param.12) | copy-start | bytes 393220
  10.7 3.9 %copy-start.4 = (bf16[2048,32]{0,1:T(8,128)(2,1)S(1)}, bf16[2048,32]{0,1:T(8,128)(2,1)}, u32[]{:S(2)}) copy-start(bf16[2048,32]{0,1:T(8,128)(2,1)} %param.11) | copy-start | bytes 393220
  10.7 4.2 %copy-start.5 = (s32[512]{0:T(512)S(1)}, s32[512]{0:T(512)}, u32[]{:S(2)}) copy-start(s32[512]{0:T(512)} %param.13) | copy-start | bytes 6148
  10.7 8.2 %copy-start.9 = (s32[512]{0:T(512)S(1)}, s32[512]{0:T(512)}, u32[]{:S(2)}) copy-start(s32[512]{0:T(512)} %param.14) | copy-start | bytes 6148
  10.7 8.2 %copy-start.6 = (s32[32,1]{0,1:T(1,128)S(1)}, s32[32,1]{0,1:T(1,128)}, u32[]{:S(2)}) copy-start(s32[32,1]{0,1:T(1,128)} %param.15) | copy-start | bytes 388
  11.6 24.6 %collective-permute-start.4 = (f32[512]{0:T(512)}, f32[512]{0:T(512)}, u32[]{:S(2)}, u32[]{:S(2)}) collective-permute-start(f32[512]{0:T(512)} %multiply_reduce_fusion), channel_id=1, source_target_pairs={{0,4},{4,0},{8,12},{12,8},{16,20},{20,16},{24,28},{28,24},{1,5},{5... | collective-permute-start | bytes 6152 | tf_op jit(solution)/shard_map/ppermute | solution.py:89
  12.0 26.9 %collective-permute-start.5 = (f32[512]{0:T(512)}, f32[512]{0:T(512)}, u32[]{:S(2)}, u32[]{:S(2)}) collective-permute-start(f32[512]{0:T(512)} %multiply_reduce_fusion), channel_id=1, source_target_pairs={{0,8},{4,12},{8,0},{12,4},{16,24},{20,28},{24,16},{28,20},{1,9},{5... | collective-permute-start | bytes 6152 | tf_op jit(solution)/shard_map/ppermute | solution.py:89
  14.6 11.0 %collective-permute-start = (bf16[2,2048,32]{1,2,0:T(8,128)(2,1)S(1)}, bf16[2,2048,32]{1,2,0:T(8,128)(2,1)S(1)}, u32[]{:S(2)}, u32[]{:S(2)}) collective-permute-start(bf16[2,2048,32]{1,2,0:T(8,128)(2,1)S(1)} %pad_maximum_fusion.2), channel_id=1, source_target_pairs={{0,4},{4,0},{8,12},{12,8},{16,20},{20,16},{24,28},{28,24},{1,5},{5... | collective-permute-start | bytes 786440 | tf_op jit(solution)/shard_map/ppermute | solution.py:71
  14.9 20.6 %collective-permute-start.11 = (s32[512]{0:T(512)S(1)}, s32[512]{0:T(512)}, u32[]{:S(2)}, u32[]{:S(2)}) collective-permute-start(s32[512]{0:T(512)S(1)} %broadcast_add_fusion), channel_id=1, source_target_pairs={{0,1},{1,2},{2,3},{4,5},{5,6},{6,7},{8,9},{9,10},{10,11},{12,13},{... | collective-permute-start | bytes 6152 | tf_op jit(solution)/shard_map/ppermute | solution.py:19
  27.3 1.2 copy-start.1
  27.6 2.5 %copy-start.7 = (s32[32,1]{0,1:T(1,128)S(1)}, s32[32,1]{0,1:T(1,128)}, u32[]{:S(2)}) copy-start(s32[32,1]{0,1:T(1,128)} %param.15) | copy-start | bytes 388
  27.6 2.5 %copy-start.16 = (s32[32]{0:T(128)S(1)}, s32[32]{0:T(128)}, u32[]{:S(2)}) copy-start(s32[32]{0:T(128)} %select_reduce_fusion.1) | copy-start | bytes 388
  27.6 6.0 %copy-start.15 = (s32[8]{0:T(128)S(1)}, s32[8]{0:T(128)}, u32[]{:S(2)}) copy-start(s32[8]{0:T(128)} %fusion.74) | copy-start | bytes 100
  28.5 6.4 %copy-start.8 = (pred[512]{0:T(512)(128)(4,1)S(1)}, pred[512]{0:T(512)(128)(4,1)}, u32[]{:S(2)}) copy-start(pred[512]{0:T(512)(128)(4,1)} %broadcast_compare_fusion.1) | copy-start | bytes 1540
  30.1 23.3 %copy-start.14 = (pred[8]{0:T(512)(128)(4,1)S(1)}, pred[8]{0:T(512)(128)(4,1)}, u32[]{:S(2)}) copy-start(pred[8]{0:T(512)(128)(4,1)} %compare_and_fusion) | copy-start | bytes 28
  30.1 68.9 %collective-permute-start.3 = (bf16[2048,384]{1,0:T(8,128)(2,1)}, bf16[2048,384]{1,0:T(8,128)(2,1)}, u32[]{:S(2)}, u32[]{:S(2)}) collective-permute-start(bf16[2048,384]{1,0:T(8,128)(2,1)} %pad_maximum_fusion), channel_id=1, source_target_pairs={{0,3},{1,2},{2,1},{3,0},{4,7},{5,6},{6,5},{7,4},{8,11},{9,10},{10,... | collective-permute-start | bytes 4718600 | tf_op jit(solution)/shard_map/ppermute | solution.py:77
  30.6 71.8 %collective-permute-start.1 = (bf16[2048,384]{1,0:T(8,128)(2,1)}, bf16[2048,384]{1,0:T(8,128)(2,1)}, u32[]{:S(2)}, u32[]{:S(2)}) collective-permute-start(bf16[2048,384]{1,0:T(8,128)(2,1)} %pad_maximum_fusion), channel_id=1, source_target_pairs={{0,1},{1,0},{2,3},{3,2},{4,5},{5,4},{6,7},{7,6},{8,9},{9,8},{10,11... | collective-permute-start | bytes 4718600 | tf_op jit(solution)/shard_map/ppermute | solution.py:77
  35.5 3.6 %collective-permute-start.6 = (f32[512]{0:T(512)}, f32[512]{0:T(512)S(1)}, u32[]{:S(2)}, u32[]{:S(2)}) collective-permute-start(f32[512]{0:T(512)} %multiply_reduce_fusion), channel_id=1, source_target_pairs={{0,12},{4,8},{8,4},{12,0},{16,28},{20,24},{24,20},{28,16},{1,13},{... | collective-permute-start | bytes 6152 | tf_op jit(solution)/shard_map/ppermute | solution.py:89
  36.2 4.8 %collective-permute-start.7 = (f32[512]{0:T(512)}, f32[512]{0:T(512)S(1)}, u32[]{:S(2)}, u32[]{:S(2)}) collective-permute-start(f32[512]{0:T(512)} %multiply_reduce_fusion), channel_id=1, source_target_pairs={{0,16},{4,20},{8,24},{12,28},{16,0},{20,4},{24,8},{28,12},{1,17},{... | collective-permute-start | bytes 6152 | tf_op jit(solution)/shard_map/ppermute | solution.py:89
  38.9 8.0 %collective-permute-start.8 = (f32[512]{0:T(512)}, f32[512]{0:T(512)S(1)}, u32[]{:S(2)}, u32[]{:S(2)}) collective-permute-start(f32[512]{0:T(512)} %multiply_reduce_fusion), channel_id=1, source_target_pairs={{0,20},{4,16},{8,28},{12,24},{16,4},{20,0},{24,12},{28,8},{1,21},{... | collective-permute-start | bytes 6152 | tf_op jit(solution)/shard_map/ppermute | solution.py:89
  39.1 65.7 %collective-permute-start.2 = (bf16[2048,384]{1,0:T(8,128)(2,1)}, bf16[2048,384]{1,0:T(8,128)(2,1)}, u32[]{:S(2)}, u32[]{:S(2)}) collective-permute-start(bf16[2048,384]{1,0:T(8,128)(2,1)} %pad_maximum_fusion), channel_id=1, source_target_pairs={{0,2},{1,3},{2,0},{3,1},{4,6},{5,7},{6,4},{7,5},{8,10},{9,11},{10,... | collective-permute-start | bytes 4718600 | tf_op jit(solution)/shard_map/ppermute | solution.py:77
  41.0 7.7 %collective-permute-start.9 = (f32[512]{0:T(512)}, f32[512]{0:T(512)S(1)}, u32[]{:S(2)}, u32[]{:S(2)}) collective-permute-start(f32[512]{0:T(512)} %multiply_reduce_fusion), channel_id=1, source_target_pairs={{0,24},{4,28},{8,16},{12,20},{16,8},{20,12},{24,0},{28,4},{1,25},{... | collective-permute-start | bytes 6152 | tf_op jit(solution)/shard_map/ppermute | solution.py:89
  46.9 5.1 %collective-permute-start.10 = (f32[512]{0:T(512)}, f32[512]{0:T(512)S(1)}, u32[]{:S(2)}, u32[]{:S(2)}) collective-permute-start(f32[512]{0:T(512)} %multiply_reduce_fusion), channel_id=1, source_target_pairs={{0,28},{4,24},{8,20},{12,16},{16,12},{20,8},{24,4},{28,0},{1,29},{... | collective-permute-start | bytes 6152 | tf_op jit(solution)/shard_map/ppermute | solution.py:89
  95.9 6.4 %copy-start.17 = (bf16[4096,1024]{1,0:T(8,128)(2,1)S(1)}, bf16[4096,1024]{1,0:T(8,128)(2,1)}, u32[]{:S(2)}) copy-start(bf16[4096,1024]{1,0:T(8,128)(2,1)} %all-gather.3.cloned.1.call-done) | copy-start | bytes 25165828
  104.8 2.6 %copy-start.2 = (f32[512,64]{0,1:T(8,128)S(1)}, f32[512,64]{0,1:T(8,128)}, u32[]{:S(2)}) copy-start(f32[512,64]{0,1:T(8,128)} %get-tuple-element.13) | copy-start | bytes 393220
  104.8 2.6 %copy-start.12 = (pred[64]{0:T(512)(128)(4,1)S(1)}, pred[64]{0:T(512)(128)(4,1)}, u32[]{:S(2)}) copy-start(pred[64]{0:T(512)(128)(4,1)} %fusion.72) | copy-start | bytes 196
  107.4 17.0 %copy-start.13 = (s32[32]{0:T(128)S(1)}, s32[32]{0:T(128)}, u32[]{:S(2)}) copy-start(s32[32]{0:T(128)} %fusion.73) | copy-start | bytes 388
  107.5 26.8 %copy-start.11 = (pred[256]{0:T(512)(128)(4,1)S(1)}, pred[256]{0:T(512)(128)(4,1)}, u32[]{:S(2)}) copy-start(pred[256]{0:T(512)(128)(4,1)} %fusion.71) | copy-start | bytes 772
  108.2 27.4 %collective-permute-start.14 = (bf16[2,512,64]{1,2,0:T(8,128)(2,1)}, bf16[2,512,64]{1,2,0:T(8,128)(2,1)}, u32[]{:S(2)}, u32[]{:S(2)}) collective-permute-start(bf16[2,512,64]{1,2,0:T(8,128)(2,1)} %pad_maximum_fusion.3), channel_id=1, source_target_pairs={{0,8},{4,12},{8,0},{12,4},{16,24},{20,28},{24,16},{28,20},{1,9},{5... | collective-permute-start | bytes 393224 | tf_op jit(solution)/shard_map/ppermute | solution.py:127
  108.2 28.4 %collective-permute-start.12 = (bf16[2,512,64]{1,2,0:T(8,128)(2,1)}, bf16[2,512,64]{1,2,0:T(8,128)(2,1)}, u32[]{:S(2)}, u32[]{:S(2)}) collective-permute-start(bf16[2,512,64]{1,2,0:T(8,128)(2,1)} %pad_maximum_fusion.3), channel_id=1, source_target_pairs={{0,1},{1,2},{2,3},{4,5},{5,6},{6,7},{8,9},{9,10},{10,11},{12,13},{... | collective-permute-start | bytes 393224 | tf_op jit(solution)/shard_map/ppermute | solution.py:19
  112.4 24.3 %collective-permute-start.13 = (bf16[2,512,64]{1,2,0:T(8,128)(2,1)}, bf16[2,512,64]{1,2,0:T(8,128)(2,1)}, u32[]{:S(2)}, u32[]{:S(2)}) collective-permute-start(bf16[2,512,64]{1,2,0:T(8,128)(2,1)} %pad_maximum_fusion.3), channel_id=1, source_target_pairs={{0,9},{1,10},{2,11},{4,13},{5,14},{6,15},{8,1},{9,2},{10,3},{12,5}... | collective-permute-start | bytes 393224 | tf_op jit(solution)/shard_map/ppermute | solution.py:136
  130.4 11.6 %all-to-all-start = ((bf16[4,16,2,512]{3,1,2,0:T(8,128)(2,1)}), bf16[4,16,2,512]{3,1,2,0:T(8,128)(2,1)}, u32[]{:S(2)}, u32[]{:S(2)}) async-start(bf16[4,16,2,512]{3,1,2,0:T(8,128)(2,1)} %copy.49), calls=%async_computation | async-start | bytes 262144 | tf_op jit(solution)/shard_map/all_to_all | solution.py:193
  139.3 1.3 copy-start.10
Sparse Core Ops, SparseCore 0:
  10.9 84.9 all-gather.2

commit v21 on v17

--- a/solution.py
+++ b/solution.py
@@ -95,6 +95,7 @@
     for shift_by in range(1, span_count + 1):
         mark_list.insert(0, shifted(marks, "gy", shift_by))
     scaling = 1.0 / jnp.sqrt(squares / D + EPSILON)
+    scaling = lax.optimization_barrier(scaling)
     query_cols = head_local * HD
     halves = 1
     half_rows = token_count // halves

time: 137 us -> 137 us (level)
    ppermute x2, waiting for transfers between devices: 0.01 us -> 55.6 us  [shifted(): return lax.ppermute(value, axis, pairs)]
    all_gather x1, waiting for transfers between devices: 52 us -> 0.35 us  [shards(): normed = lax.all_gather(local_normed[rows_of], 'gx', axis=0, tiled=False)]
    ppermute x7, waiting for transfers between devices: 4.01 us -> 0.02 us  [shards(): lax.ppermute(local_squares, 'gx', partner_route(gx_count, gx_count, k))]
    ppermute x1, starting transfers between devices: 4.89 us -> 3.32 us  [shards(): other = lax.ppermute(half_kv, ('gx', 'gy'), route)]
  transfers between devices with their start and end apart: 17 -> 17, of which waited for: 6 -> 3; matrix products, arithmetic and copies ran while one was open for 20% -> 20% of each run, Pallas kernels for 0% -> 0%
where the time goes in v21:
time: 137 us
  waiting for transfers between devices  56.6 us (41%)
  starting transfers between devices  29.7 us (22%)
  between operations  14.6 us (11%)
  matrix products  13.5 us (10%)
  other arithmetic  13.3 us (10%)
  local copies, waits for them, and re-layouts  9.46 us (7%)
    ppermute x2, waiting for transfers between devices, shifted(): return lax.ppermute(value, axis, pairs)  55.6 us
    dot_general x4, matrix products, shards(): jnp.einsum('btd,bdc->tc', rows, weights_of, preferred_element_type=jnp.fl...  11.1 us
    ppermute x7, starting transfers between devices, shards(): lax.ppermute(local_squares, 'gx', partner_route(gx_count, gx_count, k))  9.89 us
    ppermute x2, starting transfers between devices, shifted(): return lax.ppermute(value, axis, pairs)  7.72 us
    ppermute x3, starting transfers between devices, shards(): lax.ppermute(local_weights, 'gy', partner_route(gy_count, gy_count, k))  3.85 us
    sin x2, other arithmetic, rope_tables(): return lax.optimization_barrier((jnp.cos(angles), jnp.sin(angles)))  3.34 us
    all_to_all x1, starting transfers between devices, shards(): lax.all_to_all(send_kv, 'gy', split_axis=0, concat_axis=0, tiled=True)  3.33 us
    ppermute x1, starting transfers between devices, shards(): other = lax.ppermute(half_kv, ('gx', 'gy'), route)  3.32 us
  transfers between devices with their start and end apart: 17, of which 3 were waited for; matrix products, arithmetic and copies ran while one was open for 20% of the time, Pallas kernels for 0%

profile of v21, /device:TPU:0, one launch (start us, length us, event | category | flops | bytes accessed | tf_op | source)
XLA Modules:
  0.0 137.1 jit_solution(17920469244192933076)
XLA Ops:
  7.2 1.5 %convert_element_type.53 = f32[512,1024]{1,0:T(8,128)S(1)} convert(bf16[512,1024]{1,0:T(8,128)(2,1)} %param.8) | non-fusion elementwise | flops 524288 | bytes 3145728 | tf_op jit(solution)/shard_map/convert_element_type | solution.py:80
  8.8 0.8 dynamic-slice_convert_fusion
  9.6 1.2 multiply_convert_fusion
  10.9 0.2 multiply_reduce_fusion
  11.1 0.5 collective-permute-start.4
  11.6 2.6 %collective-permute-start.5 = (f32[512]{0:T(512)S(1)}, f32[512]{0:T(512)S(1)}, u32[]{:S(2)}, u32[]{:S(2)}) collective-permute-start(f32[512]{0:T(512)S(1)} %multiply_reduce_fusion), channel_id=1, source_target_pairs={{0,8},{4,12},{8,0},{12,4},{16,24},{20,28},{24,16},{28,20},{1,9},{5... | collective-permute-start | bytes 6152 | tf_op jit(solution)/shard_map/ppermute | solution.py:89
  14.4 0.2 collective-permute-start
  15.0 0.5 multiply_sine_fusion.1
  15.6 0.5 copy.32
  16.1 2.8 %multiply_sine_fusion = (f32[512,256]{0,1:T(8,128)}, f32[512,256]{0,1:T(8,128)}) fusion(f32[256]{0:T(256)S(1)} %multiply_power_fusion, f32[512]{0:T(512)S(1)} %convert_element_type.56), kind=kLoop, calls=%fused_computation.42 | loop fusion | flops 131072 | bytes 1051648 | tf_op jit(solution)/shard_map/sin | solution.py:35
  18.9 0.5 copy.33
  19.4 1.2 maximum_select_fusion
  20.5 0.3 fusion.90
  20.8 1.5 %pad_maximum_fusion = bf16[2048,384]{1,0:T(8,128)(2,1)} fusion(bf16[2048,64]{1,0:T(8,128)(2,1)S(1)} %get-tuple-element.27, bf16[2048,64]{1,0:T(8,128)(2,1)S(1)} %get-tuple-element.26, bf16[2048,256]{1,0:T(8,128)(2,1)S(1)} %copy-done.1), kind=kLoop, calls=%fused_computation.29 | loop fusion | flops 4718592 | bytes 3145728 | tf_op jit(solution)/shard_map/concatenate | solution.py:73
  22.4 2.8 %collective-permute-start.3 = (bf16[2048,384]{1,0:T(8,128)(2,1)}, bf16[2048,384]{1,0:T(8,128)(2,1)}, u32[]{:S(2)}, u32[]{:S(2)}) collective-permute-start(bf16[2048,384]{1,0:T(8,128)(2,1)} %pad_maximum_fusion), channel_id=1, source_target_pairs={{0,3},{1,2},{2,1},{3,0},{4,7},{5,6},{6,5},{7,4},{8,11},{9,10},{10,... | collective-permute-start | bytes 4718600 | tf_op jit(solution)/shard_map/ppermute | solution.py:77
  25.2 0.5 collective-permute-start.1
  25.7 2.6 %collective-permute-start.7 = (f32[512]{0:T(512)S(1)}, f32[512]{0:T(512)S(1)}, u32[]{:S(2)}, u32[]{:S(2)}) collective-permute-start(f32[512]{0:T(512)S(1)} %multiply_reduce_fusion), channel_id=1, source_target_pairs={{0,16},{4,20},{8,24},{12,28},{16,0},{20,4},{24,8},{28,12},{1,17},{... | collective-permute-start | bytes 6152 | tf_op jit(solution)/shard_map/ppermute | solution.py:89
  28.5 2.8 %collective-permute-start.9 = (f32[512]{0:T(512)S(1)}, f32[512]{0:T(512)S(1)}, u32[]{:S(2)}, u32[]{:S(2)}) collective-permute-start(f32[512]{0:T(512)S(1)} %multiply_reduce_fusion), channel_id=1, source_target_pairs={{0,24},{4,28},{8,16},{12,20},{16,8},{20,12},{24,0},{28,4},{1,25},{... | collective-permute-start | bytes 6152 | tf_op jit(solution)/shard_map/ppermute | solution.py:89
  31.3 1.1 collective-permute-start.10
  32.4 0.5 copy.38
  33.0 3.3 %collective-permute-start.11 = (s32[512]{0:T(512)S(1)}, s32[512]{0:T(512)S(1)}, u32[]{:S(2)}, u32[]{:S(2)}) collective-permute-start(s32[512]{0:T(512)S(1)} %broadcast_add_fusion), channel_id=1, source_target_pairs={{0,1},{1,2},{2,3},{4,5},{5,6},{6,7},{8,9},{9,10},{10,11},{12,13},{... | collective-permute-start | bytes 6152 | tf_op jit(solution)/shard_map/ppermute | solution.py:19
  36.4 0.6 gather_fusion
  37.1 0.5 collective-permute-start.2
  37.6 55.6 %collective-permute-done.11 = s32[512]{0:T(512)S(1)} collective-permute-done((s32[512]{0:T(512)S(1)}, s32[512]{0:T(512)S(1)}, u32[]{:S(2)}, u32[]{:S(2)}) %collective-permute-start.11) | collective-permute-done | bytes 2080 | tf_op jit(solution)/shard_map/ppermute | solution.py:19
  93.2 1.4 %fusion = pred[1024,1024]{0,1:T(32,128)(4,1)S(1)} fusion(s32[1024]{0:T(1024)S(1)} %bitcast.129, s32[1024]{0:T(1024)S(1)} %bitcast.128, s32[1024]{0:T(1024)S(1)} %pad_add_fusion, pred[1024]{0:T(1024)(128)(4,1)S(1)} %broadcast_compare_fusion), kind=kLoop, calls=%fused_computation.5 | loop fusion | flops 4194304 | bytes 1061888 | tf_op jit(solution)/shard_map/and | solution.py:162
  94.7 0.9 copy.39
  95.6 0.2 copy.40
  95.8 0.4 all-gather.3.cloned.1.call-done
  96.1 2.7 %fusion.23 = f32[512,384]{0,1:T(8,128)S(1)} fusion(bf16[2,1024,64]{1,2,0:T(8,128)(2,1)S(1)} %copy.40, bf16[2,1024,64]{1,2,0:T(8,128)(2,1)} %copy.39, bf16[2,1024,256]{1,2,0:T(8,128)(2,1)S(1)} %copy.38, bf16[4,2,512,1024]{3,2,1,0:T(8,128)(2,1)} %bitcast.140, s32[]{:T(128)S(6)} %select_n.158), kind=kOutput, calls=%fused_computation.30 | convolution fusion | flops 810024960 | bytes 4456452 | tf_op jit(solution)/shard_map/btd,bdc->tc/dot_general | solution.py:114
  98.9 3.4 %fusion.34 = f32[512,384]{0,1:T(8,128)S(1)} fusion(bf16[2,1024,384]{2,1,0:T(8,128)(2,1)} %bitcast.20, bf16[4,2,512,1024]{3,2,1,0:T(8,128)(2,1)} %bitcast.141, s32[]{:T(128)S(6)} %select_n.165), kind=kOutput, calls=%fused_computation.33 | convolution fusion | flops 805306368 | bytes 4456452 | tf_op jit(solution)/shard_map/btd,bdc->tc/dot_general | solution.py:114
  102.3 2.5 %fusion.40 = f32[512,384]{0,1:T(8,128)S(1)} fusion(f32[512,384]{0,1:T(8,128)S(1)} %fusion.23, bf16[2,1024,384]{2,1,0:T(8,128)(2,1)} %bitcast.14, bf16[4,2,512,1024]{3,2,1,0:T(8,128)(2,1)S(1)} %bitcast.142, s32[]{:T(128)S(6)} %select_n.163), kind=kOutput, calls=%fused_computation.35 | convolution fusion | flops 805502976 | bytes 5242884 | tf_op jit(solution)/shard_map/btd,bdc->tc/dot_general | solution.py:114
  104.8 2.5 %fusion.46 = f32[512,384]{0,1:T(8,128)S(1)} fusion(f32[512,384]{0,1:T(8,128)S(1)} %fusion.34, f32[512,384]{0,1:T(8,128)S(1)} %fusion.40, bf16[2,1024,384]{2,1,0:T(8,128)(2,1)} %bitcast.17, bf16[4,2,512,1024]{3,2,1,0:T(8,128)(2,1)S(1)} %bitcast.143, s32[]{:T(128)S(6)} %select_n.164, f32[512]{0:T(512)S(1)} %add_rsqrt_fusion), kind=kOutput, calls=%fused_computation.37 | convolution fusion | flops 805896192 | bytes 6031364 | tf_op jit(solution)/shard_map/btd,bdc->tc/dot_general | solution.py:114
  107.5 1.3 collective-permute-start.14
  108.8 4.4 %collective-permute-start.12 = (bf16[2,512,64]{1,2,0:T(8,128)(2,1)S(1)}, bf16[2,512,64]{1,2,0:T(8,128)(2,1)S(1)}, u32[]{:S(2)}, u32[]{:S(2)}) collective-permute-start(bf16[2,512,64]{1,2,0:T(8,128)(2,1)S(1)} %pad_maximum_fusion.3), channel_id=1, source_target_pairs={{0,1},{1,2},{2,3},{4,5},{5,6},{6,7},{8,9},{9,10},{10,11},{12,13},{... | collective-permute-start | bytes 393224 | tf_op jit(solution)/shard_map/ppermute | solution.py:19
  113.2 3.3 %collective-permute-start.13 = (bf16[2,512,64]{1,2,0:T(8,128)(2,1)S(1)}, bf16[2,512,64]{1,2,0:T(8,128)(2,1)S(1)}, u32[]{:S(2)}, u32[]{:S(2)}) collective-permute-start(bf16[2,512,64]{1,2,0:T(8,128)(2,1)S(1)} %pad_maximum_fusion.3), channel_id=1, source_target_pairs={{0,9},{1,10},{2,11},{4,13},{5,14},{6,15},{8,1},{9,2},{10,3},{12,5}... | collective-permute-start | bytes 393224 | tf_op jit(solution)/shard_map/ppermute | solution.py:137
  116.6 0.2 fusion.60
  117.2 0.2 reshape.196
  117.6 1.5 %scatter_fusion = bf16[64,2,512]{2,1,0:T(2,128)(2,1)S(1)} fusion(bf16[64,2,512]{2,1,0:T(2,128)(2,1)S(1)} %broadcast_in_dim.44, s32[32]{0:T(128)S(1)} %fusion.83, bf16[32,2,512]{2,1,0:T(2,128)(2,1)S(1)} %copy.45), kind=kCustom, calls=%fused_computation.1 | custom fusion | bytes 196736 | tf_op jit(solution)/shard_map/scatter | solution.py:192
  119.1 0.7 copy.46
  119.8 3.3 %all-to-all-start = ((bf16[4,16,2,512]{3,1,2,0:T(8,128)(2,1)}), bf16[4,16,2,512]{3,1,2,0:T(8,128)(2,1)S(1)}, u32[]{:S(2)}, u32[]{:S(2)}) async-start(bf16[4,16,2,512]{3,1,2,0:T(8,128)(2,1)} %copy.46), calls=%async_computation | async-start | bytes 262144 | tf_op jit(solution)/shard_map/all_to_all | solution.py:195
  123.3 1.0 fusion.3
  124.2 1.1 fusion.1
  125.3 1.4 %fusion.55 = bf16[1024,128]{1,0:T(8,128)(2,1)S(1)} fusion(pred[1024,1024]{0,1:T(32,128)(4,1)S(1)} %fusion, f32[1024,1024]{0,1:T(8,128)S(1)} %get-tuple-element.44, f32[1024]{0:T(1024)S(1)} %get-tuple-element.43, bf16[2,512,128]{1,2,0:T(8,128)(2,1)S(1)} %maximum_select_fusion.2, bf16[2,512,128]{1,2,0:T(8,128)(2,1)S(1)} %maximum_select_fusion.1, ...), kind=kOutput, calls=%fused_computation.41 | convolution fusion | flops 273547264 | bytes 6038528 | tf_op jit(solution)/shard_map/dot_general | solution.py:169
  126.8 0.7 copy.63
  127.5 0.6 all-to-all-done
  128.1 0.3 reshape.200
  128.4 0.9 copy.50
  129.4 0.9 copy.51
  (79 shorter events, 1.8 us)
Async XLA Ops:
  7.2 2.5 %copy-start = (bf16[512,1024]{1,0:T(8,128)(2,1)S(1)}, bf16[512,1024]{1,0:T(8,128)(2,1)}, u32[]{:S(2)}) copy-start(bf16[512,1024]{1,0:T(8,128)(2,1)} %param.8) | copy-start | bytes 3145732
  7.2 89.0 %all-gather.3.cloned.1.call-start = ((), (), s32[]{:S(2)}) async-start(), calls=%async_computation.1 | async-start | bytes 9437184 | tf_op jit(solution)/shard_map/all_gather | solution.py:105
  8.8 5.6 %copy-start.4 = (bf16[2048,32]{0,1:T(8,128)(2,1)S(1)}, bf16[2048,32]{0,1:T(8,128)(2,1)}, u32[]{:S(2)}) copy-start(bf16[2048,32]{0,1:T(8,128)(2,1)} %param.12) | copy-start | bytes 393220
  8.8 5.6 %copy-start.5 = (bf16[2048,32]{0,1:T(8,128)(2,1)S(1)}, bf16[2048,32]{0,1:T(8,128)(2,1)}, u32[]{:S(2)}) copy-start(bf16[2048,32]{0,1:T(8,128)(2,1)} %param.11) | copy-start | bytes 393220
  8.8 5.8 %copy-start.8 = (s32[512]{0:T(512)S(1)}, s32[512]{0:T(512)}, u32[]{:S(2)}) copy-start(s32[512]{0:T(512)} %param.14) | copy-start | bytes 6148
  8.8 5.8 %copy-start.7 = (s32[32,1]{0,1:T(1,128)S(1)}, s32[32,1]{0,1:T(1,128)}, u32[]{:S(2)}) copy-start(s32[32,1]{0,1:T(1,128)} %param.15) | copy-start | bytes 388
  8.8 6.2 %copy-start.6 = (s32[512]{0:T(512)S(1)}, s32[512]{0:T(512)}, u32[]{:S(2)}) copy-start(s32[512]{0:T(512)} %param.13) | copy-start | bytes 6148
  11.1 14.6 %collective-permute-start.4 = (f32[512]{0:T(512)S(1)}, f32[512]{0:T(512)S(1)}, u32[]{:S(2)}, u32[]{:S(2)}) collective-permute-start(f32[512]{0:T(512)S(1)} %multiply_reduce_fusion), channel_id=1, source_target_pairs={{0,4},{4,0},{8,12},{12,8},{16,20},{20,16},{24,28},{28,24},{1,5},{5... | collective-permute-start | bytes 6152 | tf_op jit(solution)/shard_map/ppermute | solution.py:89
  11.6 16.8 %collective-permute-start.5 = (f32[512]{0:T(512)S(1)}, f32[512]{0:T(512)S(1)}, u32[]{:S(2)}, u32[]{:S(2)}) collective-permute-start(f32[512]{0:T(512)S(1)} %multiply_reduce_fusion), channel_id=1, source_target_pairs={{0,8},{4,12},{8,0},{12,4},{16,24},{20,28},{24,16},{28,20},{1,9},{5... | collective-permute-start | bytes 6152 | tf_op jit(solution)/shard_map/ppermute | solution.py:89
  14.3 14.2 %collective-permute-start.6 = (f32[512]{0:T(512)S(1)}, f32[512]{0:T(512)S(1)}, u32[]{:S(2)}, u32[]{:S(2)}) collective-permute-start(f32[512]{0:T(512)S(1)} %multiply_reduce_fusion), channel_id=1, source_target_pairs={{0,12},{4,8},{8,4},{12,0},{16,28},{20,24},{24,20},{28,16},{1,13},{... | collective-permute-start | bytes 6152 | tf_op jit(solution)/shard_map/ppermute | solution.py:89
  14.4 4.5 %collective-permute-start = (bf16[2,2048,32]{1,2,0:T(8,128)(2,1)S(1)}, bf16[2,2048,32]{1,2,0:T(8,128)(2,1)S(1)}, u32[]{:S(2)}, u32[]{:S(2)}) collective-permute-start(bf16[2,2048,32]{1,2,0:T(8,128)(2,1)S(1)} %pad_maximum_fusion.2), channel_id=1, source_target_pairs={{0,4},{4,0},{8,12},{12,8},{16,20},{20,16},{24,28},{28,24},{1,5},{5... | collective-permute-start | bytes 786440 | tf_op jit(solution)/shard_map/ppermute | solution.py:71
  19.4 1.5 %copy-start.1 = (bf16[2048,256]{1,0:T(8,128)(2,1)S(1)}, bf16[2048,256]{1,0:T(8,128)(2,1)}, u32[]{:S(2)}) copy-start(bf16[2048,256]{1,0:T(8,128)(2,1)} %param.10) | copy-start | bytes 3145732
  22.4 76.5 %collective-permute-start.3 = (bf16[2048,384]{1,0:T(8,128)(2,1)}, bf16[2048,384]{1,0:T(8,128)(2,1)}, u32[]{:S(2)}, u32[]{:S(2)}) collective-permute-start(bf16[2048,384]{1,0:T(8,128)(2,1)} %pad_maximum_fusion), channel_id=1, source_target_pairs={{0,3},{1,2},{2,1},{3,0},{4,7},{5,6},{6,5},{7,4},{8,11},{9,10},{10,... | collective-permute-start | bytes 4718600 | tf_op jit(solution)/shard_map/ppermute | solution.py:77
  25.2 77.1 %collective-permute-start.1 = (bf16[2048,384]{1,0:T(8,128)(2,1)}, bf16[2048,384]{1,0:T(8,128)(2,1)}, u32[]{:S(2)}, u32[]{:S(2)}) collective-permute-start(bf16[2048,384]{1,0:T(8,128)(2,1)} %pad_maximum_fusion), channel_id=1, source_target_pairs={{0,1},{1,0},{2,3},{3,2},{4,5},{5,4},{6,7},{7,6},{8,9},{9,8},{10,11... | collective-permute-start | bytes 4718600 | tf_op jit(solution)/shard_map/ppermute | solution.py:77
  25.7 5.6 %collective-permute-start.7 = (f32[512]{0:T(512)S(1)}, f32[512]{0:T(512)S(1)}, u32[]{:S(2)}, u32[]{:S(2)}) collective-permute-start(f32[512]{0:T(512)S(1)} %multiply_reduce_fusion), channel_id=1, source_target_pairs={{0,16},{4,20},{8,24},{12,28},{16,0},{20,4},{24,8},{28,12},{1,17},{... | collective-permute-start | bytes 6152 | tf_op jit(solution)/shard_map/ppermute | solution.py:89
  28.4 4.7 %collective-permute-start.8 = (f32[512]{0:T(512)S(1)}, f32[512]{0:T(512)S(1)}, u32[]{:S(2)}, u32[]{:S(2)}) collective-permute-start(f32[512]{0:T(512)S(1)} %multiply_reduce_fusion), channel_id=1, source_target_pairs={{0,20},{4,16},{8,28},{12,24},{16,4},{20,0},{24,12},{28,8},{1,21},{... | collective-permute-start | bytes 6152 | tf_op jit(solution)/shard_map/ppermute | solution.py:89
  28.5 7.9 %collective-permute-start.9 = (f32[512]{0:T(512)S(1)}, f32[512]{0:T(512)S(1)}, u32[]{:S(2)}, u32[]{:S(2)}) collective-permute-start(f32[512]{0:T(512)S(1)} %multiply_reduce_fusion), channel_id=1, source_target_pairs={{0,24},{4,28},{8,16},{12,20},{16,8},{20,12},{24,0},{28,4},{1,25},{... | collective-permute-start | bytes 6152 | tf_op jit(solution)/shard_map/ppermute | solution.py:89
  31.3 5.1 %collective-permute-start.10 = (f32[512]{0:T(512)S(1)}, f32[512]{0:T(512)S(1)}, u32[]{:S(2)}, u32[]{:S(2)}) collective-permute-start(f32[512]{0:T(512)S(1)} %multiply_reduce_fusion), channel_id=1, source_target_pairs={{0,28},{4,24},{8,20},{12,16},{16,12},{20,8},{24,4},{28,0},{1,29},{... | collective-permute-start | bytes 6152 | tf_op jit(solution)/shard_map/ppermute | solution.py:89
  33.0 60.2 %collective-permute-start.11 = (s32[512]{0:T(512)S(1)}, s32[512]{0:T(512)S(1)}, u32[]{:S(2)}, u32[]{:S(2)}) collective-permute-start(s32[512]{0:T(512)S(1)} %broadcast_add_fusion), channel_id=1, source_target_pairs={{0,1},{1,2},{2,3},{4,5},{5,6},{6,7},{8,9},{9,10},{10,11},{12,13},{... | collective-permute-start | bytes 6152 | tf_op jit(solution)/shard_map/ppermute | solution.py:19
  37.1 67.7 %collective-permute-start.2 = (bf16[2048,384]{1,0:T(8,128)(2,1)}, bf16[2048,384]{1,0:T(8,128)(2,1)}, u32[]{:S(2)}, u32[]{:S(2)}) collective-permute-start(bf16[2048,384]{1,0:T(8,128)(2,1)} %pad_maximum_fusion), channel_id=1, source_target_pairs={{0,2},{1,3},{2,0},{3,1},{4,6},{5,7},{6,4},{7,5},{8,10},{9,11},{10,... | collective-permute-start | bytes 4718600 | tf_op jit(solution)/shard_map/ppermute | solution.py:77
  96.1 6.2 %copy-start.9 = (bf16[4096,1024]{1,0:T(8,128)(2,1)S(1)}, bf16[4096,1024]{1,0:T(8,128)(2,1)}, u32[]{:S(2)}) copy-start(bf16[4096,1024]{1,0:T(8,128)(2,1)} %all-gather.3.cloned.1.call-done) | copy-start | bytes 25165828
  107.3 9.3 %copy-start.2 = (f32[512,256]{0,1:T(8,128)S(1)}, f32[512,256]{0,1:T(8,128)}, u32[]{:S(2)}) copy-start(f32[512,256]{0,1:T(8,128)} %get-tuple-element.16) | copy-start | bytes 1572868
  107.3 9.3 %copy-start.3 = (f32[512,256]{0,1:T(8,128)S(1)}, f32[512,256]{0,1:T(8,128)}, u32[]{:S(2)}) copy-start(f32[512,256]{0,1:T(8,128)} %get-tuple-element.15) | copy-start | bytes 1572868
  107.5 15.6 %collective-permute-start.14 = (bf16[2,512,64]{1,2,0:T(8,128)(2,1)S(1)}, bf16[2,512,64]{1,2,0:T(8,128)(2,1)S(1)}, u32[]{:S(2)}, u32[]{:S(2)}) collective-permute-start(bf16[2,512,64]{1,2,0:T(8,128)(2,1)S(1)} %pad_maximum_fusion.3), channel_id=1, source_target_pairs={{0,8},{4,12},{8,0},{12,4},{16,24},{20,28},{24,16},{28,20},{1,9},{5... | collective-permute-start | bytes 393224 | tf_op jit(solution)/shard_map/ppermute | solution.py:128
  108.8 14.4 %collective-permute-start.12 = (bf16[2,512,64]{1,2,0:T(8,128)(2,1)S(1)}, bf16[2,512,64]{1,2,0:T(8,128)(2,1)S(1)}, u32[]{:S(2)}, u32[]{:S(2)}) collective-permute-start(bf16[2,512,64]{1,2,0:T(8,128)(2,1)S(1)} %pad_maximum_fusion.3), channel_id=1, source_target_pairs={{0,1},{1,2},{2,3},{4,5},{5,6},{6,7},{8,9},{9,10},{10,11},{12,13},{... | collective-permute-start | bytes 393224 | tf_op jit(solution)/shard_map/ppermute | solution.py:19
  113.2 10.0 %collective-permute-start.13 = (bf16[2,512,64]{1,2,0:T(8,128)(2,1)S(1)}, bf16[2,512,64]{1,2,0:T(8,128)(2,1)S(1)}, u32[]{:S(2)}, u32[]{:S(2)}) collective-permute-start(bf16[2,512,64]{1,2,0:T(8,128)(2,1)S(1)} %pad_maximum_fusion.3), channel_id=1, source_target_pairs={{0,9},{1,10},{2,11},{4,13},{5,14},{6,15},{8,1},{9,2},{10,3},{12,5}... | collective-permute-start | bytes 393224 | tf_op jit(solution)/shard_map/ppermute | solution.py:137
  119.8 8.3 %all-to-all-start = ((bf16[4,16,2,512]{3,1,2,0:T(8,128)(2,1)}), bf16[4,16,2,512]{3,1,2,0:T(8,128)(2,1)S(1)}, u32[]{:S(2)}, u32[]{:S(2)}) async-start(bf16[4,16,2,512]{3,1,2,0:T(8,128)(2,1)} %copy.46), calls=%async_computation | async-start | bytes 262144 | tf_op jit(solution)/shard_map/all_to_all | solution.py:195
Sparse Core Ops, SparseCore 0:
  11.0 85.0 all-gather.2
